TPU v7x, 128 devices: a whole 4x4x4 slice. The times are simulated.
128 devices in a mesh: lon: 16 (over y, x_hi, core), lat: 8 (over x_lo, z).
Axes of the slice: x: 4 (x_hi: 2, x_lo: 2; x = x_hi * 2 + x_lo), y: 4, z: 4, core: 2. Of those that a mesh axis runs over, the one named last changes fastest.
Arguments:
- anomalies: bfloat16 [16, 128, 80, 128], P('lat', 'lon'), may hold values from -6 to 6
- panel: float32 [16, 128, 128, 128], P('lat', 'lon'), may hold values from -6 to 6
- pair_code: int32 [16, 128, 9], P('lat', 'lon'), may hold values from 0 to 8, as said below
- pair_offset: int32 [2, 16, 128, 9], P(None, 'lat', 'lon'), may hold values from -16 to 16, as said below
Outputs:
- first_product: float32 [16, 128, 128, 128], P('lat', 'lon')
- second_product: float32 [16, 128, 128, 128], P('lat', 'lon')
Inputs may be any that keep to these rules, and one draw needn't show every extreme that they name: `pair_code`: slot 0 of every block holds code 4, the block itself; its other slots hold the eight neighbouring blocks' codes, each once. `pair_offset`: for code g the offsets are exactly (g // 3 - 1) * 8 and (g % 3 - 1) * 16.
All inputs are finite; a program needn't handle non-finite values.
Results may differ from a plain program's by a relative error of at most 0.0003.
Values may be sent and summed in bfloat16 or wider, within the bound.
No kernel may reach another device: no remote copies, remote signals or barrier semaphores. Data moves between devices by JAX's collectives and lax.ppermute only.
A program may use at most 128 MiB of HBM per device.

v0:
```python
import jax
import jax.numpy as jnp
from jax import lax
from jax.sharding import PartitionSpec as P

K = 80
COLS = 128
STRIDE = 16
RADIUS = 4


def with_halo(cells, sides, width, closed):
    for axis, dim in sides:
        count = lax.axis_size(axis)
        ends = count if closed else count - 1
        head = lax.slice_in_dim(cells, 0, width, axis=dim)
        tail = lax.slice_in_dim(cells, cells.shape[dim] - width, cells.shape[dim], axis=dim)
        cells = jnp.concatenate(
            [
                lax.ppermute(tail, axis, [(i, (i + 1) % count) for i in range(ends)]),
                cells,
                lax.ppermute(head, axis, [((i + 1) % count, i) for i in range(ends)]),
            ],
            axis=dim,
        )
    return cells


def gaspari_cohn(shift_rows, shift_cols):
    position = jnp.arange(COLS)
    row_within = position // STRIDE
    col_within = position % STRIDE
    delta_rows = shift_rows[..., None, None] + (row_within[None, :] - row_within[:, None])
    delta_cols = shift_cols[..., None, None] + (col_within[None, :] - col_within[:, None])
    squared = (delta_rows * delta_rows + delta_cols * delta_cols).astype(jnp.float32)
    scaled = jnp.sqrt(squared + 0.25) / RADIUS
    inside = (
        ((-0.25 * scaled + 0.5) * scaled + 0.625) * scaled - 5.0 / 3.0
    ) * scaled * scaled + 1.0
    outside = (
        ((((scaled / 12.0 - 0.5) * scaled + 0.625) * scaled + 5.0 / 3.0) * scaled - 5.0) * scaled
        + 4.0
        - 2.0 / (3.0 * scaled)
    )
    return jnp.where(scaled <= 1.0, inside, jnp.where(scaled <= 2.0, outside, 0.0))


def extend_members(values_in):
    taller = with_halo(values_in, (("lat", 0),), 1, False)
    return with_halo(taller, (("lon", 1),), 1, True)


def extend_panel(values_in):
    taller = with_halo(values_in, (("lat", 0),), 1, False)
    return with_halo(taller, (("lon", 1),), 1, True)


def gather_blocks(widened, slot_codes):
    lat_blocks, lon_blocks = slot_codes.shape
    flattened = widened.reshape((-1,) + widened.shape[2:])
    row_index = lax.broadcasted_iota(jnp.int32, (lat_blocks, lon_blocks), 0)
    col_index = lax.broadcasted_iota(jnp.int32, (lat_blocks, lon_blocks), 1)
    picks = (row_index + slot_codes // 3) * (lon_blocks + 2) + col_index + slot_codes % 3
    return jnp.take(flattened, picks.reshape(-1), axis=0)


def local(anomalies, panel, pair_code, pair_offset):
    lat_blocks, lon_blocks, members, columns = anomalies.shape
    pair_count = pair_code.shape[2]
    targets = anomalies.reshape(lat_blocks * lon_blocks, members, columns)
    member_wide = extend_members(anomalies)

    def tile_for(slot_index):
        sources = gather_blocks(member_wide, pair_code[:, :, slot_index])
        gram_block = jnp.einsum(
            "bki,bkj->bij", targets, sources, preferred_element_type=jnp.float32
        )
        weights = gaspari_cohn(
            pair_offset[0, :, :, slot_index].reshape(-1),
            pair_offset[1, :, :, slot_index].reshape(-1),
        )
        return gram_block * weights / (K - 1)

    kept_tiles = [tile_for(slot_index) for slot_index in range(pair_count)]
    lookup = lambda slot_index: kept_tiles[slot_index]

    def localized_product(field_in):
        field_wide = extend_panel(field_in)
        accumulated = jnp.zeros((lat_blocks * lon_blocks, columns, field_in.shape[3]), jnp.float32)
        for slot_index in range(pair_count):
            sources = gather_blocks(field_wide, pair_code[:, :, slot_index])
            accumulated = accumulated + jnp.einsum(
                "bij,bjr->bir", lookup(slot_index), sources, precision=lax.Precision.HIGHEST
            )
        return accumulated.reshape(field_in.shape)

    first_product = localized_product(panel)
    second_product = localized_product(first_product)
    return (first_product, second_product)


def solution(mesh):
    placed = (
        P("lat", "lon", None, None),
        P("lat", "lon", None, None),
        P("lat", "lon", None),
        P(None, "lat", "lon", None),
    )
    return jax.shard_map(
        local,
        mesh=mesh,
        in_specs=placed,
        out_specs=(P("lat", "lon", None, None), P("lat", "lon", None, None)),
        check_vma=False,
    )
```

profile of v0, /device:TPU:96, one launch (start us, length us, event | category | flops | bytes accessed | tf_op | source)
XLA Modules:
  0.0 181.6 jit_solution(12010333909356739309)
XLA Ops:
  2.0 2.0 %collective-permute-start.4 = (f32[1,8,128,128]{3,2,1,0:T(8,128)S(1)}, f32[1,8,128,128]{3,2,1,0:T(8,128)S(1)}, u32[]{:S(2)}, u32[]{:S(2)}) collective-permute-start(f32[1,8,128,128]{3,2,1,0:T(8,128)S(1)} %get-tuple-element.74), channel_id=1, source_target_pairs={{0,1},{1,2},{2,3},{3,4},{4,5},{5,6},{6,7},{8,9},{9,10},{10,11},{11... | collective-permute-start | bytes 1572872 | tf_op jit(solution)/shard_map/ppermute | solution.py:20
  4.0 3.8 %collective-permute-start.5 = (f32[1,8,128,128]{3,2,1,0:T(8,128)S(1)}, f32[1,8,128,128]{3,2,1,0:T(8,128)S(1)}, u32[]{:S(2)}, u32[]{:S(2)}) collective-permute-start(f32[1,8,128,128]{3,2,1,0:T(8,128)S(1)} %get-tuple-element.73), channel_id=1, source_target_pairs={{1,0},{2,1},{3,2},{4,3},{5,4},{6,5},{7,6},{9,8},{10,9},{11,10},{12... | collective-permute-start | bytes 1572872 | tf_op jit(solution)/shard_map/ppermute | solution.py:22
  8.9 4.1 %collective-permute-start = (bf16[1,8,80,128]{3,2,1,0:T(8,128)(2,1)S(1)}, bf16[1,8,80,128]{3,2,1,0:T(8,128)(2,1)S(1)}, u32[]{:S(2)}, u32[]{:S(2)}) collective-permute-start(bf16[1,8,80,128]{3,2,1,0:T(8,128)(2,1)S(1)} %get-tuple-element.78), channel_id=1, source_target_pairs={{0,1},{1,2},{2,3},{3,4},{4,5},{5,6},{6,7},{8,9},{9,10},{10,11},{11... | collective-permute-start | bytes 491528 | tf_op jit(solution)/shard_map/ppermute | solution.py:20
  13.0 1.9 %collective-permute-start.1 = (bf16[1,8,80,128]{3,2,1,0:T(8,128)(2,1)S(1)}, bf16[1,8,80,128]{3,2,1,0:T(8,128)(2,1)S(1)}, u32[]{:S(2)}, u32[]{:S(2)}) collective-permute-start(bf16[1,8,80,128]{3,2,1,0:T(8,128)(2,1)S(1)} %get-tuple-element.77), channel_id=1, source_target_pairs={{1,0},{2,1},{3,2},{4,3},{5,4},{6,5},{7,6},{9,8},{10,9},{11,10},{12... | collective-permute-start | bytes 491528 | tf_op jit(solution)/shard_map/ppermute | solution.py:22
  21.2 3.9 %collective-permute-done.1 = bf16[1,8,80,128]{3,2,1,0:T(8,128)(2,1)S(1)} collective-permute-done((bf16[1,8,80,128]{3,2,1,0:T(8,128)(2,1)S(1)}, bf16[1,8,80,128]{3,2,1,0:T(8,128)(2,1)S(1)}, u32[]{:S(2)}, u32[]{:S(2)}) %collective-permute-start.1) | collective-permute-done | bytes 163872 | tf_op jit(solution)/shard_map/ppermute | solution.py:22
  25.2 5.5 %collective-permute-start.3 = (bf16[4,1,80,128]{3,2,1,0:T(8,128)(2,1)S(1)}, bf16[4,1,80,128]{3,2,1,0:T(8,128)(2,1)S(1)}, u32[]{:S(2)}, u32[]{:S(2)}) collective-permute-start(bf16[4,1,80,128]{3,2,1,0:T(8,128)(2,1)S(1)} %get-tuple-element.76), channel_id=1, source_target_pairs={{8,0},{16,8},{24,16},{32,24},{40,32},{48,40},{56,48},{64,56},{72,6... | collective-permute-start | bytes 245768 | tf_op jit(solution)/shard_map/ppermute | solution.py:22
  30.7 2.0 %collective-permute-done.2 = bf16[4,1,80,128]{3,2,1,0:T(8,128)(2,1)S(1)} collective-permute-done((bf16[4,1,80,128]{3,2,1,0:T(8,128)(2,1)S(1)}, bf16[4,1,80,128]{3,2,1,0:T(8,128)(2,1)S(1)}, u32[]{:S(2)}, u32[]{:S(2)}) %collective-permute-start.2) | collective-permute-done | bytes 81952 | tf_op jit(solution)/shard_map/ppermute | solution.py:20
  42.1 3.8 %fusion.15 = f32[16,128,128]{1,2,0:T(8,128)} fusion(bf16[16,80,128]{2,1,0:T(8,128)(2,1)S(1)} %bitcast.121, s32[16]{0:T(128)S(1)} %add.913, s32[16]{0:T(128)S(1)} %add.910, s32[128,128]{0,1:T(8,128)S(1)} %get-tuple-element.101, s32[128,128]{0,1:T(8,128)S(1)} %get-tuple-element.102, bf16[16,80,128]{2,1,0:T(8,128)(2,1)} %gather_fusion.2, ...), kind=kOutput, calls=%fused_computation.76 | convolution fusion | flops 51544064 | bytes 1835152 | tf_op jit(solution)/shard_map/bki,bkj->bij/dot_general | solution.py:75
  45.9 2.8 %fusion.17 = f32[16,128,128]{1,2,0:T(8,128)} fusion(bf16[16,80,128]{2,1,0:T(8,128)(2,1)S(1)} %bitcast.122, s32[128,128]{0,1:T(8,128)S(1)} %get-tuple-element.101, s32[16]{0:T(128)S(1)} %add.893, s32[128,128]{0,1:T(8,128)S(1)} %get-tuple-element.102, s32[16]{0:T(128)S(1)} %add.889, bf16[16,80,128]{2,1,0:T(8,128)(2,1)S(1)} %copy-done.43, ...), kind=kOutput, calls=%fused_computation.80 | convolution fusion | flops 51544064 | bytes 1835152 | tf_op jit(solution)/shard_map/bki,bkj->bij/dot_general | solution.py:75
  48.7 2.8 %fusion.13 = f32[16,128,128]{1,2,0:T(8,128)} fusion(bf16[16,80,128]{2,1,0:T(8,128)(2,1)S(1)} %bitcast.123, s32[16]{0:T(128)S(1)} %add.932, s32[16]{0:T(128)S(1)} %add.929, s32[128,128]{0,1:T(8,128)S(1)} %get-tuple-element.101, s32[128,128]{0,1:T(8,128)S(1)} %get-tuple-element.102, bf16[16,80,128]{2,1,0:T(8,128)(2,1)S(1)} %copy-done.42, ...), kind=kOutput, calls=%fused_computation.73 | convolution fusion | flops 51544064 | bytes 1835152 | tf_op jit(solution)/shard_map/bki,bkj->bij/dot_general | solution.py:75
  51.6 2.8 %fusion.11 = f32[16,128,128]{1,2,0:T(8,128)} fusion(bf16[16,80,128]{2,1,0:T(8,128)(2,1)S(1)} %bitcast.124, s32[16]{0:T(128)S(1)} %add.951, s32[16]{0:T(128)S(1)} %add.948, s32[128,128]{0,1:T(8,128)S(1)} %get-tuple-element.101, s32[128,128]{0,1:T(8,128)S(1)} %get-tuple-element.102, bf16[16,80,128]{2,1,0:T(8,128)(2,1)S(1)} %copy-done.41, ...), kind=kOutput, calls=%fused_computation.69 | convolution fusion | flops 51544064 | bytes 1835152 | tf_op jit(solution)/shard_map/bki,bkj->bij/dot_general | solution.py:75
  54.4 2.8 %fusion.9 = f32[16,128,128]{1,2,0:T(8,128)} fusion(bf16[16,80,128]{2,1,0:T(8,128)(2,1)S(1)} %bitcast.125, s32[16]{0:T(128)S(1)} %add.970, s32[16]{0:T(128)S(1)} %add.967, s32[128,128]{0,1:T(8,128)S(1)} %get-tuple-element.101, s32[128,128]{0,1:T(8,128)S(1)} %get-tuple-element.102, bf16[16,80,128]{2,1,0:T(8,128)(2,1)S(1)} %copy-done.40, ...), kind=kOutput, calls=%fused_computation.65 | convolution fusion | flops 51544064 | bytes 1835152 | tf_op jit(solution)/shard_map/bki,bkj->bij/dot_general | solution.py:75
  57.1 2.8 %fusion.7 = f32[16,128,128]{1,2,0:T(8,128)} fusion(bf16[16,80,128]{2,1,0:T(8,128)(2,1)S(1)} %bitcast.126, s32[16]{0:T(128)S(1)} %add.989, s32[16]{0:T(128)S(1)} %add.986, s32[128,128]{0,1:T(8,128)S(1)} %get-tuple-element.101, s32[128,128]{0,1:T(8,128)S(1)} %get-tuple-element.102, bf16[16,80,128]{2,1,0:T(8,128)(2,1)S(1)} %copy-done.39, ...), kind=kOutput, calls=%fused_computation.61 | convolution fusion | flops 51544064 | bytes 1835152 | tf_op jit(solution)/shard_map/bki,bkj->bij/dot_general | solution.py:75
  59.9 3.2 %fusion.5 = f32[16,128,128]{1,2,0:T(8,128)} fusion(bf16[16,80,128]{2,1,0:T(8,128)(2,1)S(1)} %bitcast.127, s32[16]{0:T(128)S(1)} %add.1008, s32[16]{0:T(128)S(1)} %add.1005, s32[128,128]{0,1:T(8,128)S(1)} %get-tuple-element.101, s32[128,128]{0,1:T(8,128)S(1)} %get-tuple-element.102, bf16[16,80,128]{2,1,0:T(8,128)(2,1)S(1)} %copy-done.38, ...), kind=kOutput, calls=%fused_computation.57 | convolution fusion | flops 51544064 | bytes 1835152 | tf_op jit(solution)/shard_map/bki,bkj->bij/dot_general | solution.py:75
  65.8 3.9 %fusion.3 = f32[16,128,128]{1,2,0:T(8,128)} fusion(bf16[16,80,128]{2,1,0:T(8,128)(2,1)S(1)} %bitcast.128, s32[16]{0:T(128)S(1)} %add.1027, s32[16]{0:T(128)S(1)} %add.1024, s32[128,128]{0,1:T(8,128)S(1)} %get-tuple-element.101, s32[128,128]{0,1:T(8,128)S(1)} %get-tuple-element.102, bf16[16,80,128]{2,1,0:T(8,128)(2,1)} %gather_fusion.14, ...), kind=kOutput, calls=%fused_computation.53 | convolution fusion | flops 51544064 | bytes 1835152 | tf_op jit(solution)/shard_map/bki,bkj->bij/dot_general | solution.py:75
  71.0 4.4 %collective-permute-start.7 = (f32[4,1,128,128]{3,2,1,0:T(8,128)S(1)}, f32[4,1,128,128]{3,2,1,0:T(8,128)S(1)}, u32[]{:S(2)}, u32[]{:S(2)}) collective-permute-start(f32[4,1,128,128]{3,2,1,0:T(8,128)S(1)} %get-tuple-element.70), channel_id=1, source_target_pairs={{8,0},{16,8},{24,16},{32,24},{40,32},{48,40},{56,48},{64,56},{72,6... | collective-permute-start | bytes 786440 | tf_op jit(solution)/shard_map/ppermute | solution.py:22
  75.5 2.8 %fusion.1 = f32[16,128,128]{1,2,0:T(8,128)} fusion(bf16[16,80,128]{2,1,0:T(8,128)(2,1)S(1)} %bitcast.129, s32[16]{0:T(128)S(1)} %add.1046, s32[16]{0:T(128)S(1)} %add.1043, s32[128,128]{0,1:T(8,128)S(1)} %get-tuple-element.101, s32[128,128]{0,1:T(8,128)S(1)} %get-tuple-element.102, bf16[16,80,128]{2,1,0:T(8,128)(2,1)S(1)} %copy-done.37, ...), kind=kOutput, calls=%fused_computation.49 | convolution fusion | flops 51544064 | bytes 1835152 | tf_op jit(solution)/shard_map/bki,bkj->bij/dot_general | solution.py:75
  78.2 2.4 %collective-permute-done.6 = f32[4,1,128,128]{3,2,1,0:T(8,128)S(1)} collective-permute-done((f32[4,1,128,128]{3,2,1,0:T(8,128)S(1)}, f32[4,1,128,128]{3,2,1,0:T(8,128)S(1)}, u32[]{:S(2)}, u32[]{:S(2)}) %collective-permute-start.6) | collective-permute-done | bytes 262176 | tf_op jit(solution)/shard_map/ppermute | solution.py:20
  95.3 3.6 %fusion.53 = f32[16,128,128]{2,1,0:T(8,128)S(1)} fusion(f32[16,128,128]{1,2,0:T(8,128)} %fusion.15, f32[16,128,128]{2,1,0:T(8,128)} %gather_fusion.3, pred[16]{0:T(512)(128)(4,1)S(1)} %get-tuple-element.89), kind=kOutput, calls=%fused_computation.116 | convolution fusion | flops 402915328 | bytes 3145744 | tf_op jit(solution)/shard_map/bij,bjr->bir/dot_general | solution.py:92
  98.9 1.9 %convolution_add_fusion.15 = f32[16,128,128]{2,1,0:T(8,128)S(1)} fusion(f32[16,128,128]{2,1,0:T(8,128)S(1)} %fusion.53, f32[16,128,128]{1,2,0:T(8,128)S(1)} %copy-done.13, f32[16,128,128]{2,1,0:T(8,128)S(1)} %copy-done.32, pred[16]{0:T(512)(128)(4,1)S(1)} %get-tuple-element.91), kind=kOutput, calls=%fused_computation.77 | convolution fusion | flops 403177472 | bytes 4194320 | tf_op jit(solution)/shard_map/bij,bjr->bir/dot_general | solution.py:92
  104.8 2.1 %convolution_add_fusion.12 = f32[16,128,128]{2,1,0:T(8,128)S(1)} fusion(f32[16,128,128]{2,1,0:T(8,128)S(1)} %convolution_add_fusion.13, f32[16,128,128]{1,2,0:T(8,128)S(1)} %copy-done.5, f32[16,128,128]{2,1,0:T(8,128)S(1)} %copy-done.29, pred[16]{0:T(512)(128)(4,1)S(1)} %get-tuple-element.85), kind=kOutput, calls=%fused_computation.62 | convolution fusion | flops 403177472 | bytes 4194320 | tf_op jit(solution)/shard_map/bij,bjr->bir/dot_general | solution.py:92
  112.8 1.9 %convolution_add_fusion.8 = f32[16,128,128]{2,1,0:T(8,128)S(1)} fusion(f32[16,128,128]{2,1,0:T(8,128)S(1)} %convolution_add_fusion.9, f32[16,128,128]{1,2,0:T(8,128)S(1)} %copy-done.15, f32[16,128,128]{2,1,0:T(8,128)S(1)} %copy-done.24, pred[16]{0:T(512)(128)(4,1)S(1)} %get-tuple-element.49), kind=kOutput, calls=%fused_computation.46 | convolution fusion | flops 403177472 | bytes 4194320 | tf_op jit(solution)/shard_map/bij,bjr->bir/dot_general | solution.py:92
  114.8 2.9 %collective-permute-start.8 = (f32[1,8,128,128]{3,2,1,0:T(8,128)S(1)}, f32[1,8,128,128]{3,2,1,0:T(8,128)S(1)}, u32[]{:S(2)}, u32[]{:S(2)}) collective-permute-start(f32[1,8,128,128]{3,2,1,0:T(8,128)S(1)} %get-tuple-element.71), channel_id=1, source_target_pairs={{0,1},{1,2},{2,3},{3,4},{4,5},{5,6},{6,7},{8,9},{9,10},{10,11},{11... | collective-permute-start | bytes 1572872 | tf_op jit(solution)/shard_map/ppermute | solution.py:20
  117.7 2.9 %collective-permute-start.9 = (f32[1,8,128,128]{3,2,1,0:T(8,128)S(1)}, f32[1,8,128,128]{3,2,1,0:T(8,128)S(1)}, u32[]{:S(2)}, u32[]{:S(2)}) collective-permute-start(f32[1,8,128,128]{3,2,1,0:T(8,128)S(1)} %get-tuple-element.72), channel_id=1, source_target_pairs={{1,0},{2,1},{3,2},{4,3},{5,4},{6,5},{7,6},{9,8},{10,9},{11,10},{12... | collective-permute-start | bytes 1572872 | tf_op jit(solution)/shard_map/ppermute | solution.py:22
  120.7 9.3 %collective-permute-done.8 = f32[1,8,128,128]{3,2,1,0:T(8,128)S(1)} collective-permute-done((f32[1,8,128,128]{3,2,1,0:T(8,128)S(1)}, f32[1,8,128,128]{3,2,1,0:T(8,128)S(1)}, u32[]{:S(2)}, u32[]{:S(2)}) %collective-permute-start.8) | collective-permute-done | bytes 524320 | tf_op jit(solution)/shard_map/ppermute | solution.py:20
  130.0 4.0 %collective-permute-done.9 = f32[1,8,128,128]{3,2,1,0:T(8,128)S(1)} collective-permute-done((f32[1,8,128,128]{3,2,1,0:T(8,128)S(1)}, f32[1,8,128,128]{3,2,1,0:T(8,128)S(1)}, u32[]{:S(2)}, u32[]{:S(2)}) %collective-permute-start.9) | collective-permute-done | bytes 524320 | tf_op jit(solution)/shard_map/ppermute | solution.py:22
  134.1 5.5 %collective-permute-start.11 = (f32[4,1,128,128]{3,2,1,0:T(8,128)S(1)}, f32[4,1,128,128]{3,2,1,0:T(8,128)S(1)}, u32[]{:S(2)}, u32[]{:S(2)}) collective-permute-start(f32[4,1,128,128]{3,2,1,0:T(8,128)S(1)} %get-tuple-element.68), channel_id=1, source_target_pairs={{8,0},{16,8},{24,16},{32,24},{40,32},{48,40},{56,48},{64,56},{72,6... | collective-permute-start | bytes 786440 | tf_op jit(solution)/shard_map/ppermute | solution.py:22
  139.7 6.5 %collective-permute-done.10 = f32[4,1,128,128]{3,2,1,0:T(8,128)S(1)} collective-permute-done((f32[4,1,128,128]{3,2,1,0:T(8,128)S(1)}, f32[4,1,128,128]{3,2,1,0:T(8,128)S(1)}, u32[]{:S(2)}, u32[]{:S(2)}) %collective-permute-start.10) | collective-permute-done | bytes 262176 | tf_op jit(solution)/shard_map/ppermute | solution.py:20
  160.9 3.6 %fusion.43 = f32[16,128,128]{2,1,0:T(8,128)S(1)} fusion(f32[16,128,128]{1,2,0:T(8,128)} %fusion.15, f32[16,128,128]{2,1,0:T(8,128)} %gather_fusion.19, pred[16]{0:T(512)(128)(4,1)S(1)} %get-tuple-element.89), kind=kOutput, calls=%fused_computation.106 | convolution fusion | flops 402915328 | bytes 3145744 | tf_op jit(solution)/shard_map/bij,bjr->bir/dot_general | solution.py:92
  164.5 1.9 %convolution_add_fusion.7 = f32[16,128,128]{2,1,0:T(8,128)S(1)} fusion(f32[16,128,128]{2,1,0:T(8,128)S(1)} %fusion.43, f32[16,128,128]{1,2,0:T(8,128)S(1)} %copy-done.14, f32[16,128,128]{2,1,0:T(8,128)S(1)} %copy-done.26, pred[16]{0:T(512)(128)(4,1)S(1)} %get-tuple-element.91), kind=kOutput, calls=%fused_computation.45 | convolution fusion | flops 403177472 | bytes 4194320 | tf_op jit(solution)/shard_map/bij,bjr->bir/dot_general | solution.py:92
  172.4 2.2 %convolution_add_fusion.3 = f32[16,128,128]{2,1,0:T(8,128)S(1)} fusion(f32[16,128,128]{2,1,0:T(8,128)S(1)} %convolution_add_fusion.4, f32[16,128,128]{1,2,0:T(8,128)S(1)} %copy-done.4, f32[16,128,128]{2,1,0:T(8,128)S(1)} %copy-done.20, pred[16]{0:T(512)(128)(4,1)S(1)} %get-tuple-element.83), kind=kOutput, calls=%fused_computation.41 | convolution fusion | flops 403177472 | bytes 4194320 | tf_op jit(solution)/shard_map/bij,bjr->bir/dot_general | solution.py:92
  178.5 2.9 %convolution_add_fusion = f32[16,128,128]{2,1,0:T(8,128)} fusion(f32[16,128,128]{2,1,0:T(8,128)S(1)} %convolution_add_fusion.1, f32[16,128,128]{1,2,0:T(8,128)S(1)} %copy-done.16, f32[16,128,128]{2,1,0:T(8,128)S(1)} %copy-done.17, pred[16]{0:T(512)(128)(4,1)S(1)} %get-tuple-element.49), kind=kOutput, calls=%fused_computation.38 | convolution fusion | flops 403177472 | bytes 4194320 | tf_op jit(solution)/shard_map/bij,bjr->bir/dot_general | solution.py:92
  (211 shorter events, 70.8 us)
Async XLA Ops:
  0.6 20.5 %copy-start.36 = (bf16[2,8,80,128]{3,2,1,0:T(8,128)(2,1)S(1)}, bf16[2,8,80,128]{3,2,1,0:T(8,128)(2,1)}, u32[]{:S(2)}) copy-start(bf16[2,8,80,128]{3,2,1,0:T(8,128)(2,1)} %param.8) | copy-start | bytes 983044
  0.6 14.3 %copy-start.34 = (s32[2,8,9]{2,1,0:T(8,128)S(1)}, s32[2,8,9]{2,1,0:T(8,128)}, u32[]{:S(2)}) copy-start(s32[2,8,9]{2,1,0:T(8,128)} %param.10) | copy-start | bytes 1732
  0.7 16.7 %copy-start.35 = (s32[2,2,8,9]{3,2,1,0:T(8,128)S(1)}, s32[2,2,8,9]{3,2,1,0:T(8,128)}, u32[]{:S(2)}) copy-start(s32[2,2,8,9]{3,2,1,0:T(8,128)} %param.11) | copy-start | bytes 3460
  2.0 67.7 %collective-permute-start.4 = (f32[1,8,128,128]{3,2,1,0:T(8,128)S(1)}, f32[1,8,128,128]{3,2,1,0:T(8,128)S(1)}, u32[]{:S(2)}, u32[]{:S(2)}) collective-permute-start(f32[1,8,128,128]{3,2,1,0:T(8,128)S(1)} %get-tuple-element.74), channel_id=1, source_target_pairs={{0,1},{1,2},{2,3},{3,4},{4,5},{5,6},{6,7},{8,9},{9,10},{10,11},{11... | collective-permute-start | bytes 1572872 | tf_op jit(solution)/shard_map/ppermute | solution.py:20
  4.0 65.8 %collective-permute-start.5 = (f32[1,8,128,128]{3,2,1,0:T(8,128)S(1)}, f32[1,8,128,128]{3,2,1,0:T(8,128)S(1)}, u32[]{:S(2)}, u32[]{:S(2)}) collective-permute-start(f32[1,8,128,128]{3,2,1,0:T(8,128)S(1)} %get-tuple-element.73), channel_id=1, source_target_pairs={{1,0},{2,1},{3,2},{4,3},{5,4},{6,5},{7,6},{9,8},{10,9},{11,10},{12... | collective-permute-start | bytes 1572872 | tf_op jit(solution)/shard_map/ppermute | solution.py:22
  8.9 12.3 %collective-permute-start = (bf16[1,8,80,128]{3,2,1,0:T(8,128)(2,1)S(1)}, bf16[1,8,80,128]{3,2,1,0:T(8,128)(2,1)S(1)}, u32[]{:S(2)}, u32[]{:S(2)}) collective-permute-start(bf16[1,8,80,128]{3,2,1,0:T(8,128)(2,1)S(1)} %get-tuple-element.78), channel_id=1, source_target_pairs={{0,1},{1,2},{2,3},{3,4},{4,5},{5,6},{6,7},{8,9},{9,10},{10,11},{11... | collective-permute-start | bytes 491528 | tf_op jit(solution)/shard_map/ppermute | solution.py:20
  13.0 12.1 %collective-permute-start.1 = (bf16[1,8,80,128]{3,2,1,0:T(8,128)(2,1)S(1)}, bf16[1,8,80,128]{3,2,1,0:T(8,128)(2,1)S(1)}, u32[]{:S(2)}, u32[]{:S(2)}) collective-permute-start(bf16[1,8,80,128]{3,2,1,0:T(8,128)(2,1)S(1)} %get-tuple-element.77), channel_id=1, source_target_pairs={{1,0},{2,1},{3,2},{4,3},{5,4},{6,5},{7,6},{9,8},{10,9},{11,10},{12... | collective-permute-start | bytes 491528 | tf_op jit(solution)/shard_map/ppermute | solution.py:22
  25.1 7.5 %collective-permute-start.2 = (bf16[4,1,80,128]{3,2,1,0:T(8,128)(2,1)S(1)}, bf16[4,1,80,128]{3,2,1,0:T(8,128)(2,1)S(1)}, u32[]{:S(2)}, u32[]{:S(2)}) collective-permute-start(bf16[4,1,80,128]{3,2,1,0:T(8,128)(2,1)S(1)} %get-tuple-element.75), channel_id=1, source_target_pairs={{0,8},{8,16},{16,24},{24,32},{32,40},{40,48},{48,56},{56,64},{64,7... | collective-permute-start | bytes 245768 | tf_op jit(solution)/shard_map/ppermute | solution.py:20
  25.2 7.6 %collective-permute-start.3 = (bf16[4,1,80,128]{3,2,1,0:T(8,128)(2,1)S(1)}, bf16[4,1,80,128]{3,2,1,0:T(8,128)(2,1)S(1)}, u32[]{:S(2)}, u32[]{:S(2)}) collective-permute-start(bf16[4,1,80,128]{3,2,1,0:T(8,128)(2,1)S(1)} %get-tuple-element.76), channel_id=1, source_target_pairs={{8,0},{16,8},{24,16},{32,24},{40,32},{48,40},{56,48},{64,56},{72,6... | collective-permute-start | bytes 245768 | tf_op jit(solution)/shard_map/ppermute | solution.py:22
  42.1 3.8 %copy-start.43 = (bf16[16,80,128]{2,1,0:T(8,128)(2,1)S(1)}, bf16[16,80,128]{2,1,0:T(8,128)(2,1)}, u32[]{:S(2)}) copy-start(bf16[16,80,128]{2,1,0:T(8,128)(2,1)} %gather_fusion) | copy-start | bytes 983044
  45.9 2.8 %copy-start.42 = (bf16[16,80,128]{2,1,0:T(8,128)(2,1)S(1)}, bf16[16,80,128]{2,1,0:T(8,128)(2,1)}, u32[]{:S(2)}) copy-start(bf16[16,80,128]{2,1,0:T(8,128)(2,1)} %gather_fusion.4) | copy-start | bytes 983044
  48.7 2.8 %copy-start.41 = (bf16[16,80,128]{2,1,0:T(8,128)(2,1)S(1)}, bf16[16,80,128]{2,1,0:T(8,128)(2,1)}, u32[]{:S(2)}) copy-start(bf16[16,80,128]{2,1,0:T(8,128)(2,1)} %gather_fusion.6) | copy-start | bytes 983044
  51.6 2.8 %copy-start.40 = (bf16[16,80,128]{2,1,0:T(8,128)(2,1)S(1)}, bf16[16,80,128]{2,1,0:T(8,128)(2,1)}, u32[]{:S(2)}) copy-start(bf16[16,80,128]{2,1,0:T(8,128)(2,1)} %gather_fusion.8) | copy-start | bytes 983044
  54.3 2.8 %copy-start.39 = (bf16[16,80,128]{2,1,0:T(8,128)(2,1)S(1)}, bf16[16,80,128]{2,1,0:T(8,128)(2,1)}, u32[]{:S(2)}) copy-start(bf16[16,80,128]{2,1,0:T(8,128)(2,1)} %gather_fusion.10) | copy-start | bytes 983044
  57.1 2.8 %copy-start.38 = (bf16[16,80,128]{2,1,0:T(8,128)(2,1)S(1)}, bf16[16,80,128]{2,1,0:T(8,128)(2,1)}, u32[]{:S(2)}) copy-start(bf16[16,80,128]{2,1,0:T(8,128)(2,1)} %gather_fusion.12) | copy-start | bytes 983044
  65.8 3.9 %copy-start.33 = (f32[2,8,128,128]{3,2,1,0:T(8,128)S(1)}, f32[2,8,128,128]{3,2,1,0:T(8,128)}, u32[]{:S(2)}) copy-start(f32[2,8,128,128]{3,2,1,0:T(8,128)} %param.9) | copy-start | bytes 3145732
  69.6 5.8 %copy-start.37 = (bf16[16,80,128]{2,1,0:T(8,128)(2,1)S(1)}, bf16[16,80,128]{2,1,0:T(8,128)(2,1)}, u32[]{:S(2)}) copy-start(bf16[16,80,128]{2,1,0:T(8,128)(2,1)} %gather_fusion.16) | copy-start | bytes 983044
  69.9 10.7 %collective-permute-start.6 = (f32[4,1,128,128]{3,2,1,0:T(8,128)S(1)}, f32[4,1,128,128]{3,2,1,0:T(8,128)S(1)}, u32[]{:S(2)}, u32[]{:S(2)}) collective-permute-start(f32[4,1,128,128]{3,2,1,0:T(8,128)S(1)} %get-tuple-element.69), channel_id=1, source_target_pairs={{0,8},{8,16},{16,24},{24,32},{32,40},{40,48},{48,56},{56,64},{64,7... | collective-permute-start | bytes 786440 | tf_op jit(solution)/shard_map/ppermute | solution.py:20
  71.0 9.6 %collective-permute-start.7 = (f32[4,1,128,128]{3,2,1,0:T(8,128)S(1)}, f32[4,1,128,128]{3,2,1,0:T(8,128)S(1)}, u32[]{:S(2)}, u32[]{:S(2)}) collective-permute-start(f32[4,1,128,128]{3,2,1,0:T(8,128)S(1)} %get-tuple-element.70), channel_id=1, source_target_pairs={{8,0},{16,8},{24,16},{32,24},{40,32},{48,40},{56,48},{64,56},{72,6... | collective-permute-start | bytes 786440 | tf_op jit(solution)/shard_map/ppermute | solution.py:22
  95.3 3.6 %copy-start.13 = (f32[16,128,128]{1,2,0:T(8,128)S(1)}, f32[16,128,128]{1,2,0:T(8,128)}, u32[]{:S(2)}) copy-start(f32[16,128,128]{1,2,0:T(8,128)} %fusion.17) | copy-start | bytes 3145732
  95.3 3.6 %copy-start.32 = (f32[16,128,128]{2,1,0:T(8,128)S(1)}, f32[16,128,128]{2,1,0:T(8,128)}, u32[]{:S(2)}) copy-start(f32[16,128,128]{2,1,0:T(8,128)} %gather_fusion.1) | copy-start | bytes 3145732
  104.8 2.1 %copy-start.3 = (f32[16,128,128]{1,2,0:T(8,128)S(1)}, f32[16,128,128]{1,2,0:T(8,128)}, u32[]{:S(2)}) copy-start(f32[16,128,128]{1,2,0:T(8,128)} %fusion.7) | copy-start | bytes 3145732
  104.8 2.1 %copy-start.28 = (f32[16,128,128]{2,1,0:T(8,128)S(1)}, f32[16,128,128]{2,1,0:T(8,128)}, u32[]{:S(2)}) copy-start(f32[16,128,128]{2,1,0:T(8,128)} %gather_fusion.11) | copy-start | bytes 3145732
  114.7 31.7 %copy-start = (f32[16,128,128]{2,1,0:T(8,128)}, f32[16,128,128]{2,1,0:T(8,128)S(1)}, u32[]{:S(2)}) copy-start(f32[16,128,128]{2,1,0:T(8,128)S(1)} %convolution_add_fusion.8) | copy-start | bytes 3145732
  114.8 15.1 %collective-permute-start.8 = (f32[1,8,128,128]{3,2,1,0:T(8,128)S(1)}, f32[1,8,128,128]{3,2,1,0:T(8,128)S(1)}, u32[]{:S(2)}, u32[]{:S(2)}) collective-permute-start(f32[1,8,128,128]{3,2,1,0:T(8,128)S(1)} %get-tuple-element.71), channel_id=1, source_target_pairs={{0,1},{1,2},{2,3},{3,4},{4,5},{5,6},{6,7},{8,9},{9,10},{10,11},{11... | collective-permute-start | bytes 1572872 | tf_op jit(solution)/shard_map/ppermute | solution.py:20
  117.7 16.3 %collective-permute-start.9 = (f32[1,8,128,128]{3,2,1,0:T(8,128)S(1)}, f32[1,8,128,128]{3,2,1,0:T(8,128)S(1)}, u32[]{:S(2)}, u32[]{:S(2)}) collective-permute-start(f32[1,8,128,128]{3,2,1,0:T(8,128)S(1)} %get-tuple-element.72), channel_id=1, source_target_pairs={{1,0},{2,1},{3,2},{4,3},{5,4},{6,5},{7,6},{9,8},{10,9},{11,10},{12... | collective-permute-start | bytes 1572872 | tf_op jit(solution)/shard_map/ppermute | solution.py:22
  134.0 12.2 %collective-permute-start.10 = (f32[4,1,128,128]{3,2,1,0:T(8,128)S(1)}, f32[4,1,128,128]{3,2,1,0:T(8,128)S(1)}, u32[]{:S(2)}, u32[]{:S(2)}) collective-permute-start(f32[4,1,128,128]{3,2,1,0:T(8,128)S(1)} %get-tuple-element.67), channel_id=1, source_target_pairs={{0,8},{8,16},{16,24},{24,32},{32,40},{40,48},{48,56},{56,64},{64,7... | collective-permute-start | bytes 786440 | tf_op jit(solution)/shard_map/ppermute | solution.py:20
  134.1 12.1 %collective-permute-start.11 = (f32[4,1,128,128]{3,2,1,0:T(8,128)S(1)}, f32[4,1,128,128]{3,2,1,0:T(8,128)S(1)}, u32[]{:S(2)}, u32[]{:S(2)}) collective-permute-start(f32[4,1,128,128]{3,2,1,0:T(8,128)S(1)} %get-tuple-element.68), channel_id=1, source_target_pairs={{8,0},{16,8},{24,16},{32,24},{40,32},{48,40},{56,48},{64,56},{72,6... | collective-permute-start | bytes 786440 | tf_op jit(solution)/shard_map/ppermute | solution.py:22
  160.9 3.6 %copy-start.14 = (f32[16,128,128]{1,2,0:T(8,128)S(1)}, f32[16,128,128]{1,2,0:T(8,128)}, u32[]{:S(2)}) copy-start(f32[16,128,128]{1,2,0:T(8,128)} %fusion.17) | copy-start | bytes 3145732
  160.9 3.6 %copy-start.26 = (f32[16,128,128]{2,1,0:T(8,128)S(1)}, f32[16,128,128]{2,1,0:T(8,128)}, u32[]{:S(2)}) copy-start(f32[16,128,128]{2,1,0:T(8,128)} %gather_fusion.18) | copy-start | bytes 3145732
  172.3 2.2 %copy-start.2 = (f32[16,128,128]{1,2,0:T(8,128)S(1)}, f32[16,128,128]{1,2,0:T(8,128)}, u32[]{:S(2)}) copy-start(f32[16,128,128]{1,2,0:T(8,128)} %fusion.5) | copy-start | bytes 3145732
  172.3 2.2 %copy-start.19 = (f32[16,128,128]{2,1,0:T(8,128)S(1)}, f32[16,128,128]{2,1,0:T(8,128)}, u32[]{:S(2)}) copy-start(f32[16,128,128]{2,1,0:T(8,128)} %gather_fusion.24) | copy-start | bytes 3145732
  (24 other events, 46.7 us)
where the time goes:
time: 185 us; the launch traced here: 182 us
  matrix products  66.9 us (36%)
  local copies, waits for them, and re-layouts  48.3 us (26%)
  starting transfers between devices  34.5 us (19%)
  waiting for transfers between devices  28.2 us (15%)
  other arithmetic  1.93 us (1%)
  between operations  1.85 us (1%)
    gather x27, local copies, waits for them, and re-layouts, gather_blocks(): return jnp.take(flattened, picks.reshape(-1), axis=0)  40.8 us
    dot_general x18, matrix products, localized_product(): jnp.einsum('bij,bjr->bir', lookup(slot_index), sources, precision=lax.Pre...  39.2 us
    dot_general x9, matrix products, tile_for(): jnp.einsum('bki,bkj->bij', targets, sources, preferred_element_type=jnp.f...  27.7 us
    ppermute x6, starting transfers between devices, with_halo(): lax.ppermute(head, axis, [((i + 1) % count, i) for i in range(ends)])  24.1 us
    ppermute x6, waiting for transfers between devices, with_halo(): lax.ppermute(tail, axis, [(i, (i + 1) % count) for i in range(ends)])  20.2 us
    ppermute x6, starting transfers between devices, with_halo(): lax.ppermute(tail, axis, [(i, (i + 1) % count) for i in range(ends)])  10.4 us
    ppermute x6, waiting for transfers between devices, with_halo(): lax.ppermute(head, axis, [((i + 1) % count, i) for i in range(ends)])  8.01 us
  transfers between devices with their start and end apart: 12, of which 7 were waited for; matrix products, arithmetic and copies ran while one was open for 26% of the time, Pallas kernels for 0%

commit v1 on v0

v1 whole, which is shorter than its diff:
```python
import functools

import jax
import jax.numpy as jnp
from jax import lax
from jax.experimental import pallas as pl
from jax.experimental.pallas import tpu as pltpu
from jax.sharding import PartitionSpec as P

K = 80
COLS = 128
STRIDE = 16
RADIUS = 4
CODES = 9


def gaspari_cohn(shift_rows, shift_cols):
    position = jnp.arange(COLS)
    row_within = position // STRIDE
    col_within = position % STRIDE
    delta_rows = shift_rows[..., None, None] + (row_within[None, :] - row_within[:, None])
    delta_cols = shift_cols[..., None, None] + (col_within[None, :] - col_within[:, None])
    squared = (delta_rows * delta_rows + delta_cols * delta_cols).astype(jnp.float32)
    scaled = jnp.sqrt(squared + 0.25) / RADIUS
    inside = (
        ((-0.25 * scaled + 0.5) * scaled + 0.625) * scaled - 5.0 / 3.0
    ) * scaled * scaled + 1.0
    outside = (
        ((((scaled / 12.0 - 0.5) * scaled + 0.625) * scaled + 5.0 / 3.0) * scaled - 5.0) * scaled
        + 4.0
        - 2.0 / (3.0 * scaled)
    )
    return jnp.where(scaled <= 1.0, inside, jnp.where(scaled <= 2.0, outside, 0.0))


def taper_by_code():
    codes = jnp.arange(CODES, dtype=jnp.int32)
    shift_rows = (codes // 3 - 1) * (COLS // STRIDE)
    shift_cols = (codes % 3 - 1) * STRIDE
    return gaspari_cohn(shift_rows, shift_cols) / (K - 1)


def with_halo(cells):
    nlat = lax.axis_size("lat")
    nlon = lax.axis_size("lon")
    down = [(i, i + 1) for i in range(nlat - 1)]
    up = [(i + 1, i) for i in range(nlat - 1)]
    right = [(i, (i + 1) % nlon) for i in range(nlon)]
    left = [((i + 1) % nlon, i) for i in range(nlon)]

    def both(lat_pairs, lon_shift):
        return [
            (b * nlat + a, ((b + lon_shift) % nlon) * nlat + c)
            for a, c in lat_pairs
            for b in range(nlon)
        ]

    first_row, last_row = cells[:1], cells[-1:]
    north = lax.ppermute(last_row, "lat", down)
    south = lax.ppermute(first_row, "lat", up)
    west = lax.ppermute(cells[:, -1:], "lon", right)
    east = lax.ppermute(cells[:, :1], "lon", left)
    north_west = lax.ppermute(last_row[:, -1:], ("lon", "lat"), both(down, 1))
    north_east = lax.ppermute(last_row[:, :1], ("lon", "lat"), both(down, -1))
    south_west = lax.ppermute(first_row[:, -1:], ("lon", "lat"), both(up, 1))
    south_east = lax.ppermute(first_row[:, :1], ("lon", "lat"), both(up, -1))
    top = jnp.concatenate([north_west, north, north_east], axis=1)
    middle = jnp.concatenate([west, cells, east], axis=1)
    bottom = jnp.concatenate([south_west, south, south_east], axis=1)
    return jnp.concatenate([top, middle, bottom], axis=0)


def product_kernel(targets_ref, members_ref, high_ref, low_ref, taper_ref, out_ref):
    lat_blocks, lon_blocks = out_ref.shape[0], out_ref.shape[1]

    def one_block(t, carry):
        p = t // lon_blocks
        q = t % lon_blocks
        target = targets_ref[p, q]
        total = jnp.zeros(out_ref.shape[2:], jnp.float32)
        for code in range(CODES):
            dr, dc = code // 3, code % 3
            gram = jnp.dot(target, members_ref[p + dr, q + dc], preferred_element_type=jnp.float32)
            tile = gram * taper_ref[code]
            tile_high = tile.astype(jnp.bfloat16)
            tile_low = (tile - tile_high.astype(jnp.float32)).astype(jnp.bfloat16)
            field_high = high_ref[p + dr, q + dc]
            field_low = low_ref[p + dr, q + dc]
            total = total + jnp.dot(tile_high, field_high, preferred_element_type=jnp.float32)
            total = total + jnp.dot(tile_high, field_low, preferred_element_type=jnp.float32)
            total = total + jnp.dot(tile_low, field_high, preferred_element_type=jnp.float32)
        out_ref[p, q] = total
        return carry

    lax.fori_loop(0, lat_blocks * lon_blocks, one_block, 0)


def localized_product(targets, members_wide, field_in, taper):
    lat_blocks, lon_blocks, columns, rank = field_in.shape
    field_wide = with_halo(field_in)
    rounded = lax.reduce_precision(field_wide, exponent_bits=8, mantissa_bits=7)
    high = rounded.astype(jnp.bfloat16)
    low = (field_wide - rounded).astype(jnp.bfloat16)
    blocks = lat_blocks * lon_blocks
    flops = blocks * CODES * 2 * columns * (K * columns + 3 * columns * rank)
    moved = high.size * 4 + members_wide.size * 2 + targets.size * 2 + taper.size * 4 + field_in.size * 4
    vmem = pl.BlockSpec(memory_space=pltpu.VMEM)
    return pl.pallas_call(
        product_kernel,
        out_shape=jax.ShapeDtypeStruct(field_in.shape, jnp.float32),
        in_specs=[vmem] * 5,
        out_specs=vmem,
        cost_estimate=pl.CostEstimate(flops=flops, bytes_accessed=moved, transcendentals=0),
    )(targets, members_wide, high, low, taper)


def local(anomalies, panel, pair_code, pair_offset):
    del pair_code, pair_offset
    taper = taper_by_code()
    targets = jnp.swapaxes(anomalies, 2, 3)
    members_wide = with_halo(anomalies)
    first_product = localized_product(targets, members_wide, panel, taper)
    second_product = localized_product(targets, members_wide, first_product, taper)
    return (first_product, second_product)


def solution(mesh):
    placed = (
        P("lat", "lon", None, None),
        P("lat", "lon", None, None),
        P("lat", "lon", None),
        P(None, "lat", "lon", None),
    )
    return jax.shard_map(
        local,
        mesh=mesh,
        in_specs=placed,
        out_specs=(P("lat", "lon", None, None), P("lat", "lon", None, None)),
        check_vma=False,
    )
```

time: 185 us -> 155 us (0.84)
  the two profiles are of different devices: /device:TPU:96 before, /device:TPU:2 now
where the time goes in v1:
time: 155 us; the launch traced here: 154 us
  starting transfers between devices  87.1 us (56%)
  Pallas kernels  40.8 us (26%)
  waiting for transfers between devices  8.96 us (6%)
  other arithmetic  8.5 us (5%)
  local copies, waits for them, and re-layouts  7.63 us (5%)
    pallas_call x2, Pallas kernels, localized_product(): pl.pallas_call(product_kernel, out_shape=jax.ShapeDtypeStruct(field_in.sh...  40.8 us
    ppermute x3, starting transfers between devices, with_halo(): south_east = lax.ppermute(first_row[:, :1], ('lon', 'lat'), both(up, -1))  17.7 us
    ppermute x3, starting transfers between devices, with_halo(): south = lax.ppermute(first_row, 'lat', up)  16.4 us
    ppermute x3, starting transfers between devices, with_halo(): east = lax.ppermute(cells[:, :1], 'lon', left)  15.8 us
    ppermute x3, starting transfers between devices, with_halo(): north_east = lax.ppermute(last_row[:, :1], ('lon', 'lat'), both(down, -1))  10.9 us
    ppermute x3, starting transfers between devices, with_halo(): south_west = lax.ppermute(first_row[:, -1:], ('lon', 'lat'), both(up, 1))  10.9 us
    ppermute x3, starting transfers between devices, with_halo(): north = lax.ppermute(last_row, 'lat', down)  7.64 us
    ppermute x3, starting transfers between devices, with_halo(): north_west = lax.ppermute(last_row[:, -1:], ('lon', 'lat'), both(down, 1))  7.08 us
  transfers between devices with their start and end apart: 24, of which 3 were waited for; matrix products, arithmetic and copies ran while one was open for 6% of the time, Pallas kernels for 0%

profile of v1, /device:TPU:2, one launch (start us, length us, event | category | flops | bytes accessed | tf_op | source)
XLA Modules:
  0.0 154.0 jit_solution(13361719674484108124)
XLA Ops:
  1.4 3.3 %collective-permute-start = (bf16[1,1,80,128]{3,2,1,0:T(8,128)(2,1)S(1)}, bf16[1,1,80,128]{3,2,1,0:T(8,128)(2,1)S(1)}, u32[]{:S(2)}, u32[]{:S(2)}) collective-permute-start(bf16[1,1,80,128]{3,2,1,0:T(8,128)(2,1)S(1)} %get-tuple-element.22), channel_id=1, source_target_pairs={{0,9},{8,17},{16,25},{24,33},{32,41},{40,49},{48,57},{56,65},{64,7... | collective-permute-start | bytes 61448 | tf_op jit(solution)/shard_map/ppermute | solution.py:63
  4.7 5.7 %collective-permute-start.5 = (bf16[1,1,80,128]{3,2,1,0:T(8,128)(2,1)S(1)}, bf16[1,1,80,128]{3,2,1,0:T(8,128)(2,1)S(1)}, u32[]{:S(2)}, u32[]{:S(2)}) collective-permute-start(bf16[1,1,80,128]{3,2,1,0:T(8,128)(2,1)S(1)} %get-tuple-element.23), channel_id=1, source_target_pairs={{1,8},{9,16},{17,24},{25,32},{33,40},{41,48},{49,56},{57,64},{65,7... | collective-permute-start | bytes 61448 | tf_op jit(solution)/shard_map/ppermute | solution.py:65
  10.4 4.9 %collective-permute-start.2 = (bf16[1,1,80,128]{3,2,1,0:T(8,128)(2,1)S(1)}, bf16[1,1,80,128]{3,2,1,0:T(8,128)(2,1)S(1)}, u32[]{:S(2)}, u32[]{:S(2)}) collective-permute-start(bf16[1,1,80,128]{3,2,1,0:T(8,128)(2,1)S(1)} %get-tuple-element.24), channel_id=1, source_target_pairs={{0,121},{8,1},{16,9},{24,17},{32,25},{40,33},{48,41},{56,49},{64,5... | collective-permute-start | bytes 61448 | tf_op jit(solution)/shard_map/ppermute | solution.py:64
  15.2 4.6 %collective-permute-start.7 = (bf16[1,1,80,128]{3,2,1,0:T(8,128)(2,1)S(1)}, bf16[1,1,80,128]{3,2,1,0:T(8,128)(2,1)S(1)}, u32[]{:S(2)}, u32[]{:S(2)}) collective-permute-start(bf16[1,1,80,128]{3,2,1,0:T(8,128)(2,1)S(1)} %get-tuple-element.25), channel_id=1, source_target_pairs={{1,120},{9,0},{17,8},{25,16},{33,24},{41,32},{49,40},{57,48},{65,5... | collective-permute-start | bytes 61448 | tf_op jit(solution)/shard_map/ppermute | solution.py:66
  21.2 1.4 fusion.18
  22.7 1.7 %fusion.4.taper_ref = f32[9,128,128]{2,1,0:T(8,128)} fusion(s32[128,128]{1,0:T(8,128)S(1)} %get-tuple-element.30, s32[9]{0:T(128)S(1)} %get-tuple-element.32, s32[128,128]{1,0:T(8,128)S(1)} %get-tuple-element.31, s32[9]{0:T(128)S(1)} %get-tuple-element.33), kind=kLoop, calls=%fused_computation.12 | loop fusion | flops 5160960 | bytes 720968 | tf_op jit(solution)/shard_map/div | solution.py:40
  25.1 4.8 %collective-permute-start.4 = (bf16[2,1,80,128]{3,2,1,0:T(8,128)(2,1)S(1)}, bf16[2,1,80,128]{3,2,1,0:T(8,128)(2,1)S(1)}, u32[]{:S(2)}, u32[]{:S(2)}) collective-permute-start(bf16[2,1,80,128]{3,2,1,0:T(8,128)(2,1)S(1)} %get-tuple-element.29), channel_id=1, source_target_pairs={{8,0},{16,8},{24,16},{32,24},{40,32},{48,40},{56,48},{64,56},{72,6... | collective-permute-start | bytes 122888 | tf_op jit(solution)/shard_map/ppermute | solution.py:62
  29.9 1.9 %collective-permute-start.8 = (f32[1,1,128,128]{3,2,1,0:T(8,128)S(1)}, f32[1,1,128,128]{3,2,1,0:T(8,128)S(1)}, u32[]{:S(2)}, u32[]{:S(2)}) collective-permute-start(f32[1,1,128,128]{3,2,1,0:T(8,128)S(1)} %get-tuple-element.14), channel_id=1, source_target_pairs={{0,9},{8,17},{16,25},{24,33},{32,41},{40,49},{48,57},{56,65},{64,7... | collective-permute-start | bytes 196616 | tf_op jit(solution)/shard_map/ppermute | solution.py:63
  31.8 3.3 %collective-permute-start.13 = (f32[1,1,128,128]{3,2,1,0:T(8,128)S(1)}, f32[1,1,128,128]{3,2,1,0:T(8,128)}, u32[]{:S(2)}, u32[]{:S(2)}) collective-permute-start(f32[1,1,128,128]{3,2,1,0:T(8,128)S(1)} %get-tuple-element.15), channel_id=1, source_target_pairs={{1,8},{9,16},{17,24},{25,32},{33,40},{41,48},{49,56},{57,64},{65,7... | collective-permute-start | bytes 196616 | tf_op jit(solution)/shard_map/ppermute | solution.py:65
  35.2 1.9 %collective-permute-start.9 = (f32[1,8,128,128]{3,2,1,0:T(8,128)S(1)}, f32[1,8,128,128]{3,2,1,0:T(8,128)S(1)}, u32[]{:S(2)}, u32[]{:S(2)}) collective-permute-start(f32[1,8,128,128]{3,2,1,0:T(8,128)S(1)} %get-tuple-element.18), channel_id=1, source_target_pairs={{0,1},{1,2},{2,3},{3,4},{4,5},{5,6},{6,7},{8,9},{9,10},{10,11},{11... | collective-permute-start | bytes 1572872 | tf_op jit(solution)/shard_map/ppermute | solution.py:59
  37.1 6.0 %collective-permute-start.14 = (f32[1,8,128,128]{3,2,1,0:T(8,128)S(1)}, f32[1,8,128,128]{3,2,1,0:T(8,128)S(1)}, u32[]{:S(2)}, u32[]{:S(2)}) collective-permute-start(f32[1,8,128,128]{3,2,1,0:T(8,128)S(1)} %get-tuple-element.19), channel_id=1, source_target_pairs={{1,0},{2,1},{3,2},{4,3},{5,4},{6,5},{7,6},{9,8},{10,9},{11,10},{12... | collective-permute-start | bytes 1572872 | tf_op jit(solution)/shard_map/ppermute | solution.py:60
  43.9 4.1 %collective-permute-start.10 = (f32[1,1,128,128]{3,2,1,0:T(8,128)}, f32[1,1,128,128]{3,2,1,0:T(8,128)}, u32[]{:S(2)}, u32[]{:S(2)}) collective-permute-start(f32[1,1,128,128]{3,2,1,0:T(8,128)} %get-tuple-element.16), channel_id=1, source_target_pairs={{0,121},{8,1},{16,9},{24,17},{32,25},{40,33},{48,41},{56,49},{64,5... | collective-permute-start | bytes 196616 | tf_op jit(solution)/shard_map/ppermute | solution.py:64
  48.0 2.6 %collective-permute-start.1 = (bf16[1,8,80,128]{3,2,1,0:T(8,128)(2,1)}, bf16[1,8,80,128]{3,2,1,0:T(8,128)(2,1)}, u32[]{:S(2)}, u32[]{:S(2)}) collective-permute-start(bf16[1,8,80,128]{3,2,1,0:T(8,128)(2,1)} %get-tuple-element.26), channel_id=1, source_target_pairs={{0,1},{1,2},{2,3},{3,4},{4,5},{5,6},{6,7},{8,9},{9,10},{10,11},{11... | collective-permute-start | bytes 491528 | tf_op jit(solution)/shard_map/ppermute | solution.py:59
  50.7 5.5 %collective-permute-start.6 = (bf16[1,8,80,128]{3,2,1,0:T(8,128)(2,1)}, bf16[1,8,80,128]{3,2,1,0:T(8,128)(2,1)}, u32[]{:S(2)}, u32[]{:S(2)}) collective-permute-start(bf16[1,8,80,128]{3,2,1,0:T(8,128)(2,1)} %get-tuple-element.27), channel_id=1, source_target_pairs={{1,0},{2,1},{3,2},{4,3},{5,4},{6,5},{7,6},{9,8},{10,9},{11,10},{12... | collective-permute-start | bytes 491528 | tf_op jit(solution)/shard_map/ppermute | solution.py:60
  57.0 1.0 copy.4
  58.0 5.3 %collective-permute-start.15 = (f32[1,1,128,128]{3,2,1,0:T(8,128)}, f32[1,1,128,128]{3,2,1,0:T(8,128)S(1)}, u32[]{:S(2)}, u32[]{:S(2)}) collective-permute-start(f32[1,1,128,128]{3,2,1,0:T(8,128)} %get-tuple-element.17), channel_id=1, source_target_pairs={{1,120},{9,0},{17,8},{25,16},{33,24},{41,32},{49,40},{57,48},{65,5... | collective-permute-start | bytes 196616 | tf_op jit(solution)/shard_map/ppermute | solution.py:66
  63.4 5.3 %collective-permute-start.12 = (f32[2,1,128,128]{3,2,1,0:T(8,128)}, f32[2,1,128,128]{3,2,1,0:T(8,128)S(1)}, u32[]{:S(2)}, u32[]{:S(2)}) collective-permute-start(f32[2,1,128,128]{3,2,1,0:T(8,128)} %get-tuple-element.21), channel_id=1, source_target_pairs={{8,0},{16,8},{24,16},{32,24},{40,32},{48,40},{56,48},{64,56},{72,6... | collective-permute-start | bytes 393224 | tf_op jit(solution)/shard_map/ppermute | solution.py:62
  68.8 2.1 %maximum_maximum_fusion.2.members_ref = bf16[4,10,80,128]{3,2,1,0:T(8,128)(2,1)} fusion(bf16[1,1,80,128]{3,2,1,0:T(8,128)(2,1)} %copy-done.8, bf16[1,8,80,128]{3,2,1,0:T(8,128)(2,1)} %collective-permute-done.6, bf16[1,1,80,128]{3,2,1,0:T(8,128)(2,1)} %copy-done.6, bf16[2,1,80,128]{3,2,1,0:T(8,128)(2,1)} %copy-done.4, ...), kind=kLoop, calls=%fused_computation.9 | loop fusion | flops 3276800 | bytes 1638400 | tf_op jit(solution)/shard_map/concatenate | solution.py:70
  71.6 2.7 %fusion = (bf16[4,10,128,128]{3,2,1,0:T(8,128)(2,1)}, bf16[4,10,128,128]{3,2,1,0:T(8,128)(2,1)}) fusion(f32[1,1,128,128]{3,2,1,0:T(8,128)S(1)} %collective-permute-done.15, f32[1,8,128,128]{3,2,1,0:T(8,128)S(1)} %collective-permute-done.14, f32[1,1,128,128]{3,2,1,0:T(8,128)} %collective-permute-done.13, f32[2,1,128,128]{3,2,1,0:T(8,128)S(1)} %collective-permute-done.12, ...), kind=kLoop, calls=%fused_computation.4 | loop fusion | flops 7864320 | bytes 5242880 | tf_op jit(solution)/shard_map/convert_element_type | solution.py:103
  74.3 20.4 %shard_map.41 = f32[2,8,128,128]{3,2,1,0:T(8,128)} custom-call(bf16[2,8,128,80]{3,2,1,0:T(8,128)(2,1)} %bitcast.1, bf16[4,10,80,128]{3,2,1,0:T(8,128)(2,1)} %maximum_maximum_fusion.2.members_ref, bf16[4,10,128,128]{3,2,1,0:T(8,128)(2,1)} %get-tuple-element.5.high_ref, bf16[4,10,128,128]{3,2,1,0:T(8,128)(2,1)} %get-tuple-element.4.low_ref, ...), custom_call_target="tpu_custom_call" | custom-call | flops 2189426688 | bytes 5406720 | tf_op jit(solution)/shard_map/pallas_call | solution.py:108
  94.7 1.4 fusion.15
  96.1 3.1 %collective-permute-start.17 = (f32[1,8,128,128]{3,2,1,0:T(8,128)S(1)}, f32[1,8,128,128]{3,2,1,0:T(8,128)S(1)}, u32[]{:S(2)}, u32[]{:S(2)}) collective-permute-start(f32[1,8,128,128]{3,2,1,0:T(8,128)S(1)} %get-tuple-element.10), channel_id=1, source_target_pairs={{0,1},{1,2},{2,3},{3,4},{4,5},{5,6},{6,7},{8,9},{9,10},{10,11},{11... | collective-permute-start | bytes 1572872 | tf_op jit(solution)/shard_map/ppermute | solution.py:59
  99.2 4.9 %collective-permute-start.22 = (f32[1,8,128,128]{3,2,1,0:T(8,128)S(1)}, f32[1,8,128,128]{3,2,1,0:T(8,128)S(1)}, u32[]{:S(2)}, u32[]{:S(2)}) collective-permute-start(f32[1,8,128,128]{3,2,1,0:T(8,128)S(1)} %get-tuple-element.11), channel_id=1, source_target_pairs={{1,0},{2,1},{3,2},{4,3},{5,4},{6,5},{7,6},{9,8},{10,9},{11,10},{12... | collective-permute-start | bytes 1572872 | tf_op jit(solution)/shard_map/ppermute | solution.py:60
  104.1 1.9 %collective-permute-start.16 = (f32[1,1,128,128]{3,2,1,0:T(8,128)S(1)}, f32[1,1,128,128]{3,2,1,0:T(8,128)S(1)}, u32[]{:S(2)}, u32[]{:S(2)}) collective-permute-start(f32[1,1,128,128]{3,2,1,0:T(8,128)S(1)} %get-tuple-element.6), channel_id=1, source_target_pairs={{0,9},{8,17},{16,25},{24,33},{32,41},{40,49},{48,57},{56,65},{64,7... | collective-permute-start | bytes 196616 | tf_op jit(solution)/shard_map/ppermute | solution.py:63
  106.0 7.9 %collective-permute-start.23 = (f32[1,1,128,128]{3,2,1,0:T(8,128)S(1)}, f32[1,1,128,128]{3,2,1,0:T(8,128)S(1)}, u32[]{:S(2)}, u32[]{:S(2)}) collective-permute-start(f32[1,1,128,128]{3,2,1,0:T(8,128)S(1)} %get-tuple-element.7), channel_id=1, source_target_pairs={{1,120},{9,0},{17,8},{25,16},{33,24},{41,32},{49,40},{57,48},{65,5... | collective-permute-start | bytes 196616 | tf_op jit(solution)/shard_map/ppermute | solution.py:66
  113.9 1.9 %collective-permute-start.21 = (f32[1,1,128,128]{3,2,1,0:T(8,128)S(1)}, f32[1,1,128,128]{3,2,1,0:T(8,128)S(1)}, u32[]{:S(2)}, u32[]{:S(2)}) collective-permute-start(f32[1,1,128,128]{3,2,1,0:T(8,128)S(1)} %get-tuple-element.8), channel_id=1, source_target_pairs={{1,8},{9,16},{17,24},{25,32},{33,40},{41,48},{49,56},{57,64},{65,7... | collective-permute-start | bytes 196616 | tf_op jit(solution)/shard_map/ppermute | solution.py:65
  115.9 5.7 %collective-permute-start.20 = (f32[2,1,128,128]{3,2,1,0:T(8,128)S(1)}, f32[2,1,128,128]{3,2,1,0:T(8,128)S(1)}, u32[]{:S(2)}, u32[]{:S(2)}) collective-permute-start(f32[2,1,128,128]{3,2,1,0:T(8,128)S(1)} %get-tuple-element.13), channel_id=1, source_target_pairs={{8,0},{16,8},{24,16},{32,24},{40,32},{48,40},{56,48},{64,56},{72,6... | collective-permute-start | bytes 393224 | tf_op jit(solution)/shard_map/ppermute | solution.py:62
  121.6 2.4 %collective-permute-done.21 = f32[1,1,128,128]{3,2,1,0:T(8,128)S(1)} collective-permute-done((f32[1,1,128,128]{3,2,1,0:T(8,128)S(1)}, f32[1,1,128,128]{3,2,1,0:T(8,128)S(1)}, u32[]{:S(2)}, u32[]{:S(2)}) %collective-permute-start.21) | collective-permute-done | bytes 65568 | tf_op jit(solution)/shard_map/ppermute | solution.py:65
  124.0 1.9 %collective-permute-start.18 = (f32[1,1,128,128]{3,2,1,0:T(8,128)S(1)}, f32[1,1,128,128]{3,2,1,0:T(8,128)S(1)}, u32[]{:S(2)}, u32[]{:S(2)}) collective-permute-start(f32[1,1,128,128]{3,2,1,0:T(8,128)S(1)} %get-tuple-element.9), channel_id=1, source_target_pairs={{0,121},{8,1},{16,9},{24,17},{32,25},{40,33},{48,41},{56,49},{64,5... | collective-permute-start | bytes 196616 | tf_op jit(solution)/shard_map/ppermute | solution.py:64
  125.9 5.8 %collective-permute-done.18 = f32[1,1,128,128]{3,2,1,0:T(8,128)S(1)} collective-permute-done((f32[1,1,128,128]{3,2,1,0:T(8,128)S(1)}, f32[1,1,128,128]{3,2,1,0:T(8,128)S(1)}, u32[]{:S(2)}, u32[]{:S(2)}) %collective-permute-start.18) | collective-permute-done | bytes 65568 | tf_op jit(solution)/shard_map/ppermute | solution.py:64
  131.7 1.9 %fusion.1 = (bf16[4,10,128,128]{3,2,1,0:T(8,128)(2,1)}, bf16[4,10,128,128]{3,2,1,0:T(8,128)(2,1)}) fusion(f32[1,1,128,128]{3,2,1,0:T(8,128)S(1)} %collective-permute-done.23, f32[1,8,128,128]{3,2,1,0:T(8,128)S(1)} %collective-permute-done.22, f32[1,1,128,128]{3,2,1,0:T(8,128)S(1)} %collective-permute-done.21, ...), kind=kLoop, calls=%fused_computation.5 | loop fusion | flops 7864320 | bytes 5242880 | tf_op jit(solution)/shard_map/convert_element_type | solution.py:103
  133.6 20.4 %shard_map.42 = f32[2,8,128,128]{3,2,1,0:T(8,128)} custom-call(bf16[2,8,128,80]{3,2,1,0:T(8,128)(2,1)} %bitcast.2, bf16[4,10,80,128]{3,2,1,0:T(8,128)(2,1)} %maximum_maximum_fusion.2.members_ref, bf16[4,10,128,128]{3,2,1,0:T(8,128)(2,1)} %get-tuple-element.3.high_ref, bf16[4,10,128,128]{3,2,1,0:T(8,128)(2,1)} %get-tuple-element.2.low_ref, ...), custom_call_target="tpu_custom_call" | custom-call | flops 2189426688 | bytes 5406720 | tf_op jit(solution)/shard_map/pallas_call | solution.py:108
  (54 shorter events, 5.5 us)
Async XLA Ops:
  1.4 23.7 %collective-permute-start = (bf16[1,1,80,128]{3,2,1,0:T(8,128)(2,1)S(1)}, bf16[1,1,80,128]{3,2,1,0:T(8,128)(2,1)S(1)}, u32[]{:S(2)}, u32[]{:S(2)}) collective-permute-start(bf16[1,1,80,128]{3,2,1,0:T(8,128)(2,1)S(1)} %get-tuple-element.22), channel_id=1, source_target_pairs={{0,9},{8,17},{16,25},{24,33},{32,41},{40,49},{48,57},{56,65},{64,7... | collective-permute-start | bytes 61448 | tf_op jit(solution)/shard_map/ppermute | solution.py:63
  4.7 25.2 %collective-permute-start.5 = (bf16[1,1,80,128]{3,2,1,0:T(8,128)(2,1)S(1)}, bf16[1,1,80,128]{3,2,1,0:T(8,128)(2,1)S(1)}, u32[]{:S(2)}, u32[]{:S(2)}) collective-permute-start(bf16[1,1,80,128]{3,2,1,0:T(8,128)(2,1)S(1)} %get-tuple-element.23), channel_id=1, source_target_pairs={{1,8},{9,16},{17,24},{25,32},{33,40},{41,48},{49,56},{57,64},{65,7... | collective-permute-start | bytes 61448 | tf_op jit(solution)/shard_map/ppermute | solution.py:65
  10.4 21.5 %collective-permute-start.2 = (bf16[1,1,80,128]{3,2,1,0:T(8,128)(2,1)S(1)}, bf16[1,1,80,128]{3,2,1,0:T(8,128)(2,1)S(1)}, u32[]{:S(2)}, u32[]{:S(2)}) collective-permute-start(bf16[1,1,80,128]{3,2,1,0:T(8,128)(2,1)S(1)} %get-tuple-element.24), channel_id=1, source_target_pairs={{0,121},{8,1},{16,9},{24,17},{32,25},{40,33},{48,41},{56,49},{64,5... | collective-permute-start | bytes 61448 | tf_op jit(solution)/shard_map/ppermute | solution.py:64
  15.2 19.9 %collective-permute-start.7 = (bf16[1,1,80,128]{3,2,1,0:T(8,128)(2,1)S(1)}, bf16[1,1,80,128]{3,2,1,0:T(8,128)(2,1)S(1)}, u32[]{:S(2)}, u32[]{:S(2)}) collective-permute-start(bf16[1,1,80,128]{3,2,1,0:T(8,128)(2,1)S(1)} %get-tuple-element.25), channel_id=1, source_target_pairs={{1,120},{9,0},{17,8},{25,16},{33,24},{41,32},{49,40},{57,48},{65,5... | collective-permute-start | bytes 61448 | tf_op jit(solution)/shard_map/ppermute | solution.py:66
  20.6 16.5 %collective-permute-start.3 = (bf16[2,1,80,128]{3,2,1,0:T(8,128)(2,1)S(1)}, bf16[2,1,80,128]{3,2,1,0:T(8,128)(2,1)S(1)}, u32[]{:S(2)}, u32[]{:S(2)}) collective-permute-start(bf16[2,1,80,128]{3,2,1,0:T(8,128)(2,1)S(1)} %get-tuple-element.28), channel_id=1, source_target_pairs={{0,8},{8,16},{16,24},{24,32},{32,40},{40,48},{48,56},{56,64},{64,7... | collective-permute-start | bytes 122888 | tf_op jit(solution)/shard_map/ppermute | solution.py:61
  21.2 21.9 %copy-start.2 = (bf16[2,8,80,128]{3,2,1,0:T(8,128)(2,1)S(1)}, bf16[2,8,80,128]{3,2,1,0:T(8,128)(2,1)}, u32[]{:S(2)}) copy-start(bf16[2,8,80,128]{3,2,1,0:T(8,128)(2,1)} %param.4) | copy-start | bytes 983044
  25.1 31.1 %copy-start.5 = (bf16[1,1,80,128]{3,2,1,0:T(8,128)(2,1)}, bf16[1,1,80,128]{3,2,1,0:T(8,128)(2,1)S(1)}, u32[]{:S(2)}) copy-start(bf16[1,1,80,128]{3,2,1,0:T(8,128)(2,1)S(1)} %collective-permute-done) | copy-start | bytes 61444
  25.1 18.8 %collective-permute-start.4 = (bf16[2,1,80,128]{3,2,1,0:T(8,128)(2,1)S(1)}, bf16[2,1,80,128]{3,2,1,0:T(8,128)(2,1)S(1)}, u32[]{:S(2)}, u32[]{:S(2)}) collective-permute-start(bf16[2,1,80,128]{3,2,1,0:T(8,128)(2,1)S(1)} %get-tuple-element.29), channel_id=1, source_target_pairs={{8,0},{16,8},{24,16},{32,24},{40,32},{48,40},{56,48},{64,56},{72,6... | collective-permute-start | bytes 122888 | tf_op jit(solution)/shard_map/ppermute | solution.py:62
  29.9 26.3 %copy-start.6 = (bf16[1,1,80,128]{3,2,1,0:T(8,128)(2,1)}, bf16[1,1,80,128]{3,2,1,0:T(8,128)(2,1)S(1)}, u32[]{:S(2)}) copy-start(bf16[1,1,80,128]{3,2,1,0:T(8,128)(2,1)S(1)} %collective-permute-done.5) | copy-start | bytes 61444
  29.9 18.1 %collective-permute-start.8 = (f32[1,1,128,128]{3,2,1,0:T(8,128)S(1)}, f32[1,1,128,128]{3,2,1,0:T(8,128)S(1)}, u32[]{:S(2)}, u32[]{:S(2)}) collective-permute-start(f32[1,1,128,128]{3,2,1,0:T(8,128)S(1)} %get-tuple-element.14), channel_id=1, source_target_pairs={{0,9},{8,17},{16,25},{24,33},{32,41},{40,49},{48,57},{56,65},{64,7... | collective-permute-start | bytes 196616 | tf_op jit(solution)/shard_map/ppermute | solution.py:63
  31.8 24.4 %copy-start.7 = (bf16[1,1,80,128]{3,2,1,0:T(8,128)(2,1)}, bf16[1,1,80,128]{3,2,1,0:T(8,128)(2,1)S(1)}, u32[]{:S(2)}) copy-start(bf16[1,1,80,128]{3,2,1,0:T(8,128)(2,1)S(1)} %collective-permute-done.2) | copy-start | bytes 61444
  31.8 18.8 %collective-permute-start.13 = (f32[1,1,128,128]{3,2,1,0:T(8,128)S(1)}, f32[1,1,128,128]{3,2,1,0:T(8,128)}, u32[]{:S(2)}, u32[]{:S(2)}) collective-permute-start(f32[1,1,128,128]{3,2,1,0:T(8,128)S(1)} %get-tuple-element.15), channel_id=1, source_target_pairs={{1,8},{9,16},{17,24},{25,32},{33,40},{41,48},{49,56},{57,64},{65,7... | collective-permute-start | bytes 196616 | tf_op jit(solution)/shard_map/ppermute | solution.py:65
  35.1 21.1 %copy-start.8 = (bf16[1,1,80,128]{3,2,1,0:T(8,128)(2,1)}, bf16[1,1,80,128]{3,2,1,0:T(8,128)(2,1)S(1)}, u32[]{:S(2)}) copy-start(bf16[1,1,80,128]{3,2,1,0:T(8,128)(2,1)S(1)} %collective-permute-done.7) | copy-start | bytes 61444
  35.2 36.5 %collective-permute-start.9 = (f32[1,8,128,128]{3,2,1,0:T(8,128)S(1)}, f32[1,8,128,128]{3,2,1,0:T(8,128)S(1)}, u32[]{:S(2)}, u32[]{:S(2)}) collective-permute-start(f32[1,8,128,128]{3,2,1,0:T(8,128)S(1)} %get-tuple-element.18), channel_id=1, source_target_pairs={{0,1},{1,2},{2,3},{3,4},{4,5},{5,6},{6,7},{8,9},{9,10},{10,11},{11... | collective-permute-start | bytes 1572872 | tf_op jit(solution)/shard_map/ppermute | solution.py:59
  37.1 13.6 %copy-start.3 = (bf16[2,1,80,128]{3,2,1,0:T(8,128)(2,1)}, bf16[2,1,80,128]{3,2,1,0:T(8,128)(2,1)S(1)}, u32[]{:S(2)}) copy-start(bf16[2,1,80,128]{3,2,1,0:T(8,128)(2,1)S(1)} %collective-permute-done.3) | copy-start | bytes 122884
  37.1 34.5 %collective-permute-start.14 = (f32[1,8,128,128]{3,2,1,0:T(8,128)S(1)}, f32[1,8,128,128]{3,2,1,0:T(8,128)S(1)}, u32[]{:S(2)}, u32[]{:S(2)}) collective-permute-start(f32[1,8,128,128]{3,2,1,0:T(8,128)S(1)} %get-tuple-element.19), channel_id=1, source_target_pairs={{1,0},{2,1},{3,2},{4,3},{5,4},{6,5},{7,6},{9,8},{10,9},{11,10},{12... | collective-permute-start | bytes 1572872 | tf_op jit(solution)/shard_map/ppermute | solution.py:60
  43.9 6.8 %copy-start.4 = (bf16[2,1,80,128]{3,2,1,0:T(8,128)(2,1)}, bf16[2,1,80,128]{3,2,1,0:T(8,128)(2,1)S(1)}, u32[]{:S(2)}) copy-start(bf16[2,1,80,128]{3,2,1,0:T(8,128)(2,1)S(1)} %collective-permute-done.4) | copy-start | bytes 122884
  43.9 14.1 %collective-permute-start.10 = (f32[1,1,128,128]{3,2,1,0:T(8,128)}, f32[1,1,128,128]{3,2,1,0:T(8,128)}, u32[]{:S(2)}, u32[]{:S(2)}) collective-permute-start(f32[1,1,128,128]{3,2,1,0:T(8,128)} %get-tuple-element.16), channel_id=1, source_target_pairs={{0,121},{8,1},{16,9},{24,17},{32,25},{40,33},{48,41},{56,49},{64,5... | collective-permute-start | bytes 196616 | tf_op jit(solution)/shard_map/ppermute | solution.py:64
  48.0 15.3 %collective-permute-start.1 = (bf16[1,8,80,128]{3,2,1,0:T(8,128)(2,1)}, bf16[1,8,80,128]{3,2,1,0:T(8,128)(2,1)}, u32[]{:S(2)}, u32[]{:S(2)}) collective-permute-start(bf16[1,8,80,128]{3,2,1,0:T(8,128)(2,1)} %get-tuple-element.26), channel_id=1, source_target_pairs={{0,1},{1,2},{2,3},{3,4},{4,5},{5,6},{6,7},{8,9},{9,10},{10,11},{11... | collective-permute-start | bytes 491528 | tf_op jit(solution)/shard_map/ppermute | solution.py:59
  50.7 12.7 %collective-permute-start.6 = (bf16[1,8,80,128]{3,2,1,0:T(8,128)(2,1)}, bf16[1,8,80,128]{3,2,1,0:T(8,128)(2,1)}, u32[]{:S(2)}, u32[]{:S(2)}) collective-permute-start(bf16[1,8,80,128]{3,2,1,0:T(8,128)(2,1)} %get-tuple-element.27), channel_id=1, source_target_pairs={{1,0},{2,1},{3,2},{4,3},{5,4},{6,5},{7,6},{9,8},{10,9},{11,10},{12... | collective-permute-start | bytes 491528 | tf_op jit(solution)/shard_map/ppermute | solution.py:60
  58.0 12.8 %collective-permute-start.15 = (f32[1,1,128,128]{3,2,1,0:T(8,128)}, f32[1,1,128,128]{3,2,1,0:T(8,128)S(1)}, u32[]{:S(2)}, u32[]{:S(2)}) collective-permute-start(f32[1,1,128,128]{3,2,1,0:T(8,128)} %get-tuple-element.17), channel_id=1, source_target_pairs={{1,120},{9,0},{17,8},{25,16},{33,24},{41,32},{49,40},{57,48},{65,5... | collective-permute-start | bytes 196616 | tf_op jit(solution)/shard_map/ppermute | solution.py:66
  63.3 8.3 %collective-permute-start.11 = (f32[2,1,128,128]{3,2,1,0:T(8,128)}, f32[2,1,128,128]{3,2,1,0:T(8,128)S(1)}, u32[]{:S(2)}, u32[]{:S(2)}) collective-permute-start(f32[2,1,128,128]{3,2,1,0:T(8,128)} %get-tuple-element.20), channel_id=1, source_target_pairs={{0,8},{8,16},{16,24},{24,32},{32,40},{40,48},{48,56},{56,64},{64,7... | collective-permute-start | bytes 393224 | tf_op jit(solution)/shard_map/ppermute | solution.py:61
  63.4 8.2 %collective-permute-start.12 = (f32[2,1,128,128]{3,2,1,0:T(8,128)}, f32[2,1,128,128]{3,2,1,0:T(8,128)S(1)}, u32[]{:S(2)}, u32[]{:S(2)}) collective-permute-start(f32[2,1,128,128]{3,2,1,0:T(8,128)} %get-tuple-element.21), channel_id=1, source_target_pairs={{8,0},{16,8},{24,16},{32,24},{40,32},{48,40},{56,48},{64,56},{72,6... | collective-permute-start | bytes 393224 | tf_op jit(solution)/shard_map/ppermute | solution.py:62
  94.7 9.4 %copy-start.1 = (f32[2,8,128,128]{3,2,1,0:T(8,128)S(1)}, f32[2,8,128,128]{3,2,1,0:T(8,128)}, u32[]{:S(2)}) copy-start(f32[2,8,128,128]{3,2,1,0:T(8,128)} %shard_map.41) | copy-start | bytes 3145732
  96.1 35.6 %collective-permute-start.17 = (f32[1,8,128,128]{3,2,1,0:T(8,128)S(1)}, f32[1,8,128,128]{3,2,1,0:T(8,128)S(1)}, u32[]{:S(2)}, u32[]{:S(2)}) collective-permute-start(f32[1,8,128,128]{3,2,1,0:T(8,128)S(1)} %get-tuple-element.10), channel_id=1, source_target_pairs={{0,1},{1,2},{2,3},{3,4},{4,5},{5,6},{6,7},{8,9},{9,10},{10,11},{11... | collective-permute-start | bytes 1572872 | tf_op jit(solution)/shard_map/ppermute | solution.py:59
  99.2 32.5 %collective-permute-start.22 = (f32[1,8,128,128]{3,2,1,0:T(8,128)S(1)}, f32[1,8,128,128]{3,2,1,0:T(8,128)S(1)}, u32[]{:S(2)}, u32[]{:S(2)}) collective-permute-start(f32[1,8,128,128]{3,2,1,0:T(8,128)S(1)} %get-tuple-element.11), channel_id=1, source_target_pairs={{1,0},{2,1},{3,2},{4,3},{5,4},{6,5},{7,6},{9,8},{10,9},{11,10},{12... | collective-permute-start | bytes 1572872 | tf_op jit(solution)/shard_map/ppermute | solution.py:60
  104.1 11.8 %collective-permute-start.16 = (f32[1,1,128,128]{3,2,1,0:T(8,128)S(1)}, f32[1,1,128,128]{3,2,1,0:T(8,128)S(1)}, u32[]{:S(2)}, u32[]{:S(2)}) collective-permute-start(f32[1,1,128,128]{3,2,1,0:T(8,128)S(1)} %get-tuple-element.6), channel_id=1, source_target_pairs={{0,9},{8,17},{16,25},{24,33},{32,41},{40,49},{48,57},{56,65},{64,7... | collective-permute-start | bytes 196616 | tf_op jit(solution)/shard_map/ppermute | solution.py:63
  106.0 9.9 %collective-permute-start.23 = (f32[1,1,128,128]{3,2,1,0:T(8,128)S(1)}, f32[1,1,128,128]{3,2,1,0:T(8,128)S(1)}, u32[]{:S(2)}, u32[]{:S(2)}) collective-permute-start(f32[1,1,128,128]{3,2,1,0:T(8,128)S(1)} %get-tuple-element.7), channel_id=1, source_target_pairs={{1,120},{9,0},{17,8},{25,16},{33,24},{41,32},{49,40},{57,48},{65,5... | collective-permute-start | bytes 196616 | tf_op jit(solution)/shard_map/ppermute | solution.py:66
  113.9 10.1 %collective-permute-start.21 = (f32[1,1,128,128]{3,2,1,0:T(8,128)S(1)}, f32[1,1,128,128]{3,2,1,0:T(8,128)S(1)}, u32[]{:S(2)}, u32[]{:S(2)}) collective-permute-start(f32[1,1,128,128]{3,2,1,0:T(8,128)S(1)} %get-tuple-element.8), channel_id=1, source_target_pairs={{1,8},{9,16},{17,24},{25,32},{33,40},{41,48},{49,56},{57,64},{65,7... | collective-permute-start | bytes 196616 | tf_op jit(solution)/shard_map/ppermute | solution.py:65
  115.8 15.8 %collective-permute-start.19 = (f32[2,1,128,128]{3,2,1,0:T(8,128)S(1)}, f32[2,1,128,128]{3,2,1,0:T(8,128)S(1)}, u32[]{:S(2)}, u32[]{:S(2)}) collective-permute-start(f32[2,1,128,128]{3,2,1,0:T(8,128)S(1)} %get-tuple-element.12), channel_id=1, source_target_pairs={{0,8},{8,16},{16,24},{24,32},{32,40},{40,48},{48,56},{56,64},{64,7... | collective-permute-start | bytes 393224 | tf_op jit(solution)/shard_map/ppermute | solution.py:61
  115.9 15.8 %collective-permute-start.20 = (f32[2,1,128,128]{3,2,1,0:T(8,128)S(1)}, f32[2,1,128,128]{3,2,1,0:T(8,128)S(1)}, u32[]{:S(2)}, u32[]{:S(2)}) collective-permute-start(f32[2,1,128,128]{3,2,1,0:T(8,128)S(1)} %get-tuple-element.13), channel_id=1, source_target_pairs={{8,0},{16,8},{24,16},{32,24},{40,32},{48,40},{56,48},{64,56},{72,6... | collective-permute-start | bytes 393224 | tf_op jit(solution)/shard_map/ppermute | solution.py:62
  124.0 7.7 %collective-permute-start.18 = (f32[1,1,128,128]{3,2,1,0:T(8,128)S(1)}, f32[1,1,128,128]{3,2,1,0:T(8,128)S(1)}, u32[]{:S(2)}, u32[]{:S(2)}) collective-permute-start(f32[1,1,128,128]{3,2,1,0:T(8,128)S(1)} %get-tuple-element.9), channel_id=1, source_target_pairs={{0,121},{8,1},{16,9},{24,17},{32,25},{40,33},{48,41},{56,49},{64,5... | collective-permute-start | bytes 196616 | tf_op jit(solution)/shard_map/ppermute | solution.py:64
  (1 other events, 3.2 us)

commit v2 on v1

--- a/solution.py
+++ b/solution.py
@@ -70,22 +70,24 @@
     return jnp.concatenate([top, middle, bottom], axis=0)
 
 
-def product_kernel(targets_ref, members_ref, high_ref, low_ref, taper_ref, out_ref):
-    lat_blocks, lon_blocks = out_ref.shape[0], out_ref.shape[1]
+def product_kernel(field_at, targets_ref, members_ref, field_ref, taper_ref, out_ref):
+    lat_blocks, lon_blocks, columns, rank = out_ref.shape
 
     def one_block(t, carry):
         p = t // lon_blocks
         q = t % lon_blocks
         target = targets_ref[p, q]
-        total = jnp.zeros(out_ref.shape[2:], jnp.float32)
+        total = jnp.zeros((columns, rank), jnp.float32)
         for code in range(CODES):
             dr, dc = code // 3, code % 3
-            gram = jnp.dot(target, members_ref[p + dr, q + dc], preferred_element_type=jnp.float32)
+            gram = jnp.dot(
+                target, members_ref[p + dr, q + dc, :K, :], preferred_element_type=jnp.float32
+            )
             tile = gram * taper_ref[code]
             tile_high = tile.astype(jnp.bfloat16)
             tile_low = (tile - tile_high.astype(jnp.float32)).astype(jnp.bfloat16)
-            field_high = high_ref[p + dr, q + dc]
-            field_low = low_ref[p + dr, q + dc]
+            field_high = field_ref[p + dr, q + dc, field_at : field_at + columns, :]
+            field_low = field_ref[p + dr, q + dc, field_at + columns : field_at + 2 * columns, :]
             total = total + jnp.dot(tile_high, field_high, preferred_element_type=jnp.float32)
             total = total + jnp.dot(tile_high, field_low, preferred_element_type=jnp.float32)
             total = total + jnp.dot(tile_low, field_high, preferred_element_type=jnp.float32)
@@ -95,32 +97,36 @@
     lax.fori_loop(0, lat_blocks * lon_blocks, one_block, 0)
 
 
-def localized_product(targets, members_wide, field_in, taper):
-    lat_blocks, lon_blocks, columns, rank = field_in.shape
-    field_wide = with_halo(field_in)
-    rounded = lax.reduce_precision(field_wide, exponent_bits=8, mantissa_bits=7)
-    high = rounded.astype(jnp.bfloat16)
-    low = (field_wide - rounded).astype(jnp.bfloat16)
+def split_high_low(field):
+    rounded = lax.reduce_precision(field, exponent_bits=8, mantissa_bits=7)
+    return rounded.astype(jnp.bfloat16), (field - rounded).astype(jnp.bfloat16)
+
+
+def localized_product(targets, members_wide, field_wide, field_at, out_like):
+    lat_blocks, lon_blocks, columns, rank = out_like.shape
+    taper = taper_by_code()
     blocks = lat_blocks * lon_blocks
     flops = blocks * CODES * 2 * columns * (K * columns + 3 * columns * rank)
-    moved = high.size * 4 + members_wide.size * 2 + targets.size * 2 + taper.size * 4 + field_in.size * 4
+    moved = field_wide.size * 2 + members_wide.size * 2 + targets.size * 2 + taper.size * 4 + out_like.size * 4
     vmem = pl.BlockSpec(memory_space=pltpu.VMEM)
     return pl.pallas_call(
-        product_kernel,
-        out_shape=jax.ShapeDtypeStruct(field_in.shape, jnp.float32),
-        in_specs=[vmem] * 5,
+        functools.partial(product_kernel, field_at),
+        out_shape=jax.ShapeDtypeStruct(out_like.shape, jnp.float32),
+        in_specs=[vmem] * 4,
         out_specs=vmem,
         cost_estimate=pl.CostEstimate(flops=flops, bytes_accessed=moved, transcendentals=0),
-    )(targets, members_wide, high, low, taper)
+    )(targets, members_wide, field_wide, taper)
 
 
 def local(anomalies, panel, pair_code, pair_offset):
     del pair_code, pair_offset
-    taper = taper_by_code()
     targets = jnp.swapaxes(anomalies, 2, 3)
-    members_wide = with_halo(anomalies)
-    first_product = localized_product(targets, members_wide, panel, taper)
-    second_product = localized_product(targets, members_wide, first_product, taper)
+    panel_high, panel_low = split_high_low(panel)
+    first_wide = with_halo(jnp.concatenate([anomalies, panel_high, panel_low], axis=2))
+    first_product = localized_product(targets, first_wide, first_wide, K, panel)
+    product_high, product_low = split_high_low(first_product)
+    second_wide = with_halo(jnp.concatenate([product_high, product_low], axis=2))
+    second_product = localized_product(targets, first_wide, second_wide, 0, first_product)
     return (first_product, second_product)
 
 

time: 155 us -> 135 us (0.87)
  starting transfers between devices: 87.1 us -> 57 us
  waiting for transfers between devices: 8.96 us -> 16.8 us
  local copies, waits for them, and re-layouts: 7.63 us -> 1.1 us
  other arithmetic: 8.5 us -> 14.4 us
  Pallas kernels: 40.8 us -> 42.6 us
    ppermute x3 -> x2, starting transfers between devices: 17.7 us -> 9.33 us  [with_halo(): south_east = lax.ppermute(first_row[:, :1], ('lon', 'lat'), both(up, -1))]
    ppermute x3 -> x2, waiting for transfers between devices: 0.75 us -> 7.51 us  [with_halo(): west = lax.ppermute(cells[:, -1:], 'lon', right)]
    ppermute x3 -> x2, starting transfers between devices: 16.4 us -> 10.8 us  [with_halo(): south = lax.ppermute(first_row, 'lat', up)]
    ppermute x3 -> x2, starting transfers between devices: 15.8 us -> 10.7 us  [with_halo(): east = lax.ppermute(cells[:, :1], 'lon', left)]
    concatenate x1 -> x2, other arithmetic: 2.11 us -> 7.16 us  [with_halo(): return jnp.concatenate([top, middle, bottom], axis=0)]
    ppermute x3 -> x2, waiting for transfers between devices: 5.77 us -> 1.33 us  [with_halo(): north_east = lax.ppermute(last_row[:, :1], ('lon', 'lat'), both(down, -1))]
    ppermute x3 -> x2, waiting for transfers between devices: 0.01 us -> 4.33 us  [with_halo(): north_west = lax.ppermute(last_row[:, -1:], ('lon', 'lat'), both(down, 1))]
    ppermute x3 -> x2, waiting for transfers between devices: 0.01 us -> 3.66 us  [with_halo(): south_east = lax.ppermute(first_row[:, :1], ('lon', 'lat'), both(up, -1))]
  transfers between devices with their start and end apart: 24 -> 16, of which waited for: 3 -> 4; matrix products, arithmetic and copies ran while one was open for 6% -> 3% of each run, Pallas kernels for 0% -> 0%
where the time goes in v2:
time: 135 us; the launch traced here: 133 us
  starting transfers between devices  57 us (42%)
  Pallas kernels  42.6 us (32%)
  waiting for transfers between devices  16.8 us (12%)
  other arithmetic  14.4 us (11%)
    pallas_call x2, Pallas kernels, localized_product(): pl.pallas_call(functools.partial(product_kernel, field_at), out_shape=jax...  42.6 us
    ppermute x2, starting transfers between devices, with_halo(): south = lax.ppermute(first_row, 'lat', up)  10.8 us
    ppermute x2, starting transfers between devices, with_halo(): east = lax.ppermute(cells[:, :1], 'lon', left)  10.7 us
    ppermute x2, starting transfers between devices, with_halo(): south_east = lax.ppermute(first_row[:, :1], ('lon', 'lat'), both(up, -1))  9.33 us
    ppermute x2, starting transfers between devices, with_halo(): north_east = lax.ppermute(last_row[:, :1], ('lon', 'lat'), both(down, -1))  8.17 us
    ppermute x2, starting transfers between devices, with_halo(): south_west = lax.ppermute(first_row[:, -1:], ('lon', 'lat'), both(up, 1))  7.67 us
    ppermute x2, waiting for transfers between devices, with_halo(): west = lax.ppermute(cells[:, -1:], 'lon', right)  7.51 us
    concatenate x2, other arithmetic, with_halo(): return jnp.concatenate([top, middle, bottom], axis=0)  7.16 us
  transfers between devices with their start and end apart: 16, of which 4 were waited for; matrix products, arithmetic and copies ran while one was open for 3% of the time, Pallas kernels for 0%

profile of v2, /device:TPU:2, one launch (start us, length us, event | category | flops | bytes accessed | tf_op | source)
XLA Modules:
  0.0 132.9 jit_solution(16077530309638193545)
XLA Ops:
  0.6 1.5 %reduce-precision_convert_fusion.1 = (bf16[2,8,128,128]{3,2,1,0:T(8,128)(2,1)S(1)}, bf16[2,8,128,128]{3,2,1,0:T(8,128)(2,1)S(1)}) fusion(f32[2,8,128,128]{3,2,1,0:T(8,128)} %param.5), kind=kLoop, calls=%fused_computation.17 | loop fusion | flops 1048576 | bytes 2097152 | tf_op jit(solution)/shard_map/convert_element_type | solution.py:102
  2.2 1.5 %pad_maximum_fusion.6 = (bf16[1,1,336,128]{3,2,1,0:T(8,128)(2,1)S(1)}, bf16[1,1,336,128]{3,2,1,0:T(8,128)(2,1)S(1)}, bf16[1,1,336,128]{3,2,1,0:T(8,128)(2,1)S(1)}, bf16[1,1,336,128]{3,2,1,0:T(8,128)(2,1)}) fusion(bf16[2,8,128,128]{3,2,1,0:T(8,128)(2,1)S(1)} %get-tuple-element.21, bf16[2,8,128,128]{3,2,1,0:T(8,128)(2,1)S(1)} %get-tuple-element.20, ...), kind=kLoop, calls=%fused_computation.46 | loop fusion | flops 1032192 | bytes 1720320 | tf_op jit(solution)/shard_map/slice | solution.py:63
  3.6 3.3 %collective-permute-start = (bf16[1,1,336,128]{3,2,1,0:T(8,128)(2,1)S(1)}, bf16[1,1,336,128]{3,2,1,0:T(8,128)(2,1)S(1)}, u32[]{:S(2)}, u32[]{:S(2)}) collective-permute-start(bf16[1,1,336,128]{3,2,1,0:T(8,128)(2,1)S(1)} %get-tuple-element.2), channel_id=1, source_target_pairs={{0,9},{8,17},{16,25},{24,33},{32,41},{40,49},{48,57},{56,65},{64,7... | collective-permute-start | bytes 258056 | tf_op jit(solution)/shard_map/ppermute | solution.py:63
  6.9 7.4 %collective-permute-start.7 = (bf16[1,1,336,128]{3,2,1,0:T(8,128)(2,1)S(1)}, bf16[1,1,336,128]{3,2,1,0:T(8,128)(2,1)}, u32[]{:S(2)}, u32[]{:S(2)}) collective-permute-start(bf16[1,1,336,128]{3,2,1,0:T(8,128)(2,1)S(1)} %get-tuple-element.3), channel_id=1, source_target_pairs={{1,120},{9,0},{17,8},{25,16},{33,24},{41,32},{49,40},{57,48},{65,5... | collective-permute-start | bytes 258056 | tf_op jit(solution)/shard_map/ppermute | solution.py:66
  14.3 1.9 %collective-permute-start.5 = (bf16[1,1,336,128]{3,2,1,0:T(8,128)(2,1)S(1)}, bf16[1,1,336,128]{3,2,1,0:T(8,128)(2,1)}, u32[]{:S(2)}, u32[]{:S(2)}) collective-permute-start(bf16[1,1,336,128]{3,2,1,0:T(8,128)(2,1)S(1)} %get-tuple-element.4), channel_id=1, source_target_pairs={{1,8},{9,16},{17,24},{25,32},{33,40},{41,48},{49,56},{57,64},{65,7... | collective-permute-start | bytes 258056 | tf_op jit(solution)/shard_map/ppermute | solution.py:65
  16.3 0.1 pad_maximum_fusion
  16.4 0.1 fusion.20
  16.5 3.2 %collective-permute-start.1 = (bf16[1,8,336,128]{3,2,1,0:T(8,128)(2,1)S(1)}, bf16[1,8,336,128]{3,2,1,0:T(8,128)(2,1)S(1)}, u32[]{:S(2)}, u32[]{:S(2)}) collective-permute-start(bf16[1,8,336,128]{3,2,1,0:T(8,128)(2,1)S(1)} %get-tuple-element.6), channel_id=1, source_target_pairs={{0,1},{1,2},{2,3},{3,4},{4,5},{5,6},{6,7},{8,9},{9,10},{10,11},{11... | collective-permute-start | bytes 2064392 | tf_op jit(solution)/shard_map/ppermute | solution.py:59
  19.7 4.7 %collective-permute-start.6 = (bf16[1,8,336,128]{3,2,1,0:T(8,128)(2,1)S(1)}, bf16[1,8,336,128]{3,2,1,0:T(8,128)(2,1)}, u32[]{:S(2)}, u32[]{:S(2)}) collective-permute-start(bf16[1,8,336,128]{3,2,1,0:T(8,128)(2,1)S(1)} %get-tuple-element.7), channel_id=1, source_target_pairs={{1,0},{2,1},{3,2},{4,3},{5,4},{6,5},{7,6},{9,8},{10,9},{11,10},{12... | collective-permute-start | bytes 2064392 | tf_op jit(solution)/shard_map/ppermute | solution.py:60
  24.4 0.8 pad_maximum_fusion.2
  25.2 0.1 broadcast_subtract_fusion
  25.3 6.3 %collective-permute-start.2 = (bf16[1,1,336,128]{3,2,1,0:T(8,128)(2,1)}, bf16[1,1,336,128]{3,2,1,0:T(8,128)(2,1)}, u32[]{:S(2)}, u32[]{:S(2)}) collective-permute-start(bf16[1,1,336,128]{3,2,1,0:T(8,128)(2,1)} %get-tuple-element.5), channel_id=1, source_target_pairs={{0,121},{8,1},{16,9},{24,17},{32,25},{40,33},{48,41},{56,49},{64,5... | collective-permute-start | bytes 258056 | tf_op jit(solution)/shard_map/ppermute | solution.py:64
  31.6 0.1 collective-permute-start.3
  31.7 5.3 %collective-permute-start.4 = (bf16[2,1,336,128]{3,2,1,0:T(8,128)(2,1)}, bf16[2,1,336,128]{3,2,1,0:T(8,128)(2,1)}, u32[]{:S(2)}, u32[]{:S(2)}) collective-permute-start(bf16[2,1,336,128]{3,2,1,0:T(8,128)(2,1)} %get-tuple-element.9), channel_id=1, source_target_pairs={{8,0},{16,8},{24,16},{32,24},{40,32},{48,40},{56,48},{64,56},{72,6... | collective-permute-start | bytes 516104 | tf_op jit(solution)/shard_map/ppermute | solution.py:62
  37.0 1.7 %fusion.4.taper_ref = f32[9,128,128]{2,1,0:T(8,128)} fusion(s32[128,128]{1,0:T(8,128)S(1)} %get-tuple-element.22, s32[9]{0:T(128)S(1)} %get-tuple-element.24, s32[128,128]{1,0:T(8,128)S(1)} %get-tuple-element.23, s32[9]{0:T(128)S(1)} %get-tuple-element.25), kind=kLoop, calls=%fused_computation.24 | loop fusion | flops 5160960 | bytes 720968 | tf_op jit(solution)/shard_map/div | solution.py:40
  38.8 1.0 copy.4
  39.8 1.3 collective-permute-done.2
  41.1 7.5 %collective-permute-done.3 = bf16[2,1,336,128]{3,2,1,0:T(8,128)(2,1)} collective-permute-done((bf16[2,1,336,128]{3,2,1,0:T(8,128)(2,1)}, bf16[2,1,336,128]{3,2,1,0:T(8,128)(2,1)}, u32[]{:S(2)}, u32[]{:S(2)}) %collective-permute-start.3) | collective-permute-done | bytes 172064 | tf_op jit(solution)/shard_map/ppermute | solution.py:61
  48.6 4.6 %maximum_maximum_fusion.members_ref.field_ref = bf16[4,10,336,128]{3,2,1,0:T(8,128)(2,1)} fusion(bf16[1,1,336,128]{3,2,1,0:T(8,128)(2,1)} %collective-permute-done.7, bf16[1,8,336,128]{3,2,1,0:T(8,128)(2,1)} %collective-permute-done.6, bf16[1,1,336,128]{3,2,1,0:T(8,128)(2,1)} %collective-permute-done.5, bf16[2,1,336,128]{3,2,1,0:T(8,128)(2,1)} %collective-permute-done.4, ...), kind=kLoop, calls=%fused_computation | loop fusion | flops 37847040 | bytes 6881280 | tf_op jit(solution)/shard_map/concatenate | solution.py:70
  53.2 21.4 %shard_map.41 = f32[2,8,128,128]{3,2,1,0:T(8,128)} custom-call(bf16[2,8,128,80]{3,2,1,0:T(8,128)(2,1)} %bitcast.1, bf16[4,10,336,128]{3,2,1,0:T(8,128)(2,1)} %maximum_maximum_fusion.members_ref.field_ref, bf16[4,10,336,128]{3,2,1,0:T(8,128)(2,1)} %maximum_maximum_fusion.members_ref.field_ref, f32[9,128,128]{2,1,0:T(8,128)} %fusion.4.taper_ref), custom_call_target="tpu_custom_call" | custom-call | flops 2189426688 | bytes 8847360 | tf_op jit(solution)/shard_map/pallas_call | solution.py:112
  74.6 1.5 %reduce-precision_convert_fusion = (bf16[2,8,128,128]{3,2,1,0:T(8,128)(2,1)S(1)}, bf16[2,8,128,128]{3,2,1,0:T(8,128)(2,1)S(1)}) fusion(f32[2,8,128,128]{3,2,1,0:T(8,128)} %shard_map.41), kind=kLoop, calls=%fused_computation.15 | loop fusion | flops 1048576 | bytes 2097152 | tf_op jit(solution)/shard_map/convert_element_type | solution.py:102
  76.2 1.9 %collective-permute-start.9 = (bf16[1,8,256,128]{3,2,1,0:T(8,128)(2,1)S(1)}, bf16[1,8,256,128]{3,2,1,0:T(8,128)(2,1)S(1)}, u32[]{:S(2)}, u32[]{:S(2)}) collective-permute-start(bf16[1,8,256,128]{3,2,1,0:T(8,128)(2,1)S(1)} %get-tuple-element.14), channel_id=1, source_target_pairs={{0,1},{1,2},{2,3},{3,4},{4,5},{5,6},{6,7},{8,9},{9,10},{10,11},{11... | collective-permute-start | bytes 1572872 | tf_op jit(solution)/shard_map/ppermute | solution.py:59
  78.1 6.0 %collective-permute-start.14 = (bf16[1,8,256,128]{3,2,1,0:T(8,128)(2,1)S(1)}, bf16[1,8,256,128]{3,2,1,0:T(8,128)(2,1)S(1)}, u32[]{:S(2)}, u32[]{:S(2)}) collective-permute-start(bf16[1,8,256,128]{3,2,1,0:T(8,128)(2,1)S(1)} %get-tuple-element.15), channel_id=1, source_target_pairs={{1,0},{2,1},{3,2},{4,3},{5,4},{6,5},{7,6},{9,8},{10,9},{11,10},{12... | collective-permute-start | bytes 1572872 | tf_op jit(solution)/shard_map/ppermute | solution.py:60
  84.2 1.9 %collective-permute-start.8 = (bf16[1,1,256,128]{3,2,1,0:T(8,128)(2,1)S(1)}, bf16[1,1,256,128]{3,2,1,0:T(8,128)(2,1)S(1)}, u32[]{:S(2)}, u32[]{:S(2)}) collective-permute-start(bf16[1,1,256,128]{3,2,1,0:T(8,128)(2,1)S(1)} %get-tuple-element.10), channel_id=1, source_target_pairs={{0,9},{8,17},{16,25},{24,33},{32,41},{40,49},{48,57},{56,65},{64,7... | collective-permute-start | bytes 196616 | tf_op jit(solution)/shard_map/ppermute | solution.py:63
  86.1 1.9 %collective-permute-start.10 = (bf16[1,1,256,128]{3,2,1,0:T(8,128)(2,1)S(1)}, bf16[1,1,256,128]{3,2,1,0:T(8,128)(2,1)S(1)}, u32[]{:S(2)}, u32[]{:S(2)}) collective-permute-start(bf16[1,1,256,128]{3,2,1,0:T(8,128)(2,1)S(1)} %get-tuple-element.11), channel_id=1, source_target_pairs={{0,121},{8,1},{16,9},{24,17},{32,25},{40,33},{48,41},{56,49},{64,5... | collective-permute-start | bytes 196616 | tf_op jit(solution)/shard_map/ppermute | solution.py:64
  88.0 5.8 %collective-permute-start.13 = (bf16[1,1,256,128]{3,2,1,0:T(8,128)(2,1)S(1)}, bf16[1,1,256,128]{3,2,1,0:T(8,128)(2,1)S(1)}, u32[]{:S(2)}, u32[]{:S(2)}) collective-permute-start(bf16[1,1,256,128]{3,2,1,0:T(8,128)(2,1)S(1)} %get-tuple-element.12), channel_id=1, source_target_pairs={{1,8},{9,16},{17,24},{25,32},{33,40},{41,48},{49,56},{57,64},{65,7... | collective-permute-start | bytes 196616 | tf_op jit(solution)/shard_map/ppermute | solution.py:65
  93.8 4.3 %collective-permute-done.8 = bf16[1,1,256,128]{3,2,1,0:T(8,128)(2,1)S(1)} collective-permute-done((bf16[1,1,256,128]{3,2,1,0:T(8,128)(2,1)S(1)}, bf16[1,1,256,128]{3,2,1,0:T(8,128)(2,1)S(1)}, u32[]{:S(2)}, u32[]{:S(2)}) %collective-permute-start.8) | collective-permute-done | bytes 65568 | tf_op jit(solution)/shard_map/ppermute | solution.py:63
  98.1 5.4 %collective-permute-start.12 = (bf16[2,1,256,128]{3,2,1,0:T(8,128)(2,1)S(1)}, bf16[2,1,256,128]{3,2,1,0:T(8,128)(2,1)S(1)}, u32[]{:S(2)}, u32[]{:S(2)}) collective-permute-start(bf16[2,1,256,128]{3,2,1,0:T(8,128)(2,1)S(1)} %get-tuple-element.17), channel_id=1, source_target_pairs={{8,0},{16,8},{24,16},{32,24},{40,32},{48,40},{56,48},{64,56},{72,6... | collective-permute-start | bytes 393224 | tf_op jit(solution)/shard_map/ppermute | solution.py:62
  103.5 1.9 %collective-permute-start.15 = (bf16[1,1,256,128]{3,2,1,0:T(8,128)(2,1)S(1)}, bf16[1,1,256,128]{3,2,1,0:T(8,128)(2,1)S(1)}, u32[]{:S(2)}, u32[]{:S(2)}) collective-permute-start(bf16[1,1,256,128]{3,2,1,0:T(8,128)(2,1)S(1)} %get-tuple-element.13), channel_id=1, source_target_pairs={{1,120},{9,0},{17,8},{25,16},{33,24},{41,32},{49,40},{57,48},{65,5... | collective-permute-start | bytes 196616 | tf_op jit(solution)/shard_map/ppermute | solution.py:66
  105.4 3.7 %collective-permute-done.15 = bf16[1,1,256,128]{3,2,1,0:T(8,128)(2,1)S(1)} collective-permute-done((bf16[1,1,256,128]{3,2,1,0:T(8,128)(2,1)S(1)}, bf16[1,1,256,128]{3,2,1,0:T(8,128)(2,1)S(1)}, u32[]{:S(2)}, u32[]{:S(2)}) %collective-permute-start.15) | collective-permute-done | bytes 65568 | tf_op jit(solution)/shard_map/ppermute | solution.py:66
  109.1 2.6 %maximum_maximum_fusion.1.field_ref = bf16[4,10,256,128]{3,2,1,0:T(8,128)(2,1)} fusion(bf16[1,1,256,128]{3,2,1,0:T(8,128)(2,1)S(1)} %collective-permute-done.15, bf16[1,8,256,128]{3,2,1,0:T(8,128)(2,1)S(1)} %collective-permute-done.14, bf16[1,1,256,128]{3,2,1,0:T(8,128)(2,1)S(1)} %collective-permute-done.13, ...), kind=kLoop, calls=%fused_computation.1 | loop fusion | flops 26214400 | bytes 5242880 | tf_op jit(solution)/shard_map/concatenate | solution.py:70
  111.7 21.2 %shard_map.42 = f32[2,8,128,128]{3,2,1,0:T(8,128)} custom-call(bf16[2,8,128,80]{3,2,1,0:T(8,128)(2,1)} %bitcast.2, bf16[4,10,336,128]{3,2,1,0:T(8,128)(2,1)} %maximum_maximum_fusion.members_ref.field_ref, bf16[4,10,256,128]{3,2,1,0:T(8,128)(2,1)} %maximum_maximum_fusion.1.field_ref, f32[9,128,128]{2,1,0:T(8,128)} %fusion.4.taper_ref), custom_call_target="tpu_custom_call" | custom-call | flops 2189426688 | bytes 8028160 | tf_op jit(solution)/shard_map/pallas_call | solution.py:112
  (21 shorter events, 0.2 us)
Async XLA Ops:
  0.6 15.6 %copy-start = (bf16[2,8,80,128]{3,2,1,0:T(8,128)(2,1)S(1)}, bf16[2,8,80,128]{3,2,1,0:T(8,128)(2,1)}, u32[]{:S(2)}) copy-start(bf16[2,8,80,128]{3,2,1,0:T(8,128)(2,1)} %param.4) | copy-start | bytes 983044
  3.6 21.7 %collective-permute-start = (bf16[1,1,336,128]{3,2,1,0:T(8,128)(2,1)S(1)}, bf16[1,1,336,128]{3,2,1,0:T(8,128)(2,1)S(1)}, u32[]{:S(2)}, u32[]{:S(2)}) collective-permute-start(bf16[1,1,336,128]{3,2,1,0:T(8,128)(2,1)S(1)} %get-tuple-element.2), channel_id=1, source_target_pairs={{0,9},{8,17},{16,25},{24,33},{32,41},{40,49},{48,57},{56,65},{64,7... | collective-permute-start | bytes 258056 | tf_op jit(solution)/shard_map/ppermute | solution.py:63
  6.9 24.7 %collective-permute-start.7 = (bf16[1,1,336,128]{3,2,1,0:T(8,128)(2,1)S(1)}, bf16[1,1,336,128]{3,2,1,0:T(8,128)(2,1)}, u32[]{:S(2)}, u32[]{:S(2)}) collective-permute-start(bf16[1,1,336,128]{3,2,1,0:T(8,128)(2,1)S(1)} %get-tuple-element.3), channel_id=1, source_target_pairs={{1,120},{9,0},{17,8},{25,16},{33,24},{41,32},{49,40},{57,48},{65,5... | collective-permute-start | bytes 258056 | tf_op jit(solution)/shard_map/ppermute | solution.py:66
  14.3 17.4 %collective-permute-start.5 = (bf16[1,1,336,128]{3,2,1,0:T(8,128)(2,1)S(1)}, bf16[1,1,336,128]{3,2,1,0:T(8,128)(2,1)}, u32[]{:S(2)}, u32[]{:S(2)}) collective-permute-start(bf16[1,1,336,128]{3,2,1,0:T(8,128)(2,1)S(1)} %get-tuple-element.4), channel_id=1, source_target_pairs={{1,8},{9,16},{17,24},{25,32},{33,40},{41,48},{49,56},{57,64},{65,7... | collective-permute-start | bytes 258056 | tf_op jit(solution)/shard_map/ppermute | solution.py:65
  16.5 32.1 %collective-permute-start.1 = (bf16[1,8,336,128]{3,2,1,0:T(8,128)(2,1)S(1)}, bf16[1,8,336,128]{3,2,1,0:T(8,128)(2,1)S(1)}, u32[]{:S(2)}, u32[]{:S(2)}) collective-permute-start(bf16[1,8,336,128]{3,2,1,0:T(8,128)(2,1)S(1)} %get-tuple-element.6), channel_id=1, source_target_pairs={{0,1},{1,2},{2,3},{3,4},{4,5},{5,6},{6,7},{8,9},{9,10},{10,11},{11... | collective-permute-start | bytes 2064392 | tf_op jit(solution)/shard_map/ppermute | solution.py:59
  19.7 28.9 %collective-permute-start.6 = (bf16[1,8,336,128]{3,2,1,0:T(8,128)(2,1)S(1)}, bf16[1,8,336,128]{3,2,1,0:T(8,128)(2,1)}, u32[]{:S(2)}, u32[]{:S(2)}) collective-permute-start(bf16[1,8,336,128]{3,2,1,0:T(8,128)(2,1)S(1)} %get-tuple-element.7), channel_id=1, source_target_pairs={{1,0},{2,1},{3,2},{4,3},{5,4},{6,5},{7,6},{9,8},{10,9},{11,10},{12... | collective-permute-start | bytes 2064392 | tf_op jit(solution)/shard_map/ppermute | solution.py:60
  25.3 15.8 %collective-permute-start.2 = (bf16[1,1,336,128]{3,2,1,0:T(8,128)(2,1)}, bf16[1,1,336,128]{3,2,1,0:T(8,128)(2,1)}, u32[]{:S(2)}, u32[]{:S(2)}) collective-permute-start(bf16[1,1,336,128]{3,2,1,0:T(8,128)(2,1)} %get-tuple-element.5), channel_id=1, source_target_pairs={{0,121},{8,1},{16,9},{24,17},{32,25},{40,33},{48,41},{56,49},{64,5... | collective-permute-start | bytes 258056 | tf_op jit(solution)/shard_map/ppermute | solution.py:64
  31.6 17.0 %collective-permute-start.3 = (bf16[2,1,336,128]{3,2,1,0:T(8,128)(2,1)}, bf16[2,1,336,128]{3,2,1,0:T(8,128)(2,1)}, u32[]{:S(2)}, u32[]{:S(2)}) collective-permute-start(bf16[2,1,336,128]{3,2,1,0:T(8,128)(2,1)} %get-tuple-element.8), channel_id=1, source_target_pairs={{0,8},{8,16},{16,24},{24,32},{32,40},{40,48},{48,56},{56,64},{64,7... | collective-permute-start | bytes 516104 | tf_op jit(solution)/shard_map/ppermute | solution.py:61
  31.7 16.9 %collective-permute-start.4 = (bf16[2,1,336,128]{3,2,1,0:T(8,128)(2,1)}, bf16[2,1,336,128]{3,2,1,0:T(8,128)(2,1)}, u32[]{:S(2)}, u32[]{:S(2)}) collective-permute-start(bf16[2,1,336,128]{3,2,1,0:T(8,128)(2,1)} %get-tuple-element.9), channel_id=1, source_target_pairs={{8,0},{16,8},{24,16},{32,24},{40,32},{48,40},{56,48},{64,56},{72,6... | collective-permute-start | bytes 516104 | tf_op jit(solution)/shard_map/ppermute | solution.py:62
  76.2 32.9 %collective-permute-start.9 = (bf16[1,8,256,128]{3,2,1,0:T(8,128)(2,1)S(1)}, bf16[1,8,256,128]{3,2,1,0:T(8,128)(2,1)S(1)}, u32[]{:S(2)}, u32[]{:S(2)}) collective-permute-start(bf16[1,8,256,128]{3,2,1,0:T(8,128)(2,1)S(1)} %get-tuple-element.14), channel_id=1, source_target_pairs={{0,1},{1,2},{2,3},{3,4},{4,5},{5,6},{6,7},{8,9},{9,10},{10,11},{11... | collective-permute-start | bytes 1572872 | tf_op jit(solution)/shard_map/ppermute | solution.py:59
  78.1 31.0 %collective-permute-start.14 = (bf16[1,8,256,128]{3,2,1,0:T(8,128)(2,1)S(1)}, bf16[1,8,256,128]{3,2,1,0:T(8,128)(2,1)S(1)}, u32[]{:S(2)}, u32[]{:S(2)}) collective-permute-start(bf16[1,8,256,128]{3,2,1,0:T(8,128)(2,1)S(1)} %get-tuple-element.15), channel_id=1, source_target_pairs={{1,0},{2,1},{3,2},{4,3},{5,4},{6,5},{7,6},{9,8},{10,9},{11,10},{12... | collective-permute-start | bytes 1572872 | tf_op jit(solution)/shard_map/ppermute | solution.py:60
  84.2 14.0 %collective-permute-start.8 = (bf16[1,1,256,128]{3,2,1,0:T(8,128)(2,1)S(1)}, bf16[1,1,256,128]{3,2,1,0:T(8,128)(2,1)S(1)}, u32[]{:S(2)}, u32[]{:S(2)}) collective-permute-start(bf16[1,1,256,128]{3,2,1,0:T(8,128)(2,1)S(1)} %get-tuple-element.10), channel_id=1, source_target_pairs={{0,9},{8,17},{16,25},{24,33},{32,41},{40,49},{48,57},{56,65},{64,7... | collective-permute-start | bytes 196616 | tf_op jit(solution)/shard_map/ppermute | solution.py:63
  86.1 12.1 %collective-permute-start.10 = (bf16[1,1,256,128]{3,2,1,0:T(8,128)(2,1)S(1)}, bf16[1,1,256,128]{3,2,1,0:T(8,128)(2,1)S(1)}, u32[]{:S(2)}, u32[]{:S(2)}) collective-permute-start(bf16[1,1,256,128]{3,2,1,0:T(8,128)(2,1)S(1)} %get-tuple-element.11), channel_id=1, source_target_pairs={{0,121},{8,1},{16,9},{24,17},{32,25},{40,33},{48,41},{56,49},{64,5... | collective-permute-start | bytes 196616 | tf_op jit(solution)/shard_map/ppermute | solution.py:64
  88.0 15.5 %collective-permute-start.13 = (bf16[1,1,256,128]{3,2,1,0:T(8,128)(2,1)S(1)}, bf16[1,1,256,128]{3,2,1,0:T(8,128)(2,1)S(1)}, u32[]{:S(2)}, u32[]{:S(2)}) collective-permute-start(bf16[1,1,256,128]{3,2,1,0:T(8,128)(2,1)S(1)} %get-tuple-element.12), channel_id=1, source_target_pairs={{1,8},{9,16},{17,24},{25,32},{33,40},{41,48},{49,56},{57,64},{65,7... | collective-permute-start | bytes 196616 | tf_op jit(solution)/shard_map/ppermute | solution.py:65
  98.1 10.9 %collective-permute-start.11 = (bf16[2,1,256,128]{3,2,1,0:T(8,128)(2,1)S(1)}, bf16[2,1,256,128]{3,2,1,0:T(8,128)(2,1)S(1)}, u32[]{:S(2)}, u32[]{:S(2)}) collective-permute-start(bf16[2,1,256,128]{3,2,1,0:T(8,128)(2,1)S(1)} %get-tuple-element.16), channel_id=1, source_target_pairs={{0,8},{8,16},{16,24},{24,32},{32,40},{40,48},{48,56},{56,64},{64,7... | collective-permute-start | bytes 393224 | tf_op jit(solution)/shard_map/ppermute | solution.py:61
  98.1 10.9 %collective-permute-start.12 = (bf16[2,1,256,128]{3,2,1,0:T(8,128)(2,1)S(1)}, bf16[2,1,256,128]{3,2,1,0:T(8,128)(2,1)S(1)}, u32[]{:S(2)}, u32[]{:S(2)}) collective-permute-start(bf16[2,1,256,128]{3,2,1,0:T(8,128)(2,1)S(1)} %get-tuple-element.17), channel_id=1, source_target_pairs={{8,0},{16,8},{24,16},{32,24},{40,32},{48,40},{56,48},{64,56},{72,6... | collective-permute-start | bytes 393224 | tf_op jit(solution)/shard_map/ppermute | solution.py:62
  103.5 5.6 %collective-permute-start.15 = (bf16[1,1,256,128]{3,2,1,0:T(8,128)(2,1)S(1)}, bf16[1,1,256,128]{3,2,1,0:T(8,128)(2,1)S(1)}, u32[]{:S(2)}, u32[]{:S(2)}) collective-permute-start(bf16[1,1,256,128]{3,2,1,0:T(8,128)(2,1)S(1)} %get-tuple-element.13), channel_id=1, source_target_pairs={{1,120},{9,0},{17,8},{25,16},{33,24},{41,32},{49,40},{57,48},{65,5... | collective-permute-start | bytes 196616 | tf_op jit(solution)/shard_map/ppermute | solution.py:66

commit v3 on v2

--- a/solution.py
+++ b/solution.py
@@ -43,31 +43,12 @@
 def with_halo(cells):
     nlat = lax.axis_size("lat")
     nlon = lax.axis_size("lon")
-    down = [(i, i + 1) for i in range(nlat - 1)]
-    up = [(i + 1, i) for i in range(nlat - 1)]
-    right = [(i, (i + 1) % nlon) for i in range(nlon)]
-    left = [((i + 1) % nlon, i) for i in range(nlon)]
-
-    def both(lat_pairs, lon_shift):
-        return [
-            (b * nlat + a, ((b + lon_shift) % nlon) * nlat + c)
-            for a, c in lat_pairs
-            for b in range(nlon)
-        ]
-
-    first_row, last_row = cells[:1], cells[-1:]
-    north = lax.ppermute(last_row, "lat", down)
-    south = lax.ppermute(first_row, "lat", up)
-    west = lax.ppermute(cells[:, -1:], "lon", right)
-    east = lax.ppermute(cells[:, :1], "lon", left)
-    north_west = lax.ppermute(last_row[:, -1:], ("lon", "lat"), both(down, 1))
-    north_east = lax.ppermute(last_row[:, :1], ("lon", "lat"), both(down, -1))
-    south_west = lax.ppermute(first_row[:, -1:], ("lon", "lat"), both(up, 1))
-    south_east = lax.ppermute(first_row[:, :1], ("lon", "lat"), both(up, -1))
-    top = jnp.concatenate([north_west, north, north_east], axis=1)
-    middle = jnp.concatenate([west, cells, east], axis=1)
-    bottom = jnp.concatenate([south_west, south, south_east], axis=1)
-    return jnp.concatenate([top, middle, bottom], axis=0)
+    west = lax.ppermute(cells[:, -1:], "lon", [(i, (i + 1) % nlon) for i in range(nlon)])
+    east = lax.ppermute(cells[:, :1], "lon", [((i + 1) % nlon, i) for i in range(nlon)])
+    wider = jnp.concatenate([west, cells, east], axis=1)
+    north = lax.ppermute(wider[-1:], "lat", [(i, i + 1) for i in range(nlat - 1)])
+    south = lax.ppermute(wider[:1], "lat", [(i + 1, i) for i in range(nlat - 1)])
+    return jnp.concatenate([north, wider, south], axis=0)
 
 
 def product_kernel(field_at, targets_ref, members_ref, field_ref, taper_ref, out_ref):

time: 135 us -> 121 us (0.90)
  starting transfers between devices: 57 us -> 27.3 us
  waiting for transfers between devices: 16.8 us -> 35.5 us
  other arithmetic: 14.4 us -> 11.4 us
    ppermute x16 -> x8, starting transfers between devices: 57 us -> 27.3 us  [the longest x2 10.7 us: with_halo(): lax.ppermute(cells[:, :1], 'lon', [((i + 1) % nlon, i) for i in range(nlo...]
    ppermute x16 -> x8, waiting for transfers between devices: 16.8 us -> 35.5 us  [the longest x2 25.7 us: with_halo(): lax.ppermute(wider[-1:], 'lat', [(i, i + 1) for i in range(nlat - 1)])]
    concatenate x5 -> x4, other arithmetic: 7.34 us -> 5.74 us  [the longest x2 5.54 us: with_halo(): return jnp.concatenate([north, wider, south], axis=0)]
    slice x3 -> x2, other arithmetic: 2.23 us -> 0.85 us  [with_halo(): cells[:, -1:]]
  transfers between devices with their start and end apart: 16 -> 8, of which waited for: 4 -> 6; matrix products, arithmetic and copies ran while one was open for 3% -> 2% of each run, Pallas kernels for 0% -> 0%
where the time goes in v3:
time: 121 us; the launch traced here: 120 us
  Pallas kernels  42.6 us (35%)
  waiting for transfers between devices  35.5 us (29%)
  starting transfers between devices  27.3 us (23%)
  other arithmetic  11.4 us (9%)
  local copies, waits for them, and re-layouts  2.42 us (2%)
    pallas_call x2, Pallas kernels, localized_product(): pl.pallas_call(functools.partial(product_kernel, field_at), out_shape=jax...  42.6 us
    ppermute x2, waiting for transfers between devices, with_halo(): lax.ppermute(wider[-1:], 'lat', [(i, i + 1) for i in range(nlat - 1)])  25.7 us
    ppermute x2, starting transfers between devices, with_halo(): lax.ppermute(cells[:, :1], 'lon', [((i + 1) % nlon, i) for i in range(nlo...  10.7 us
    ppermute x2, starting transfers between devices, with_halo(): lax.ppermute(wider[:1], 'lat', [(i + 1, i) for i in range(nlat - 1)])  9.23 us
    ppermute x2, starting transfers between devices, with_halo(): lax.ppermute(wider[-1:], 'lat', [(i, i + 1) for i in range(nlat - 1)])  7.21 us
    ppermute x2, waiting for transfers between devices, with_halo(): lax.ppermute(cells[:, -1:], 'lon', [(i, (i + 1) % nlon) for i in range(nl...  6.87 us
    concatenate x2, other arithmetic, with_halo(): return jnp.concatenate([north, wider, south], axis=0)  5.54 us
    convert_element_type x2, other arithmetic, split_high_low(): rounded.astype(jnp.bfloat16)  3.01 us
  transfers between devices with their start and end apart: 8, of which 6 were waited for; matrix products, arithmetic and copies ran while one was open for 2% of the time, Pallas kernels for 0%

profile of v3, /device:TPU:2, one launch (start us, length us, event | category | flops | bytes accessed | tf_op | source)
XLA Modules:
  0.0 120.0 jit_solution(4474091366541877585)
XLA Ops:
  0.6 0.0 copy-start
  0.6 1.5 %reduce-precision_convert_fusion.1 = (bf16[2,8,128,128]{3,2,1,0:T(8,128)(2,1)S(1)}, bf16[2,8,128,128]{3,2,1,0:T(8,128)(2,1)S(1)}) fusion(f32[2,8,128,128]{3,2,1,0:T(8,128)} %param.5), kind=kLoop, calls=%fused_computation.6 | loop fusion | flops 1048576 | bytes 2097152 | tf_op jit(solution)/shard_map/convert_element_type | solution.py:83
  2.2 0.8 pad_maximum_fusion.6
  3.0 0.1 collective-permute-start
  3.1 5.3 %collective-permute-start.1 = (bf16[2,1,336,128]{3,2,1,0:T(8,128)(2,1)S(1)}, bf16[2,1,336,128]{3,2,1,0:T(8,128)(2,1)S(1)}, u32[]{:S(2)}, u32[]{:S(2)}) collective-permute-start(bf16[2,1,336,128]{3,2,1,0:T(8,128)(2,1)S(1)} %get-tuple-element.5), channel_id=1, source_target_pairs={{8,0},{16,8},{24,16},{32,24},{40,32},{48,40},{56,48},{64,56},{72,6... | collective-permute-start | bytes 516104 | tf_op jit(solution)/shard_map/ppermute | solution.py:47
  8.4 3.1 %collective-permute-done = bf16[2,1,336,128]{3,2,1,0:T(8,128)(2,1)S(1)} collective-permute-done((bf16[2,1,336,128]{3,2,1,0:T(8,128)(2,1)S(1)}, bf16[2,1,336,128]{3,2,1,0:T(8,128)(2,1)S(1)}, u32[]{:S(2)}, u32[]{:S(2)}) %collective-permute-start) | collective-permute-done | bytes 172064 | tf_op jit(solution)/shard_map/ppermute | solution.py:46
  11.5 0.0 collective-permute-done.1
  11.5 0.0 copy-done
  11.5 0.1 pad_maximum_fusion.2
  11.7 1.3 %fusion.14 = (bf16[1,10,336,128]{3,2,1,0:T(8,128)(2,1)}, bf16[1,10,336,128]{3,2,1,0:T(8,128)(2,1)}) fusion(bf16[2,10,336,128]{3,2,1,0:T(8,128)(2,1)S(1)} %pad_maximum_fusion.2), kind=kLoop, calls=%fused_computation.47 | loop fusion | bytes 3440640 | tf_op jit(solution)/shard_map/slice | solution.py:49
  13.0 3.8 %collective-permute-start.2 = (bf16[1,10,336,128]{3,2,1,0:T(8,128)(2,1)}, bf16[1,10,336,128]{3,2,1,0:T(8,128)(2,1)S(1)}, u32[]{:S(2)}, u32[]{:S(2)}) collective-permute-start(bf16[1,10,336,128]{3,2,1,0:T(8,128)(2,1)} %get-tuple-element.2), channel_id=1, source_target_pairs={{0,1},{1,2},{2,3},{3,4},{4,5},{5,6},{6,7},{8,9},{9,10},{10,11},{11... | collective-permute-start | bytes 2580488 | tf_op jit(solution)/shard_map/ppermute | solution.py:49
  16.8 4.1 %collective-permute-start.3 = (bf16[1,10,336,128]{3,2,1,0:T(8,128)(2,1)}, bf16[1,10,336,128]{3,2,1,0:T(8,128)(2,1)S(1)}, u32[]{:S(2)}, u32[]{:S(2)}) collective-permute-start(bf16[1,10,336,128]{3,2,1,0:T(8,128)(2,1)} %get-tuple-element.3), channel_id=1, source_target_pairs={{1,0},{2,1},{3,2},{4,3},{5,4},{6,5},{7,6},{9,8},{10,9},{11,10},{12... | collective-permute-start | bytes 2580488 | tf_op jit(solution)/shard_map/ppermute | solution.py:50
  20.9 1.0 copy.4
  22.0 0.1 broadcast_subtract_fusion
  22.1 1.7 %fusion.4.taper_ref = f32[9,128,128]{2,1,0:T(8,128)} fusion(s32[128,128]{1,0:T(8,128)S(1)} %get-tuple-element.14, s32[9]{0:T(128)S(1)} %get-tuple-element.16, s32[128,128]{1,0:T(8,128)S(1)} %get-tuple-element.15, s32[9]{0:T(128)S(1)} %get-tuple-element.17), kind=kLoop, calls=%fused_computation.13 | loop fusion | flops 5160960 | bytes 720968 | tf_op jit(solution)/shard_map/div | solution.py:40
  23.8 15.1 %collective-permute-done.2 = bf16[1,10,336,128]{3,2,1,0:T(8,128)(2,1)S(1)} collective-permute-done((bf16[1,10,336,128]{3,2,1,0:T(8,128)(2,1)}, bf16[1,10,336,128]{3,2,1,0:T(8,128)(2,1)S(1)}, u32[]{:S(2)}, u32[]{:S(2)}) %collective-permute-start.2) | collective-permute-done | bytes 860192 | tf_op jit(solution)/shard_map/ppermute | solution.py:49
  38.9 1.7 %collective-permute-done.3 = bf16[1,10,336,128]{3,2,1,0:T(8,128)(2,1)S(1)} collective-permute-done((bf16[1,10,336,128]{3,2,1,0:T(8,128)(2,1)}, bf16[1,10,336,128]{3,2,1,0:T(8,128)(2,1)S(1)}, u32[]{:S(2)}, u32[]{:S(2)}) %collective-permute-start.3) | collective-permute-done | bytes 860192 | tf_op jit(solution)/shard_map/ppermute | solution.py:50
  40.7 3.3 %pad_maximum_fusion.members_ref.field_ref = bf16[4,10,336,128]{3,2,1,0:T(8,128)(2,1)} fusion(bf16[1,10,336,128]{3,2,1,0:T(8,128)(2,1)S(1)} %collective-permute-done.3, bf16[2,1,336,128]{3,2,1,0:T(8,128)(2,1)S(1)} %collective-permute-done.1, bf16[2,8,128,128]{3,2,1,0:T(8,128)(2,1)S(1)} %get-tuple-element.13, bf16[2,8,128,128]{3,2,1,0:T(8,128)(2,1)S(1)} %get-tuple-element.12, ...), kind=kLoop, calls=%fused_computation | loop fusion | flops 24084480 | bytes 6881280 | tf_op jit(solution)/shard_map/concatenate | solution.py:51
  43.9 21.4 %shard_map.41 = f32[2,8,128,128]{3,2,1,0:T(8,128)} custom-call(bf16[2,8,128,80]{3,2,1,0:T(8,128)(2,1)} %bitcast.1, bf16[4,10,336,128]{3,2,1,0:T(8,128)(2,1)} %pad_maximum_fusion.members_ref.field_ref, bf16[4,10,336,128]{3,2,1,0:T(8,128)(2,1)} %pad_maximum_fusion.members_ref.field_ref, f32[9,128,128]{2,1,0:T(8,128)} %fusion.4.taper_ref), custom_call_target="tpu_custom_call" | custom-call | flops 2189426688 | bytes 8847360 | tf_op jit(solution)/shard_map/pallas_call | solution.py:93
  65.4 1.5 %reduce-precision_convert_fusion = (bf16[2,8,128,128]{3,2,1,0:T(8,128)(2,1)S(1)}, bf16[2,8,128,128]{3,2,1,0:T(8,128)(2,1)S(1)}) fusion(f32[2,8,128,128]{3,2,1,0:T(8,128)} %shard_map.41), kind=kLoop, calls=%fused_computation.4 | loop fusion | flops 1048576 | bytes 2097152 | tf_op jit(solution)/shard_map/convert_element_type | solution.py:83
  66.9 0.1 collective-permute-start.4
  67.0 5.3 %collective-permute-start.5 = (bf16[2,1,256,128]{3,2,1,0:T(8,128)(2,1)S(1)}, bf16[2,1,256,128]{3,2,1,0:T(8,128)(2,1)S(1)}, u32[]{:S(2)}, u32[]{:S(2)}) collective-permute-start(bf16[2,1,256,128]{3,2,1,0:T(8,128)(2,1)S(1)} %get-tuple-element.9), channel_id=1, source_target_pairs={{8,0},{16,8},{24,16},{32,24},{40,32},{48,40},{56,48},{64,56},{72,6... | collective-permute-start | bytes 393224 | tf_op jit(solution)/shard_map/ppermute | solution.py:47
  72.3 3.8 %collective-permute-done.4 = bf16[2,1,256,128]{3,2,1,0:T(8,128)(2,1)S(1)} collective-permute-done((bf16[2,1,256,128]{3,2,1,0:T(8,128)(2,1)S(1)}, bf16[2,1,256,128]{3,2,1,0:T(8,128)(2,1)S(1)}, u32[]{:S(2)}, u32[]{:S(2)}) %collective-permute-start.4) | collective-permute-done | bytes 131104 | tf_op jit(solution)/shard_map/ppermute | solution.py:46
  76.1 0.0 collective-permute-done.5
  76.1 0.1 pad_maximum_fusion.3
  76.2 0.1 fusion.15
  76.3 3.4 %collective-permute-start.6 = (bf16[1,10,256,128]{3,2,1,0:T(8,128)(2,1)S(1)}, bf16[1,10,256,128]{3,2,1,0:T(8,128)(2,1)S(1)}, u32[]{:S(2)}, u32[]{:S(2)}) collective-permute-start(bf16[1,10,256,128]{3,2,1,0:T(8,128)(2,1)S(1)} %get-tuple-element.6), channel_id=1, source_target_pairs={{0,1},{1,2},{2,3},{3,4},{4,5},{5,6},{6,7},{8,9},{9,10},{10,11},{11... | collective-permute-start | bytes 1966088 | tf_op jit(solution)/shard_map/ppermute | solution.py:49
  79.7 5.1 %collective-permute-start.7 = (bf16[1,10,256,128]{3,2,1,0:T(8,128)(2,1)S(1)}, bf16[1,10,256,128]{3,2,1,0:T(8,128)(2,1)S(1)}, u32[]{:S(2)}, u32[]{:S(2)}) collective-permute-start(bf16[1,10,256,128]{3,2,1,0:T(8,128)(2,1)S(1)} %get-tuple-element.7), channel_id=1, source_target_pairs={{1,0},{2,1},{3,2},{4,3},{5,4},{6,5},{7,6},{9,8},{10,9},{11,10},{12... | collective-permute-start | bytes 1966088 | tf_op jit(solution)/shard_map/ppermute | solution.py:50
  84.8 10.6 %collective-permute-done.6 = bf16[1,10,256,128]{3,2,1,0:T(8,128)(2,1)S(1)} collective-permute-done((bf16[1,10,256,128]{3,2,1,0:T(8,128)(2,1)S(1)}, bf16[1,10,256,128]{3,2,1,0:T(8,128)(2,1)S(1)}, u32[]{:S(2)}, u32[]{:S(2)}) %collective-permute-start.6) | collective-permute-done | bytes 655392 | tf_op jit(solution)/shard_map/ppermute | solution.py:49
  95.4 1.2 collective-permute-done.7
  96.6 2.3 %pad_maximum_fusion.1.field_ref = bf16[4,10,256,128]{3,2,1,0:T(8,128)(2,1)} fusion(bf16[1,10,256,128]{3,2,1,0:T(8,128)(2,1)S(1)} %collective-permute-done.7, bf16[2,1,256,128]{3,2,1,0:T(8,128)(2,1)S(1)} %collective-permute-done.5, bf16[2,8,128,128]{3,2,1,0:T(8,128)(2,1)S(1)} %get-tuple-element.11, bf16[2,8,128,128]{3,2,1,0:T(8,128)(2,1)S(1)} %get-tuple-element.10, ...), kind=kLoop, calls=%fused_computation.1 | loop fusion | flops 15728640 | bytes 5242880 | tf_op jit(solution)/shard_map/concatenate | solution.py:51
  98.9 21.2 %shard_map.42 = f32[2,8,128,128]{3,2,1,0:T(8,128)} custom-call(bf16[2,8,128,80]{3,2,1,0:T(8,128)(2,1)} %bitcast.2, bf16[4,10,336,128]{3,2,1,0:T(8,128)(2,1)} %pad_maximum_fusion.members_ref.field_ref, bf16[4,10,256,128]{3,2,1,0:T(8,128)(2,1)} %pad_maximum_fusion.1.field_ref, f32[9,128,128]{2,1,0:T(8,128)} %fusion.4.taper_ref), custom_call_target="tpu_custom_call" | custom-call | flops 2189426688 | bytes 8028160 | tf_op jit(solution)/shard_map/pallas_call | solution.py:93
  (4 shorter events, 0.0 us)
Async XLA Ops:
  0.6 10.9 %copy-start = (bf16[2,8,80,128]{3,2,1,0:T(8,128)(2,1)S(1)}, bf16[2,8,80,128]{3,2,1,0:T(8,128)(2,1)}, u32[]{:S(2)}) copy-start(bf16[2,8,80,128]{3,2,1,0:T(8,128)(2,1)} %param.4) | copy-start | bytes 983044
  3.0 8.5 %collective-permute-start = (bf16[2,1,336,128]{3,2,1,0:T(8,128)(2,1)S(1)}, bf16[2,1,336,128]{3,2,1,0:T(8,128)(2,1)S(1)}, u32[]{:S(2)}, u32[]{:S(2)}) collective-permute-start(bf16[2,1,336,128]{3,2,1,0:T(8,128)(2,1)S(1)} %get-tuple-element.4), channel_id=1, source_target_pairs={{0,8},{8,16},{16,24},{24,32},{32,40},{40,48},{48,56},{56,64},{64,7... | collective-permute-start | bytes 516104 | tf_op jit(solution)/shard_map/ppermute | solution.py:46
  3.1 8.4 %collective-permute-start.1 = (bf16[2,1,336,128]{3,2,1,0:T(8,128)(2,1)S(1)}, bf16[2,1,336,128]{3,2,1,0:T(8,128)(2,1)S(1)}, u32[]{:S(2)}, u32[]{:S(2)}) collective-permute-start(bf16[2,1,336,128]{3,2,1,0:T(8,128)(2,1)S(1)} %get-tuple-element.5), channel_id=1, source_target_pairs={{8,0},{16,8},{24,16},{32,24},{40,32},{48,40},{56,48},{64,56},{72,6... | collective-permute-start | bytes 516104 | tf_op jit(solution)/shard_map/ppermute | solution.py:47
  13.0 26.0 %collective-permute-start.2 = (bf16[1,10,336,128]{3,2,1,0:T(8,128)(2,1)}, bf16[1,10,336,128]{3,2,1,0:T(8,128)(2,1)S(1)}, u32[]{:S(2)}, u32[]{:S(2)}) collective-permute-start(bf16[1,10,336,128]{3,2,1,0:T(8,128)(2,1)} %get-tuple-element.2), channel_id=1, source_target_pairs={{0,1},{1,2},{2,3},{3,4},{4,5},{5,6},{6,7},{8,9},{9,10},{10,11},{11... | collective-permute-start | bytes 2580488 | tf_op jit(solution)/shard_map/ppermute | solution.py:49
  16.8 23.9 %collective-permute-start.3 = (bf16[1,10,336,128]{3,2,1,0:T(8,128)(2,1)}, bf16[1,10,336,128]{3,2,1,0:T(8,128)(2,1)S(1)}, u32[]{:S(2)}, u32[]{:S(2)}) collective-permute-start(bf16[1,10,336,128]{3,2,1,0:T(8,128)(2,1)} %get-tuple-element.3), channel_id=1, source_target_pairs={{1,0},{2,1},{3,2},{4,3},{5,4},{6,5},{7,6},{9,8},{10,9},{11,10},{12... | collective-permute-start | bytes 2580488 | tf_op jit(solution)/shard_map/ppermute | solution.py:50
  66.9 9.2 %collective-permute-start.4 = (bf16[2,1,256,128]{3,2,1,0:T(8,128)(2,1)S(1)}, bf16[2,1,256,128]{3,2,1,0:T(8,128)(2,1)S(1)}, u32[]{:S(2)}, u32[]{:S(2)}) collective-permute-start(bf16[2,1,256,128]{3,2,1,0:T(8,128)(2,1)S(1)} %get-tuple-element.8), channel_id=1, source_target_pairs={{0,8},{8,16},{16,24},{24,32},{32,40},{40,48},{48,56},{56,64},{64,7... | collective-permute-start | bytes 393224 | tf_op jit(solution)/shard_map/ppermute | solution.py:46
  67.0 9.1 %collective-permute-start.5 = (bf16[2,1,256,128]{3,2,1,0:T(8,128)(2,1)S(1)}, bf16[2,1,256,128]{3,2,1,0:T(8,128)(2,1)S(1)}, u32[]{:S(2)}, u32[]{:S(2)}) collective-permute-start(bf16[2,1,256,128]{3,2,1,0:T(8,128)(2,1)S(1)} %get-tuple-element.9), channel_id=1, source_target_pairs={{8,0},{16,8},{24,16},{32,24},{40,32},{48,40},{56,48},{64,56},{72,6... | collective-permute-start | bytes 393224 | tf_op jit(solution)/shard_map/ppermute | solution.py:47
  76.3 19.1 %collective-permute-start.6 = (bf16[1,10,256,128]{3,2,1,0:T(8,128)(2,1)S(1)}, bf16[1,10,256,128]{3,2,1,0:T(8,128)(2,1)S(1)}, u32[]{:S(2)}, u32[]{:S(2)}) collective-permute-start(bf16[1,10,256,128]{3,2,1,0:T(8,128)(2,1)S(1)} %get-tuple-element.6), channel_id=1, source_target_pairs={{0,1},{1,2},{2,3},{3,4},{4,5},{5,6},{6,7},{8,9},{9,10},{10,11},{11... | collective-permute-start | bytes 1966088 | tf_op jit(solution)/shard_map/ppermute | solution.py:49
  79.7 16.9 %collective-permute-start.7 = (bf16[1,10,256,128]{3,2,1,0:T(8,128)(2,1)S(1)}, bf16[1,10,256,128]{3,2,1,0:T(8,128)(2,1)S(1)}, u32[]{:S(2)}, u32[]{:S(2)}) collective-permute-start(bf16[1,10,256,128]{3,2,1,0:T(8,128)(2,1)S(1)} %get-tuple-element.7), channel_id=1, source_target_pairs={{1,0},{2,1},{3,2},{4,3},{5,4},{6,5},{7,6},{9,8},{10,9},{11,10},{12... | collective-permute-start | bytes 1966088 | tf_op jit(solution)/shard_map/ppermute | solution.py:50

commit v4 on v3

--- a/solution.py
+++ b/solution.py
@@ -37,7 +37,8 @@
     codes = jnp.arange(CODES, dtype=jnp.int32)
     shift_rows = (codes // 3 - 1) * (COLS // STRIDE)
     shift_cols = (codes % 3 - 1) * STRIDE
-    return gaspari_cohn(shift_rows, shift_cols) / (K - 1)
+    table = gaspari_cohn(shift_rows, shift_cols) / (K - 1)
+    return table.reshape(3, 3 * COLS, COLS)
 
 
 def with_halo(cells):
@@ -53,29 +54,41 @@
 
 def product_kernel(field_at, targets_ref, members_ref, field_ref, taper_ref, out_ref):
     lat_blocks, lon_blocks, columns, rank = out_ref.shape
+    out_ref[...] = jnp.zeros(out_ref.shape, jnp.float32)
+    for p in range(lat_blocks):
+        for dr in range(3):
+            row = p + dr
 
-    def one_block(t, carry):
-        p = t // lon_blocks
-        q = t % lon_blocks
-        target = targets_ref[p, q]
-        total = jnp.zeros((columns, rank), jnp.float32)
-        for code in range(CODES):
-            dr, dc = code // 3, code % 3
-            gram = jnp.dot(
-                target, members_ref[p + dr, q + dc, :K, :], preferred_element_type=jnp.float32
-            )
-            tile = gram * taper_ref[code]
-            tile_high = tile.astype(jnp.bfloat16)
-            tile_low = (tile - tile_high.astype(jnp.float32)).astype(jnp.bfloat16)
-            field_high = field_ref[p + dr, q + dc, field_at : field_at + columns, :]
-            field_low = field_ref[p + dr, q + dc, field_at + columns : field_at + 2 * columns, :]
-            total = total + jnp.dot(tile_high, field_high, preferred_element_type=jnp.float32)
-            total = total + jnp.dot(tile_high, field_low, preferred_element_type=jnp.float32)
-            total = total + jnp.dot(tile_low, field_high, preferred_element_type=jnp.float32)
-        out_ref[p, q] = total
-        return carry
+            def step(c, carry, p=p, dr=dr, row=row):
+                lhs = jnp.concatenate(
+                    [targets_ref[p, jnp.clip(c - k, 0, lon_blocks - 1)] for k in range(3)], axis=0
+                )
+                gram = jnp.dot(lhs, members_ref[row, c, :K, :], preferred_element_type=jnp.float32)
+                tile = gram * taper_ref[dr]
+                high = tile.astype(jnp.bfloat16)
+                low = (tile - high.astype(jnp.float32)).astype(jnp.bfloat16)
+                field_high = field_ref[row, c, field_at : field_at + columns, :]
+                field_low = field_ref[row, c, field_at + columns : field_at + 2 * columns, :]
+                both = jnp.dot(
+                    jnp.concatenate([high, low], axis=0), field_high, preferred_element_type=jnp.float32
+                )
+                cross = jnp.dot(high, field_low, preferred_element_type=jnp.float32)
+                for k in range(3):
+                    q = c - k
+                    part = (
+                        both[k * columns : (k + 1) * columns]
+                        + both[(3 + k) * columns : (4 + k) * columns]
+                        + cross[k * columns : (k + 1) * columns]
+                    )
 
-    lax.fori_loop(0, lat_blocks * lon_blocks, one_block, 0)
+                    @pl.when((q >= 0) & (q < lon_blocks))
+                    def _(q=q, part=part):
+                        at = jnp.clip(q, 0, lon_blocks - 1)
+                        out_ref[p, at] = out_ref[p, at] + part
+
+                return carry
+
+            lax.fori_loop(0, lon_blocks + 2, step, 0)
 
 
 def split_high_low(field):

time: 121 us -> 132 us (1.091)
  Pallas kernels: 42.6 us -> 55 us
    pallas_call x2, Pallas kernels: 42.6 us -> 55 us  [localized_product(): pl.pallas_call(functools.partial(product_kernel, field_at), out_shape=jax...]
where the time goes in v4:
time: 132 us; the launch traced here: 131 us
  Pallas kernels  55 us (42%)
  waiting for transfers between devices  34.9 us (26%)
  starting transfers between devices  27.3 us (21%)
  other arithmetic  11.6 us (9%)
  local copies, waits for them, and re-layouts  1.45 us (1%)
    pallas_call x2, Pallas kernels, localized_product(): pl.pallas_call(functools.partial(product_kernel, field_at), out_shape=jax...  55 us
    ppermute x2, waiting for transfers between devices, with_halo(): lax.ppermute(wider[-1:], 'lat', [(i, i + 1) for i in range(nlat - 1)])  26.4 us
    ppermute x2, starting transfers between devices, with_halo(): lax.ppermute(cells[:, :1], 'lon', [((i + 1) % nlon, i) for i in range(nlo...  10.7 us
    ppermute x2, starting transfers between devices, with_halo(): lax.ppermute(wider[:1], 'lat', [(i + 1, i) for i in range(nlat - 1)])  9.23 us
    ppermute x2, starting transfers between devices, with_halo(): lax.ppermute(wider[-1:], 'lat', [(i, i + 1) for i in range(nlat - 1)])  7.23 us
    ppermute x2, waiting for transfers between devices, with_halo(): lax.ppermute(cells[:, -1:], 'lon', [(i, (i + 1) % nlon) for i in range(nl...  5.74 us
    concatenate x2, other arithmetic, with_halo(): return jnp.concatenate([north, wider, south], axis=0)  5.58 us
    convert_element_type x2, other arithmetic, split_high_low(): rounded.astype(jnp.bfloat16)  3.01 us
  transfers between devices with their start and end apart: 8, of which 6 were waited for; matrix products, arithmetic and copies ran while one was open for 2% of the time, Pallas kernels for 0%

profile of v4, /device:TPU:2, one launch (start us, length us, event | category | flops | bytes accessed | tf_op | source)
XLA Modules:
  0.0 131.1 jit_solution(4774810257556131554)
XLA Ops:
  0.6 0.0 copy-start
  0.6 1.5 %reduce-precision_convert_fusion.1 = (bf16[2,8,128,128]{3,2,1,0:T(8,128)(2,1)S(1)}, bf16[2,8,128,128]{3,2,1,0:T(8,128)(2,1)S(1)}) fusion(f32[2,8,128,128]{3,2,1,0:T(8,128)} %param.5), kind=kLoop, calls=%fused_computation.6 | loop fusion | flops 1048576 | bytes 2097152 | tf_op jit(solution)/shard_map/convert_element_type | solution.py:96
  2.2 0.8 pad_maximum_fusion.6
  3.0 0.1 collective-permute-start
  3.1 5.3 %collective-permute-start.1 = (bf16[2,1,336,128]{3,2,1,0:T(8,128)(2,1)S(1)}, bf16[2,1,336,128]{3,2,1,0:T(8,128)(2,1)S(1)}, u32[]{:S(2)}, u32[]{:S(2)}) collective-permute-start(bf16[2,1,336,128]{3,2,1,0:T(8,128)(2,1)S(1)} %get-tuple-element.5), channel_id=1, source_target_pairs={{8,0},{16,8},{24,16},{32,24},{40,32},{48,40},{56,48},{64,56},{72,6... | collective-permute-start | bytes 516104 | tf_op jit(solution)/shard_map/ppermute | solution.py:48
  8.5 1.0 copy.4
  9.5 0.1 broadcast_bitcast_fusion
  9.6 0.1 broadcast_bitcast_fusion.1
  9.7 1.9 %collective-permute-done = bf16[2,1,336,128]{3,2,1,0:T(8,128)(2,1)S(1)} collective-permute-done((bf16[2,1,336,128]{3,2,1,0:T(8,128)(2,1)S(1)}, bf16[2,1,336,128]{3,2,1,0:T(8,128)(2,1)S(1)}, u32[]{:S(2)}, u32[]{:S(2)}) %collective-permute-start) | collective-permute-done | bytes 172064 | tf_op jit(solution)/shard_map/ppermute | solution.py:47
  11.5 0.1 pad_maximum_fusion.2
  11.7 0.1 fusion.41
  11.8 3.8 %collective-permute-start.2 = (bf16[1,10,336,128]{3,2,1,0:T(8,128)(2,1)S(1)}, bf16[1,10,336,128]{3,2,1,0:T(8,128)(2,1)S(1)}, u32[]{:S(2)}, u32[]{:S(2)}) collective-permute-start(bf16[1,10,336,128]{3,2,1,0:T(8,128)(2,1)S(1)} %get-tuple-element.2), channel_id=1, source_target_pairs={{0,1},{1,2},{2,3},{3,4},{4,5},{5,6},{6,7},{8,9},{9,10},{10,11},{11... | collective-permute-start | bytes 2580488 | tf_op jit(solution)/shard_map/ppermute | solution.py:50
  15.6 4.1 %collective-permute-start.3 = (bf16[1,10,336,128]{3,2,1,0:T(8,128)(2,1)S(1)}, bf16[1,10,336,128]{3,2,1,0:T(8,128)(2,1)S(1)}, u32[]{:S(2)}, u32[]{:S(2)}) collective-permute-start(bf16[1,10,336,128]{3,2,1,0:T(8,128)(2,1)S(1)} %get-tuple-element.3), channel_id=1, source_target_pairs={{1,0},{2,1},{3,2},{4,3},{5,4},{6,5},{7,6},{9,8},{10,9},{11,10},{12... | collective-permute-start | bytes 2580488 | tf_op jit(solution)/shard_map/ppermute | solution.py:51
  19.8 0.1 broadcast_subtract_fusion
  19.8 0.1 broadcast_subtract_fusion.1
  20.0 1.8 %fusion.4.taper_ref = f32[3,384,128]{2,1,0:T(8,128)} fusion(s32[3,384]{1,0:T(4,128)S(1)} %get-tuple-element.14, s32[3,384]{1,0:T(4,128)S(1)} %get-tuple-element.15, s32[3,384,128]{2,1,0:T(8,128)S(1)} %bitcast.172, s32[3,384,128]{2,1,0:T(8,128)S(1)} %bitcast.171), kind=kLoop, calls=%fused_computation.13 | loop fusion | flops 5160960 | bytes 1778688 | tf_op jit(solution)/shard_map/div | solution.py:40
  21.8 15.8 %collective-permute-done.2 = bf16[1,10,336,128]{3,2,1,0:T(8,128)(2,1)S(1)} collective-permute-done((bf16[1,10,336,128]{3,2,1,0:T(8,128)(2,1)S(1)}, bf16[1,10,336,128]{3,2,1,0:T(8,128)(2,1)S(1)}, u32[]{:S(2)}, u32[]{:S(2)}) %collective-permute-start.2) | collective-permute-done | bytes 860192 | tf_op jit(solution)/shard_map/ppermute | solution.py:50
  37.6 1.6 %collective-permute-done.3 = bf16[1,10,336,128]{3,2,1,0:T(8,128)(2,1)S(1)} collective-permute-done((bf16[1,10,336,128]{3,2,1,0:T(8,128)(2,1)S(1)}, bf16[1,10,336,128]{3,2,1,0:T(8,128)(2,1)S(1)}, u32[]{:S(2)}, u32[]{:S(2)}) %collective-permute-start.3) | collective-permute-done | bytes 860192 | tf_op jit(solution)/shard_map/ppermute | solution.py:51
  39.2 3.3 %pad_maximum_fusion.members_ref.field_ref = bf16[4,10,336,128]{3,2,1,0:T(8,128)(2,1)} fusion(bf16[1,10,336,128]{3,2,1,0:T(8,128)(2,1)S(1)} %collective-permute-done.3, bf16[2,1,336,128]{3,2,1,0:T(8,128)(2,1)S(1)} %collective-permute-done.1, bf16[2,8,128,128]{3,2,1,0:T(8,128)(2,1)S(1)} %get-tuple-element.13, bf16[2,8,128,128]{3,2,1,0:T(8,128)(2,1)S(1)} %get-tuple-element.12, ...), kind=kLoop, calls=%fused_computation | loop fusion | flops 24084480 | bytes 6881280 | tf_op jit(solution)/shard_map/concatenate | solution.py:52
  42.5 27.7 %shard_map.41 = f32[2,8,128,128]{3,2,1,0:T(8,128)} custom-call(bf16[2,8,128,80]{3,2,1,0:T(8,128)(2,1)} %bitcast.169, bf16[4,10,336,128]{3,2,1,0:T(8,128)(2,1)} %pad_maximum_fusion.members_ref.field_ref, bf16[4,10,336,128]{3,2,1,0:T(8,128)(2,1)} %pad_maximum_fusion.members_ref.field_ref, f32[3,384,128]{2,1,0:T(8,128)} %fusion.4.taper_ref), custom_call_target="tpu_custom_call" | custom-call | flops 2189426688 | bytes 8847360 | tf_op jit(solution)/shard_map/pallas_call | solution.py:106
  70.2 1.5 %reduce-precision_convert_fusion = (bf16[2,8,128,128]{3,2,1,0:T(8,128)(2,1)S(1)}, bf16[2,8,128,128]{3,2,1,0:T(8,128)(2,1)S(1)}) fusion(f32[2,8,128,128]{3,2,1,0:T(8,128)} %shard_map.41), kind=kLoop, calls=%fused_computation.4 | loop fusion | flops 1048576 | bytes 2097152 | tf_op jit(solution)/shard_map/convert_element_type | solution.py:96
  71.7 0.1 collective-permute-start.4
  71.8 5.3 %collective-permute-start.5 = (bf16[2,1,256,128]{3,2,1,0:T(8,128)(2,1)S(1)}, bf16[2,1,256,128]{3,2,1,0:T(8,128)(2,1)S(1)}, u32[]{:S(2)}, u32[]{:S(2)}) collective-permute-start(bf16[2,1,256,128]{3,2,1,0:T(8,128)(2,1)S(1)} %get-tuple-element.9), channel_id=1, source_target_pairs={{8,0},{16,8},{24,16},{32,24},{40,32},{48,40},{56,48},{64,56},{72,6... | collective-permute-start | bytes 393224 | tf_op jit(solution)/shard_map/ppermute | solution.py:48
  77.1 3.9 %collective-permute-done.4 = bf16[2,1,256,128]{3,2,1,0:T(8,128)(2,1)S(1)} collective-permute-done((bf16[2,1,256,128]{3,2,1,0:T(8,128)(2,1)S(1)}, bf16[2,1,256,128]{3,2,1,0:T(8,128)(2,1)S(1)}, u32[]{:S(2)}, u32[]{:S(2)}) %collective-permute-start.4) | collective-permute-done | bytes 131104 | tf_op jit(solution)/shard_map/ppermute | solution.py:47
  81.0 0.1 pad_maximum_fusion.3
  81.1 0.1 fusion.42
  81.2 3.4 %collective-permute-start.6 = (bf16[1,10,256,128]{3,2,1,0:T(8,128)(2,1)S(1)}, bf16[1,10,256,128]{3,2,1,0:T(8,128)(2,1)S(1)}, u32[]{:S(2)}, u32[]{:S(2)}) collective-permute-start(bf16[1,10,256,128]{3,2,1,0:T(8,128)(2,1)S(1)} %get-tuple-element.6), channel_id=1, source_target_pairs={{0,1},{1,2},{2,3},{3,4},{4,5},{5,6},{6,7},{8,9},{9,10},{10,11},{11... | collective-permute-start | bytes 1966088 | tf_op jit(solution)/shard_map/ppermute | solution.py:50
  84.6 5.1 %collective-permute-start.7 = (bf16[1,10,256,128]{3,2,1,0:T(8,128)(2,1)S(1)}, bf16[1,10,256,128]{3,2,1,0:T(8,128)(2,1)S(1)}, u32[]{:S(2)}, u32[]{:S(2)}) collective-permute-start(bf16[1,10,256,128]{3,2,1,0:T(8,128)(2,1)S(1)} %get-tuple-element.7), channel_id=1, source_target_pairs={{1,0},{2,1},{3,2},{4,3},{5,4},{6,5},{7,6},{9,8},{10,9},{11,10},{12... | collective-permute-start | bytes 1966088 | tf_op jit(solution)/shard_map/ppermute | solution.py:51
  89.7 10.6 %collective-permute-done.6 = bf16[1,10,256,128]{3,2,1,0:T(8,128)(2,1)S(1)} collective-permute-done((bf16[1,10,256,128]{3,2,1,0:T(8,128)(2,1)S(1)}, bf16[1,10,256,128]{3,2,1,0:T(8,128)(2,1)S(1)}, u32[]{:S(2)}, u32[]{:S(2)}) %collective-permute-start.6) | collective-permute-done | bytes 655392 | tf_op jit(solution)/shard_map/ppermute | solution.py:50
  100.3 1.2 collective-permute-done.7
  101.5 2.3 %pad_maximum_fusion.1.field_ref = bf16[4,10,256,128]{3,2,1,0:T(8,128)(2,1)} fusion(bf16[1,10,256,128]{3,2,1,0:T(8,128)(2,1)S(1)} %collective-permute-done.7, bf16[2,1,256,128]{3,2,1,0:T(8,128)(2,1)S(1)} %collective-permute-done.5, bf16[2,8,128,128]{3,2,1,0:T(8,128)(2,1)S(1)} %get-tuple-element.11, bf16[2,8,128,128]{3,2,1,0:T(8,128)(2,1)S(1)} %get-tuple-element.10, ...), kind=kLoop, calls=%fused_computation.1 | loop fusion | flops 15728640 | bytes 5242880 | tf_op jit(solution)/shard_map/concatenate | solution.py:52
  103.8 27.3 %shard_map.42 = f32[2,8,128,128]{3,2,1,0:T(8,128)} custom-call(bf16[2,8,128,80]{3,2,1,0:T(8,128)(2,1)} %bitcast.170, bf16[4,10,336,128]{3,2,1,0:T(8,128)(2,1)} %pad_maximum_fusion.members_ref.field_ref, bf16[4,10,256,128]{3,2,1,0:T(8,128)(2,1)} %pad_maximum_fusion.1.field_ref, f32[3,384,128]{2,1,0:T(8,128)} %fusion.4.taper_ref), custom_call_target="tpu_custom_call" | custom-call | flops 2189426688 | bytes 8028160 | tf_op jit(solution)/shard_map/pallas_call | solution.py:106
  (11 shorter events, 0.2 us)
Async XLA Ops:
  0.6 7.9 %copy-start = (bf16[2,8,80,128]{3,2,1,0:T(8,128)(2,1)S(1)}, bf16[2,8,80,128]{3,2,1,0:T(8,128)(2,1)}, u32[]{:S(2)}) copy-start(bf16[2,8,80,128]{3,2,1,0:T(8,128)(2,1)} %param.4) | copy-start | bytes 983044
  3.0 8.5 %collective-permute-start = (bf16[2,1,336,128]{3,2,1,0:T(8,128)(2,1)S(1)}, bf16[2,1,336,128]{3,2,1,0:T(8,128)(2,1)S(1)}, u32[]{:S(2)}, u32[]{:S(2)}) collective-permute-start(bf16[2,1,336,128]{3,2,1,0:T(8,128)(2,1)S(1)} %get-tuple-element.4), channel_id=1, source_target_pairs={{0,8},{8,16},{16,24},{24,32},{32,40},{40,48},{48,56},{56,64},{64,7... | collective-permute-start | bytes 516104 | tf_op jit(solution)/shard_map/ppermute | solution.py:47
  3.1 8.4 %collective-permute-start.1 = (bf16[2,1,336,128]{3,2,1,0:T(8,128)(2,1)S(1)}, bf16[2,1,336,128]{3,2,1,0:T(8,128)(2,1)S(1)}, u32[]{:S(2)}, u32[]{:S(2)}) collective-permute-start(bf16[2,1,336,128]{3,2,1,0:T(8,128)(2,1)S(1)} %get-tuple-element.5), channel_id=1, source_target_pairs={{8,0},{16,8},{24,16},{32,24},{40,32},{48,40},{56,48},{64,56},{72,6... | collective-permute-start | bytes 516104 | tf_op jit(solution)/shard_map/ppermute | solution.py:48
  11.8 25.8 %collective-permute-start.2 = (bf16[1,10,336,128]{3,2,1,0:T(8,128)(2,1)S(1)}, bf16[1,10,336,128]{3,2,1,0:T(8,128)(2,1)S(1)}, u32[]{:S(2)}, u32[]{:S(2)}) collective-permute-start(bf16[1,10,336,128]{3,2,1,0:T(8,128)(2,1)S(1)} %get-tuple-element.2), channel_id=1, source_target_pairs={{0,1},{1,2},{2,3},{3,4},{4,5},{5,6},{6,7},{8,9},{9,10},{10,11},{11... | collective-permute-start | bytes 2580488 | tf_op jit(solution)/shard_map/ppermute | solution.py:50
  15.6 23.6 %collective-permute-start.3 = (bf16[1,10,336,128]{3,2,1,0:T(8,128)(2,1)S(1)}, bf16[1,10,336,128]{3,2,1,0:T(8,128)(2,1)S(1)}, u32[]{:S(2)}, u32[]{:S(2)}) collective-permute-start(bf16[1,10,336,128]{3,2,1,0:T(8,128)(2,1)S(1)} %get-tuple-element.3), channel_id=1, source_target_pairs={{1,0},{2,1},{3,2},{4,3},{5,4},{6,5},{7,6},{9,8},{10,9},{11,10},{12... | collective-permute-start | bytes 2580488 | tf_op jit(solution)/shard_map/ppermute | solution.py:51
  71.7 9.3 %collective-permute-start.4 = (bf16[2,1,256,128]{3,2,1,0:T(8,128)(2,1)S(1)}, bf16[2,1,256,128]{3,2,1,0:T(8,128)(2,1)S(1)}, u32[]{:S(2)}, u32[]{:S(2)}) collective-permute-start(bf16[2,1,256,128]{3,2,1,0:T(8,128)(2,1)S(1)} %get-tuple-element.8), channel_id=1, source_target_pairs={{0,8},{8,16},{16,24},{24,32},{32,40},{40,48},{48,56},{56,64},{64,7... | collective-permute-start | bytes 393224 | tf_op jit(solution)/shard_map/ppermute | solution.py:47
  71.8 9.2 %collective-permute-start.5 = (bf16[2,1,256,128]{3,2,1,0:T(8,128)(2,1)S(1)}, bf16[2,1,256,128]{3,2,1,0:T(8,128)(2,1)S(1)}, u32[]{:S(2)}, u32[]{:S(2)}) collective-permute-start(bf16[2,1,256,128]{3,2,1,0:T(8,128)(2,1)S(1)} %get-tuple-element.9), channel_id=1, source_target_pairs={{8,0},{16,8},{24,16},{32,24},{40,32},{48,40},{56,48},{64,56},{72,6... | collective-permute-start | bytes 393224 | tf_op jit(solution)/shard_map/ppermute | solution.py:48
  81.2 19.1 %collective-permute-start.6 = (bf16[1,10,256,128]{3,2,1,0:T(8,128)(2,1)S(1)}, bf16[1,10,256,128]{3,2,1,0:T(8,128)(2,1)S(1)}, u32[]{:S(2)}, u32[]{:S(2)}) collective-permute-start(bf16[1,10,256,128]{3,2,1,0:T(8,128)(2,1)S(1)} %get-tuple-element.6), channel_id=1, source_target_pairs={{0,1},{1,2},{2,3},{3,4},{4,5},{5,6},{6,7},{8,9},{9,10},{10,11},{11... | collective-permute-start | bytes 1966088 | tf_op jit(solution)/shard_map/ppermute | solution.py:50
  84.6 16.9 %collective-permute-start.7 = (bf16[1,10,256,128]{3,2,1,0:T(8,128)(2,1)S(1)}, bf16[1,10,256,128]{3,2,1,0:T(8,128)(2,1)S(1)}, u32[]{:S(2)}, u32[]{:S(2)}) collective-permute-start(bf16[1,10,256,128]{3,2,1,0:T(8,128)(2,1)S(1)} %get-tuple-element.7), channel_id=1, source_target_pairs={{1,0},{2,1},{3,2},{4,3},{5,4},{6,5},{7,6},{9,8},{10,9},{11,10},{12... | collective-permute-start | bytes 1966088 | tf_op jit(solution)/shard_map/ppermute | solution.py:51

commit v5 on v3

v5 whole, which is shorter than its diff:
```python
import functools

import jax
import jax.numpy as jnp
from jax import lax
from jax.experimental import pallas as pl
from jax.experimental.pallas import tpu as pltpu
from jax.sharding import PartitionSpec as P

K = 80
COLS = 128
STRIDE = 16
RADIUS = 4
CODES = 9


def gaspari_cohn(shift_rows, shift_cols):
    position = jnp.arange(COLS)
    row_within = position // STRIDE
    col_within = position % STRIDE
    delta_rows = shift_rows[..., None, None] + (row_within[None, :] - row_within[:, None])
    delta_cols = shift_cols[..., None, None] + (col_within[None, :] - col_within[:, None])
    squared = (delta_rows * delta_rows + delta_cols * delta_cols).astype(jnp.float32)
    scaled = jnp.sqrt(squared + 0.25) / RADIUS
    inside = (
        ((-0.25 * scaled + 0.5) * scaled + 0.625) * scaled - 5.0 / 3.0
    ) * scaled * scaled + 1.0
    outside = (
        ((((scaled / 12.0 - 0.5) * scaled + 0.625) * scaled + 5.0 / 3.0) * scaled - 5.0) * scaled
        + 4.0
        - 2.0 / (3.0 * scaled)
    )
    return jnp.where(scaled <= 1.0, inside, jnp.where(scaled <= 2.0, outside, 0.0))


def taper_by_code():
    codes = jnp.arange(CODES, dtype=jnp.int32)
    shift_rows = (codes // 3 - 1) * (COLS // STRIDE)
    shift_cols = (codes % 3 - 1) * STRIDE
    return gaspari_cohn(shift_rows, shift_cols) / (K - 1)


def with_halo(cells):
    nlat = lax.axis_size("lat")
    nlon = lax.axis_size("lon")
    west = lax.ppermute(cells[:, -1:], "lon", [(i, (i + 1) % nlon) for i in range(nlon)])
    east = lax.ppermute(cells[:, :1], "lon", [((i + 1) % nlon, i) for i in range(nlon)])
    wider = jnp.concatenate([west, cells, east], axis=1)
    north = lax.ppermute(wider[-1:], "lat", [(i, i + 1) for i in range(nlat - 1)])
    south = lax.ppermute(wider[:1], "lat", [(i + 1, i) for i in range(nlat - 1)])
    return north, wider, south


def rows_kernel(plan, field_at, with_partial, targets_ref, taper_ref, *rest):
    out_ref = rest[-1]
    partial_ref = rest[0] if with_partial else None
    sources = rest[1:-1] if with_partial else rest[:-1]
    lat_blocks, lon_blocks, columns, rank = out_ref.shape
    for p in range(lat_blocks):

        def one_block(q, carry, p=p, uses=plan[p]):
            target = targets_ref[p, q]
            if with_partial:
                total = partial_ref[p, q]
            else:
                total = jnp.zeros((columns, rank), jnp.float32)
            for dr, members_at, field_from, row in uses:
                members_ref, field_ref = sources[members_at], sources[field_from]
                for dc in range(3):
                    gram = jnp.dot(
                        target, members_ref[row, q + dc, :K, :], preferred_element_type=jnp.float32
                    )
                    tile = gram * taper_ref[dr * 3 + dc]
                    tile_high = tile.astype(jnp.bfloat16)
                    tile_low = (tile - tile_high.astype(jnp.float32)).astype(jnp.bfloat16)
                    field_high = field_ref[row, q + dc, field_at : field_at + columns, :]
                    field_low = field_ref[row, q + dc, field_at + columns : field_at + 2 * columns, :]
                    total = total + jnp.dot(tile_high, field_high, preferred_element_type=jnp.float32)
                    total = total + jnp.dot(tile_high, field_low, preferred_element_type=jnp.float32)
                    total = total + jnp.dot(tile_low, field_high, preferred_element_type=jnp.float32)
            out_ref[p, q] = total
            return carry

        lax.fori_loop(0, lon_blocks, one_block, 0)


def rows_call(plan, field_at, targets, taper, partial, sources, out_like):
    lat_blocks, lon_blocks, columns, rank = out_like.shape
    codes = sum(3 * len(uses) for uses in plan)
    flops = lon_blocks * codes * 2 * columns * (K * columns + 3 * columns * rank)
    operands = [targets, taper] + ([partial] if partial is not None else []) + list(sources)
    moved = sum(x.size * x.dtype.itemsize for x in operands) + out_like.size * 4
    vmem = pl.BlockSpec(memory_space=pltpu.VMEM)
    return pl.pallas_call(
        functools.partial(rows_kernel, plan, field_at, partial is not None),
        out_shape=jax.ShapeDtypeStruct(out_like.shape, jnp.float32),
        in_specs=[vmem] * len(operands),
        out_specs=vmem,
        cost_estimate=pl.CostEstimate(flops=flops, bytes_accessed=moved, transcendentals=0),
    )(*operands)


def split_high_low(field):
    rounded = lax.reduce_precision(field, exponent_bits=8, mantissa_bits=7)
    return rounded.astype(jnp.bfloat16), (field - rounded).astype(jnp.bfloat16)


def own_plan(lat_blocks, members, field):
    return tuple(
        tuple((dr, members, field, p + dr - 1) for dr in range(3) if 0 <= p + dr - 1 < lat_blocks)
        for p in range(lat_blocks)
    )


def halo_plan(lat_blocks, members, field):
    return tuple(
        tuple(
            (dr, members[p + dr > 0], field[p + dr > 0], 0)
            for dr in range(3)
            if not 0 <= p + dr - 1 < lat_blocks
        )
        for p in range(lat_blocks)
    )


def local(anomalies, panel, pair_code, pair_offset):
    del pair_code, pair_offset
    lat_blocks = anomalies.shape[0]
    taper = taper_by_code()
    targets = jnp.swapaxes(anomalies, 2, 3)
    panel_high, panel_low = split_high_low(panel)
    north, wider, south = with_halo(jnp.concatenate([anomalies, panel_high, panel_low], axis=2))
    partial = rows_call(own_plan(lat_blocks, 0, 0), K, targets, taper, None, (wider,), panel)
    first_product = rows_call(
        halo_plan(lat_blocks, (0, 1), (0, 1)), K, targets, taper, partial, (north, south), panel
    )
    product_high, product_low = split_high_low(first_product)
    north2, wider2, south2 = with_halo(jnp.concatenate([product_high, product_low], axis=2))
    partial = rows_call(own_plan(lat_blocks, 0, 1), 0, targets, taper, None, (wider, wider2), panel)
    second_product = rows_call(
        halo_plan(lat_blocks, (0, 1), (2, 3)),
        0,
        targets,
        taper,
        partial,
        (north, south, north2, south2),
        panel,
    )
    return (first_product, second_product)


def solution(mesh):
    placed = (
        P("lat", "lon", None, None),
        P("lat", "lon", None, None),
        P("lat", "lon", None),
        P(None, "lat", "lon", None),
    )
    return jax.shard_map(
        local,
        mesh=mesh,
        in_specs=placed,
        out_specs=(P("lat", "lon", None, None), P("lat", "lon", None, None)),
        check_vma=False,
    )
```

time: 121 us -> 104 us (0.86)
  waiting for transfers between devices: 35.5 us -> 12.3 us
  Pallas kernels: 42.6 us -> 54.4 us
  other arithmetic: 11.4 us -> 5.14 us
  local copies, waits for them, and re-layouts: 2.42 us -> 6.25 us
  starting transfers between devices: 27.3 us -> 24.5 us
    ppermute x2, waiting for transfers between devices: 25.7 us -> 6.03 us  [with_halo(): lax.ppermute(wider[-1:], 'lat', [(i, i + 1) for i in range(nlat - 1)])]
    pallas_call x2 -> x4, Pallas kernels: 42.6 us -> 54.4 us  [rows_call(): pl.pallas_call(functools.partial(rows_kernel, plan, field_at, partial is...]
    concatenate x2 -> x0, other arithmetic: 5.54 us -> none  [with_halo(): return jnp.concatenate([north, wider, south], axis=0)]
    unnamed x3 -> x15, local copies, waits for them, and re-layouts: 1.04 us -> 4.04 us
    ppermute x2, waiting for transfers between devices: 2.91 us -> 0.51 us  [with_halo(): lax.ppermute(wider[:1], 'lat', [(i + 1, i) for i in range(nlat - 1)])]
    ppermute x2, starting transfers between devices: 9.23 us -> 7.81 us  [with_halo(): lax.ppermute(wider[:1], 'lat', [(i + 1, i) for i in range(nlat - 1)])]
    ppermute x2, starting transfers between devices: 7.21 us -> 5.84 us  [with_halo(): lax.ppermute(wider[-1:], 'lat', [(i, i + 1) for i in range(nlat - 1)])]
  transfers between devices with their start and end apart: 8 -> 8, of which waited for: 6 -> 4; matrix products, arithmetic and copies ran while one was open for 2% -> 3% of each run, Pallas kernels for 0% -> 30%
where the time goes in v5:
time: 104 us; the launch traced here: 103 us
  Pallas kernels  54.4 us (52%)
  starting transfers between devices  24.5 us (24%)
  waiting for transfers between devices  12.3 us (12%)
  local copies, waits for them, and re-layouts  6.25 us (6%)
  other arithmetic  5.14 us (5%)
    pallas_call x4, Pallas kernels, rows_call(): pl.pallas_call(functools.partial(rows_kernel, plan, field_at, partial is...  54.4 us
    ppermute x2, starting transfers between devices, with_halo(): lax.ppermute(cells[:, :1], 'lon', [((i + 1) % nlon, i) for i in range(nlo...  10.7 us
    ppermute x2, starting transfers between devices, with_halo(): lax.ppermute(wider[:1], 'lat', [(i + 1, i) for i in range(nlat - 1)])  7.81 us
    ppermute x2, waiting for transfers between devices, with_halo(): lax.ppermute(wider[-1:], 'lat', [(i, i + 1) for i in range(nlat - 1)])  6.03 us
    ppermute x2, starting transfers between devices, with_halo(): lax.ppermute(wider[-1:], 'lat', [(i, i + 1) for i in range(nlat - 1)])  5.84 us
    ppermute x2, waiting for transfers between devices, with_halo(): lax.ppermute(cells[:, -1:], 'lon', [(i, (i + 1) % nlon) for i in range(nl...  5.79 us
    unnamed x15, local copies, waits for them, and re-layouts  4.04 us
    convert_element_type x2, other arithmetic, split_high_low(): rounded.astype(jnp.bfloat16)  3.01 us
  transfers between devices with their start and end apart: 8, of which 4 were waited for; matrix products, arithmetic and copies ran while one was open for 3% of the time, Pallas kernels for 30%

profile of v5, /device:TPU:2, one launch (start us, length us, event | category | flops | bytes accessed | tf_op | source)
XLA Modules:
  0.0 103.4 jit_solution(1119622374159531367)
XLA Ops:
  0.6 1.5 %reduce-precision_convert_fusion.1 = (bf16[2,8,128,128]{3,2,1,0:T(8,128)(2,1)S(1)}, bf16[2,8,128,128]{3,2,1,0:T(8,128)(2,1)S(1)}) fusion(f32[2,8,128,128]{3,2,1,0:T(8,128)} %param.5), kind=kLoop, calls=%fused_computation.4 | loop fusion | flops 1048576 | bytes 2097152 | tf_op jit(solution)/shard_map/convert_element_type | solution.py:105
  2.2 0.1 collective-permute-start
  2.3 5.3 %collective-permute-start.1 = (bf16[2,1,336,128]{3,2,1,0:T(8,128)(2,1)S(1)}, bf16[2,1,336,128]{3,2,1,0:T(8,128)(2,1)S(1)}, u32[]{:S(2)}, u32[]{:S(2)}) collective-permute-start(bf16[2,1,336,128]{3,2,1,0:T(8,128)(2,1)S(1)} %get-tuple-element.5), channel_id=1, source_target_pairs={{8,0},{16,8},{24,16},{32,24},{40,32},{48,40},{56,48},{64,56},{72,6... | collective-permute-start | bytes 516104 | tf_op jit(solution)/shard_map/ppermute | solution.py:47
  7.6 1.0 copy.4
  8.7 2.1 %collective-permute-done = bf16[2,1,336,128]{3,2,1,0:T(8,128)(2,1)S(1)} collective-permute-done((bf16[2,1,336,128]{3,2,1,0:T(8,128)(2,1)S(1)}, bf16[2,1,336,128]{3,2,1,0:T(8,128)(2,1)S(1)}, u32[]{:S(2)}, u32[]{:S(2)}) %collective-permute-start) | collective-permute-done | bytes 172064 | tf_op jit(solution)/shard_map/ppermute | solution.py:46
  10.7 0.1 pad_maximum_fusion.rest_0_
  10.9 1.1 %fusion.14 = (bf16[1,10,336,128]{3,2,1,0:T(8,128)(2,1)}, bf16[1,10,336,128]{3,2,1,0:T(8,128)(2,1)S(1)}) fusion(bf16[2,10,336,128]{3,2,1,0:T(8,128)(2,1)S(1)} %pad_maximum_fusion.rest_0_), kind=kLoop, calls=%fused_computation.45 | loop fusion | bytes 3440640 | tf_op jit(solution)/shard_map/slice | solution.py:50
  12.0 0.4 copy-done
  12.4 5.9 %collective-permute-start.3 = (bf16[1,10,336,128]{3,2,1,0:T(8,128)(2,1)}, bf16[1,10,336,128]{3,2,1,0:T(8,128)(2,1)S(1)}, u32[]{:S(2)}, u32[]{:S(2)}) collective-permute-start(bf16[1,10,336,128]{3,2,1,0:T(8,128)(2,1)} %get-tuple-element.2), channel_id=1, source_target_pairs={{1,0},{2,1},{3,2},{4,3},{5,4},{6,5},{7,6},{9,8},{10,9},{11,10},{12... | collective-permute-start | bytes 2580488 | tf_op jit(solution)/shard_map/ppermute | solution.py:50
  18.3 1.9 %collective-permute-start.2 = (bf16[1,10,336,128]{3,2,1,0:T(8,128)(2,1)S(1)}, bf16[1,10,336,128]{3,2,1,0:T(8,128)(2,1)S(1)}, u32[]{:S(2)}, u32[]{:S(2)}) collective-permute-start(bf16[1,10,336,128]{3,2,1,0:T(8,128)(2,1)S(1)} %get-tuple-element.3), channel_id=1, source_target_pairs={{0,1},{1,2},{2,3},{3,4},{4,5},{5,6},{6,7},{8,9},{9,10},{10,11},{11... | collective-permute-start | bytes 2580488 | tf_op jit(solution)/shard_map/ppermute | solution.py:49
  20.2 0.1 broadcast_subtract_fusion
  20.3 1.7 %fusion.4.taper_ref = f32[9,128,128]{2,1,0:T(8,128)} fusion(s32[128,128]{1,0:T(8,128)S(1)} %get-tuple-element.14, s32[9]{0:T(128)S(1)} %get-tuple-element.16, s32[128,128]{1,0:T(8,128)S(1)} %get-tuple-element.15, s32[9]{0:T(128)S(1)} %get-tuple-element.17), kind=kLoop, calls=%fused_computation.11 | loop fusion | flops 5160960 | bytes 720968 | tf_op jit(solution)/shard_map/div | solution.py:40
  22.1 15.5 %shard_map.41.rest_0_ = f32[2,8,128,128]{3,2,1,0:T(8,128)} custom-call(bf16[2,8,128,80]{3,2,1,0:T(8,128)(2,1)} %bitcast.1, f32[9,128,128]{2,1,0:T(8,128)} %fusion.4.taper_ref, bf16[2,10,336,128]{3,2,1,0:T(8,128)(2,1)} %copy-done), custom_call_target="tpu_custom_call" | custom-call | flops 1459617792 | bytes 3686400 | tf_op jit(solution)/shard_map/pallas_call | solution.py:94
  37.5 0.5 collective-permute-done.3.rest_2_
  38.0 6.0 %collective-permute-done.2.rest_1_ = bf16[1,10,336,128]{3,2,1,0:T(8,128)(2,1)S(1)} collective-permute-done((bf16[1,10,336,128]{3,2,1,0:T(8,128)(2,1)S(1)}, bf16[1,10,336,128]{3,2,1,0:T(8,128)(2,1)S(1)}, u32[]{:S(2)}, u32[]{:S(2)}) %collective-permute-start.2) | collective-permute-done | bytes 860192 | tf_op jit(solution)/shard_map/ppermute | solution.py:49
  44.1 0.9 copy-done.3
  45.0 11.4 %shard_map.42 = f32[2,8,128,128]{3,2,1,0:T(8,128)} custom-call(bf16[2,8,128,80]{3,2,1,0:T(8,128)(2,1)} %bitcast.2, f32[9,128,128]{2,1,0:T(8,128)} %fusion.4.taper_ref, f32[2,8,128,128]{3,2,1,0:T(8,128)} %shard_map.41.rest_0_, bf16[1,10,336,128]{3,2,1,0:T(8,128)(2,1)} %copy-done.3, bf16[1,10,336,128]{3,2,1,0:T(8,128)(2,1)} %copy-done.2), custom_call_target="tpu_custom_call" | custom-call | flops 729808896 | bytes 4734976 | tf_op jit(solution)/shard_map/pallas_call | solution.py:94
  56.3 1.5 %reduce-precision_convert_fusion = (bf16[2,8,128,128]{3,2,1,0:T(8,128)(2,1)S(1)}, bf16[2,8,128,128]{3,2,1,0:T(8,128)(2,1)S(1)}) fusion(f32[2,8,128,128]{3,2,1,0:T(8,128)} %shard_map.42), kind=kLoop, calls=%fused_computation.2 | loop fusion | flops 1048576 | bytes 2097152 | tf_op jit(solution)/shard_map/convert_element_type | solution.py:105
  57.9 0.1 collective-permute-start.4
  57.9 5.3 %collective-permute-start.5 = (bf16[2,1,256,128]{3,2,1,0:T(8,128)(2,1)S(1)}, bf16[2,1,256,128]{3,2,1,0:T(8,128)(2,1)S(1)}, u32[]{:S(2)}, u32[]{:S(2)}) collective-permute-start(bf16[2,1,256,128]{3,2,1,0:T(8,128)(2,1)S(1)} %get-tuple-element.9), channel_id=1, source_target_pairs={{8,0},{16,8},{24,16},{32,24},{40,32},{48,40},{56,48},{64,56},{72,6... | collective-permute-start | bytes 393224 | tf_op jit(solution)/shard_map/ppermute | solution.py:47
  63.3 3.7 %collective-permute-done.4 = bf16[2,1,256,128]{3,2,1,0:T(8,128)(2,1)S(1)} collective-permute-done((bf16[2,1,256,128]{3,2,1,0:T(8,128)(2,1)S(1)}, bf16[2,1,256,128]{3,2,1,0:T(8,128)(2,1)S(1)}, u32[]{:S(2)}, u32[]{:S(2)}) %collective-permute-start.4) | collective-permute-done | bytes 131104 | tf_op jit(solution)/shard_map/ppermute | solution.py:46
  67.0 0.0 collective-permute-done.5
  67.0 0.1 pad_maximum_fusion.1.rest_1_
  67.2 1.1 %fusion.15 = (bf16[1,10,256,128]{3,2,1,0:T(8,128)(2,1)}, bf16[1,10,256,128]{3,2,1,0:T(8,128)(2,1)S(1)}) fusion(bf16[2,10,256,128]{3,2,1,0:T(8,128)(2,1)S(1)} %pad_maximum_fusion.1.rest_1_), kind=kLoop, calls=%fused_computation.46 | loop fusion | bytes 2621440 | tf_op jit(solution)/shard_map/slice | solution.py:50
  68.2 1.9 %collective-permute-start.7 = (bf16[1,10,256,128]{3,2,1,0:T(8,128)(2,1)}, bf16[1,10,256,128]{3,2,1,0:T(8,128)(2,1)S(1)}, u32[]{:S(2)}, u32[]{:S(2)}) collective-permute-start(bf16[1,10,256,128]{3,2,1,0:T(8,128)(2,1)} %get-tuple-element.6), channel_id=1, source_target_pairs={{1,0},{2,1},{3,2},{4,3},{5,4},{6,5},{7,6},{9,8},{10,9},{11,10},{12... | collective-permute-start | bytes 1966088 | tf_op jit(solution)/shard_map/ppermute | solution.py:50
  70.2 3.9 %collective-permute-start.6 = (bf16[1,10,256,128]{3,2,1,0:T(8,128)(2,1)S(1)}, bf16[1,10,256,128]{3,2,1,0:T(8,128)(2,1)S(1)}, u32[]{:S(2)}, u32[]{:S(2)}) collective-permute-start(bf16[1,10,256,128]{3,2,1,0:T(8,128)(2,1)S(1)} %get-tuple-element.7), channel_id=1, source_target_pairs={{0,1},{1,2},{2,3},{3,4},{4,5},{5,6},{6,7},{8,9},{9,10},{10,11},{11... | collective-permute-start | bytes 1966088 | tf_op jit(solution)/shard_map/ppermute | solution.py:49
  74.1 15.8 %shard_map.43.rest_0_ = f32[2,8,128,128]{3,2,1,0:T(8,128)} custom-call(bf16[2,8,128,80]{3,2,1,0:T(8,128)(2,1)} %bitcast.3, f32[9,128,128]{2,1,0:T(8,128)} %fusion.4.taper_ref, bf16[2,10,336,128]{3,2,1,0:T(8,128)(2,1)} %copy-done, bf16[2,10,256,128]{3,2,1,0:T(8,128)(2,1)} %copy-done.1), custom_call_target="tpu_custom_call" | custom-call | flops 1459617792 | bytes 4997120 | tf_op jit(solution)/shard_map/pallas_call | solution.py:94
  90.0 0.0 collective-permute-done.7.rest_4_
  90.0 0.0 collective-permute-done.6.rest_3_
  90.0 0.8 copy-done.5
  90.8 0.9 copy-done.6
  91.7 11.7 %shard_map.44 = f32[2,8,128,128]{3,2,1,0:T(8,128)} custom-call(bf16[2,8,128,80]{3,2,1,0:T(8,128)(2,1)} %bitcast.4, f32[9,128,128]{2,1,0:T(8,128)} %fusion.4.taper_ref, f32[2,8,128,128]{3,2,1,0:T(8,128)} %shard_map.43.rest_0_, bf16[1,10,336,128]{3,2,1,0:T(8,128)(2,1)} %copy-done.3, bf16[1,10,336,128]{3,2,1,0:T(8,128)(2,1)} %copy-done.2, ...), custom_call_target="tpu_custom_call" | custom-call | flops 729808896 | bytes 6045696 | tf_op jit(solution)/shard_map/pallas_call | solution.py:94
  (16 shorter events, 0.1 us)
Async XLA Ops:
  0.6 1.5 %copy-start.4 = (bf16[2,8,80,128]{3,2,1,0:T(8,128)(2,1)S(1)}, bf16[2,8,80,128]{3,2,1,0:T(8,128)(2,1)}, u32[]{:S(2)}) copy-start(bf16[2,8,80,128]{3,2,1,0:T(8,128)(2,1)} %param.4) | copy-start | bytes 983044
  2.2 8.5 %collective-permute-start = (bf16[2,1,336,128]{3,2,1,0:T(8,128)(2,1)S(1)}, bf16[2,1,336,128]{3,2,1,0:T(8,128)(2,1)S(1)}, u32[]{:S(2)}, u32[]{:S(2)}) collective-permute-start(bf16[2,1,336,128]{3,2,1,0:T(8,128)(2,1)S(1)} %get-tuple-element.4), channel_id=1, source_target_pairs={{0,8},{8,16},{16,24},{24,32},{32,40},{40,48},{48,56},{56,64},{64,7... | collective-permute-start | bytes 516104 | tf_op jit(solution)/shard_map/ppermute | solution.py:46
  2.3 8.4 %collective-permute-start.1 = (bf16[2,1,336,128]{3,2,1,0:T(8,128)(2,1)S(1)}, bf16[2,1,336,128]{3,2,1,0:T(8,128)(2,1)S(1)}, u32[]{:S(2)}, u32[]{:S(2)}) collective-permute-start(bf16[2,1,336,128]{3,2,1,0:T(8,128)(2,1)S(1)} %get-tuple-element.5), channel_id=1, source_target_pairs={{8,0},{16,8},{24,16},{32,24},{40,32},{48,40},{56,48},{64,56},{72,6... | collective-permute-start | bytes 516104 | tf_op jit(solution)/shard_map/ppermute | solution.py:47
  10.9 1.5 %copy-start = (bf16[2,10,336,128]{3,2,1,0:T(8,128)(2,1)}, bf16[2,10,336,128]{3,2,1,0:T(8,128)(2,1)S(1)}, u32[]{:S(2)}) copy-start(bf16[2,10,336,128]{3,2,1,0:T(8,128)(2,1)S(1)} %pad_maximum_fusion.rest_0_) | copy-start | bytes 5160964
  12.4 25.7 %collective-permute-start.3 = (bf16[1,10,336,128]{3,2,1,0:T(8,128)(2,1)}, bf16[1,10,336,128]{3,2,1,0:T(8,128)(2,1)S(1)}, u32[]{:S(2)}, u32[]{:S(2)}) collective-permute-start(bf16[1,10,336,128]{3,2,1,0:T(8,128)(2,1)} %get-tuple-element.2), channel_id=1, source_target_pairs={{1,0},{2,1},{3,2},{4,3},{5,4},{6,5},{7,6},{9,8},{10,9},{11,10},{12... | collective-permute-start | bytes 2580488 | tf_op jit(solution)/shard_map/ppermute | solution.py:50
  18.3 25.8 %collective-permute-start.2 = (bf16[1,10,336,128]{3,2,1,0:T(8,128)(2,1)S(1)}, bf16[1,10,336,128]{3,2,1,0:T(8,128)(2,1)S(1)}, u32[]{:S(2)}, u32[]{:S(2)}) collective-permute-start(bf16[1,10,336,128]{3,2,1,0:T(8,128)(2,1)S(1)} %get-tuple-element.3), channel_id=1, source_target_pairs={{0,1},{1,2},{2,3},{3,4},{4,5},{5,6},{6,7},{8,9},{9,10},{10,11},{11... | collective-permute-start | bytes 2580488 | tf_op jit(solution)/shard_map/ppermute | solution.py:49
  38.0 6.0 %copy-start.2 = (bf16[1,10,336,128]{3,2,1,0:T(8,128)(2,1)}, bf16[1,10,336,128]{3,2,1,0:T(8,128)(2,1)S(1)}, u32[]{:S(2)}) copy-start(bf16[1,10,336,128]{3,2,1,0:T(8,128)(2,1)S(1)} %collective-permute-done.3.rest_2_) | copy-start | bytes 2580484
  44.1 0.9 copy-start.3
  57.9 9.2 %collective-permute-start.4 = (bf16[2,1,256,128]{3,2,1,0:T(8,128)(2,1)S(1)}, bf16[2,1,256,128]{3,2,1,0:T(8,128)(2,1)S(1)}, u32[]{:S(2)}, u32[]{:S(2)}) collective-permute-start(bf16[2,1,256,128]{3,2,1,0:T(8,128)(2,1)S(1)} %get-tuple-element.8), channel_id=1, source_target_pairs={{0,8},{8,16},{16,24},{24,32},{32,40},{40,48},{48,56},{56,64},{64,7... | collective-permute-start | bytes 393224 | tf_op jit(solution)/shard_map/ppermute | solution.py:46
  57.9 9.1 %collective-permute-start.5 = (bf16[2,1,256,128]{3,2,1,0:T(8,128)(2,1)S(1)}, bf16[2,1,256,128]{3,2,1,0:T(8,128)(2,1)S(1)}, u32[]{:S(2)}, u32[]{:S(2)}) collective-permute-start(bf16[2,1,256,128]{3,2,1,0:T(8,128)(2,1)S(1)} %get-tuple-element.9), channel_id=1, source_target_pairs={{8,0},{16,8},{24,16},{32,24},{40,32},{48,40},{56,48},{64,56},{72,6... | collective-permute-start | bytes 393224 | tf_op jit(solution)/shard_map/ppermute | solution.py:47
  67.2 6.9 %copy-start.1 = (bf16[2,10,256,128]{3,2,1,0:T(8,128)(2,1)}, bf16[2,10,256,128]{3,2,1,0:T(8,128)(2,1)S(1)}, u32[]{:S(2)}) copy-start(bf16[2,10,256,128]{3,2,1,0:T(8,128)(2,1)S(1)} %pad_maximum_fusion.1.rest_1_) | copy-start | bytes 3932164
  68.2 21.7 %collective-permute-start.7 = (bf16[1,10,256,128]{3,2,1,0:T(8,128)(2,1)}, bf16[1,10,256,128]{3,2,1,0:T(8,128)(2,1)S(1)}, u32[]{:S(2)}, u32[]{:S(2)}) collective-permute-start(bf16[1,10,256,128]{3,2,1,0:T(8,128)(2,1)} %get-tuple-element.6), channel_id=1, source_target_pairs={{1,0},{2,1},{3,2},{4,3},{5,4},{6,5},{7,6},{9,8},{10,9},{11,10},{12... | collective-permute-start | bytes 1966088 | tf_op jit(solution)/shard_map/ppermute | solution.py:50
  70.2 19.8 %collective-permute-start.6 = (bf16[1,10,256,128]{3,2,1,0:T(8,128)(2,1)S(1)}, bf16[1,10,256,128]{3,2,1,0:T(8,128)(2,1)S(1)}, u32[]{:S(2)}, u32[]{:S(2)}) collective-permute-start(bf16[1,10,256,128]{3,2,1,0:T(8,128)(2,1)S(1)} %get-tuple-element.7), channel_id=1, source_target_pairs={{0,1},{1,2},{2,3},{3,4},{4,5},{5,6},{6,7},{8,9},{9,10},{10,11},{11... | collective-permute-start | bytes 1966088 | tf_op jit(solution)/shard_map/ppermute | solution.py:49
  90.0 0.8 copy-start.5
  90.8 0.9 copy-start.6

commit v6 on v5

--- a/solution.py
+++ b/solution.py
@@ -40,15 +40,18 @@
     return gaspari_cohn(shift_rows, shift_cols) / (K - 1)
 
 
-def with_halo(cells):
+def lon_halo(cells, depth):
+    nlon = lax.axis_size("lon")
+    west = lax.ppermute(cells[:, -depth:], "lon", [(i, (i + 1) % nlon) for i in range(nlon)])
+    east = lax.ppermute(cells[:, :depth], "lon", [((i + 1) % nlon, i) for i in range(nlon)])
+    return jnp.concatenate([west, cells, east], axis=1)
+
+
+def lat_halo(rows):
     nlat = lax.axis_size("lat")
-    nlon = lax.axis_size("lon")
-    west = lax.ppermute(cells[:, -1:], "lon", [(i, (i + 1) % nlon) for i in range(nlon)])
-    east = lax.ppermute(cells[:, :1], "lon", [((i + 1) % nlon, i) for i in range(nlon)])
-    wider = jnp.concatenate([west, cells, east], axis=1)
-    north = lax.ppermute(wider[-1:], "lat", [(i, i + 1) for i in range(nlat - 1)])
-    south = lax.ppermute(wider[:1], "lat", [(i + 1, i) for i in range(nlat - 1)])
-    return north, wider, south
+    north = lax.ppermute(rows[-1:], "lat", [(i, i + 1) for i in range(nlat - 1)])
+    south = lax.ppermute(rows[:1], "lat", [(i + 1, i) for i in range(nlat - 1)])
+    return north, south
 
 
 def rows_kernel(plan, field_at, with_partial, targets_ref, taper_ref, *rest):
@@ -64,17 +67,20 @@
                 total = partial_ref[p, q]
             else:
                 total = jnp.zeros((columns, rank), jnp.float32)
-            for dr, members_at, field_from, row in uses:
+            for dr, members_at, field_from, row, members_off, field_off in uses:
                 members_ref, field_ref = sources[members_at], sources[field_from]
                 for dc in range(3):
                     gram = jnp.dot(
-                        target, members_ref[row, q + dc, :K, :], preferred_element_type=jnp.float32
+                        target,
+                        members_ref[row, q + dc + members_off, :K, :],
+                        preferred_element_type=jnp.float32,
                     )
                     tile = gram * taper_ref[dr * 3 + dc]
                     tile_high = tile.astype(jnp.bfloat16)
                     tile_low = (tile - tile_high.astype(jnp.float32)).astype(jnp.bfloat16)
-                    field_high = field_ref[row, q + dc, field_at : field_at + columns, :]
-                    field_low = field_ref[row, q + dc, field_at + columns : field_at + 2 * columns, :]
+                    partner = field_ref.at[row, q + dc + field_off]
+                    field_high = partner[field_at : field_at + columns, :]
+                    field_low = partner[field_at + columns : field_at + 2 * columns, :]
                     total = total + jnp.dot(tile_high, field_high, preferred_element_type=jnp.float32)
                     total = total + jnp.dot(tile_high, field_low, preferred_element_type=jnp.float32)
                     total = total + jnp.dot(tile_low, field_high, preferred_element_type=jnp.float32)
@@ -105,17 +111,17 @@
     return rounded.astype(jnp.bfloat16), (field - rounded).astype(jnp.bfloat16)
 
 
-def own_plan(lat_blocks, members, field):
+def own_plan(lat_blocks, members, field, offsets):
     return tuple(
-        tuple((dr, members, field, p + dr - 1) for dr in range(3) if 0 <= p + dr - 1 < lat_blocks)
+        tuple((dr, members, field, p + dr - 1) + offsets for dr in range(3) if 0 <= p + dr - 1 < lat_blocks)
         for p in range(lat_blocks)
     )
 
 
-def halo_plan(lat_blocks, members, field):
+def halo_plan(lat_blocks, members, field, offsets):
     return tuple(
         tuple(
-            (dr, members[p + dr > 0], field[p + dr > 0], 0)
+            (dr, members[p + dr > 0], field[p + dr > 0], 0) + offsets
             for dr in range(3)
             if not 0 <= p + dr - 1 < lat_blocks
         )
@@ -125,20 +131,25 @@
 
 def local(anomalies, panel, pair_code, pair_offset):
     del pair_code, pair_offset
-    lat_blocks = anomalies.shape[0]
+    lat_blocks, lon_blocks = anomalies.shape[:2]
     taper = taper_by_code()
+    panel_high, panel_low = split_high_low(panel)
+    wider = lon_halo(jnp.concatenate([anomalies, panel_high, panel_low], axis=2), 2)
+    north, south = lat_halo(wider)
+    targets_wide = jnp.swapaxes(wider[:, 1 : lon_blocks + 3, :K, :], 2, 3)
+    like_wide = jax.ShapeDtypeStruct((lat_blocks, lon_blocks + 2) + panel.shape[2:], jnp.float32)
+    partial = rows_call(own_plan(lat_blocks, 0, 0, (0, 0)), K, targets_wide, taper, None, (wider,), like_wide)
+    product_wide = rows_call(
+        halo_plan(lat_blocks, (0, 1), (0, 1), (0, 0)), K, targets_wide, taper, partial, (north, south), like_wide
+    )
+    first_product = product_wide[:, 1 : lon_blocks + 1]
+    product_high, product_low = split_high_low(product_wide)
+    message = jnp.concatenate([product_high, product_low], axis=2)
+    north2, south2 = lat_halo(message)
     targets = jnp.swapaxes(anomalies, 2, 3)
-    panel_high, panel_low = split_high_low(panel)
-    north, wider, south = with_halo(jnp.concatenate([anomalies, panel_high, panel_low], axis=2))
-    partial = rows_call(own_plan(lat_blocks, 0, 0), K, targets, taper, None, (wider,), panel)
-    first_product = rows_call(
-        halo_plan(lat_blocks, (0, 1), (0, 1)), K, targets, taper, partial, (north, south), panel
-    )
-    product_high, product_low = split_high_low(first_product)
-    north2, wider2, south2 = with_halo(jnp.concatenate([product_high, product_low], axis=2))
-    partial = rows_call(own_plan(lat_blocks, 0, 1), 0, targets, taper, None, (wider, wider2), panel)
+    partial = rows_call(own_plan(lat_blocks, 0, 1, (1, 0)), 0, targets, taper, None, (wider, message), panel)
     second_product = rows_call(
-        halo_plan(lat_blocks, (0, 1), (2, 3)),
+        halo_plan(lat_blocks, (0, 1), (2, 3), (1, 0)),
         0,
         targets,
         taper,

time: 104 us -> 105 us (level)
  Pallas kernels: 54.4 us -> 60.5 us
  starting transfers between devices: 24.5 us -> 18.8 us
  other arithmetic: 5.14 us -> 7.7 us
    pallas_call x4, Pallas kernels: 54.4 us -> 60.5 us  [rows_call(): pl.pallas_call(functools.partial(rows_kernel, plan, field_at, partial is...]
    ppermute x8 -> x6, starting transfers between devices: 24.5 us -> 18.8 us  [the longest x2 7.5 us: lat_halo(): south = lax.ppermute(rows[:1], 'lat', [(i + 1, i) for i in range(nlat - 1)])]
    concatenate x2 -> x3, other arithmetic: 0.25 us -> 2.63 us  [the longest x2 2.45 us: local(): message = jnp.concatenate([product_high, product_low], axis=2)]
    unnamed x15 -> x11, local copies, waits for them, and re-layouts: 4.04 us -> 1.99 us
    transpose x0 -> x2, local copies, waits for them, and re-layouts: none -> 1.14 us  [local(): targets_wide = jnp.swapaxes(wider[:, 1:lon_blocks + 3, :K, :], 2, 3)]
    ppermute x8 -> x6, waiting for transfers between devices: 12.3 us -> 11.4 us  [the longest x1 5.83 us: lon_halo(): lax.ppermute(cells[:, -depth:], 'lon', [(i, (i + 1) % nlon) for i in rang...]
  transfers between devices with their start and end apart: 8 -> 6, of which waited for: 4 -> 2; matrix products, arithmetic and copies ran while one was open for 3% -> 6% of each run, Pallas kernels for 30% -> 33%
where the time goes in v6:
time: 105 us
  Pallas kernels  60.5 us (58%)
  starting transfers between devices  18.8 us (18%)
  waiting for transfers between devices  11.4 us (11%)
  other arithmetic  7.7 us (7%)
  local copies, waits for them, and re-layouts  5.73 us (5%)
    pallas_call x4, Pallas kernels, rows_call(): pl.pallas_call(functools.partial(rows_kernel, plan, field_at, partial is...  60.5 us
    ppermute x2, starting transfers between devices, lat_halo(): south = lax.ppermute(rows[:1], 'lat', [(i + 1, i) for i in range(nlat - 1)])  7.5 us
    ppermute x2, starting transfers between devices, lat_halo(): lax.ppermute(rows[-1:], 'lat', [(i, i + 1) for i in range(nlat - 1)])  5.84 us
    ppermute x1, waiting for transfers between devices, lon_halo(): lax.ppermute(cells[:, -depth:], 'lon', [(i, (i + 1) % nlon) for i in rang...  5.83 us
    ppermute x2, waiting for transfers between devices, lat_halo(): lax.ppermute(rows[-1:], 'lat', [(i, i + 1) for i in range(nlat - 1)])  5.52 us
    ppermute x1, starting transfers between devices, lon_halo(): lax.ppermute(cells[:, :depth], 'lon', [((i + 1) % nlon, i) for i in range...  5.35 us
    convert_element_type x2, other arithmetic, split_high_low(): rounded.astype(jnp.bfloat16)  3.18 us
    concatenate x2, other arithmetic, local(): message = jnp.concatenate([product_high, product_low], axis=2)  2.45 us
  transfers between devices with their start and end apart: 6, of which 2 were waited for; matrix products, arithmetic and copies ran while one was open for 6% of the time, Pallas kernels for 33%

profile of v6, /device:TPU:2, one launch (start us, length us, event | category | flops | bytes accessed | tf_op | source)
XLA Modules:
  0.0 104.8 jit_solution(9055608600594117704)
XLA Ops:
  0.6 0.0 copy-start.4
  0.6 1.5 %reduce-precision_convert_fusion.1 = (bf16[2,8,128,128]{3,2,1,0:T(8,128)(2,1)S(1)}, bf16[2,8,128,128]{3,2,1,0:T(8,128)(2,1)S(1)}) fusion(f32[2,8,128,128]{3,2,1,0:T(8,128)} %param.5), kind=kLoop, calls=%fused_computation.9 | loop fusion | flops 1048576 | bytes 2097152 | tf_op jit(solution)/shard_map/convert_element_type | solution.py:111
  2.2 0.0 copy-done.4
  2.2 0.1 collective-permute-start
  2.3 5.3 %collective-permute-start.1 = (bf16[2,2,336,128]{3,2,1,0:T(8,128)(2,1)S(1)}, bf16[2,2,336,128]{3,2,1,0:T(8,128)(2,1)S(1)}, u32[]{:S(2)}, u32[]{:S(2)}) collective-permute-start(bf16[2,2,336,128]{3,2,1,0:T(8,128)(2,1)S(1)} %get-tuple-element.5), channel_id=1, source_target_pairs={{8,0},{16,8},{24,16},{32,24},{40,32},{48,40},{56,48},{64,56},{72,6... | collective-permute-start | bytes 1032200 | tf_op jit(solution)/shard_map/ppermute | solution.py:46
  7.7 5.8 %collective-permute-done = bf16[2,2,336,128]{3,2,1,0:T(8,128)(2,1)S(1)} collective-permute-done((bf16[2,2,336,128]{3,2,1,0:T(8,128)(2,1)S(1)}, bf16[2,2,336,128]{3,2,1,0:T(8,128)(2,1)S(1)}, u32[]{:S(2)}, u32[]{:S(2)}) %collective-permute-start) | collective-permute-done | bytes 344096 | tf_op jit(solution)/shard_map/ppermute | solution.py:45
  13.5 0.0 collective-permute-done.1
  13.5 0.2 pad_maximum_fusion.rest_0_
  13.7 0.0 copy-start
  13.7 1.6 %fusion.16 = (bf16[1,12,336,128]{3,2,1,0:T(8,128)(2,1)}, bf16[1,12,336,128]{3,2,1,0:T(8,128)(2,1)}) fusion(bf16[2,12,336,128]{3,2,1,0:T(8,128)(2,1)S(1)} %pad_maximum_fusion.rest_0_), kind=kLoop, calls=%fused_computation.50 | loop fusion | bytes 4128768 | tf_op jit(solution)/shard_map/slice | solution.py:53
  15.3 5.6 %collective-permute-start.3 = (bf16[1,12,336,128]{3,2,1,0:T(8,128)(2,1)}, bf16[1,12,336,128]{3,2,1,0:T(8,128)(2,1)S(1)}, u32[]{:S(2)}, u32[]{:S(2)}) collective-permute-start(bf16[1,12,336,128]{3,2,1,0:T(8,128)(2,1)} %get-tuple-element.2), channel_id=1, source_target_pairs={{1,0},{2,1},{3,2},{4,3},{5,4},{6,5},{7,6},{9,8},{10,9},{11,10},{12... | collective-permute-start | bytes 3096584 | tf_op jit(solution)/shard_map/ppermute | solution.py:53
  20.9 1.9 %collective-permute-start.2 = (bf16[1,12,336,128]{3,2,1,0:T(8,128)(2,1)}, bf16[1,12,336,128]{3,2,1,0:T(8,128)(2,1)S(1)}, u32[]{:S(2)}, u32[]{:S(2)}) collective-permute-start(bf16[1,12,336,128]{3,2,1,0:T(8,128)(2,1)} %get-tuple-element.3), channel_id=1, source_target_pairs={{0,1},{1,2},{2,3},{3,4},{4,5},{5,6},{6,7},{8,9},{9,10},{10,11},{11... | collective-permute-start | bytes 3096584 | tf_op jit(solution)/shard_map/ppermute | solution.py:52
  22.8 0.1 broadcast_subtract_fusion
  22.9 1.7 %fusion.6.taper_ref = f32[9,128,128]{2,1,0:T(8,128)} fusion(s32[128,128]{1,0:T(8,128)S(1)} %get-tuple-element.12, s32[9]{0:T(128)S(1)} %get-tuple-element.14, s32[128,128]{1,0:T(8,128)S(1)} %get-tuple-element.13, s32[9]{0:T(128)S(1)} %get-tuple-element.15), kind=kLoop, calls=%fused_computation.17 | loop fusion | flops 5160960 | bytes 720968 | tf_op jit(solution)/shard_map/div | solution.py:40
  24.7 1.1 %copy.5.targets_ref = bf16[2,10,128,80]{3,2,1,0:T(8,128)(2,1)} copy(bf16[2,10,128,80]{2,3,1,0:T(8,128)(2,1)S(1)} %slice_bitcast_fusion) | data formatting | bytes 819200 | tf_op jit(solution)/shard_map/transpose | solution.py:139
  25.8 18.9 %shard_map.41.rest_0_ = f32[2,10,128,128]{3,2,1,0:T(8,128)} custom-call(bf16[2,10,128,80]{3,2,1,0:T(8,128)(2,1)} %copy.5.targets_ref, f32[9,128,128]{2,1,0:T(8,128)} %fusion.6.taper_ref, bf16[2,12,336,128]{3,2,1,0:T(8,128)(2,1)} %copy-done), custom_call_target="tpu_custom_call" | custom-call | flops 1824522240 | bytes 4374528 | tf_op jit(solution)/shard_map/pallas_call | solution.py:100
  44.7 0.0 collective-permute-done.3.rest_2_
  44.7 5.5 %collective-permute-done.2.rest_1_ = bf16[1,12,336,128]{3,2,1,0:T(8,128)(2,1)S(1)} collective-permute-done((bf16[1,12,336,128]{3,2,1,0:T(8,128)(2,1)}, bf16[1,12,336,128]{3,2,1,0:T(8,128)(2,1)S(1)}, u32[]{:S(2)}, u32[]{:S(2)}) %collective-permute-start.2) | collective-permute-done | bytes 1032224 | tf_op jit(solution)/shard_map/ppermute | solution.py:52
  50.2 1.0 copy-done.3
  51.2 13.9 %shard_map.42 = f32[2,10,128,128]{3,2,1,0:T(8,128)} custom-call(bf16[2,10,128,80]{3,2,1,0:T(8,128)(2,1)} %copy.5.targets_ref, f32[9,128,128]{2,1,0:T(8,128)} %fusion.6.taper_ref, f32[2,10,128,128]{3,2,1,0:T(8,128)} %shard_map.41.rest_0_, bf16[1,12,336,128]{3,2,1,0:T(8,128)(2,1)} %copy-done.3, bf16[1,12,336,128]{3,2,1,0:T(8,128)(2,1)} %copy-done.2), custom_call_target="tpu_custom_call" | custom-call | flops 912261120 | bytes 5685248 | tf_op jit(solution)/shard_map/pallas_call | solution.py:100
  65.1 1.7 %reduce-precision_convert_fusion = (bf16[2,10,128,128]{3,2,1,0:T(8,128)(2,1)S(1)}, bf16[2,10,128,128]{3,2,1,0:T(8,128)(2,1)S(1)}) fusion(f32[2,10,128,128]{3,2,1,0:T(8,128)} %shard_map.42), kind=kLoop, calls=%fused_computation.2 | loop fusion | flops 1310720 | bytes 2621440 | tf_op jit(solution)/shard_map/convert_element_type | solution.py:111
  66.7 1.2 %fusion.3 = (bf16[1,10,256,128]{3,2,1,0:T(8,128)(2,1)}, bf16[1,10,256,128]{3,2,1,0:T(8,128)(2,1)}) fusion(bf16[2,10,128,128]{3,2,1,0:T(8,128)(2,1)S(1)} %get-tuple-element.8, bf16[2,10,128,128]{3,2,1,0:T(8,128)(2,1)S(1)} %get-tuple-element.9), kind=kLoop, calls=%fused_computation.14 | loop fusion | flops 2621440 | bytes 2621440 | tf_op jit(solution)/shard_map/concatenate | solution.py:147
  67.9 1.9 %collective-permute-start.5 = (bf16[1,10,256,128]{3,2,1,0:T(8,128)(2,1)}, bf16[1,10,256,128]{3,2,1,0:T(8,128)(2,1)}, u32[]{:S(2)}, u32[]{:S(2)}) collective-permute-start(bf16[1,10,256,128]{3,2,1,0:T(8,128)(2,1)} %get-tuple-element.6), channel_id=1, source_target_pairs={{1,0},{2,1},{3,2},{4,3},{5,4},{6,5},{7,6},{9,8},{10,9},{11,10},{12... | collective-permute-start | bytes 1966088 | tf_op jit(solution)/shard_map/ppermute | solution.py:53
  69.9 3.9 %collective-permute-start.4 = (bf16[1,10,256,128]{3,2,1,0:T(8,128)(2,1)}, bf16[1,10,256,128]{3,2,1,0:T(8,128)(2,1)}, u32[]{:S(2)}, u32[]{:S(2)}) collective-permute-start(bf16[1,10,256,128]{3,2,1,0:T(8,128)(2,1)} %get-tuple-element.7), channel_id=1, source_target_pairs={{0,1},{1,2},{2,3},{3,4},{4,5},{5,6},{6,7},{8,9},{9,10},{10,11},{11... | collective-permute-start | bytes 1966088 | tf_op jit(solution)/shard_map/ppermute | solution.py:52
  73.8 1.0 copy.6
  74.8 0.0 copy-done.1
  74.8 1.0 slice.35
  75.8 1.3 %pad_maximum_fusion.1.rest_1_ = bf16[2,10,256,128]{3,2,1,0:T(8,128)(2,1)} fusion(bf16[2,10,128,128]{3,2,1,0:T(8,128)(2,1)S(1)} %get-tuple-element.9, bf16[2,10,128,128]{3,2,1,0:T(8,128)(2,1)S(1)} %get-tuple-element.8), kind=kLoop, calls=%fused_computation.5 | loop fusion | flops 2621440 | bytes 2621440 | tf_op jit(solution)/shard_map/concatenate | solution.py:147
  77.1 15.9 %shard_map.43.rest_0_ = f32[2,8,128,128]{3,2,1,0:T(8,128)} custom-call(bf16[2,8,128,80]{3,2,1,0:T(8,128)(2,1)} %bitcast.3, f32[9,128,128]{2,1,0:T(8,128)} %fusion.6.taper_ref, bf16[2,12,336,128]{3,2,1,0:T(8,128)(2,1)} %copy-done, bf16[2,10,256,128]{3,2,1,0:T(8,128)(2,1)} %pad_maximum_fusion.1.rest_1_), custom_call_target="tpu_custom_call" | custom-call | flops 1459617792 | bytes 5341184 | tf_op jit(solution)/shard_map/pallas_call | solution.py:100
  93.0 0.0 collective-permute-done.5.rest_4_
  93.0 0.0 collective-permute-done.4.rest_3_
  93.0 11.8 %shard_map.44 = f32[2,8,128,128]{3,2,1,0:T(8,128)} custom-call(bf16[2,8,128,80]{3,2,1,0:T(8,128)(2,1)} %bitcast.4, f32[9,128,128]{2,1,0:T(8,128)} %fusion.6.taper_ref, f32[2,8,128,128]{3,2,1,0:T(8,128)} %shard_map.43.rest_0_, bf16[1,12,336,128]{3,2,1,0:T(8,128)(2,1)} %copy-done.3, bf16[1,12,336,128]{3,2,1,0:T(8,128)(2,1)} %copy-done.2, ...), custom_call_target="tpu_custom_call" | custom-call | flops 729808896 | bytes 6389760 | tf_op jit(solution)/shard_map/pallas_call | solution.py:100
  (10 shorter events, 0.1 us)
Async XLA Ops:
  0.6 1.5 %copy-start.4 = (bf16[2,8,80,128]{3,2,1,0:T(8,128)(2,1)S(1)}, bf16[2,8,80,128]{3,2,1,0:T(8,128)(2,1)}, u32[]{:S(2)}) copy-start(bf16[2,8,80,128]{3,2,1,0:T(8,128)(2,1)} %param.4) | copy-start | bytes 983044
  2.2 11.3 %collective-permute-start = (bf16[2,2,336,128]{3,2,1,0:T(8,128)(2,1)S(1)}, bf16[2,2,336,128]{3,2,1,0:T(8,128)(2,1)S(1)}, u32[]{:S(2)}, u32[]{:S(2)}) collective-permute-start(bf16[2,2,336,128]{3,2,1,0:T(8,128)(2,1)S(1)} %get-tuple-element.4), channel_id=1, source_target_pairs={{0,8},{8,16},{16,24},{24,32},{32,40},{40,48},{48,56},{56,64},{64,7... | collective-permute-start | bytes 1032200 | tf_op jit(solution)/shard_map/ppermute | solution.py:45
  2.3 11.2 %collective-permute-start.1 = (bf16[2,2,336,128]{3,2,1,0:T(8,128)(2,1)S(1)}, bf16[2,2,336,128]{3,2,1,0:T(8,128)(2,1)S(1)}, u32[]{:S(2)}, u32[]{:S(2)}) collective-permute-start(bf16[2,2,336,128]{3,2,1,0:T(8,128)(2,1)S(1)} %get-tuple-element.5), channel_id=1, source_target_pairs={{8,0},{16,8},{24,16},{32,24},{40,32},{48,40},{56,48},{64,56},{72,6... | collective-permute-start | bytes 1032200 | tf_op jit(solution)/shard_map/ppermute | solution.py:46
  13.7 10.9 %copy-start = (bf16[2,12,336,128]{3,2,1,0:T(8,128)(2,1)}, bf16[2,12,336,128]{3,2,1,0:T(8,128)(2,1)S(1)}, u32[]{:S(2)}) copy-start(bf16[2,12,336,128]{3,2,1,0:T(8,128)(2,1)S(1)} %pad_maximum_fusion.rest_0_) | copy-start | bytes 6193156
  15.3 29.4 %collective-permute-start.3 = (bf16[1,12,336,128]{3,2,1,0:T(8,128)(2,1)}, bf16[1,12,336,128]{3,2,1,0:T(8,128)(2,1)S(1)}, u32[]{:S(2)}, u32[]{:S(2)}) collective-permute-start(bf16[1,12,336,128]{3,2,1,0:T(8,128)(2,1)} %get-tuple-element.2), channel_id=1, source_target_pairs={{1,0},{2,1},{3,2},{4,3},{5,4},{6,5},{7,6},{9,8},{10,9},{11,10},{12... | collective-permute-start | bytes 3096584 | tf_op jit(solution)/shard_map/ppermute | solution.py:53
  20.9 29.3 %collective-permute-start.2 = (bf16[1,12,336,128]{3,2,1,0:T(8,128)(2,1)}, bf16[1,12,336,128]{3,2,1,0:T(8,128)(2,1)S(1)}, u32[]{:S(2)}, u32[]{:S(2)}) collective-permute-start(bf16[1,12,336,128]{3,2,1,0:T(8,128)(2,1)} %get-tuple-element.3), channel_id=1, source_target_pairs={{0,1},{1,2},{2,3},{3,4},{4,5},{5,6},{6,7},{8,9},{9,10},{10,11},{11... | collective-permute-start | bytes 3096584 | tf_op jit(solution)/shard_map/ppermute | solution.py:52
  44.7 5.5 %copy-start.2 = (bf16[1,12,336,128]{3,2,1,0:T(8,128)(2,1)}, bf16[1,12,336,128]{3,2,1,0:T(8,128)(2,1)S(1)}, u32[]{:S(2)}) copy-start(bf16[1,12,336,128]{3,2,1,0:T(8,128)(2,1)S(1)} %collective-permute-done.3.rest_2_) | copy-start | bytes 3096580
  50.2 1.0 copy-start.3
  66.7 8.1 %copy-start.1 = (f32[2,10,128,128]{3,2,1,0:T(8,128)S(1)}, f32[2,10,128,128]{3,2,1,0:T(8,128)}, u32[]{:S(2)}) copy-start(f32[2,10,128,128]{3,2,1,0:T(8,128)} %shard_map.42) | copy-start | bytes 3932164
  67.9 25.1 %collective-permute-start.5 = (bf16[1,10,256,128]{3,2,1,0:T(8,128)(2,1)}, bf16[1,10,256,128]{3,2,1,0:T(8,128)(2,1)}, u32[]{:S(2)}, u32[]{:S(2)}) collective-permute-start(bf16[1,10,256,128]{3,2,1,0:T(8,128)(2,1)} %get-tuple-element.6), channel_id=1, source_target_pairs={{1,0},{2,1},{3,2},{4,3},{5,4},{6,5},{7,6},{9,8},{10,9},{11,10},{12... | collective-permute-start | bytes 1966088 | tf_op jit(solution)/shard_map/ppermute | solution.py:53
  69.9 23.2 %collective-permute-start.4 = (bf16[1,10,256,128]{3,2,1,0:T(8,128)(2,1)}, bf16[1,10,256,128]{3,2,1,0:T(8,128)(2,1)}, u32[]{:S(2)}, u32[]{:S(2)}) collective-permute-start(bf16[1,10,256,128]{3,2,1,0:T(8,128)(2,1)} %get-tuple-element.7), channel_id=1, source_target_pairs={{0,1},{1,2},{2,3},{3,4},{4,5},{5,6},{6,7},{8,9},{9,10},{10,11},{11... | collective-permute-start | bytes 1966088 | tf_op jit(solution)/shard_map/ppermute | solution.py:52

commit v7 on v6

--- a/solution.py
+++ b/solution.py
@@ -47,32 +47,36 @@
     return jnp.concatenate([west, cells, east], axis=1)
 
 
-def lat_halo(rows):
+def lat_halo(first_row, last_row):
     nlat = lax.axis_size("lat")
-    north = lax.ppermute(rows[-1:], "lat", [(i, i + 1) for i in range(nlat - 1)])
-    south = lax.ppermute(rows[:1], "lat", [(i + 1, i) for i in range(nlat - 1)])
+    north = lax.ppermute(last_row, "lat", [(i, i + 1) for i in range(nlat - 1)])
+    south = lax.ppermute(first_row, "lat", [(i + 1, i) for i in range(nlat - 1)])
     return north, south
 
 
-def rows_kernel(plan, field_at, with_partial, targets_ref, taper_ref, *rest):
-    out_ref = rest[-1]
+def rows_kernel(plan, field_at, with_partial, target_off, emit, targets_ref, taper_ref, *rest):
+    outs = rest[-(1 + len(emit)) :] if emit else rest[-1:]
+    rest = rest[: len(rest) - len(outs)]
+    out_ref = outs[0]
     partial_ref = rest[0] if with_partial else None
-    sources = rest[1:-1] if with_partial else rest[:-1]
-    lat_blocks, lon_blocks, columns, rank = out_ref.shape
+    sources = rest[1:] if with_partial else rest
+    columns, rank = out_ref.shape[2:]
+    lat_blocks = out_ref.shape[0]
+    lon_blocks = partial_ref.shape[1] if emit else out_ref.shape[1]
     for p in range(lat_blocks):
 
         def one_block(q, carry, p=p, uses=plan[p]):
-            target = targets_ref[p, q]
+            target = targets_ref[p, q + target_off]
             if with_partial:
                 total = partial_ref[p, q]
             else:
                 total = jnp.zeros((columns, rank), jnp.float32)
-            for dr, members_at, field_from, row, members_off, field_off in uses:
+            for dr, members_at, members_row, field_from, row, members_off, field_off in uses:
                 members_ref, field_ref = sources[members_at], sources[field_from]
                 for dc in range(3):
                     gram = jnp.dot(
                         target,
-                        members_ref[row, q + dc + members_off, :K, :],
+                        members_ref[members_row, q + dc + members_off, :K, :],
                         preferred_element_type=jnp.float32,
                     )
                     tile = gram * taper_ref[dr * 3 + dc]
@@ -84,26 +88,44 @@
                     total = total + jnp.dot(tile_high, field_high, preferred_element_type=jnp.float32)
                     total = total + jnp.dot(tile_high, field_low, preferred_element_type=jnp.float32)
                     total = total + jnp.dot(tile_low, field_high, preferred_element_type=jnp.float32)
-            out_ref[p, q] = total
+            if emit:
+                inner = out_ref.shape[1]
+                shift = (lon_blocks - inner) // 2
+
+                @pl.when((q >= shift) & (q < shift + inner))
+                def _():
+                    out_ref[p, jnp.clip(q - shift, 0, inner - 1)] = total
+
+                high = total.astype(jnp.bfloat16)
+                low = (total - high.astype(jnp.float32)).astype(jnp.bfloat16)
+                row_ref = outs[1 + emit[p]]
+                row_ref[0, q, :columns, :] = high
+                row_ref[0, q, columns:, :] = low
+            else:
+                out_ref[p, q] = total
             return carry
 
         lax.fori_loop(0, lon_blocks, one_block, 0)
 
 
-def rows_call(plan, field_at, targets, taper, partial, sources, out_like):
-    lat_blocks, lon_blocks, columns, rank = out_like.shape
+def rows_call(plan, field_at, targets, taper, partial, sources, out_like, target_off=0, emit=()):
+    lat_blocks, lon_blocks, columns, rank = (partial if emit else out_like).shape
     codes = sum(3 * len(uses) for uses in plan)
     flops = lon_blocks * codes * 2 * columns * (K * columns + 3 * columns * rank)
     operands = [targets, taper] + ([partial] if partial is not None else []) + list(sources)
-    moved = sum(x.size * x.dtype.itemsize for x in operands) + out_like.size * 4
+    shapes = [jax.ShapeDtypeStruct(out_like.shape, jnp.float32)]
+    if emit:
+        shapes += [jax.ShapeDtypeStruct((1, lon_blocks, 2 * columns, rank), jnp.bfloat16)] * len(emit)
+    moved = sum(x.size * x.dtype.itemsize for x in operands + shapes)
     vmem = pl.BlockSpec(memory_space=pltpu.VMEM)
-    return pl.pallas_call(
-        functools.partial(rows_kernel, plan, field_at, partial is not None),
-        out_shape=jax.ShapeDtypeStruct(out_like.shape, jnp.float32),
+    result = pl.pallas_call(
+        functools.partial(rows_kernel, plan, field_at, partial is not None, target_off, emit),
+        out_shape=tuple(shapes) if emit else shapes[0],
         in_specs=[vmem] * len(operands),
-        out_specs=vmem,
+        out_specs=tuple([vmem] * len(shapes)) if emit else vmem,
         cost_estimate=pl.CostEstimate(flops=flops, bytes_accessed=moved, transcendentals=0),
     )(*operands)
+    return result
 
 
 def split_high_low(field):
@@ -111,9 +133,14 @@
     return rounded.astype(jnp.bfloat16), (field - rounded).astype(jnp.bfloat16)
 
 
-def own_plan(lat_blocks, members, field, offsets):
+def own_plan(lat_blocks, members, fields, offsets):
     return tuple(
-        tuple((dr, members, field, p + dr - 1) + offsets for dr in range(3) if 0 <= p + dr - 1 < lat_blocks)
+        tuple(
+            (dr, members, p + dr - 1, fields[p + dr - 1], p + dr - 1 if len(set(fields)) == 1 else 0)
+            + offsets
+            for dr in range(3)
+            if 0 <= p + dr - 1 < lat_blocks
+        )
         for p in range(lat_blocks)
     )
 
@@ -121,7 +148,7 @@
 def halo_plan(lat_blocks, members, field, offsets):
     return tuple(
         tuple(
-            (dr, members[p + dr > 0], field[p + dr > 0], 0) + offsets
+            (dr, members[p + dr > 0], 0, field[p + dr > 0], 0) + offsets
             for dr in range(3)
             if not 0 <= p + dr - 1 < lat_blocks
         )
@@ -135,27 +162,43 @@
     taper = taper_by_code()
     panel_high, panel_low = split_high_low(panel)
     wider = lon_halo(jnp.concatenate([anomalies, panel_high, panel_low], axis=2), 2)
-    north, south = lat_halo(wider)
+    north, south = lat_halo(wider[:1], wider[-1:])
     targets_wide = jnp.swapaxes(wider[:, 1 : lon_blocks + 3, :K, :], 2, 3)
     like_wide = jax.ShapeDtypeStruct((lat_blocks, lon_blocks + 2) + panel.shape[2:], jnp.float32)
-    partial = rows_call(own_plan(lat_blocks, 0, 0, (0, 0)), K, targets_wide, taper, None, (wider,), like_wide)
-    product_wide = rows_call(
-        halo_plan(lat_blocks, (0, 1), (0, 1), (0, 0)), K, targets_wide, taper, partial, (north, south), like_wide
-    )
-    first_product = product_wide[:, 1 : lon_blocks + 1]
-    product_high, product_low = split_high_low(product_wide)
-    message = jnp.concatenate([product_high, product_low], axis=2)
-    north2, south2 = lat_halo(message)
-    targets = jnp.swapaxes(anomalies, 2, 3)
-    partial = rows_call(own_plan(lat_blocks, 0, 1, (1, 0)), 0, targets, taper, None, (wider, message), panel)
+    own_fields = (0,) * lat_blocks
+    partial = rows_call(own_plan(lat_blocks, 0, own_fields, (0, 0)), K, targets_wide, taper, None, (wider,), like_wide)
+    emit = tuple(0 if p == 0 else 1 for p in range(lat_blocks))
+    first_product, first_row, last_row = rows_call(
+        halo_plan(lat_blocks, (0, 1), (0, 1), (0, 0)),
+        K,
+        targets_wide,
+        taper,
+        partial,
+        (north, south),
+        panel,
+        emit=emit,
+    )
+    north2, south2 = lat_halo(first_row, last_row)
+    row_fields = (1, 2) if lat_blocks == 2 else None
+    partial = rows_call(
+        own_plan(lat_blocks, 0, row_fields, (1, 0)),
+        0,
+        targets_wide,
+        taper,
+        None,
+        (wider, first_row, last_row),
+        panel,
+        target_off=1,
+    )
     second_product = rows_call(
         halo_plan(lat_blocks, (0, 1), (2, 3), (1, 0)),
         0,
-        targets,
+        targets_wide,
         taper,
         partial,
         (north, south, north2, south2),
         panel,
+        target_off=1,
     )
     return (first_product, second_product)
 

time: 105 us -> 101 us (0.962)
  other arithmetic: 7.7 us -> 3.57 us
  local copies, waits for them, and re-layouts: 5.73 us -> 3.58 us
  waiting for transfers between devices: 11.4 us -> 12.9 us
    concatenate x2 -> x0, other arithmetic: 2.45 us -> none  [local(): message = jnp.concatenate([product_high, product_low], axis=2)]
    convert_element_type x2 -> x1, other arithmetic: 3.18 us -> 1.53 us  [split_high_low(): rounded.astype(jnp.bfloat16)]
    ppermute x4, waiting for transfers between devices: 5.53 us -> 7.07 us  [the longest x2 7.07 us: lat_halo(): north = lax.ppermute(last_row, 'lat', [(i, i + 1) for i in range(nlat - 1)])]
    unnamed x11 -> x10, local copies, waits for them, and re-layouts: 1.99 us -> 0.88 us
    slice x2 -> x1, local copies, waits for them, and re-layouts: 2.6 us -> 1.57 us  [local(): north, south = lat_halo(wider[:1], wider[-1:])]
  transfers between devices with their start and end apart: 6 -> 6, of which waited for: 2 -> 3; matrix products, arithmetic and copies ran while one was open for 6% -> 3% of each run, Pallas kernels for 33% -> 35%
where the time goes in v7:
time: 101 us
  Pallas kernels  61 us (60%)
  starting transfers between devices  18.8 us (19%)
  waiting for transfers between devices  12.9 us (13%)
  local copies, waits for them, and re-layouts  3.58 us (4%)
  other arithmetic  3.57 us (4%)
    pallas_call x4, Pallas kernels, rows_call(): pl.pallas_call(functools.partial(rows_kernel, plan, field_at, partial is...  61 us
    ppermute x2, starting transfers between devices, lat_halo(): lax.ppermute(first_row, 'lat', [(i + 1, i) for i in range(nlat - 1)])  7.5 us
    ppermute x2, waiting for transfers between devices, lat_halo(): north = lax.ppermute(last_row, 'lat', [(i, i + 1) for i in range(nlat - 1)])  7.07 us
    ppermute x2, starting transfers between devices, lat_halo(): north = lax.ppermute(last_row, 'lat', [(i, i + 1) for i in range(nlat - 1)])  5.84 us
    ppermute x1, waiting for transfers between devices, lon_halo(): lax.ppermute(cells[:, -depth:], 'lon', [(i, (i + 1) % nlon) for i in rang...  5.83 us
    ppermute x1, starting transfers between devices, lon_halo(): lax.ppermute(cells[:, :depth], 'lon', [((i + 1) % nlon, i) for i in range...  5.35 us
  transfers between devices with their start and end apart: 6, of which 3 were waited for; matrix products, arithmetic and copies ran while one was open for 3% of the time, Pallas kernels for 35%

profile of v7, /device:TPU:2, one launch (start us, length us, event | category | flops | bytes accessed | tf_op | source)
XLA Modules:
  0.0 100.6 jit_solution(3551565540033847061)
XLA Ops:
  0.6 0.0 copy-start.2
  0.6 1.5 %reduce-precision_convert_fusion = (bf16[2,8,128,128]{3,2,1,0:T(8,128)(2,1)S(1)}, bf16[2,8,128,128]{3,2,1,0:T(8,128)(2,1)S(1)}) fusion(f32[2,8,128,128]{3,2,1,0:T(8,128)} %param.5), kind=kLoop, calls=%fused_computation.2 | loop fusion | flops 1048576 | bytes 2097152 | tf_op jit(solution)/shard_map/convert_element_type | solution.py:133
  2.2 0.0 copy-done.2
  2.2 0.1 collective-permute-start
  2.3 5.3 %collective-permute-start.1 = (bf16[2,2,336,128]{3,2,1,0:T(8,128)(2,1)S(1)}, bf16[2,2,336,128]{3,2,1,0:T(8,128)(2,1)S(1)}, u32[]{:S(2)}, u32[]{:S(2)}) collective-permute-start(bf16[2,2,336,128]{3,2,1,0:T(8,128)(2,1)S(1)} %get-tuple-element.11), channel_id=1, source_target_pairs={{8,0},{16,8},{24,16},{32,24},{40,32},{48,40},{56,48},{64,56},{72,6... | collective-permute-start | bytes 1032200 | tf_op jit(solution)/shard_map/ppermute | solution.py:46
  7.7 5.8 %collective-permute-done = bf16[2,2,336,128]{3,2,1,0:T(8,128)(2,1)S(1)} collective-permute-done((bf16[2,2,336,128]{3,2,1,0:T(8,128)(2,1)S(1)}, bf16[2,2,336,128]{3,2,1,0:T(8,128)(2,1)S(1)}, u32[]{:S(2)}, u32[]{:S(2)}) %collective-permute-start) | collective-permute-done | bytes 344096 | tf_op jit(solution)/shard_map/ppermute | solution.py:45
  13.5 0.0 collective-permute-done.1
  13.5 0.2 pad_maximum_fusion.rest_0_
  13.7 0.0 copy-start
  13.7 1.6 %fusion.13 = (bf16[1,12,336,128]{3,2,1,0:T(8,128)(2,1)}, bf16[1,12,336,128]{3,2,1,0:T(8,128)(2,1)}) fusion(bf16[2,12,336,128]{3,2,1,0:T(8,128)(2,1)S(1)} %pad_maximum_fusion.rest_0_), kind=kLoop, calls=%fused_computation.40 | loop fusion | bytes 4128768 | tf_op jit(solution)/shard_map/slice | solution.py:165
  15.3 5.6 %collective-permute-start.3 = (bf16[1,12,336,128]{3,2,1,0:T(8,128)(2,1)}, bf16[1,12,336,128]{3,2,1,0:T(8,128)(2,1)S(1)}, u32[]{:S(2)}, u32[]{:S(2)}) collective-permute-start(bf16[1,12,336,128]{3,2,1,0:T(8,128)(2,1)} %get-tuple-element.8), channel_id=1, source_target_pairs={{1,0},{2,1},{3,2},{4,3},{5,4},{6,5},{7,6},{9,8},{10,9},{11,10},{12... | collective-permute-start | bytes 3096584 | tf_op jit(solution)/shard_map/ppermute | solution.py:53
  20.9 1.9 %collective-permute-start.2 = (bf16[1,12,336,128]{3,2,1,0:T(8,128)(2,1)}, bf16[1,12,336,128]{3,2,1,0:T(8,128)(2,1)}, u32[]{:S(2)}, u32[]{:S(2)}) collective-permute-start(bf16[1,12,336,128]{3,2,1,0:T(8,128)(2,1)} %get-tuple-element.9), channel_id=1, source_target_pairs={{0,1},{1,2},{2,3},{3,4},{4,5},{5,6},{6,7},{8,9},{9,10},{10,11},{11... | collective-permute-start | bytes 3096584 | tf_op jit(solution)/shard_map/ppermute | solution.py:52
  22.8 0.1 broadcast_subtract_fusion
  22.9 1.7 %fusion.3.taper_ref = f32[9,128,128]{2,1,0:T(8,128)} fusion(s32[128,128]{1,0:T(8,128)S(1)} %get-tuple-element.14, s32[9]{0:T(128)S(1)} %get-tuple-element.16, s32[128,128]{1,0:T(8,128)S(1)} %get-tuple-element.15, s32[9]{0:T(128)S(1)} %get-tuple-element.17), kind=kLoop, calls=%fused_computation.7 | loop fusion | flops 5160960 | bytes 720968 | tf_op jit(solution)/shard_map/div | solution.py:40
  24.6 0.0 copy-done
  24.7 1.1 %copy.5.targets_ref = bf16[2,10,128,80]{3,2,1,0:T(8,128)(2,1)} copy(bf16[2,10,128,80]{2,3,1,0:T(8,128)(2,1)S(1)} %slice_bitcast_fusion) | data formatting | bytes 819200 | tf_op jit(solution)/shard_map/transpose | solution.py:166
  25.8 18.9 %shard_map.41.rest_0_ = f32[2,10,128,128]{3,2,1,0:T(8,128)} custom-call(bf16[2,10,128,80]{3,2,1,0:T(8,128)(2,1)} %copy.5.targets_ref, f32[9,128,128]{2,1,0:T(8,128)} %fusion.3.taper_ref, bf16[2,12,336,128]{3,2,1,0:T(8,128)(2,1)} %copy-done), custom_call_target="tpu_custom_call" | custom-call | flops 1824522240 | bytes 4374528 | tf_op jit(solution)/shard_map/pallas_call | solution.py:121
  44.7 0.0 collective-permute-done.3.rest_2_
  44.7 0.0 copy-start.1
  44.7 5.7 %collective-permute-done.2.rest_1_ = bf16[1,12,336,128]{3,2,1,0:T(8,128)(2,1)} collective-permute-done((bf16[1,12,336,128]{3,2,1,0:T(8,128)(2,1)}, bf16[1,12,336,128]{3,2,1,0:T(8,128)(2,1)}, u32[]{:S(2)}, u32[]{:S(2)}) %collective-permute-start.2) | collective-permute-done | bytes 1032224 | tf_op jit(solution)/shard_map/ppermute | solution.py:52
  50.4 0.0 copy-done.1
  50.4 14.3 %shard_map.42 = (f32[2,8,128,128]{3,2,1,0:T(8,128)}, bf16[1,10,256,128]{3,2,1,0:T(8,128)(2,1)}, bf16[1,10,256,128]{3,2,1,0:T(8,128)(2,1)}) custom-call(bf16[2,10,128,80]{3,2,1,0:T(8,128)(2,1)} %copy.5.targets_ref, f32[9,128,128]{2,1,0:T(8,128)} %fusion.3.taper_ref, f32[2,10,128,128]{3,2,1,0:T(8,128)} %shard_map.41.rest_0_, ...), custom_call_target="tpu_custom_call" | custom-call | flops 912261120 | bytes 6733824 | tf_op jit(solution)/shard_map/pallas_call | solution.py:121
  64.7 1.9 %collective-permute-start.5 = (bf16[1,10,256,128]{3,2,1,0:T(8,128)(2,1)}, bf16[1,10,256,128]{3,2,1,0:T(8,128)(2,1)S(1)}, u32[]{:S(2)}, u32[]{:S(2)}) collective-permute-start(bf16[1,10,256,128]{3,2,1,0:T(8,128)(2,1)} %get-tuple-element.6.rest_1_), channel_id=1, source_target_pairs={{1,0},{2,1},{3,2},{4,3},{5,4},{6,5},{7,6},{9,8},{10,9},{11,10},{12... | collective-permute-start | bytes 1966088 | tf_op jit(solution)/shard_map/ppermute | solution.py:53
  66.6 3.9 %collective-permute-start.4 = (bf16[1,10,256,128]{3,2,1,0:T(8,128)(2,1)}, bf16[1,10,256,128]{3,2,1,0:T(8,128)(2,1)S(1)}, u32[]{:S(2)}, u32[]{:S(2)}) collective-permute-start(bf16[1,10,256,128]{3,2,1,0:T(8,128)(2,1)} %get-tuple-element.7.rest_2_), channel_id=1, source_target_pairs={{0,1},{1,2},{2,3},{3,4},{4,5},{5,6},{6,7},{8,9},{9,10},{10,11},{11... | collective-permute-start | bytes 1966088 | tf_op jit(solution)/shard_map/ppermute | solution.py:52
  70.5 15.9 %shard_map.43.rest_0_ = f32[2,8,128,128]{3,2,1,0:T(8,128)} custom-call(bf16[2,10,128,80]{3,2,1,0:T(8,128)(2,1)} %copy.5.targets_ref, f32[9,128,128]{2,1,0:T(8,128)} %fusion.3.taper_ref, bf16[2,12,336,128]{3,2,1,0:T(8,128)(2,1)} %copy-done, bf16[1,10,256,128]{3,2,1,0:T(8,128)(2,1)} %get-tuple-element.6.rest_1_, bf16[1,10,256,128]{3,2,1,0:T(8,128)(2,1)} %get-tuple-element.7.rest_2_), custom_call_target="tpu_custom_call" | custom-call | flops 1459617792 | bytes 5423104 | tf_op jit(solution)/shard_map/pallas_call | solution.py:121
  86.4 0.0 collective-permute-done.5.rest_4_
  86.4 0.0 copy-start.3
  86.4 1.4 %collective-permute-done.4.rest_3_ = bf16[1,10,256,128]{3,2,1,0:T(8,128)(2,1)S(1)} collective-permute-done((bf16[1,10,256,128]{3,2,1,0:T(8,128)(2,1)}, bf16[1,10,256,128]{3,2,1,0:T(8,128)(2,1)S(1)}, u32[]{:S(2)}, u32[]{:S(2)}) %collective-permute-start.4) | collective-permute-done | bytes 655392 | tf_op jit(solution)/shard_map/ppermute | solution.py:52
  87.8 0.0 copy-done.3
  87.8 0.0 copy-start.4
  87.8 0.9 copy-done.4
  88.7 11.9 %shard_map.44 = f32[2,8,128,128]{3,2,1,0:T(8,128)} custom-call(bf16[2,10,128,80]{3,2,1,0:T(8,128)(2,1)} %copy.5.targets_ref, f32[9,128,128]{2,1,0:T(8,128)} %fusion.3.taper_ref, f32[2,8,128,128]{3,2,1,0:T(8,128)} %shard_map.43.rest_0_, bf16[1,12,336,128]{3,2,1,0:T(8,128)(2,1)} %collective-permute-done.2.rest_1_, bf16[1,12,336,128]{3,2,1,0:T(8,128)(2,1)} %copy-done.1, ...), custom_call_target="tpu_custom_call" | custom-call | flops 729808896 | bytes 6471680 | tf_op jit(solution)/shard_map/pallas_call | solution.py:121
  (5 shorter events, 0.1 us)
Async XLA Ops:
  0.6 1.5 %copy-start.2 = (bf16[2,8,80,128]{3,2,1,0:T(8,128)(2,1)S(1)}, bf16[2,8,80,128]{3,2,1,0:T(8,128)(2,1)}, u32[]{:S(2)}) copy-start(bf16[2,8,80,128]{3,2,1,0:T(8,128)(2,1)} %param.4) | copy-start | bytes 983044
  2.2 11.3 %collective-permute-start = (bf16[2,2,336,128]{3,2,1,0:T(8,128)(2,1)S(1)}, bf16[2,2,336,128]{3,2,1,0:T(8,128)(2,1)S(1)}, u32[]{:S(2)}, u32[]{:S(2)}) collective-permute-start(bf16[2,2,336,128]{3,2,1,0:T(8,128)(2,1)S(1)} %get-tuple-element.10), channel_id=1, source_target_pairs={{0,8},{8,16},{16,24},{24,32},{32,40},{40,48},{48,56},{56,64},{64,7... | collective-permute-start | bytes 1032200 | tf_op jit(solution)/shard_map/ppermute | solution.py:45
  2.3 11.2 %collective-permute-start.1 = (bf16[2,2,336,128]{3,2,1,0:T(8,128)(2,1)S(1)}, bf16[2,2,336,128]{3,2,1,0:T(8,128)(2,1)S(1)}, u32[]{:S(2)}, u32[]{:S(2)}) collective-permute-start(bf16[2,2,336,128]{3,2,1,0:T(8,128)(2,1)S(1)} %get-tuple-element.11), channel_id=1, source_target_pairs={{8,0},{16,8},{24,16},{32,24},{40,32},{48,40},{56,48},{64,56},{72,6... | collective-permute-start | bytes 1032200 | tf_op jit(solution)/shard_map/ppermute | solution.py:46
  13.7 10.9 %copy-start = (bf16[2,12,336,128]{3,2,1,0:T(8,128)(2,1)}, bf16[2,12,336,128]{3,2,1,0:T(8,128)(2,1)S(1)}, u32[]{:S(2)}) copy-start(bf16[2,12,336,128]{3,2,1,0:T(8,128)(2,1)S(1)} %pad_maximum_fusion.rest_0_) | copy-start | bytes 6193156
  15.3 29.4 %collective-permute-start.3 = (bf16[1,12,336,128]{3,2,1,0:T(8,128)(2,1)}, bf16[1,12,336,128]{3,2,1,0:T(8,128)(2,1)S(1)}, u32[]{:S(2)}, u32[]{:S(2)}) collective-permute-start(bf16[1,12,336,128]{3,2,1,0:T(8,128)(2,1)} %get-tuple-element.8), channel_id=1, source_target_pairs={{1,0},{2,1},{3,2},{4,3},{5,4},{6,5},{7,6},{9,8},{10,9},{11,10},{12... | collective-permute-start | bytes 3096584 | tf_op jit(solution)/shard_map/ppermute | solution.py:53
  20.9 29.5 %collective-permute-start.2 = (bf16[1,12,336,128]{3,2,1,0:T(8,128)(2,1)}, bf16[1,12,336,128]{3,2,1,0:T(8,128)(2,1)}, u32[]{:S(2)}, u32[]{:S(2)}) collective-permute-start(bf16[1,12,336,128]{3,2,1,0:T(8,128)(2,1)} %get-tuple-element.9), channel_id=1, source_target_pairs={{0,1},{1,2},{2,3},{3,4},{4,5},{5,6},{6,7},{8,9},{9,10},{10,11},{11... | collective-permute-start | bytes 3096584 | tf_op jit(solution)/shard_map/ppermute | solution.py:52
  44.7 5.7 %copy-start.1 = (bf16[1,12,336,128]{3,2,1,0:T(8,128)(2,1)}, bf16[1,12,336,128]{3,2,1,0:T(8,128)(2,1)S(1)}, u32[]{:S(2)}) copy-start(bf16[1,12,336,128]{3,2,1,0:T(8,128)(2,1)S(1)} %collective-permute-done.3.rest_2_) | copy-start | bytes 3096580
  64.7 21.8 %collective-permute-start.5 = (bf16[1,10,256,128]{3,2,1,0:T(8,128)(2,1)}, bf16[1,10,256,128]{3,2,1,0:T(8,128)(2,1)S(1)}, u32[]{:S(2)}, u32[]{:S(2)}) collective-permute-start(bf16[1,10,256,128]{3,2,1,0:T(8,128)(2,1)} %get-tuple-element.6.rest_1_), channel_id=1, source_target_pairs={{1,0},{2,1},{3,2},{4,3},{5,4},{6,5},{7,6},{9,8},{10,9},{11,10},{12... | collective-permute-start | bytes 1966088 | tf_op jit(solution)/shard_map/ppermute | solution.py:53
  66.6 21.2 %collective-permute-start.4 = (bf16[1,10,256,128]{3,2,1,0:T(8,128)(2,1)}, bf16[1,10,256,128]{3,2,1,0:T(8,128)(2,1)S(1)}, u32[]{:S(2)}, u32[]{:S(2)}) collective-permute-start(bf16[1,10,256,128]{3,2,1,0:T(8,128)(2,1)} %get-tuple-element.7.rest_2_), channel_id=1, source_target_pairs={{0,1},{1,2},{2,3},{3,4},{4,5},{5,6},{6,7},{8,9},{9,10},{10,11},{11... | collective-permute-start | bytes 1966088 | tf_op jit(solution)/shard_map/ppermute | solution.py:52
  86.4 1.4 %copy-start.3 = (bf16[1,10,256,128]{3,2,1,0:T(8,128)(2,1)}, bf16[1,10,256,128]{3,2,1,0:T(8,128)(2,1)S(1)}, u32[]{:S(2)}) copy-start(bf16[1,10,256,128]{3,2,1,0:T(8,128)(2,1)S(1)} %collective-permute-done.5.rest_4_) | copy-start | bytes 1966084
  87.8 0.9 copy-start.4

commit v8 on v7

--- a/solution.py
+++ b/solution.py
@@ -1,4 +1,6 @@
 import functools
+
+import numpy as np
 
 import jax
 import jax.numpy as jnp
@@ -14,37 +16,35 @@
 CODES = 9
 
 
-def gaspari_cohn(shift_rows, shift_cols):
-    position = jnp.arange(COLS)
+def taper_by_code():
+    codes = np.arange(CODES)
+    shift_rows = ((codes // 3 - 1) * (COLS // STRIDE))[:, None, None]
+    shift_cols = ((codes % 3 - 1) * STRIDE)[:, None, None]
+    position = np.arange(COLS)
     row_within = position // STRIDE
     col_within = position % STRIDE
-    delta_rows = shift_rows[..., None, None] + (row_within[None, :] - row_within[:, None])
-    delta_cols = shift_cols[..., None, None] + (col_within[None, :] - col_within[:, None])
-    squared = (delta_rows * delta_rows + delta_cols * delta_cols).astype(jnp.float32)
-    scaled = jnp.sqrt(squared + 0.25) / RADIUS
+    delta_rows = shift_rows + (row_within[None, :] - row_within[:, None])
+    delta_cols = shift_cols + (col_within[None, :] - col_within[:, None])
+    squared = (delta_rows * delta_rows + delta_cols * delta_cols).astype(np.float32)
+    f = np.float32
+    scaled = np.sqrt(squared + f(0.25)) / f(RADIUS)
     inside = (
-        ((-0.25 * scaled + 0.5) * scaled + 0.625) * scaled - 5.0 / 3.0
-    ) * scaled * scaled + 1.0
+        ((f(-0.25) * scaled + f(0.5)) * scaled + f(0.625)) * scaled - f(5.0 / 3.0)
+    ) * scaled * scaled + f(1.0)
     outside = (
-        ((((scaled / 12.0 - 0.5) * scaled + 0.625) * scaled + 5.0 / 3.0) * scaled - 5.0) * scaled
-        + 4.0
-        - 2.0 / (3.0 * scaled)
-    )
-    return jnp.where(scaled <= 1.0, inside, jnp.where(scaled <= 2.0, outside, 0.0))
-
-
-def taper_by_code():
-    codes = jnp.arange(CODES, dtype=jnp.int32)
-    shift_rows = (codes // 3 - 1) * (COLS // STRIDE)
-    shift_cols = (codes % 3 - 1) * STRIDE
-    return gaspari_cohn(shift_rows, shift_cols) / (K - 1)
+        ((((scaled / f(12.0) - f(0.5)) * scaled + f(0.625)) * scaled + f(5.0 / 3.0)) * scaled - f(5.0)) * scaled
+        + f(4.0)
+        - f(2.0) / (f(3.0) * scaled)
+    )
+    table = np.where(scaled <= 1.0, inside, np.where(scaled <= 2.0, outside, f(0.0))).astype(np.float32)
+    return jnp.asarray(table / f(K - 1))
 
 
 def lon_halo(cells, depth):
     nlon = lax.axis_size("lon")
     west = lax.ppermute(cells[:, -depth:], "lon", [(i, (i + 1) % nlon) for i in range(nlon)])
     east = lax.ppermute(cells[:, :depth], "lon", [((i + 1) % nlon, i) for i in range(nlon)])
-    return jnp.concatenate([west, cells, east], axis=1)
+    return jnp.concatenate([west, cells, east], axis=1), west, east
 
 
 def lat_halo(first_row, last_row):
@@ -54,7 +54,7 @@
     return north, south
 
 
-def rows_kernel(plan, field_at, with_partial, target_off, emit, targets_ref, taper_ref, *rest):
+def rows_kernel(plan, field_at, with_partial, target_off, emit, targets_ref, edges_ref, taper_ref, *rest):
     outs = rest[-(1 + len(emit)) :] if emit else rest[-1:]
     rest = rest[: len(rest) - len(outs)]
     out_ref = outs[0]
@@ -65,8 +65,11 @@
     lon_blocks = partial_ref.shape[1] if emit else out_ref.shape[1]
     for p in range(lat_blocks):
 
-        def one_block(q, carry, p=p, uses=plan[p]):
-            target = targets_ref[p, q + target_off]
+        def one_block(q, carry, p=p, uses=plan[p], side=None):
+            if side is None:
+                target = targets_ref[p, q + target_off]
+            else:
+                target = edges_ref[p, side]
             if with_partial:
                 total = partial_ref[p, q]
             else:
@@ -105,21 +108,42 @@
                 out_ref[p, q] = total
             return carry
 
-        lax.fori_loop(0, lon_blocks, one_block, 0)
-
-
-def rows_call(plan, field_at, targets, taper, partial, sources, out_like, target_off=0, emit=()):
+        if edges_ref is None:
+            lax.fori_loop(0, lon_blocks, one_block, 0)
+        else:
+            one_block(0, 0, side=0)
+            lax.fori_loop(1, lon_blocks - 1, one_block, 0)
+            one_block(lon_blocks - 1, 0, side=1)
+
+
+def kernel_with_edges(*args):
+    return rows_kernel(*args)
+
+
+def kernel_without_edges(plan, field_at, with_partial, target_off, emit, targets_ref, *rest):
+    return rows_kernel(plan, field_at, with_partial, target_off, emit, targets_ref, None, *rest)
+
+
+def rows_call(plan, field_at, targets, taper, partial, sources, out_like, target_off=0, emit=(), edges=None):
     lat_blocks, lon_blocks, columns, rank = (partial if emit else out_like).shape
     codes = sum(3 * len(uses) for uses in plan)
     flops = lon_blocks * codes * 2 * columns * (K * columns + 3 * columns * rank)
-    operands = [targets, taper] + ([partial] if partial is not None else []) + list(sources)
+    operands = [targets] + ([edges] if edges is not None else []) + [taper]
+    operands += ([partial] if partial is not None else []) + list(sources)
     shapes = [jax.ShapeDtypeStruct(out_like.shape, jnp.float32)]
     if emit:
         shapes += [jax.ShapeDtypeStruct((1, lon_blocks, 2 * columns, rank), jnp.bfloat16)] * len(emit)
     moved = sum(x.size * x.dtype.itemsize for x in operands + shapes)
     vmem = pl.BlockSpec(memory_space=pltpu.VMEM)
     result = pl.pallas_call(
-        functools.partial(rows_kernel, plan, field_at, partial is not None, target_off, emit),
+        functools.partial(
+            kernel_with_edges if edges is not None else kernel_without_edges,
+            plan,
+            field_at,
+            partial is not None,
+            target_off,
+            emit,
+        ),
         out_shape=tuple(shapes) if emit else shapes[0],
         in_specs=[vmem] * len(operands),
         out_specs=tuple([vmem] * len(shapes)) if emit else vmem,
@@ -161,44 +185,55 @@
     lat_blocks, lon_blocks = anomalies.shape[:2]
     taper = taper_by_code()
     panel_high, panel_low = split_high_low(panel)
-    wider = lon_halo(jnp.concatenate([anomalies, panel_high, panel_low], axis=2), 2)
+    wider, west, east = lon_halo(jnp.concatenate([anomalies, panel_high, panel_low], axis=2), 2)
     north, south = lat_halo(wider[:1], wider[-1:])
-    targets_wide = jnp.swapaxes(wider[:, 1 : lon_blocks + 3, :K, :], 2, 3)
+    targets = jnp.swapaxes(anomalies, 2, 3)
+    edges = jnp.swapaxes(jnp.concatenate([west[:, 1:, :K, :], east[:, :1, :K, :]], axis=1), 2, 3)
     like_wide = jax.ShapeDtypeStruct((lat_blocks, lon_blocks + 2) + panel.shape[2:], jnp.float32)
     own_fields = (0,) * lat_blocks
-    partial = rows_call(own_plan(lat_blocks, 0, own_fields, (0, 0)), K, targets_wide, taper, None, (wider,), like_wide)
+    partial = rows_call(
+        own_plan(lat_blocks, 0, own_fields, (0, 0)),
+        K,
+        targets,
+        taper,
+        None,
+        (wider,),
+        like_wide,
+        target_off=-1,
+        edges=edges,
+    )
     emit = tuple(0 if p == 0 else 1 for p in range(lat_blocks))
     first_product, first_row, last_row = rows_call(
         halo_plan(lat_blocks, (0, 1), (0, 1), (0, 0)),
         K,
-        targets_wide,
+        targets,
         taper,
         partial,
         (north, south),
         panel,
+        target_off=-1,
         emit=emit,
+        edges=edges,
     )
     north2, south2 = lat_halo(first_row, last_row)
     row_fields = (1, 2) if lat_blocks == 2 else None
     partial = rows_call(
         own_plan(lat_blocks, 0, row_fields, (1, 0)),
         0,
-        targets_wide,
+        targets,
         taper,
         None,
         (wider, first_row, last_row),
         panel,
-        target_off=1,
     )
     second_product = rows_call(
         halo_plan(lat_blocks, (0, 1), (2, 3), (1, 0)),
         0,
-        targets_wide,
+        targets,
         taper,
         partial,
         (north, south, north2, south2),
         panel,
-        target_off=1,
     )
     return (first_product, second_product)
 

time: 101 us -> 101 us (level)
  local copies, waits for them, and re-layouts: 3.58 us -> 5.64 us
  other arithmetic: 3.57 us -> 1.77 us
  waiting for transfers between devices: 12.9 us -> 14.5 us
  Pallas kernels: 61 us -> 59.6 us
    unnamed x10 -> x13, local copies, waits for them, and re-layouts: 0.88 us -> 3.27 us
    div x1 -> x0, other arithmetic: 1.7 us -> none  [taper_by_code(): return gaspari_cohn(shift_rows, shift_cols) / (K - 1)]
    pallas_call x4, Pallas kernels: 61 us -> 59.6 us  [rows_call(): pl.pallas_call(functools.partial(kernel_with_edges if edges is not None e...]
    ppermute x2, waiting for transfers between devices: 7.07 us -> 8.09 us  [lat_halo(): north = lax.ppermute(last_row, 'lat', [(i, i + 1) for i in range(nlat - 1)])]
  transfers between devices with their start and end apart: 6 -> 6, of which waited for: 3 -> 4; matrix products, arithmetic and copies ran while one was open for 3% -> 2% of each run, Pallas kernels for 35% -> 34%
where the time goes in v8:
time: 101 us
  Pallas kernels  59.6 us (59%)
  starting transfers between devices  18.8 us (19%)
  waiting for transfers between devices  14.5 us (14%)
  local copies, waits for them, and re-layouts  5.64 us (6%)
  other arithmetic  1.77 us (2%)
    pallas_call x4, Pallas kernels, rows_call(): pl.pallas_call(functools.partial(kernel_with_edges if edges is not None e...  59.6 us
    ppermute x2, waiting for transfers between devices, lat_halo(): north = lax.ppermute(last_row, 'lat', [(i, i + 1) for i in range(nlat - 1)])  8.09 us
    ppermute x2, starting transfers between devices, lat_halo(): lax.ppermute(first_row, 'lat', [(i + 1, i) for i in range(nlat - 1)])  7.5 us
    ppermute x1, waiting for transfers between devices, lon_halo(): lax.ppermute(cells[:, -depth:], 'lon', [(i, (i + 1) % nlon) for i in rang...  5.85 us
    ppermute x2, starting transfers between devices, lat_halo(): north = lax.ppermute(last_row, 'lat', [(i, i + 1) for i in range(nlat - 1)])  5.84 us
    ppermute x1, starting transfers between devices, lon_halo(): lax.ppermute(cells[:, :depth], 'lon', [((i + 1) % nlon, i) for i in range...  5.35 us
    unnamed x13, local copies, waits for them, and re-layouts  3.27 us
  transfers between devices with their start and end apart: 6, of which 4 were waited for; matrix products, arithmetic and copies ran while one was open for 2% of the time, Pallas kernels for 34%

profile of v8, /device:TPU:2, one launch (start us, length us, event | category | flops | bytes accessed | tf_op | source)
XLA Modules:
  0.0 100.9 jit_solution(16723809489445615151)
XLA Ops:
  0.6 0.0 copy-start.3
  0.6 1.5 %reduce-precision_convert_fusion = (bf16[2,8,128,128]{3,2,1,0:T(8,128)(2,1)S(1)}, bf16[2,8,128,128]{3,2,1,0:T(8,128)(2,1)S(1)}) fusion(f32[2,8,128,128]{3,2,1,0:T(8,128)} %param.6), kind=kLoop, calls=%fused_computation.2 | loop fusion | flops 1048576 | bytes 2097152 | tf_op jit(solution)/shard_map/convert_element_type | solution.py:157
  2.2 0.0 copy-done.3
  2.2 0.1 collective-permute-start
  2.3 5.3 %collective-permute-start.1 = (bf16[2,2,336,128]{3,2,1,0:T(8,128)(2,1)S(1)}, bf16[2,2,336,128]{3,2,1,0:T(8,128)(2,1)S(1)}, u32[]{:S(2)}, u32[]{:S(2)}) collective-permute-start(bf16[2,2,336,128]{3,2,1,0:T(8,128)(2,1)S(1)} %get-tuple-element.11), channel_id=1, source_target_pairs={{8,0},{16,8},{24,16},{32,24},{40,32},{48,40},{56,48},{64,56},{72,6... | collective-permute-start | bytes 1032200 | tf_op jit(solution)/shard_map/ppermute | solution.py:46
  7.7 5.8 %collective-permute-done = bf16[2,2,336,128]{3,2,1,0:T(8,128)(2,1)S(1)} collective-permute-done((bf16[2,2,336,128]{3,2,1,0:T(8,128)(2,1)S(1)}, bf16[2,2,336,128]{3,2,1,0:T(8,128)(2,1)S(1)}, u32[]{:S(2)}, u32[]{:S(2)}) %collective-permute-start) | collective-permute-done | bytes 344096 | tf_op jit(solution)/shard_map/ppermute | solution.py:45
  13.5 0.0 collective-permute-done.1
  13.5 0.2 pad_maximum_fusion.args_3_.rest_1_
  13.7 0.0 copy-start
  13.7 1.6 %fusion.1 = (bf16[1,12,336,128]{3,2,1,0:T(8,128)(2,1)}, bf16[1,12,336,128]{3,2,1,0:T(8,128)(2,1)}) fusion(bf16[2,12,336,128]{3,2,1,0:T(8,128)(2,1)S(1)} %pad_maximum_fusion.args_3_.rest_1_), kind=kLoop, calls=%fused_computation.8 | loop fusion | bytes 4128768 | tf_op jit(solution)/shard_map/slice | solution.py:189
  15.3 0.4 copy-done
  15.7 5.6 %collective-permute-start.3 = (bf16[1,12,336,128]{3,2,1,0:T(8,128)(2,1)}, bf16[1,12,336,128]{3,2,1,0:T(8,128)(2,1)S(1)}, u32[]{:S(2)}, u32[]{:S(2)}) collective-permute-start(bf16[1,12,336,128]{3,2,1,0:T(8,128)(2,1)} %get-tuple-element.8), channel_id=1, source_target_pairs={{1,0},{2,1},{3,2},{4,3},{5,4},{6,5},{7,6},{9,8},{10,9},{11,10},{12... | collective-permute-start | bytes 3096584 | tf_op jit(solution)/shard_map/ppermute | solution.py:53
  21.3 1.9 %collective-permute-start.2 = (bf16[1,12,336,128]{3,2,1,0:T(8,128)(2,1)}, bf16[1,12,336,128]{3,2,1,0:T(8,128)(2,1)S(1)}, u32[]{:S(2)}, u32[]{:S(2)}) collective-permute-start(bf16[1,12,336,128]{3,2,1,0:T(8,128)(2,1)} %get-tuple-element.9), channel_id=1, source_target_pairs={{0,1},{1,2},{2,3},{3,4},{4,5},{5,6},{6,7},{8,9},{9,10},{10,11},{11... | collective-permute-start | bytes 3096584 | tf_op jit(solution)/shard_map/ppermute | solution.py:52
  23.3 1.0 %copy.5 = bf16[2,8,80,128]{2,3,1,0:T(8,128)(2,1)} copy(bf16[2,8,80,128]{3,2,1,0:T(8,128)(2,1)S(1)} %copy-done.3) | data formatting | bytes 655360 | tf_op args[0]
  24.3 0.8 copy.7.args_1_
  25.1 18.4 %shard_map.50.args_3_ = f32[2,10,128,128]{3,2,1,0:T(8,128)} custom-call(bf16[2,8,128,80]{3,2,1,0:T(8,128)(2,1)} %bitcast.3, bf16[2,2,128,80]{3,2,1,0:T(8,128)(2,1)} %copy.7.args_1_, f32[9,128,128]{2,1,0:T(8,128)} %constant.2.clone.args_2_.rest_0_, bf16[2,12,336,128]{3,2,1,0:T(8,128)(2,1)} %copy-done), custom_call_target="tpu_custom_call" | custom-call | flops 1824522240 | bytes 4374528 | tf_op jit(solution)/shard_map/pallas_call | solution.py:138
  43.5 0.5 collective-permute-done.3.args_5_.rest_3_
  44.0 0.0 copy-start.1
  44.0 6.7 %collective-permute-done.2.args_4_.rest_2_ = bf16[1,12,336,128]{3,2,1,0:T(8,128)(2,1)S(1)} collective-permute-done((bf16[1,12,336,128]{3,2,1,0:T(8,128)(2,1)}, bf16[1,12,336,128]{3,2,1,0:T(8,128)(2,1)S(1)}, u32[]{:S(2)}, u32[]{:S(2)}) %collective-permute-start.2) | collective-permute-done | bytes 1032224 | tf_op jit(solution)/shard_map/ppermute | solution.py:52
  50.7 0.0 copy-done.1
  50.7 0.0 copy-start.2
  50.7 1.0 copy-done.2
  51.6 13.4 %shard_map.51 = (f32[2,8,128,128]{3,2,1,0:T(8,128)}, bf16[1,10,256,128]{3,2,1,0:T(8,128)(2,1)}, bf16[1,10,256,128]{3,2,1,0:T(8,128)(2,1)}) custom-call(bf16[2,8,128,80]{3,2,1,0:T(8,128)(2,1)} %bitcast.4, bf16[2,2,128,80]{3,2,1,0:T(8,128)(2,1)} %copy.7.args_1_, f32[9,128,128]{2,1,0:T(8,128)} %constant.2.clone.args_2_.rest_0_, ...), custom_call_target="tpu_custom_call" | custom-call | flops 912261120 | bytes 6733824 | tf_op jit(solution)/shard_map/pallas_call | solution.py:138
  65.1 1.9 %collective-permute-start.5 = (bf16[1,10,256,128]{3,2,1,0:T(8,128)(2,1)}, bf16[1,10,256,128]{3,2,1,0:T(8,128)(2,1)S(1)}, u32[]{:S(2)}, u32[]{:S(2)}) collective-permute-start(bf16[1,10,256,128]{3,2,1,0:T(8,128)(2,1)} %get-tuple-element.6.rest_2_), channel_id=1, source_target_pairs={{1,0},{2,1},{3,2},{4,3},{5,4},{6,5},{7,6},{9,8},{10,9},{11,10},{12... | collective-permute-start | bytes 1966088 | tf_op jit(solution)/shard_map/ppermute | solution.py:53
  67.0 3.9 %collective-permute-start.4 = (bf16[1,10,256,128]{3,2,1,0:T(8,128)(2,1)}, bf16[1,10,256,128]{3,2,1,0:T(8,128)(2,1)S(1)}, u32[]{:S(2)}, u32[]{:S(2)}) collective-permute-start(bf16[1,10,256,128]{3,2,1,0:T(8,128)(2,1)} %get-tuple-element.7.rest_3_), channel_id=1, source_target_pairs={{0,1},{1,2},{2,3},{3,4},{4,5},{5,6},{6,7},{8,9},{9,10},{10,11},{11... | collective-permute-start | bytes 1966088 | tf_op jit(solution)/shard_map/ppermute | solution.py:52
  70.9 15.9 %shard_map.52.rest_1_ = f32[2,8,128,128]{3,2,1,0:T(8,128)} custom-call(bf16[2,8,128,80]{3,2,1,0:T(8,128)(2,1)} %bitcast.5, f32[9,128,128]{2,1,0:T(8,128)} %constant.2.clone.args_2_.rest_0_, bf16[2,12,336,128]{3,2,1,0:T(8,128)(2,1)} %copy-done, bf16[1,10,256,128]{3,2,1,0:T(8,128)(2,1)} %get-tuple-element.6.rest_2_, ...), custom_call_target="tpu_custom_call" | custom-call | flops 1459617792 | bytes 5341184 | tf_op jit(solution)/shard_map/pallas_call | solution.py:138
  86.8 0.0 collective-permute-done.5.rest_5_
  86.8 0.0 copy-start.4
  86.8 1.4 %collective-permute-done.4.rest_4_ = bf16[1,10,256,128]{3,2,1,0:T(8,128)(2,1)S(1)} collective-permute-done((bf16[1,10,256,128]{3,2,1,0:T(8,128)(2,1)}, bf16[1,10,256,128]{3,2,1,0:T(8,128)(2,1)S(1)}, u32[]{:S(2)}, u32[]{:S(2)}) %collective-permute-start.4) | collective-permute-done | bytes 655392 | tf_op jit(solution)/shard_map/ppermute | solution.py:52
  88.2 0.0 copy-done.4
  88.2 0.9 copy-done.5
  89.1 11.8 %shard_map.53 = f32[2,8,128,128]{3,2,1,0:T(8,128)} custom-call(bf16[2,8,128,80]{3,2,1,0:T(8,128)(2,1)} %bitcast.6, f32[9,128,128]{2,1,0:T(8,128)} %constant.2.clone.args_2_.rest_0_, f32[2,8,128,128]{3,2,1,0:T(8,128)} %shard_map.52.rest_1_, bf16[1,12,336,128]{3,2,1,0:T(8,128)(2,1)} %copy-done.2, bf16[1,12,336,128]{3,2,1,0:T(8,128)(2,1)} %copy-done.1, ...), custom_call_target="tpu_custom_call" | custom-call | flops 729808896 | bytes 6389760 | tf_op jit(solution)/shard_map/pallas_call | solution.py:138
  (5 shorter events, 0.1 us)
Async XLA Ops:
  0.6 1.5 %copy-start.3 = (bf16[2,8,80,128]{3,2,1,0:T(8,128)(2,1)S(1)}, bf16[2,8,80,128]{3,2,1,0:T(8,128)(2,1)}, u32[]{:S(2)}) copy-start(bf16[2,8,80,128]{3,2,1,0:T(8,128)(2,1)} %param.5) | copy-start | bytes 983044
  2.2 11.3 %collective-permute-start = (bf16[2,2,336,128]{3,2,1,0:T(8,128)(2,1)S(1)}, bf16[2,2,336,128]{3,2,1,0:T(8,128)(2,1)S(1)}, u32[]{:S(2)}, u32[]{:S(2)}) collective-permute-start(bf16[2,2,336,128]{3,2,1,0:T(8,128)(2,1)S(1)} %get-tuple-element.10), channel_id=1, source_target_pairs={{0,8},{8,16},{16,24},{24,32},{32,40},{40,48},{48,56},{56,64},{64,7... | collective-permute-start | bytes 1032200 | tf_op jit(solution)/shard_map/ppermute | solution.py:45
  2.3 11.2 %collective-permute-start.1 = (bf16[2,2,336,128]{3,2,1,0:T(8,128)(2,1)S(1)}, bf16[2,2,336,128]{3,2,1,0:T(8,128)(2,1)S(1)}, u32[]{:S(2)}, u32[]{:S(2)}) collective-permute-start(bf16[2,2,336,128]{3,2,1,0:T(8,128)(2,1)S(1)} %get-tuple-element.11), channel_id=1, source_target_pairs={{8,0},{16,8},{24,16},{32,24},{40,32},{48,40},{56,48},{64,56},{72,6... | collective-permute-start | bytes 1032200 | tf_op jit(solution)/shard_map/ppermute | solution.py:46
  13.7 2.0 %copy-start = (bf16[2,12,336,128]{3,2,1,0:T(8,128)(2,1)}, bf16[2,12,336,128]{3,2,1,0:T(8,128)(2,1)S(1)}, u32[]{:S(2)}) copy-start(bf16[2,12,336,128]{3,2,1,0:T(8,128)(2,1)S(1)} %pad_maximum_fusion.args_3_.rest_1_) | copy-start | bytes 6193156
  15.7 28.3 %collective-permute-start.3 = (bf16[1,12,336,128]{3,2,1,0:T(8,128)(2,1)}, bf16[1,12,336,128]{3,2,1,0:T(8,128)(2,1)S(1)}, u32[]{:S(2)}, u32[]{:S(2)}) collective-permute-start(bf16[1,12,336,128]{3,2,1,0:T(8,128)(2,1)} %get-tuple-element.8), channel_id=1, source_target_pairs={{1,0},{2,1},{3,2},{4,3},{5,4},{6,5},{7,6},{9,8},{10,9},{11,10},{12... | collective-permute-start | bytes 3096584 | tf_op jit(solution)/shard_map/ppermute | solution.py:53
  21.3 29.3 %collective-permute-start.2 = (bf16[1,12,336,128]{3,2,1,0:T(8,128)(2,1)}, bf16[1,12,336,128]{3,2,1,0:T(8,128)(2,1)S(1)}, u32[]{:S(2)}, u32[]{:S(2)}) collective-permute-start(bf16[1,12,336,128]{3,2,1,0:T(8,128)(2,1)} %get-tuple-element.9), channel_id=1, source_target_pairs={{0,1},{1,2},{2,3},{3,4},{4,5},{5,6},{6,7},{8,9},{9,10},{10,11},{11... | collective-permute-start | bytes 3096584 | tf_op jit(solution)/shard_map/ppermute | solution.py:52
  44.0 6.7 %copy-start.1 = (bf16[1,12,336,128]{3,2,1,0:T(8,128)(2,1)}, bf16[1,12,336,128]{3,2,1,0:T(8,128)(2,1)S(1)}, u32[]{:S(2)}) copy-start(bf16[1,12,336,128]{3,2,1,0:T(8,128)(2,1)S(1)} %collective-permute-done.3.args_5_.rest_3_) | copy-start | bytes 3096580
  50.7 1.0 copy-start.2
  65.1 21.7 %collective-permute-start.5 = (bf16[1,10,256,128]{3,2,1,0:T(8,128)(2,1)}, bf16[1,10,256,128]{3,2,1,0:T(8,128)(2,1)S(1)}, u32[]{:S(2)}, u32[]{:S(2)}) collective-permute-start(bf16[1,10,256,128]{3,2,1,0:T(8,128)(2,1)} %get-tuple-element.6.rest_2_), channel_id=1, source_target_pairs={{1,0},{2,1},{3,2},{4,3},{5,4},{6,5},{7,6},{9,8},{10,9},{11,10},{12... | collective-permute-start | bytes 1966088 | tf_op jit(solution)/shard_map/ppermute | solution.py:53
  67.0 21.2 %collective-permute-start.4 = (bf16[1,10,256,128]{3,2,1,0:T(8,128)(2,1)}, bf16[1,10,256,128]{3,2,1,0:T(8,128)(2,1)S(1)}, u32[]{:S(2)}, u32[]{:S(2)}) collective-permute-start(bf16[1,10,256,128]{3,2,1,0:T(8,128)(2,1)} %get-tuple-element.7.rest_3_), channel_id=1, source_target_pairs={{0,1},{1,2},{2,3},{3,4},{4,5},{5,6},{6,7},{8,9},{9,10},{10,11},{11... | collective-permute-start | bytes 1966088 | tf_op jit(solution)/shard_map/ppermute | solution.py:52
  86.8 1.4 %copy-start.4 = (bf16[1,10,256,128]{3,2,1,0:T(8,128)(2,1)}, bf16[1,10,256,128]{3,2,1,0:T(8,128)(2,1)S(1)}, u32[]{:S(2)}) copy-start(bf16[1,10,256,128]{3,2,1,0:T(8,128)(2,1)S(1)} %collective-permute-done.5.rest_5_) | copy-start | bytes 1966084
  88.2 0.9 copy-start.5

commit v9 on v8

--- a/solution.py
+++ b/solution.py
@@ -74,7 +74,7 @@
                 total = partial_ref[p, q]
             else:
                 total = jnp.zeros((columns, rank), jnp.float32)
-            for dr, members_at, members_row, field_from, row, members_off, field_off in uses:
+            for dr, members_at, members_row, field_from, row, members_off, field_off, trim in uses:
                 members_ref, field_ref = sources[members_at], sources[field_from]
                 for dc in range(3):
                     gram = jnp.dot(
@@ -86,8 +86,20 @@
                     tile_high = tile.astype(jnp.bfloat16)
                     tile_low = (tile - tile_high.astype(jnp.float32)).astype(jnp.bfloat16)
                     partner = field_ref.at[row, q + dc + field_off]
-                    field_high = partner[field_at : field_at + columns, :]
-                    field_low = partner[field_at + columns : field_at + 2 * columns, :]
+                    if trim:
+                        kept = columns - STRIDE
+                        pad = jnp.zeros((STRIDE, rank), jnp.bfloat16)
+                        field_high = partner[field_at : field_at + kept, :]
+                        field_low = partner[field_at + kept : field_at + 2 * kept, :]
+                        if trim == 1:
+                            field_high = jnp.concatenate([pad, field_high], axis=0)
+                            field_low = jnp.concatenate([pad, field_low], axis=0)
+                        else:
+                            field_high = jnp.concatenate([field_high, pad], axis=0)
+                            field_low = jnp.concatenate([field_low, pad], axis=0)
+                    else:
+                        field_high = partner[field_at : field_at + columns, :]
+                        field_low = partner[field_at + columns : field_at + 2 * columns, :]
                     total = total + jnp.dot(tile_high, field_high, preferred_element_type=jnp.float32)
                     total = total + jnp.dot(tile_high, field_low, preferred_element_type=jnp.float32)
                     total = total + jnp.dot(tile_low, field_high, preferred_element_type=jnp.float32)
@@ -162,6 +174,7 @@
         tuple(
             (dr, members, p + dr - 1, fields[p + dr - 1], p + dr - 1 if len(set(fields)) == 1 else 0)
             + offsets
+            + (0,)
             for dr in range(3)
             if 0 <= p + dr - 1 < lat_blocks
         )
@@ -169,10 +182,12 @@
     )
 
 
-def halo_plan(lat_blocks, members, field, offsets):
+def halo_plan(lat_blocks, members, field, offsets, trimmed=False):
     return tuple(
         tuple(
-            (dr, members[p + dr > 0], 0, field[p + dr > 0], 0) + offsets
+            (dr, members[p + dr > 0], 0, field[p + dr > 0], 0)
+            + offsets
+            + ((1 if p + dr == 0 else 2) if trimmed else 0,)
             for dr in range(3)
             if not 0 <= p + dr - 1 < lat_blocks
         )
@@ -186,7 +201,14 @@
     taper = taper_by_code()
     panel_high, panel_low = split_high_low(panel)
     wider, west, east = lon_halo(jnp.concatenate([anomalies, panel_high, panel_low], axis=2), 2)
-    north, south = lat_halo(wider[:1], wider[-1:])
+    kept = COLS - STRIDE
+    going_north = jnp.concatenate(
+        [wider[:1, :, :K], wider[:1, :, K : K + kept], wider[:1, :, K + COLS : K + COLS + kept]], axis=2
+    )
+    going_south = jnp.concatenate(
+        [wider[-1:, :, :K], wider[-1:, :, K + STRIDE : K + COLS], wider[-1:, :, K + COLS + STRIDE :]], axis=2
+    )
+    north, south = lat_halo(going_north, going_south)
     targets = jnp.swapaxes(anomalies, 2, 3)
     edges = jnp.swapaxes(jnp.concatenate([west[:, 1:, :K, :], east[:, :1, :K, :]], axis=1), 2, 3)
     like_wide = jax.ShapeDtypeStruct((lat_blocks, lon_blocks + 2) + panel.shape[2:], jnp.float32)
@@ -204,7 +226,7 @@
     )
     emit = tuple(0 if p == 0 else 1 for p in range(lat_blocks))
     first_product, first_row, last_row = rows_call(
-        halo_plan(lat_blocks, (0, 1), (0, 1), (0, 0)),
+        halo_plan(lat_blocks, (0, 1), (0, 1), (0, 0), trimmed=True),
         K,
         targets,
         taper,

time: 101 us -> 99.6 us (0.986)
  waiting for transfers between devices: 14.5 us -> 8.85 us
  starting transfers between devices: 18.8 us -> 20.5 us
  other arithmetic: 1.77 us -> 3 us
    ppermute x2, waiting for transfers between devices: 8.09 us -> 2.99 us  [lat_halo(): north = lax.ppermute(last_row, 'lat', [(i, i + 1) for i in range(nlat - 1)])]
    ppermute x2, starting transfers between devices: 7.5 us -> 9.34 us  [lat_halo(): lax.ppermute(first_row, 'lat', [(i + 1, i) for i in range(nlat - 1)])]
    slice x1 -> x3, local copies, waits for them, and re-layouts: 1.59 us -> 0.14 us  [the longest x1 0.07 us: local(): wider[:1, :, K + COLS:K + COLS + kept]]
    unnamed x13 -> x15, local copies, waits for them, and re-layouts: 3.27 us -> 4.61 us
    concatenate x0 -> x2, other arithmetic: none -> 1.23 us  [the longest x1 1.17 us: local(): jnp.concatenate([wider[-1:, :, :K], wider[-1:, :, K + STRIDE:K + COLS], w...]
  transfers between devices with their start and end apart: 6 -> 6, of which waited for: 4 -> 2; matrix products, arithmetic and copies ran while one was open for 2% -> 3% of each run, Pallas kernels for 34% -> 35%
where the time goes in v9:
time: 99.6 us; the launch traced here: 98.9 us
  Pallas kernels  59.5 us (60%)
  starting transfers between devices  20.5 us (21%)
  waiting for transfers between devices  8.85 us (9%)
  local copies, waits for them, and re-layouts  6.31 us (6%)
  other arithmetic  3 us (3%)
    pallas_call x4, Pallas kernels, rows_call(): pl.pallas_call(functools.partial(kernel_with_edges if edges is not None e...  59.5 us
    ppermute x2, starting transfers between devices, lat_halo(): lax.ppermute(first_row, 'lat', [(i + 1, i) for i in range(nlat - 1)])  9.34 us
    ppermute x1, waiting for transfers between devices, lon_halo(): lax.ppermute(cells[:, -depth:], 'lon', [(i, (i + 1) % nlon) for i in rang...  5.85 us
    ppermute x2, starting transfers between devices, lat_halo(): north = lax.ppermute(last_row, 'lat', [(i, i + 1) for i in range(nlat - 1)])  5.73 us
    ppermute x1, starting transfers between devices, lon_halo(): lax.ppermute(cells[:, :depth], 'lon', [((i + 1) % nlon, i) for i in range...  5.35 us
    unnamed x15, local copies, waits for them, and re-layouts  4.61 us
    ppermute x2, waiting for transfers between devices, lat_halo(): north = lax.ppermute(last_row, 'lat', [(i, i + 1) for i in range(nlat - 1)])  2.99 us
  transfers between devices with their start and end apart: 6, of which 2 were waited for; matrix products, arithmetic and copies ran while one was open for 3% of the time, Pallas kernels for 35%

profile of v9, /device:TPU:2, one launch (start us, length us, event | category | flops | bytes accessed | tf_op | source)
XLA Modules:
  0.0 98.9 jit_solution(5236693501522422180)
XLA Ops:
  0.6 0.0 copy-start.3
  0.6 1.5 %reduce-precision_convert_fusion = (bf16[2,8,128,128]{3,2,1,0:T(8,128)(2,1)S(1)}, bf16[2,8,128,128]{3,2,1,0:T(8,128)(2,1)S(1)}) fusion(f32[2,8,128,128]{3,2,1,0:T(8,128)} %param.6), kind=kLoop, calls=%fused_computation.2 | loop fusion | flops 1048576 | bytes 2097152 | tf_op jit(solution)/shard_map/convert_element_type | solution.py:169
  2.2 0.0 copy-done.3
  2.2 0.1 collective-permute-start
  2.3 5.3 %collective-permute-start.1 = (bf16[2,2,336,128]{3,2,1,0:T(8,128)(2,1)S(1)}, bf16[2,2,336,128]{3,2,1,0:T(8,128)(2,1)S(1)}, u32[]{:S(2)}, u32[]{:S(2)}) collective-permute-start(bf16[2,2,336,128]{3,2,1,0:T(8,128)(2,1)S(1)} %get-tuple-element.12), channel_id=1, source_target_pairs={{8,0},{16,8},{24,16},{32,24},{40,32},{48,40},{56,48},{64,56},{72,6... | collective-permute-start | bytes 1032200 | tf_op jit(solution)/shard_map/ppermute | solution.py:46
  7.7 5.8 %collective-permute-done = bf16[2,2,336,128]{3,2,1,0:T(8,128)(2,1)S(1)} collective-permute-done((bf16[2,2,336,128]{3,2,1,0:T(8,128)(2,1)S(1)}, bf16[2,2,336,128]{3,2,1,0:T(8,128)(2,1)S(1)}, u32[]{:S(2)}, u32[]{:S(2)}) %collective-permute-start) | collective-permute-done | bytes 344096 | tf_op jit(solution)/shard_map/ppermute | solution.py:45
  13.5 0.0 collective-permute-done.1
  13.5 0.2 pad_maximum_fusion.args_3_.rest_1_
  13.7 0.5 copy-done.6
  14.3 0.1 fusion.1
  14.4 1.2 %pad_maximum_fusion.1 = bf16[1,12,304,128]{3,2,1,0:T(8,128)(2,1)} fusion(bf16[1,12,112,128]{3,2,1,0:T(8,128)(2,1)S(1)} %get-tuple-element.9, bf16[1,12,112,128]{3,2,1,0:T(8,128)(2,1)S(1)} %get-tuple-element.10, bf16[1,12,80,128]{3,2,1,0:T(8,128)(2,1)S(1)} %slice.40), kind=kLoop, calls=%fused_computation.4 | loop fusion | flops 2801664 | bytes 1867776 | tf_op jit(solution)/shard_map/concatenate | solution.py:208
  15.6 0.3 copy-done
  15.9 3.8 %collective-permute-start.2 = (bf16[1,12,304,128]{3,2,1,0:T(8,128)(2,1)}, bf16[1,12,304,128]{3,2,1,0:T(8,128)(2,1)S(1)}, u32[]{:S(2)}, u32[]{:S(2)}) collective-permute-start(bf16[1,12,304,128]{3,2,1,0:T(8,128)(2,1)} %pad_maximum_fusion.1), channel_id=1, source_target_pairs={{0,1},{1,2},{2,3},{3,4},{4,5},{5,6},{6,7},{8,9},{9,10},{10,11},{11... | collective-permute-start | bytes 2801672 | tf_op jit(solution)/shard_map/ppermute | solution.py:52
  19.7 0.1 pad_maximum_fusion.2
  19.8 4.1 %collective-permute-start.3 = (bf16[1,12,304,128]{3,2,1,0:T(8,128)(2,1)S(1)}, bf16[1,12,304,128]{3,2,1,0:T(8,128)(2,1)S(1)}, u32[]{:S(2)}, u32[]{:S(2)}) collective-permute-start(bf16[1,12,304,128]{3,2,1,0:T(8,128)(2,1)S(1)} %pad_maximum_fusion.2), channel_id=1, source_target_pairs={{1,0},{2,1},{3,2},{4,3},{5,4},{6,5},{7,6},{9,8},{10,9},{11,10},{12... | collective-permute-start | bytes 2801672 | tf_op jit(solution)/shard_map/ppermute | solution.py:53
  23.9 1.0 %copy.5 = bf16[2,8,80,128]{2,3,1,0:T(8,128)(2,1)} copy(bf16[2,8,80,128]{3,2,1,0:T(8,128)(2,1)S(1)} %copy-done.3) | data formatting | bytes 655360 | tf_op args[0]
  24.9 0.8 slice.39
  25.7 0.8 copy.7.args_1_
  26.5 18.4 %shard_map.50.args_3_ = f32[2,10,128,128]{3,2,1,0:T(8,128)} custom-call(bf16[2,8,128,80]{3,2,1,0:T(8,128)(2,1)} %bitcast.3, bf16[2,2,128,80]{3,2,1,0:T(8,128)(2,1)} %copy.7.args_1_, f32[9,128,128]{2,1,0:T(8,128)} %constant.2.clone.args_2_.rest_0_, bf16[2,12,336,128]{3,2,1,0:T(8,128)(2,1)} %copy-done), custom_call_target="tpu_custom_call" | custom-call | flops 1824522240 | bytes 4374528 | tf_op jit(solution)/shard_map/pallas_call | solution.py:150
  44.9 0.0 collective-permute-done.2.args_4_.rest_2_
  44.9 0.0 collective-permute-done.3.args_5_.rest_3_
  44.9 0.9 copy-done.1
  45.8 0.9 copy-done.2
  46.8 13.4 %shard_map.51 = (f32[2,8,128,128]{3,2,1,0:T(8,128)}, bf16[1,10,256,128]{3,2,1,0:T(8,128)(2,1)}, bf16[1,10,256,128]{3,2,1,0:T(8,128)(2,1)}) custom-call(bf16[2,8,128,80]{3,2,1,0:T(8,128)(2,1)} %bitcast.4, bf16[2,2,128,80]{3,2,1,0:T(8,128)(2,1)} %copy.7.args_1_, f32[9,128,128]{2,1,0:T(8,128)} %constant.2.clone.args_2_.rest_0_, ...), custom_call_target="tpu_custom_call" | custom-call | flops 912261120 | bytes 6537216 | tf_op jit(solution)/shard_map/pallas_call | solution.py:150
  60.2 5.2 %collective-permute-start.5 = (bf16[1,10,256,128]{3,2,1,0:T(8,128)(2,1)}, bf16[1,10,256,128]{3,2,1,0:T(8,128)(2,1)S(1)}, u32[]{:S(2)}, u32[]{:S(2)}) collective-permute-start(bf16[1,10,256,128]{3,2,1,0:T(8,128)(2,1)} %get-tuple-element.6.rest_2_), channel_id=1, source_target_pairs={{1,0},{2,1},{3,2},{4,3},{5,4},{6,5},{7,6},{9,8},{10,9},{11,10},{12... | collective-permute-start | bytes 1966088 | tf_op jit(solution)/shard_map/ppermute | solution.py:53
  65.4 1.9 %collective-permute-start.4 = (bf16[1,10,256,128]{3,2,1,0:T(8,128)(2,1)}, bf16[1,10,256,128]{3,2,1,0:T(8,128)(2,1)S(1)}, u32[]{:S(2)}, u32[]{:S(2)}) collective-permute-start(bf16[1,10,256,128]{3,2,1,0:T(8,128)(2,1)} %get-tuple-element.7.rest_3_), channel_id=1, source_target_pairs={{0,1},{1,2},{2,3},{3,4},{4,5},{5,6},{6,7},{8,9},{9,10},{10,11},{11... | collective-permute-start | bytes 1966088 | tf_op jit(solution)/shard_map/ppermute | solution.py:52
  67.4 15.9 %shard_map.52.rest_1_ = f32[2,8,128,128]{3,2,1,0:T(8,128)} custom-call(bf16[2,8,128,80]{3,2,1,0:T(8,128)(2,1)} %bitcast.5, f32[9,128,128]{2,1,0:T(8,128)} %constant.2.clone.args_2_.rest_0_, bf16[2,12,336,128]{3,2,1,0:T(8,128)(2,1)} %copy-done, bf16[1,10,256,128]{3,2,1,0:T(8,128)(2,1)} %get-tuple-element.6.rest_2_, ...), custom_call_target="tpu_custom_call" | custom-call | flops 1459617792 | bytes 5341184 | tf_op jit(solution)/shard_map/pallas_call | solution.py:150
  83.3 0.0 collective-permute-done.5.rest_5_
  83.3 3.0 %collective-permute-done.4.rest_4_ = bf16[1,10,256,128]{3,2,1,0:T(8,128)(2,1)S(1)} collective-permute-done((bf16[1,10,256,128]{3,2,1,0:T(8,128)(2,1)}, bf16[1,10,256,128]{3,2,1,0:T(8,128)(2,1)S(1)}, u32[]{:S(2)}, u32[]{:S(2)}) %collective-permute-start.4) | collective-permute-done | bytes 655392 | tf_op jit(solution)/shard_map/ppermute | solution.py:52
  86.2 0.0 copy-done.4
  86.3 0.9 copy-done.5
  87.1 11.8 %shard_map.53 = f32[2,8,128,128]{3,2,1,0:T(8,128)} custom-call(bf16[2,8,128,80]{3,2,1,0:T(8,128)(2,1)} %bitcast.6, f32[9,128,128]{2,1,0:T(8,128)} %constant.2.clone.args_2_.rest_0_, f32[2,8,128,128]{3,2,1,0:T(8,128)} %shard_map.52.rest_1_, bf16[1,12,304,128]{3,2,1,0:T(8,128)(2,1)} %copy-done.1, bf16[1,12,304,128]{3,2,1,0:T(8,128)(2,1)} %copy-done.2, ...), custom_call_target="tpu_custom_call" | custom-call | flops 729808896 | bytes 6193152 | tf_op jit(solution)/shard_map/pallas_call | solution.py:150
  (11 shorter events, 0.1 us)
Async XLA Ops:
  0.6 1.5 %copy-start.3 = (bf16[2,8,80,128]{3,2,1,0:T(8,128)(2,1)S(1)}, bf16[2,8,80,128]{3,2,1,0:T(8,128)(2,1)}, u32[]{:S(2)}) copy-start(bf16[2,8,80,128]{3,2,1,0:T(8,128)(2,1)} %param.5) | copy-start | bytes 983044
  2.2 11.3 %collective-permute-start = (bf16[2,2,336,128]{3,2,1,0:T(8,128)(2,1)S(1)}, bf16[2,2,336,128]{3,2,1,0:T(8,128)(2,1)S(1)}, u32[]{:S(2)}, u32[]{:S(2)}) collective-permute-start(bf16[2,2,336,128]{3,2,1,0:T(8,128)(2,1)S(1)} %get-tuple-element.11), channel_id=1, source_target_pairs={{0,8},{8,16},{16,24},{24,32},{32,40},{40,48},{48,56},{56,64},{64,7... | collective-permute-start | bytes 1032200 | tf_op jit(solution)/shard_map/ppermute | solution.py:45
  2.3 11.2 %collective-permute-start.1 = (bf16[2,2,336,128]{3,2,1,0:T(8,128)(2,1)S(1)}, bf16[2,2,336,128]{3,2,1,0:T(8,128)(2,1)S(1)}, u32[]{:S(2)}, u32[]{:S(2)}) collective-permute-start(bf16[2,2,336,128]{3,2,1,0:T(8,128)(2,1)S(1)} %get-tuple-element.12), channel_id=1, source_target_pairs={{8,0},{16,8},{24,16},{32,24},{40,32},{48,40},{56,48},{64,56},{72,6... | collective-permute-start | bytes 1032200 | tf_op jit(solution)/shard_map/ppermute | solution.py:46
  13.5 0.7 copy-start.6
  14.3 1.6 %copy-start = (bf16[2,12,336,128]{3,2,1,0:T(8,128)(2,1)}, bf16[2,12,336,128]{3,2,1,0:T(8,128)(2,1)S(1)}, u32[]{:S(2)}) copy-start(bf16[2,12,336,128]{3,2,1,0:T(8,128)(2,1)S(1)} %pad_maximum_fusion.args_3_.rest_1_) | copy-start | bytes 6193156
  15.9 29.0 %collective-permute-start.2 = (bf16[1,12,304,128]{3,2,1,0:T(8,128)(2,1)}, bf16[1,12,304,128]{3,2,1,0:T(8,128)(2,1)S(1)}, u32[]{:S(2)}, u32[]{:S(2)}) collective-permute-start(bf16[1,12,304,128]{3,2,1,0:T(8,128)(2,1)} %pad_maximum_fusion.1), channel_id=1, source_target_pairs={{0,1},{1,2},{2,3},{3,4},{4,5},{5,6},{6,7},{8,9},{9,10},{10,11},{11... | collective-permute-start | bytes 2801672 | tf_op jit(solution)/shard_map/ppermute | solution.py:52
  19.8 25.1 %collective-permute-start.3 = (bf16[1,12,304,128]{3,2,1,0:T(8,128)(2,1)S(1)}, bf16[1,12,304,128]{3,2,1,0:T(8,128)(2,1)S(1)}, u32[]{:S(2)}, u32[]{:S(2)}) collective-permute-start(bf16[1,12,304,128]{3,2,1,0:T(8,128)(2,1)S(1)} %pad_maximum_fusion.2), channel_id=1, source_target_pairs={{1,0},{2,1},{3,2},{4,3},{5,4},{6,5},{7,6},{9,8},{10,9},{11,10},{12... | collective-permute-start | bytes 2801672 | tf_op jit(solution)/shard_map/ppermute | solution.py:53
  44.9 0.9 copy-start.1
  45.8 0.9 copy-start.2
  60.2 23.0 %collective-permute-start.5 = (bf16[1,10,256,128]{3,2,1,0:T(8,128)(2,1)}, bf16[1,10,256,128]{3,2,1,0:T(8,128)(2,1)S(1)}, u32[]{:S(2)}, u32[]{:S(2)}) collective-permute-start(bf16[1,10,256,128]{3,2,1,0:T(8,128)(2,1)} %get-tuple-element.6.rest_2_), channel_id=1, source_target_pairs={{1,0},{2,1},{3,2},{4,3},{5,4},{6,5},{7,6},{9,8},{10,9},{11,10},{12... | collective-permute-start | bytes 1966088 | tf_op jit(solution)/shard_map/ppermute | solution.py:53
  65.4 20.8 %collective-permute-start.4 = (bf16[1,10,256,128]{3,2,1,0:T(8,128)(2,1)}, bf16[1,10,256,128]{3,2,1,0:T(8,128)(2,1)S(1)}, u32[]{:S(2)}, u32[]{:S(2)}) collective-permute-start(bf16[1,10,256,128]{3,2,1,0:T(8,128)(2,1)} %get-tuple-element.7.rest_3_), channel_id=1, source_target_pairs={{0,1},{1,2},{2,3},{3,4},{4,5},{5,6},{6,7},{8,9},{9,10},{10,11},{11... | collective-permute-start | bytes 1966088 | tf_op jit(solution)/shard_map/ppermute | solution.py:52
  83.3 3.0 %copy-start.4 = (bf16[1,10,256,128]{3,2,1,0:T(8,128)(2,1)}, bf16[1,10,256,128]{3,2,1,0:T(8,128)(2,1)S(1)}, u32[]{:S(2)}) copy-start(bf16[1,10,256,128]{3,2,1,0:T(8,128)(2,1)S(1)} %collective-permute-done.5.rest_5_) | copy-start | bytes 1966084
  86.2 0.9 copy-start.5

commit v10 on v9

--- a/solution.py
+++ b/solution.py
@@ -202,13 +202,23 @@
     panel_high, panel_low = split_high_low(panel)
     wider, west, east = lon_halo(jnp.concatenate([anomalies, panel_high, panel_low], axis=2), 2)
     kept = COLS - STRIDE
-    going_north = jnp.concatenate(
-        [wider[:1, :, :K], wider[:1, :, K : K + kept], wider[:1, :, K + COLS : K + COLS + kept]], axis=2
-    )
-    going_south = jnp.concatenate(
-        [wider[-1:, :, :K], wider[-1:, :, K + STRIDE : K + COLS], wider[-1:, :, K + COLS + STRIDE :]], axis=2
-    )
-    north, south = lat_halo(going_north, going_south)
+
+    def for_south_halo(rows):
+        return jnp.concatenate(
+            [rows[:, :, :K], rows[:, :, K : K + kept], rows[:, :, K + COLS : K + COLS + kept]], axis=2
+        )
+
+    def for_north_halo(rows):
+        return jnp.concatenate(
+            [rows[:, :, :K], rows[:, :, K + STRIDE : K + COLS], rows[:, :, K + COLS + STRIDE :]], axis=2
+        )
+
+    message = jnp.concatenate([anomalies, panel_high, panel_low], axis=2)
+    north_own, south_own = lat_halo(for_south_halo(message[:1]), for_north_halo(message[-1:]))
+    corners = jnp.concatenate([west, east], axis=1)
+    north_corners, south_corners = lat_halo(for_south_halo(corners[:1]), for_north_halo(corners[-1:]))
+    north = jnp.concatenate([north_corners[:, :2], north_own, north_corners[:, 2:]], axis=1)
+    south = jnp.concatenate([south_corners[:, :2], south_own, south_corners[:, 2:]], axis=1)
     targets = jnp.swapaxes(anomalies, 2, 3)
     edges = jnp.swapaxes(jnp.concatenate([west[:, 1:, :K, :], east[:, :1, :K, :]], axis=1), 2, 3)
     like_wide = jax.ShapeDtypeStruct((lat_blocks, lon_blocks + 2) + panel.shape[2:], jnp.float32)

time: 99.6 us -> 103 us (1.034)
  waiting for transfers between devices: 8.85 us -> 0.02 us
  other arithmetic: 3 us -> 10.1 us
  starting transfers between devices: 20.5 us -> 26.9 us
  local copies, waits for them, and re-layouts: 6.31 us -> 4.68 us
    ppermute x2 -> x3, starting transfers between devices: 9.34 us -> 15.8 us  [lat_halo(): lax.ppermute(first_row, 'lat', [(i + 1, i) for i in range(nlat - 1)])]
    ppermute x1, waiting for transfers between devices: 5.85 us -> 0.01 us  [lon_halo(): lax.ppermute(cells[:, -depth:], 'lon', [(i, (i + 1) % nlon) for i in rang...]
    concatenate x2 -> x6, other arithmetic: 1.23 us -> 6.38 us  [the longest x1 2.1 us: local(): jnp.concatenate([north_corners[:, :2], north_own, north_corners[:, 2:]],...]
    ppermute x2 -> x3, waiting for transfers between devices: 2.99 us -> 0.01 us  [lat_halo(): north = lax.ppermute(last_row, 'lat', [(i, i + 1) for i in range(nlat - 1)])]
    unnamed x15 -> x8, local copies, waits for them, and re-layouts: 4.61 us -> 2.74 us
    concatenate x1, other arithmetic: 0.18 us -> 1.43 us  [lon_halo(): return (jnp.concatenate([west, cells, east], axis=1), west, east)]
    ppermute x2 -> x3, starting transfers between devices: 5.73 us -> 5.74 us  [lat_halo(): north = lax.ppermute(last_row, 'lat', [(i, i + 1) for i in range(nlat - 1)])]
  transfers between devices with their start and end apart: 6 -> 8, of which waited for: 2 -> 0; matrix products, arithmetic and copies ran while one was open for 3% -> 10% of each run, Pallas kernels for 35% -> 34%
where the time goes in v10:
time: 103 us; the launch traced here: 102 us
  Pallas kernels  59.5 us (58%)
  starting transfers between devices  26.9 us (26%)
  other arithmetic  10.1 us (10%)
  local copies, waits for them, and re-layouts  4.68 us (5%)
    pallas_call x4, Pallas kernels, rows_call(): pl.pallas_call(functools.partial(kernel_with_edges if edges is not None e...  59.5 us
    ppermute x3, starting transfers between devices, lat_halo(): lax.ppermute(first_row, 'lat', [(i + 1, i) for i in range(nlat - 1)])  15.8 us
    ppermute x3, starting transfers between devices, lat_halo(): north = lax.ppermute(last_row, 'lat', [(i, i + 1) for i in range(nlat - 1)])  5.74 us
    ppermute x1, starting transfers between devices, lon_halo(): lax.ppermute(cells[:, :depth], 'lon', [((i + 1) % nlon, i) for i in range...  5.36 us
    unnamed x8, local copies, waits for them, and re-layouts  2.74 us
    concatenate x1, other arithmetic, local(): jnp.concatenate([north_corners[:, :2], north_own, north_corners[:, 2:]],...  2.1 us
  transfers between devices with their start and end apart: 8, of which 0 were waited for; matrix products, arithmetic and copies ran while one was open for 10% of the time, Pallas kernels for 34%

profile of v10, /device:TPU:2, one launch (start us, length us, event | category | flops | bytes accessed | tf_op | source)
XLA Modules:
  0.0 102.0 jit_solution(13160575834014687292)
XLA Ops:
  0.6 0.0 copy-start
  0.6 1.5 %reduce-precision_convert_fusion = (bf16[2,8,128,128]{3,2,1,0:T(8,128)(2,1)S(1)}, bf16[2,8,128,128]{3,2,1,0:T(8,128)(2,1)S(1)}) fusion(f32[2,8,128,128]{3,2,1,0:T(8,128)} %param.6), kind=kLoop, calls=%fused_computation.2 | loop fusion | flops 1048576 | bytes 2097152 | tf_op jit(solution)/shard_map/convert_element_type | solution.py:169
  2.2 0.8 pad_maximum_fusion.6
  3.0 0.0 collective-permute-start
  3.0 5.4 %collective-permute-start.1 = (bf16[2,2,336,128]{3,2,1,0:T(8,128)(2,1)S(1)}, bf16[2,2,336,128]{3,2,1,0:T(8,128)(2,1)S(1)}, u32[]{:S(2)}, u32[]{:S(2)}) collective-permute-start(bf16[2,2,336,128]{3,2,1,0:T(8,128)(2,1)S(1)} %get-tuple-element.9), channel_id=1, source_target_pairs={{8,0},{16,8},{24,16},{32,24},{40,32},{48,40},{56,48},{64,56},{72,6... | collective-permute-start | bytes 1032200 | tf_op jit(solution)/shard_map/ppermute | solution.py:46
  8.4 0.9 fusion.3
  9.2 5.9 %collective-permute-start.5 = (bf16[1,8,304,128]{3,2,1,0:T(8,128)(2,1)}, bf16[1,8,304,128]{3,2,1,0:T(8,128)(2,1)S(1)}, u32[]{:S(2)}, u32[]{:S(2)}) collective-permute-start(bf16[1,8,304,128]{3,2,1,0:T(8,128)(2,1)} %fusion.3), channel_id=1, source_target_pairs={{1,0},{2,1},{3,2},{4,3},{5,4},{6,5},{7,6},{9,8},{10,9},{11,10},{12... | collective-permute-start | bytes 1867784 | tf_op jit(solution)/shard_map/ppermute | solution.py:53
  15.2 0.9 pad_maximum_fusion.3
  16.0 1.9 %collective-permute-start.3 = (bf16[1,8,304,128]{3,2,1,0:T(8,128)(2,1)}, bf16[1,8,304,128]{3,2,1,0:T(8,128)(2,1)}, u32[]{:S(2)}, u32[]{:S(2)}) collective-permute-start(bf16[1,8,304,128]{3,2,1,0:T(8,128)(2,1)} %pad_maximum_fusion.3), channel_id=1, source_target_pairs={{0,1},{1,2},{2,3},{3,4},{4,5},{5,6},{6,7},{8,9},{9,10},{10,11},{11... | collective-permute-start | bytes 1867784 | tf_op jit(solution)/shard_map/ppermute | solution.py:52
  18.0 1.0 copy.5
  19.0 0.0 collective-permute-done
  19.2 0.8 copy.7.args_1_
  19.9 0.7 pad_maximum_fusion.7
  20.7 1.9 %collective-permute-start.2 = (bf16[1,4,304,128]{3,2,1,0:T(8,128)(2,1)}, bf16[1,4,304,128]{3,2,1,0:T(8,128)(2,1)}, u32[]{:S(2)}, u32[]{:S(2)}) collective-permute-start(bf16[1,4,304,128]{3,2,1,0:T(8,128)(2,1)} %pad_maximum_fusion.7), channel_id=1, source_target_pairs={{0,1},{1,2},{2,3},{3,4},{4,5},{5,6},{6,7},{8,9},{9,10},{10,11},{11... | collective-permute-start | bytes 933896 | tf_op jit(solution)/shard_map/ppermute | solution.py:52
  22.6 0.7 pad_maximum_fusion.8
  23.4 6.0 %collective-permute-start.4 = (bf16[1,4,304,128]{3,2,1,0:T(8,128)(2,1)}, bf16[1,4,304,128]{3,2,1,0:T(8,128)(2,1)S(1)}, u32[]{:S(2)}, u32[]{:S(2)}) collective-permute-start(bf16[1,4,304,128]{3,2,1,0:T(8,128)(2,1)} %pad_maximum_fusion.8), channel_id=1, source_target_pairs={{1,0},{2,1},{3,2},{4,3},{5,4},{6,5},{7,6},{9,8},{10,9},{11,10},{12... | collective-permute-start | bytes 933896 | tf_op jit(solution)/shard_map/ppermute | solution.py:53
  29.4 1.4 %pad_maximum_fusion.args_3_.rest_1_ = bf16[2,12,336,128]{3,2,1,0:T(8,128)(2,1)} fusion(bf16[2,2,336,128]{3,2,1,0:T(8,128)(2,1)S(1)} %collective-permute-done.1, bf16[2,8,128,128]{3,2,1,0:T(8,128)(2,1)S(1)} %get-tuple-element.11, bf16[2,8,128,128]{3,2,1,0:T(8,128)(2,1)S(1)} %get-tuple-element.10, bf16[2,8,80,128]{3,2,1,0:T(8,128)(2,1)S(1)} %copy-done, ...), kind=kLoop, calls=%fused_computation | loop fusion | flops 10321920 | bytes 4128768 | tf_op jit(solution)/shard_map/concatenate | solution.py:47
  30.8 18.4 %shard_map.50.args_3_ = f32[2,10,128,128]{3,2,1,0:T(8,128)} custom-call(bf16[2,8,128,80]{3,2,1,0:T(8,128)(2,1)} %bitcast.3, bf16[2,2,128,80]{3,2,1,0:T(8,128)(2,1)} %copy.7.args_1_, f32[9,128,128]{2,1,0:T(8,128)} %constant.2.clone.args_2_.rest_0_, bf16[2,12,336,128]{3,2,1,0:T(8,128)(2,1)} %pad_maximum_fusion.args_3_.rest_1_), custom_call_target="tpu_custom_call" | custom-call | flops 1824522240 | bytes 4374528 | tf_op jit(solution)/shard_map/pallas_call | solution.py:150
  49.2 0.0 collective-permute-done.2
  49.2 1.0 fusion.7
  50.2 0.0 collective-permute-done.3
  50.2 2.1 %pad_maximum_fusion.1.args_4_.rest_2_ = bf16[1,12,304,128]{3,2,1,0:T(8,128)(2,1)} fusion(bf16[1,2,304,128]{3,2,1,0:T(8,128)(2,1)S(1)} %get-tuple-element.20, bf16[1,8,304,128]{3,2,1,0:T(8,128)(2,1)} %collective-permute-done.3, bf16[1,2,304,128]{3,2,1,0:T(8,128)(2,1)S(1)} %get-tuple-element.19), kind=kLoop, calls=%fused_computation.6 | loop fusion | flops 933888 | bytes 1867776 | tf_op jit(solution)/shard_map/concatenate | solution.py:220
  52.3 0.0 collective-permute-done.4
  52.4 0.0 collective-permute-done.5
  52.4 1.0 %pad_maximum_fusion.2.args_5_.rest_3_ = bf16[1,12,304,128]{3,2,1,0:T(8,128)(2,1)} fusion(bf16[1,2,304,128]{3,2,1,0:T(8,128)(2,1)S(1)} %get-tuple-element.18, bf16[1,8,304,128]{3,2,1,0:T(8,128)(2,1)S(1)} %collective-permute-done.5, bf16[1,2,304,128]{3,2,1,0:T(8,128)(2,1)S(1)} %get-tuple-element.17), kind=kLoop, calls=%fused_computation.7 | loop fusion | flops 933888 | bytes 1867776 | tf_op jit(solution)/shard_map/concatenate | solution.py:221
  53.4 13.4 %shard_map.51 = (f32[2,8,128,128]{3,2,1,0:T(8,128)}, bf16[1,10,256,128]{3,2,1,0:T(8,128)(2,1)}, bf16[1,10,256,128]{3,2,1,0:T(8,128)(2,1)}) custom-call(bf16[2,8,128,80]{3,2,1,0:T(8,128)(2,1)} %bitcast.4, bf16[2,2,128,80]{3,2,1,0:T(8,128)(2,1)} %copy.7.args_1_, f32[9,128,128]{2,1,0:T(8,128)} %constant.2.clone.args_2_.rest_0_, ...), custom_call_target="tpu_custom_call" | custom-call | flops 912261120 | bytes 6537216 | tf_op jit(solution)/shard_map/pallas_call | solution.py:150
  66.8 3.9 %collective-permute-start.7 = (bf16[1,10,256,128]{3,2,1,0:T(8,128)(2,1)}, bf16[1,10,256,128]{3,2,1,0:T(8,128)(2,1)S(1)}, u32[]{:S(2)}, u32[]{:S(2)}) collective-permute-start(bf16[1,10,256,128]{3,2,1,0:T(8,128)(2,1)} %get-tuple-element.6.rest_2_), channel_id=1, source_target_pairs={{1,0},{2,1},{3,2},{4,3},{5,4},{6,5},{7,6},{9,8},{10,9},{11,10},{12... | collective-permute-start | bytes 1966088 | tf_op jit(solution)/shard_map/ppermute | solution.py:53
  70.8 1.9 %collective-permute-start.6 = (bf16[1,10,256,128]{3,2,1,0:T(8,128)(2,1)}, bf16[1,10,256,128]{3,2,1,0:T(8,128)(2,1)S(1)}, u32[]{:S(2)}, u32[]{:S(2)}) collective-permute-start(bf16[1,10,256,128]{3,2,1,0:T(8,128)(2,1)} %get-tuple-element.7.rest_3_), channel_id=1, source_target_pairs={{0,1},{1,2},{2,3},{3,4},{4,5},{5,6},{6,7},{8,9},{9,10},{10,11},{11... | collective-permute-start | bytes 1966088 | tf_op jit(solution)/shard_map/ppermute | solution.py:52
  72.7 15.9 %shard_map.52.rest_1_ = f32[2,8,128,128]{3,2,1,0:T(8,128)} custom-call(bf16[2,8,128,80]{3,2,1,0:T(8,128)(2,1)} %bitcast.5, f32[9,128,128]{2,1,0:T(8,128)} %constant.2.clone.args_2_.rest_0_, bf16[2,12,336,128]{3,2,1,0:T(8,128)(2,1)} %pad_maximum_fusion.args_3_.rest_1_, bf16[1,10,256,128]{3,2,1,0:T(8,128)(2,1)} %get-tuple-element.6.rest_2_, ...), custom_call_target="tpu_custom_call" | custom-call | flops 1459617792 | bytes 5341184 | tf_op jit(solution)/shard_map/pallas_call | solution.py:150
  88.6 0.8 copy-done.1
  89.4 0.8 copy-done.2
  90.3 11.8 %shard_map.53 = f32[2,8,128,128]{3,2,1,0:T(8,128)} custom-call(bf16[2,8,128,80]{3,2,1,0:T(8,128)(2,1)} %bitcast.6, f32[9,128,128]{2,1,0:T(8,128)} %constant.2.clone.args_2_.rest_0_, f32[2,8,128,128]{3,2,1,0:T(8,128)} %shard_map.52.rest_1_, bf16[1,12,304,128]{3,2,1,0:T(8,128)(2,1)} %pad_maximum_fusion.1.args_4_.rest_2_, ...), custom_call_target="tpu_custom_call" | custom-call | flops 729808896 | bytes 6193152 | tf_op jit(solution)/shard_map/pallas_call | solution.py:150
  (19 shorter events, 0.2 us)
Async XLA Ops:
  0.6 1.6 %copy-start = (bf16[2,8,80,128]{3,2,1,0:T(8,128)(2,1)S(1)}, bf16[2,8,80,128]{3,2,1,0:T(8,128)(2,1)}, u32[]{:S(2)}) copy-start(bf16[2,8,80,128]{3,2,1,0:T(8,128)(2,1)} %param.5) | copy-start | bytes 983044
  3.0 12.2 %slice-start = ((bf16[2,8,80,128]{3,2,1,0:T(8,128)(2,1)}), bf16[1,8,80,128]{3,2,1,0:T(8,128)(2,1)S(1)}, s32[]{:S(2)}) async-start(bf16[2,8,80,128]{3,2,1,0:T(8,128)(2,1)} %param.5), calls=%async_computation | async-start | bytes 327680 | tf_op jit(solution)/shard_map/slice | solution.py:213
  3.0 16.0 %collective-permute-start = (bf16[2,2,336,128]{3,2,1,0:T(8,128)(2,1)}, bf16[2,2,336,128]{3,2,1,0:T(8,128)(2,1)S(1)}, u32[]{:S(2)}, u32[]{:S(2)}) collective-permute-start(bf16[2,2,336,128]{3,2,1,0:T(8,128)(2,1)} %get-tuple-element.8), channel_id=1, source_target_pairs={{0,8},{8,16},{16,24},{24,32},{32,40},{40,48},{48,56},{56,64},{64,7... | collective-permute-start | bytes 1032200 | tf_op jit(solution)/shard_map/ppermute | solution.py:45
  3.0 16.0 %collective-permute-start.1 = (bf16[2,2,336,128]{3,2,1,0:T(8,128)(2,1)S(1)}, bf16[2,2,336,128]{3,2,1,0:T(8,128)(2,1)S(1)}, u32[]{:S(2)}, u32[]{:S(2)}) collective-permute-start(bf16[2,2,336,128]{3,2,1,0:T(8,128)(2,1)S(1)} %get-tuple-element.9), channel_id=1, source_target_pairs={{8,0},{16,8},{24,16},{32,24},{40,32},{48,40},{56,48},{64,56},{72,6... | collective-permute-start | bytes 1032200 | tf_op jit(solution)/shard_map/ppermute | solution.py:46
  9.2 43.2 %collective-permute-start.5 = (bf16[1,8,304,128]{3,2,1,0:T(8,128)(2,1)}, bf16[1,8,304,128]{3,2,1,0:T(8,128)(2,1)S(1)}, u32[]{:S(2)}, u32[]{:S(2)}) collective-permute-start(bf16[1,8,304,128]{3,2,1,0:T(8,128)(2,1)} %fusion.3), channel_id=1, source_target_pairs={{1,0},{2,1},{3,2},{4,3},{5,4},{6,5},{7,6},{9,8},{10,9},{11,10},{12... | collective-permute-start | bytes 1867784 | tf_op jit(solution)/shard_map/ppermute | solution.py:53
  16.0 34.2 %collective-permute-start.3 = (bf16[1,8,304,128]{3,2,1,0:T(8,128)(2,1)}, bf16[1,8,304,128]{3,2,1,0:T(8,128)(2,1)}, u32[]{:S(2)}, u32[]{:S(2)}) collective-permute-start(bf16[1,8,304,128]{3,2,1,0:T(8,128)(2,1)} %pad_maximum_fusion.3), channel_id=1, source_target_pairs={{0,1},{1,2},{2,3},{3,4},{4,5},{5,6},{6,7},{8,9},{9,10},{10,11},{11... | collective-permute-start | bytes 1867784 | tf_op jit(solution)/shard_map/ppermute | solution.py:52
  20.7 28.5 %collective-permute-start.2 = (bf16[1,4,304,128]{3,2,1,0:T(8,128)(2,1)}, bf16[1,4,304,128]{3,2,1,0:T(8,128)(2,1)}, u32[]{:S(2)}, u32[]{:S(2)}) collective-permute-start(bf16[1,4,304,128]{3,2,1,0:T(8,128)(2,1)} %pad_maximum_fusion.7), channel_id=1, source_target_pairs={{0,1},{1,2},{2,3},{3,4},{4,5},{5,6},{6,7},{8,9},{9,10},{10,11},{11... | collective-permute-start | bytes 933896 | tf_op jit(solution)/shard_map/ppermute | solution.py:52
  23.4 29.0 %collective-permute-start.4 = (bf16[1,4,304,128]{3,2,1,0:T(8,128)(2,1)}, bf16[1,4,304,128]{3,2,1,0:T(8,128)(2,1)S(1)}, u32[]{:S(2)}, u32[]{:S(2)}) collective-permute-start(bf16[1,4,304,128]{3,2,1,0:T(8,128)(2,1)} %pad_maximum_fusion.8), channel_id=1, source_target_pairs={{1,0},{2,1},{3,2},{4,3},{5,4},{6,5},{7,6},{9,8},{10,9},{11,10},{12... | collective-permute-start | bytes 933896 | tf_op jit(solution)/shard_map/ppermute | solution.py:53
  66.8 21.7 %collective-permute-start.7 = (bf16[1,10,256,128]{3,2,1,0:T(8,128)(2,1)}, bf16[1,10,256,128]{3,2,1,0:T(8,128)(2,1)S(1)}, u32[]{:S(2)}, u32[]{:S(2)}) collective-permute-start(bf16[1,10,256,128]{3,2,1,0:T(8,128)(2,1)} %get-tuple-element.6.rest_2_), channel_id=1, source_target_pairs={{1,0},{2,1},{3,2},{4,3},{5,4},{6,5},{7,6},{9,8},{10,9},{11,10},{12... | collective-permute-start | bytes 1966088 | tf_op jit(solution)/shard_map/ppermute | solution.py:53
  70.8 17.8 %collective-permute-start.6 = (bf16[1,10,256,128]{3,2,1,0:T(8,128)(2,1)}, bf16[1,10,256,128]{3,2,1,0:T(8,128)(2,1)S(1)}, u32[]{:S(2)}, u32[]{:S(2)}) collective-permute-start(bf16[1,10,256,128]{3,2,1,0:T(8,128)(2,1)} %get-tuple-element.7.rest_3_), channel_id=1, source_target_pairs={{0,1},{1,2},{2,3},{3,4},{4,5},{5,6},{6,7},{8,9},{9,10},{10,11},{11... | collective-permute-start | bytes 1966088 | tf_op jit(solution)/shard_map/ppermute | solution.py:52
  88.6 0.9 copy-start.1
  89.4 0.8 copy-start.2

commit v11 on v9

--- a/solution.py
+++ b/solution.py
@@ -239,22 +239,25 @@
     )
     north2, south2 = lat_halo(first_row, last_row)
     row_fields = (1, 2) if lat_blocks == 2 else None
+    members = wider[:, 1 : lon_blocks + 3, :K]
+    members_north = north[:, 1 : lon_blocks + 3, :K]
+    members_south = south[:, 1 : lon_blocks + 3, :K]
     partial = rows_call(
-        own_plan(lat_blocks, 0, row_fields, (1, 0)),
+        own_plan(lat_blocks, 0, row_fields, (0, 0)),
         0,
         targets,
         taper,
         None,
-        (wider, first_row, last_row),
+        (members, first_row, last_row),
         panel,
     )
     second_product = rows_call(
-        halo_plan(lat_blocks, (0, 1), (2, 3), (1, 0)),
+        halo_plan(lat_blocks, (0, 1), (2, 3), (0, 0)),
         0,
         targets,
         taper,
         partial,
-        (north, south, north2, south2),
+        (members_north, members_south, north2, south2),
         panel,
     )
     return (first_product, second_product)

time: 99.6 us -> 102 us (1.024)
  local copies, waits for them, and re-layouts: 6.31 us -> 12.1 us
  waiting for transfers between devices: 8.85 us -> 5.86 us
    slice x0 -> x3, local copies, waits for them, and re-layouts: none -> 5.05 us  [the longest x1 1.79 us: local(): members = wider[:, 1:lon_blocks + 3, :K]]
    ppermute x2, waiting for transfers between devices: 2.99 us -> 0.01 us  [lat_halo(): north = lax.ppermute(last_row, 'lat', [(i, i + 1) for i in range(nlat - 1)])]
  transfers between devices with their start and end apart: 6 -> 6, of which waited for: 2 -> 1; matrix products, arithmetic and copies ran while one was open for 3% -> 8% of each run, Pallas kernels for 35% -> 34%
where the time goes in v11:
time: 102 us; the launch traced here: 101 us
  Pallas kernels  58.5 us (57%)
  starting transfers between devices  20.5 us (20%)
  local copies, waits for them, and re-layouts  12.1 us (12%)
  waiting for transfers between devices  5.86 us (6%)
  other arithmetic  2.99 us (3%)
    pallas_call x4, Pallas kernels, rows_call(): pl.pallas_call(functools.partial(kernel_with_edges if edges is not None e...  58.5 us
    ppermute x2, starting transfers between devices, lat_halo(): lax.ppermute(first_row, 'lat', [(i + 1, i) for i in range(nlat - 1)])  9.38 us
    ppermute x1, waiting for transfers between devices, lon_halo(): lax.ppermute(cells[:, -depth:], 'lon', [(i, (i + 1) % nlon) for i in rang...  5.85 us
    ppermute x2, starting transfers between devices, lat_halo(): north = lax.ppermute(last_row, 'lat', [(i, i + 1) for i in range(nlat - 1)])  5.73 us
    unnamed x15, local copies, waits for them, and re-layouts  5.4 us
    ppermute x1, starting transfers between devices, lon_halo(): lax.ppermute(cells[:, :depth], 'lon', [((i + 1) % nlon, i) for i in range...  5.35 us
  transfers between devices with their start and end apart: 6, of which 1 were waited for; matrix products, arithmetic and copies ran while one was open for 8% of the time, Pallas kernels for 34%

profile of v11, /device:TPU:2, one launch (start us, length us, event | category | flops | bytes accessed | tf_op | source)
XLA Modules:
  0.0 100.8 jit_solution(12541870559540182016)
XLA Ops:
  0.6 1.5 %reduce-precision_convert_fusion = (bf16[2,8,128,128]{3,2,1,0:T(8,128)(2,1)S(1)}, bf16[2,8,128,128]{3,2,1,0:T(8,128)(2,1)S(1)}) fusion(f32[2,8,128,128]{3,2,1,0:T(8,128)} %param.6), kind=kLoop, calls=%fused_computation.2 | loop fusion | flops 1048576 | bytes 2097152 | tf_op jit(solution)/shard_map/convert_element_type | solution.py:169
  2.2 0.1 collective-permute-start
  2.3 5.3 %collective-permute-start.1 = (bf16[2,2,336,128]{3,2,1,0:T(8,128)(2,1)S(1)}, bf16[2,2,336,128]{3,2,1,0:T(8,128)(2,1)S(1)}, u32[]{:S(2)}, u32[]{:S(2)}) collective-permute-start(bf16[2,2,336,128]{3,2,1,0:T(8,128)(2,1)S(1)} %get-tuple-element.12), channel_id=1, source_target_pairs={{8,0},{16,8},{24,16},{32,24},{40,32},{48,40},{56,48},{64,56},{72,6... | collective-permute-start | bytes 1032200 | tf_op jit(solution)/shard_map/ppermute | solution.py:46
  7.7 5.8 %collective-permute-done = bf16[2,2,336,128]{3,2,1,0:T(8,128)(2,1)S(1)} collective-permute-done((bf16[2,2,336,128]{3,2,1,0:T(8,128)(2,1)S(1)}, bf16[2,2,336,128]{3,2,1,0:T(8,128)(2,1)S(1)}, u32[]{:S(2)}, u32[]{:S(2)}) %collective-permute-start) | collective-permute-done | bytes 344096 | tf_op jit(solution)/shard_map/ppermute | solution.py:45
  13.5 0.0 collective-permute-done.1
  13.5 0.2 pad_maximum_fusion.args_3_
  13.7 0.5 copy-done.6
  14.3 0.1 fusion.1
  14.4 1.2 %pad_maximum_fusion.1 = bf16[1,12,304,128]{3,2,1,0:T(8,128)(2,1)} fusion(bf16[1,12,112,128]{3,2,1,0:T(8,128)(2,1)S(1)} %get-tuple-element.9, bf16[1,12,112,128]{3,2,1,0:T(8,128)(2,1)S(1)} %get-tuple-element.10, bf16[1,12,80,128]{3,2,1,0:T(8,128)(2,1)S(1)} %slice.52), kind=kLoop, calls=%fused_computation.4 | loop fusion | flops 2801664 | bytes 1867776 | tf_op jit(solution)/shard_map/concatenate | solution.py:208
  15.6 0.3 copy-done
  15.9 3.8 %collective-permute-start.2 = (bf16[1,12,304,128]{3,2,1,0:T(8,128)(2,1)}, bf16[1,12,304,128]{3,2,1,0:T(8,128)(2,1)S(1)}, u32[]{:S(2)}, u32[]{:S(2)}) collective-permute-start(bf16[1,12,304,128]{3,2,1,0:T(8,128)(2,1)} %pad_maximum_fusion.1), channel_id=1, source_target_pairs={{0,1},{1,2},{2,3},{3,4},{4,5},{5,6},{6,7},{8,9},{9,10},{10,11},{11... | collective-permute-start | bytes 2801672 | tf_op jit(solution)/shard_map/ppermute | solution.py:52
  19.7 0.1 pad_maximum_fusion.2
  19.8 4.1 %collective-permute-start.3 = (bf16[1,12,304,128]{3,2,1,0:T(8,128)(2,1)S(1)}, bf16[1,12,304,128]{3,2,1,0:T(8,128)(2,1)S(1)}, u32[]{:S(2)}, u32[]{:S(2)}) collective-permute-start(bf16[1,12,304,128]{3,2,1,0:T(8,128)(2,1)S(1)} %pad_maximum_fusion.2), channel_id=1, source_target_pairs={{1,0},{2,1},{3,2},{4,3},{5,4},{6,5},{7,6},{9,8},{10,9},{11,10},{12... | collective-permute-start | bytes 2801672 | tf_op jit(solution)/shard_map/ppermute | solution.py:53
  23.9 1.0 copy.5
  24.9 0.8 slice.51
  25.7 0.8 copy.7.args_1_
  26.5 18.4 %shard_map.50.args_3_ = f32[2,10,128,128]{3,2,1,0:T(8,128)} custom-call(bf16[2,8,128,80]{3,2,1,0:T(8,128)(2,1)} %bitcast.3, bf16[2,2,128,80]{3,2,1,0:T(8,128)(2,1)} %copy.7.args_1_, f32[9,128,128]{2,1,0:T(8,128)} %constant.2.clone.args_2_.rest_0_, bf16[2,12,336,128]{3,2,1,0:T(8,128)(2,1)} %copy-done), custom_call_target="tpu_custom_call" | custom-call | flops 1824522240 | bytes 4374528 | tf_op jit(solution)/shard_map/pallas_call | solution.py:150
  44.9 0.0 collective-permute-done.2.args_4_
  44.9 0.0 collective-permute-done.3.args_5_
  44.9 0.9 copy-done.2
  45.8 0.9 copy-done.3
  46.7 13.4 %shard_map.51 = (f32[2,8,128,128]{3,2,1,0:T(8,128)}, bf16[1,10,256,128]{3,2,1,0:T(8,128)(2,1)}, bf16[1,10,256,128]{3,2,1,0:T(8,128)(2,1)}) custom-call(bf16[2,8,128,80]{3,2,1,0:T(8,128)(2,1)} %bitcast.4, bf16[2,2,128,80]{3,2,1,0:T(8,128)(2,1)} %copy.7.args_1_, f32[9,128,128]{2,1,0:T(8,128)} %constant.2.clone.args_2_.rest_0_, ...), custom_call_target="tpu_custom_call" | custom-call | flops 912261120 | bytes 6537216 | tf_op jit(solution)/shard_map/pallas_call | solution.py:150
  60.1 5.3 %collective-permute-start.5 = (bf16[1,10,256,128]{3,2,1,0:T(8,128)(2,1)}, bf16[1,10,256,128]{3,2,1,0:T(8,128)(2,1)S(1)}, u32[]{:S(2)}, u32[]{:S(2)}) collective-permute-start(bf16[1,10,256,128]{3,2,1,0:T(8,128)(2,1)} %get-tuple-element.6.rest_2_), channel_id=1, source_target_pairs={{1,0},{2,1},{3,2},{4,3},{5,4},{6,5},{7,6},{9,8},{10,9},{11,10},{12... | collective-permute-start | bytes 1966088 | tf_op jit(solution)/shard_map/ppermute | solution.py:53
  65.4 1.9 %collective-permute-start.4 = (bf16[1,10,256,128]{3,2,1,0:T(8,128)(2,1)}, bf16[1,10,256,128]{3,2,1,0:T(8,128)(2,1)S(1)}, u32[]{:S(2)}, u32[]{:S(2)}) collective-permute-start(bf16[1,10,256,128]{3,2,1,0:T(8,128)(2,1)} %get-tuple-element.7.rest_3_), channel_id=1, source_target_pairs={{0,1},{1,2},{2,3},{3,4},{4,5},{5,6},{6,7},{8,9},{9,10},{10,11},{11... | collective-permute-start | bytes 1966088 | tf_op jit(solution)/shard_map/ppermute | solution.py:52
  67.3 1.8 %slice.57.rest_1_ = bf16[2,10,80,128]{3,2,1,0:T(8,128)(2,1)} slice(bf16[2,12,336,128]{3,2,1,0:T(8,128)(2,1)} %copy-done), slice={[0:2], [1:11], [0:80], [0:128]} | slice | bytes 819200 | tf_op jit(solution)/shard_map/slice | solution.py:242
  69.1 1.6 %slice.58.rest_2_ = bf16[1,10,80,128]{3,2,1,0:T(8,128)(2,1)} slice(bf16[1,12,304,128]{3,2,1,0:T(8,128)(2,1)} %copy-done.2), slice={[0:1], [1:11], [0:80], [0:128]} | slice | bytes 409600 | tf_op jit(solution)/shard_map/slice | solution.py:243
  70.7 1.6 %slice.59.rest_3_ = bf16[1,10,80,128]{3,2,1,0:T(8,128)(2,1)} slice(bf16[1,12,304,128]{3,2,1,0:T(8,128)(2,1)} %copy-done.3), slice={[0:1], [1:11], [0:80], [0:128]} | slice | bytes 409600 | tf_op jit(solution)/shard_map/slice | solution.py:244
  72.4 15.4 %shard_map.52.rest_1_ = f32[2,8,128,128]{3,2,1,0:T(8,128)} custom-call(bf16[2,8,128,80]{3,2,1,0:T(8,128)(2,1)} %bitcast.5, f32[9,128,128]{2,1,0:T(8,128)} %constant.2.clone.args_2_.rest_0_, bf16[2,10,80,128]{3,2,1,0:T(8,128)(2,1)} %slice.57.rest_1_, bf16[1,10,256,128]{3,2,1,0:T(8,128)(2,1)} %get-tuple-element.6.rest_2_, ...), custom_call_target="tpu_custom_call" | custom-call | flops 1459617792 | bytes 3686400 | tf_op jit(solution)/shard_map/pallas_call | solution.py:150
  87.8 0.0 collective-permute-done.4.rest_4_
  87.8 0.9 copy-done.4
  88.6 0.8 copy-done.5
  89.5 11.3 %shard_map.53 = f32[2,8,128,128]{3,2,1,0:T(8,128)} custom-call(bf16[2,8,128,80]{3,2,1,0:T(8,128)(2,1)} %bitcast.6, f32[9,128,128]{2,1,0:T(8,128)} %constant.2.clone.args_2_.rest_0_, f32[2,8,128,128]{3,2,1,0:T(8,128)} %shard_map.52.rest_1_, bf16[1,10,80,128]{3,2,1,0:T(8,128)(2,1)} %slice.58.rest_2_, bf16[1,10,80,128]{3,2,1,0:T(8,128)(2,1)} %slice.59.rest_3_, ...), custom_call_target="tpu_custom_call" | custom-call | flops 729808896 | bytes 4734976 | tf_op jit(solution)/shard_map/pallas_call | solution.py:150
  (14 shorter events, 0.1 us)
Async XLA Ops:
  0.6 1.5 %copy-start.1 = (bf16[2,8,80,128]{3,2,1,0:T(8,128)(2,1)S(1)}, bf16[2,8,80,128]{3,2,1,0:T(8,128)(2,1)}, u32[]{:S(2)}) copy-start(bf16[2,8,80,128]{3,2,1,0:T(8,128)(2,1)} %param.5) | copy-start | bytes 983044
  2.2 11.3 %collective-permute-start = (bf16[2,2,336,128]{3,2,1,0:T(8,128)(2,1)S(1)}, bf16[2,2,336,128]{3,2,1,0:T(8,128)(2,1)S(1)}, u32[]{:S(2)}, u32[]{:S(2)}) collective-permute-start(bf16[2,2,336,128]{3,2,1,0:T(8,128)(2,1)S(1)} %get-tuple-element.11), channel_id=1, source_target_pairs={{0,8},{8,16},{16,24},{24,32},{32,40},{40,48},{48,56},{56,64},{64,7... | collective-permute-start | bytes 1032200 | tf_op jit(solution)/shard_map/ppermute | solution.py:45
  2.3 11.2 %collective-permute-start.1 = (bf16[2,2,336,128]{3,2,1,0:T(8,128)(2,1)S(1)}, bf16[2,2,336,128]{3,2,1,0:T(8,128)(2,1)S(1)}, u32[]{:S(2)}, u32[]{:S(2)}) collective-permute-start(bf16[2,2,336,128]{3,2,1,0:T(8,128)(2,1)S(1)} %get-tuple-element.12), channel_id=1, source_target_pairs={{8,0},{16,8},{24,16},{32,24},{40,32},{48,40},{56,48},{64,56},{72,6... | collective-permute-start | bytes 1032200 | tf_op jit(solution)/shard_map/ppermute | solution.py:46
  13.5 0.7 copy-start.6
  14.3 1.6 %copy-start = (bf16[2,12,336,128]{3,2,1,0:T(8,128)(2,1)}, bf16[2,12,336,128]{3,2,1,0:T(8,128)(2,1)S(1)}, u32[]{:S(2)}) copy-start(bf16[2,12,336,128]{3,2,1,0:T(8,128)(2,1)S(1)} %pad_maximum_fusion.args_3_) | copy-start | bytes 6193156
  15.9 29.0 %collective-permute-start.2 = (bf16[1,12,304,128]{3,2,1,0:T(8,128)(2,1)}, bf16[1,12,304,128]{3,2,1,0:T(8,128)(2,1)S(1)}, u32[]{:S(2)}, u32[]{:S(2)}) collective-permute-start(bf16[1,12,304,128]{3,2,1,0:T(8,128)(2,1)} %pad_maximum_fusion.1), channel_id=1, source_target_pairs={{0,1},{1,2},{2,3},{3,4},{4,5},{5,6},{6,7},{8,9},{9,10},{10,11},{11... | collective-permute-start | bytes 2801672 | tf_op jit(solution)/shard_map/ppermute | solution.py:52
  19.8 25.1 %collective-permute-start.3 = (bf16[1,12,304,128]{3,2,1,0:T(8,128)(2,1)S(1)}, bf16[1,12,304,128]{3,2,1,0:T(8,128)(2,1)S(1)}, u32[]{:S(2)}, u32[]{:S(2)}) collective-permute-start(bf16[1,12,304,128]{3,2,1,0:T(8,128)(2,1)S(1)} %pad_maximum_fusion.2), channel_id=1, source_target_pairs={{1,0},{2,1},{3,2},{4,3},{5,4},{6,5},{7,6},{9,8},{10,9},{11,10},{12... | collective-permute-start | bytes 2801672 | tf_op jit(solution)/shard_map/ppermute | solution.py:53
  44.9 0.9 copy-start.2
  45.8 0.9 copy-start.3
  60.1 27.6 %collective-permute-start.5 = (bf16[1,10,256,128]{3,2,1,0:T(8,128)(2,1)}, bf16[1,10,256,128]{3,2,1,0:T(8,128)(2,1)S(1)}, u32[]{:S(2)}, u32[]{:S(2)}) collective-permute-start(bf16[1,10,256,128]{3,2,1,0:T(8,128)(2,1)} %get-tuple-element.6.rest_2_), channel_id=1, source_target_pairs={{1,0},{2,1},{3,2},{4,3},{5,4},{6,5},{7,6},{9,8},{10,9},{11,10},{12... | collective-permute-start | bytes 1966088 | tf_op jit(solution)/shard_map/ppermute | solution.py:53
  65.4 22.4 %collective-permute-start.4 = (bf16[1,10,256,128]{3,2,1,0:T(8,128)(2,1)}, bf16[1,10,256,128]{3,2,1,0:T(8,128)(2,1)S(1)}, u32[]{:S(2)}, u32[]{:S(2)}) collective-permute-start(bf16[1,10,256,128]{3,2,1,0:T(8,128)(2,1)} %get-tuple-element.7.rest_3_), channel_id=1, source_target_pairs={{0,1},{1,2},{2,3},{3,4},{4,5},{5,6},{6,7},{8,9},{9,10},{10,11},{11... | collective-permute-start | bytes 1966088 | tf_op jit(solution)/shard_map/ppermute | solution.py:52
  87.8 0.9 copy-start.4
  88.6 0.8 copy-start.5

commit v12 on v11

--- a/solution.py
+++ b/solution.py
@@ -54,12 +54,15 @@
     return north, south
 
 
-def rows_kernel(plan, field_at, with_partial, target_off, emit, targets_ref, edges_ref, taper_ref, *rest):
-    outs = rest[-(1 + len(emit)) :] if emit else rest[-1:]
-    rest = rest[: len(rest) - len(outs)]
+def rows_kernel(plan, field_at, with_partial, target_off, emit, copies, targets_ref, edges_ref, taper_ref, *rest):
+    count = 1 + len(emit) + len(copies)
+    outs = rest[-count:]
+    rest = rest[: len(rest) - count]
     out_ref = outs[0]
     partial_ref = rest[0] if with_partial else None
     sources = rest[1:] if with_partial else rest
+    for (source, first, end), copy_ref in zip(copies, outs[1 + len(emit) :]):
+        copy_ref[...] = sources[source][:, first:end, :K, :]
     columns, rank = out_ref.shape[2:]
     lat_blocks = out_ref.shape[0]
     lon_blocks = partial_ref.shape[1] if emit else out_ref.shape[1]
@@ -132,11 +135,13 @@
     return rows_kernel(*args)
 
 
-def kernel_without_edges(plan, field_at, with_partial, target_off, emit, targets_ref, *rest):
-    return rows_kernel(plan, field_at, with_partial, target_off, emit, targets_ref, None, *rest)
-
-
-def rows_call(plan, field_at, targets, taper, partial, sources, out_like, target_off=0, emit=(), edges=None):
+def kernel_without_edges(plan, field_at, with_partial, target_off, emit, copies, targets_ref, *rest):
+    return rows_kernel(plan, field_at, with_partial, target_off, emit, copies, targets_ref, None, *rest)
+
+
+def rows_call(
+    plan, field_at, targets, taper, partial, sources, out_like, target_off=0, emit=(), edges=None, copies=()
+):
     lat_blocks, lon_blocks, columns, rank = (partial if emit else out_like).shape
     codes = sum(3 * len(uses) for uses in plan)
     flops = lon_blocks * codes * 2 * columns * (K * columns + 3 * columns * rank)
@@ -145,6 +150,10 @@
     shapes = [jax.ShapeDtypeStruct(out_like.shape, jnp.float32)]
     if emit:
         shapes += [jax.ShapeDtypeStruct((1, lon_blocks, 2 * columns, rank), jnp.bfloat16)] * len(emit)
+    for source, first, end in copies:
+        held = sources[source]
+        shapes.append(jax.ShapeDtypeStruct((held.shape[0], end - first, K, held.shape[3]), held.dtype))
+    several = len(shapes) > 1
     moved = sum(x.size * x.dtype.itemsize for x in operands + shapes)
     vmem = pl.BlockSpec(memory_space=pltpu.VMEM)
     result = pl.pallas_call(
@@ -155,10 +164,11 @@
             partial is not None,
             target_off,
             emit,
+            copies,
         ),
-        out_shape=tuple(shapes) if emit else shapes[0],
+        out_shape=tuple(shapes) if several else shapes[0],
         in_specs=[vmem] * len(operands),
-        out_specs=tuple([vmem] * len(shapes)) if emit else vmem,
+        out_specs=tuple([vmem] * len(shapes)) if several else vmem,
         cost_estimate=pl.CostEstimate(flops=flops, bytes_accessed=moved, transcendentals=0),
     )(*operands)
     return result
@@ -213,7 +223,8 @@
     edges = jnp.swapaxes(jnp.concatenate([west[:, 1:, :K, :], east[:, :1, :K, :]], axis=1), 2, 3)
     like_wide = jax.ShapeDtypeStruct((lat_blocks, lon_blocks + 2) + panel.shape[2:], jnp.float32)
     own_fields = (0,) * lat_blocks
-    partial = rows_call(
+    span = (1, lon_blocks + 3)
+    partial, members = rows_call(
         own_plan(lat_blocks, 0, own_fields, (0, 0)),
         K,
         targets,
@@ -223,9 +234,10 @@
         like_wide,
         target_off=-1,
         edges=edges,
+        copies=((0,) + span,),
     )
     emit = tuple(0 if p == 0 else 1 for p in range(lat_blocks))
-    first_product, first_row, last_row = rows_call(
+    first_product, first_row, last_row, members_north, members_south = rows_call(
         halo_plan(lat_blocks, (0, 1), (0, 1), (0, 0), trimmed=True),
         K,
         targets,
@@ -236,12 +248,10 @@
         target_off=-1,
         emit=emit,
         edges=edges,
+        copies=((0,) + span, (1,) + span),
     )
     north2, south2 = lat_halo(first_row, last_row)
     row_fields = (1, 2) if lat_blocks == 2 else None
-    members = wider[:, 1 : lon_blocks + 3, :K]
-    members_north = north[:, 1 : lon_blocks + 3, :K]
-    members_south = south[:, 1 : lon_blocks + 3, :K]
     partial = rows_call(
         own_plan(lat_blocks, 0, row_fields, (0, 0)),
         0,

time: 102 us -> 99.3 us (0.974)
  local copies, waits for them, and re-layouts: 12.1 us -> 5.61 us
  waiting for transfers between devices: 5.86 us -> 9.33 us
    slice x3 -> x0, local copies, waits for them, and re-layouts: 5.05 us -> none  [the longest x1 1.79 us: local(): members = wider[:, 1:lon_blocks + 3, :K]]
    ppermute x2, waiting for transfers between devices: 0.01 us -> 3.47 us  [lat_halo(): north = lax.ppermute(last_row, 'lat', [(i, i + 1) for i in range(nlat - 1)])]
    unnamed x15, local copies, waits for them, and re-layouts: 5.4 us -> 3.91 us
  transfers between devices with their start and end apart: 6 -> 6, of which waited for: 1 -> 2; matrix products, arithmetic and copies ran while one was open for 8% -> 3% of each run, Pallas kernels for 34% -> 34%
where the time goes in v12:
time: 99.3 us; the launch traced here: 98.6 us
  Pallas kernels  58.8 us (59%)
  starting transfers between devices  21.1 us (21%)
  waiting for transfers between devices  9.33 us (9%)
  local copies, waits for them, and re-layouts  5.61 us (6%)
  other arithmetic  3.03 us (3%)
    pallas_call x4, Pallas kernels, rows_call(): pl.pallas_call(functools.partial(kernel_with_edges if edges is not None e...  58.8 us
    ppermute x2, starting transfers between devices, lat_halo(): lax.ppermute(first_row, 'lat', [(i + 1, i) for i in range(nlat - 1)])  9.93 us
    ppermute x1, waiting for transfers between devices, lon_halo(): lax.ppermute(cells[:, -depth:], 'lon', [(i, (i + 1) % nlon) for i in rang...  5.85 us
    ppermute x2, starting transfers between devices, lat_halo(): north = lax.ppermute(last_row, 'lat', [(i, i + 1) for i in range(nlat - 1)])  5.73 us
    ppermute x1, starting transfers between devices, lon_halo(): lax.ppermute(cells[:, :depth], 'lon', [((i + 1) % nlon, i) for i in range...  5.35 us
    unnamed x15, local copies, waits for them, and re-layouts  3.91 us
    ppermute x2, waiting for transfers between devices, lat_halo(): north = lax.ppermute(last_row, 'lat', [(i, i + 1) for i in range(nlat - 1)])  3.47 us
  transfers between devices with their start and end apart: 6, of which 2 were waited for; matrix products, arithmetic and copies ran while one was open for 3% of the time, Pallas kernels for 34%

profile of v12, /device:TPU:2, one launch (start us, length us, event | category | flops | bytes accessed | tf_op | source)
XLA Modules:
  0.0 98.6 jit_solution(11788609141143241327)
XLA Ops:
  0.6 0.0 copy-start.1
  0.6 1.5 %reduce-precision_convert_fusion = (bf16[2,8,128,128]{3,2,1,0:T(8,128)(2,1)S(1)}, bf16[2,8,128,128]{3,2,1,0:T(8,128)(2,1)S(1)}) fusion(f32[2,8,128,128]{3,2,1,0:T(8,128)} %param.6), kind=kLoop, calls=%fused_computation.2 | loop fusion | flops 1048576 | bytes 2097152 | tf_op jit(solution)/shard_map/convert_element_type | solution.py:179
  2.2 0.0 copy-done.1
  2.2 0.1 collective-permute-start
  2.3 5.3 %collective-permute-start.1 = (bf16[2,2,336,128]{3,2,1,0:T(8,128)(2,1)S(1)}, bf16[2,2,336,128]{3,2,1,0:T(8,128)(2,1)S(1)}, u32[]{:S(2)}, u32[]{:S(2)}) collective-permute-start(bf16[2,2,336,128]{3,2,1,0:T(8,128)(2,1)S(1)} %get-tuple-element.20), channel_id=1, source_target_pairs={{8,0},{16,8},{24,16},{32,24},{40,32},{48,40},{56,48},{64,56},{72,6... | collective-permute-start | bytes 1032200 | tf_op jit(solution)/shard_map/ppermute | solution.py:46
  7.7 5.8 %collective-permute-done = bf16[2,2,336,128]{3,2,1,0:T(8,128)(2,1)S(1)} collective-permute-done((bf16[2,2,336,128]{3,2,1,0:T(8,128)(2,1)S(1)}, bf16[2,2,336,128]{3,2,1,0:T(8,128)(2,1)S(1)}, u32[]{:S(2)}, u32[]{:S(2)}) %collective-permute-start) | collective-permute-done | bytes 344096 | tf_op jit(solution)/shard_map/ppermute | solution.py:45
  13.5 0.0 collective-permute-done.1
  13.5 0.2 pad_maximum_fusion.args_3_
  13.7 0.5 copy-done.6
  14.3 0.1 fusion.1
  14.4 1.2 %pad_maximum_fusion.1 = bf16[1,12,304,128]{3,2,1,0:T(8,128)(2,1)} fusion(bf16[1,12,112,128]{3,2,1,0:T(8,128)(2,1)S(1)} %get-tuple-element.17, bf16[1,12,112,128]{3,2,1,0:T(8,128)(2,1)S(1)} %get-tuple-element.18, bf16[1,12,80,128]{3,2,1,0:T(8,128)(2,1)S(1)} %slice.40), kind=kLoop, calls=%fused_computation.4 | loop fusion | flops 2801664 | bytes 1867776 | tf_op jit(solution)/shard_map/concatenate | solution.py:218
  15.6 0.2 copy-done
  15.9 3.8 %collective-permute-start.2 = (bf16[1,12,304,128]{3,2,1,0:T(8,128)(2,1)}, bf16[1,12,304,128]{3,2,1,0:T(8,128)(2,1)S(1)}, u32[]{:S(2)}, u32[]{:S(2)}) collective-permute-start(bf16[1,12,304,128]{3,2,1,0:T(8,128)(2,1)} %pad_maximum_fusion.1), channel_id=1, source_target_pairs={{0,1},{1,2},{2,3},{3,4},{4,5},{5,6},{6,7},{8,9},{9,10},{10,11},{11... | collective-permute-start | bytes 2801672 | tf_op jit(solution)/shard_map/ppermute | solution.py:52
  19.7 0.1 pad_maximum_fusion.2
  19.7 4.1 %collective-permute-start.3 = (bf16[1,12,304,128]{3,2,1,0:T(8,128)(2,1)S(1)}, bf16[1,12,304,128]{3,2,1,0:T(8,128)(2,1)S(1)}, u32[]{:S(2)}, u32[]{:S(2)}) collective-permute-start(bf16[1,12,304,128]{3,2,1,0:T(8,128)(2,1)S(1)} %pad_maximum_fusion.2), channel_id=1, source_target_pairs={{1,0},{2,1},{3,2},{4,3},{5,4},{6,5},{7,6},{9,8},{10,9},{11,10},{12... | collective-permute-start | bytes 2801672 | tf_op jit(solution)/shard_map/ppermute | solution.py:53
  23.9 1.0 %copy.5 = bf16[2,8,80,128]{2,3,1,0:T(8,128)(2,1)} copy(bf16[2,8,80,128]{3,2,1,0:T(8,128)(2,1)S(1)} %copy-done.1) | data formatting | bytes 655360 | tf_op args[0]
  24.9 0.8 slice.39
  25.7 0.8 copy.7.args_1_
  26.5 18.4 %shard_map.50 = (f32[2,10,128,128]{3,2,1,0:T(8,128)}, bf16[2,10,80,128]{3,2,1,0:T(8,128)(2,1)}) custom-call(bf16[2,8,128,80]{3,2,1,0:T(8,128)(2,1)} %bitcast.3, bf16[2,2,128,80]{3,2,1,0:T(8,128)(2,1)} %copy.7.args_1_, f32[9,128,128]{2,1,0:T(8,128)} %constant.2.clone.args_2_.rest_0_, bf16[2,12,336,128]{3,2,1,0:T(8,128)(2,1)} %copy-done), custom_call_target="tpu_custom_call" | custom-call | flops 1824522240 | bytes 4784128 | tf_op jit(solution)/shard_map/pallas_call | solution.py:159
  44.9 0.0 collective-permute-done.2.args_4_
  44.9 0.0 collective-permute-done.3.args_5_
  44.9 0.0 copy-start.3
  44.9 0.9 copy-done.2
  45.8 0.3 copy-done.3
  46.2 13.6 %shard_map.51 = (f32[2,8,128,128]{3,2,1,0:T(8,128)}, bf16[1,10,256,128]{3,2,1,0:T(8,128)(2,1)}, bf16[1,10,256,128]{3,2,1,0:T(8,128)(2,1)}, bf16[1,10,80,128]{3,2,1,0:T(8,128)(2,1)}, bf16[1,10,80,128]{3,2,1,0:T(8,128)(2,1)}) custom-call(bf16[2,8,128,80]{3,2,1,0:T(8,128)(2,1)} %bitcast.4, bf16[2,2,128,80]{3,2,1,0:T(8,128)(2,1)} %copy.7.args_1_, ...), custom_call_target="tpu_custom_call" | custom-call | flops 912261120 | bytes 6946816 | tf_op jit(solution)/shard_map/pallas_call | solution.py:159
  59.8 5.8 %collective-permute-start.5 = (bf16[1,10,256,128]{3,2,1,0:T(8,128)(2,1)}, bf16[1,10,256,128]{3,2,1,0:T(8,128)(2,1)S(1)}, u32[]{:S(2)}, u32[]{:S(2)}) collective-permute-start(bf16[1,10,256,128]{3,2,1,0:T(8,128)(2,1)} %get-tuple-element.12.rest_2_), channel_id=1, source_target_pairs={{1,0},{2,1},{3,2},{4,3},{5,4},{6,5},{7,6},{9,8},{10,9},{11,10},{12... | collective-permute-start | bytes 1966088 | tf_op jit(solution)/shard_map/ppermute | solution.py:53
  65.6 1.9 %collective-permute-start.4 = (bf16[1,10,256,128]{3,2,1,0:T(8,128)(2,1)}, bf16[1,10,256,128]{3,2,1,0:T(8,128)(2,1)S(1)}, u32[]{:S(2)}, u32[]{:S(2)}) collective-permute-start(bf16[1,10,256,128]{3,2,1,0:T(8,128)(2,1)} %get-tuple-element.13.rest_3_), channel_id=1, source_target_pairs={{0,1},{1,2},{2,3},{3,4},{4,5},{5,6},{6,7},{8,9},{9,10},{10,11},{11... | collective-permute-start | bytes 1966088 | tf_op jit(solution)/shard_map/ppermute | solution.py:52
  67.5 15.4 %shard_map.52.rest_1_ = f32[2,8,128,128]{3,2,1,0:T(8,128)} custom-call(bf16[2,8,128,80]{3,2,1,0:T(8,128)(2,1)} %bitcast.5, f32[9,128,128]{2,1,0:T(8,128)} %constant.2.clone.args_2_.rest_0_, bf16[2,10,80,128]{3,2,1,0:T(8,128)(2,1)} %get-tuple-element.11.rest_1_, bf16[1,10,256,128]{3,2,1,0:T(8,128)(2,1)} %get-tuple-element.12.rest_2_, ...), custom_call_target="tpu_custom_call" | custom-call | flops 1459617792 | bytes 3686400 | tf_op jit(solution)/shard_map/pallas_call | solution.py:159
  82.9 0.0 collective-permute-done.5.rest_5_
  82.9 3.5 %collective-permute-done.4.rest_4_ = bf16[1,10,256,128]{3,2,1,0:T(8,128)(2,1)S(1)} collective-permute-done((bf16[1,10,256,128]{3,2,1,0:T(8,128)(2,1)}, bf16[1,10,256,128]{3,2,1,0:T(8,128)(2,1)S(1)}, u32[]{:S(2)}, u32[]{:S(2)}) %collective-permute-start.4) | collective-permute-done | bytes 655392 | tf_op jit(solution)/shard_map/ppermute | solution.py:52
  86.4 0.9 copy-done.5
  87.2 11.3 %shard_map.53 = f32[2,8,128,128]{3,2,1,0:T(8,128)} custom-call(bf16[2,8,128,80]{3,2,1,0:T(8,128)(2,1)} %bitcast.6, f32[9,128,128]{2,1,0:T(8,128)} %constant.2.clone.args_2_.rest_0_, f32[2,8,128,128]{3,2,1,0:T(8,128)} %shard_map.52.rest_1_, bf16[1,10,80,128]{3,2,1,0:T(8,128)(2,1)} %get-tuple-element.14.rest_2_, ...), custom_call_target="tpu_custom_call" | custom-call | flops 729808896 | bytes 4734976 | tf_op jit(solution)/shard_map/pallas_call | solution.py:159
  (11 shorter events, 0.1 us)
Async XLA Ops:
  0.6 1.5 %copy-start.1 = (bf16[2,8,80,128]{3,2,1,0:T(8,128)(2,1)S(1)}, bf16[2,8,80,128]{3,2,1,0:T(8,128)(2,1)}, u32[]{:S(2)}) copy-start(bf16[2,8,80,128]{3,2,1,0:T(8,128)(2,1)} %param.5) | copy-start | bytes 983044
  2.2 11.3 %collective-permute-start = (bf16[2,2,336,128]{3,2,1,0:T(8,128)(2,1)S(1)}, bf16[2,2,336,128]{3,2,1,0:T(8,128)(2,1)S(1)}, u32[]{:S(2)}, u32[]{:S(2)}) collective-permute-start(bf16[2,2,336,128]{3,2,1,0:T(8,128)(2,1)S(1)} %get-tuple-element.19), channel_id=1, source_target_pairs={{0,8},{8,16},{16,24},{24,32},{32,40},{40,48},{48,56},{56,64},{64,7... | collective-permute-start | bytes 1032200 | tf_op jit(solution)/shard_map/ppermute | solution.py:45
  2.3 11.2 %collective-permute-start.1 = (bf16[2,2,336,128]{3,2,1,0:T(8,128)(2,1)S(1)}, bf16[2,2,336,128]{3,2,1,0:T(8,128)(2,1)S(1)}, u32[]{:S(2)}, u32[]{:S(2)}) collective-permute-start(bf16[2,2,336,128]{3,2,1,0:T(8,128)(2,1)S(1)} %get-tuple-element.20), channel_id=1, source_target_pairs={{8,0},{16,8},{24,16},{32,24},{40,32},{48,40},{56,48},{64,56},{72,6... | collective-permute-start | bytes 1032200 | tf_op jit(solution)/shard_map/ppermute | solution.py:46
  13.5 0.7 copy-start.6
  14.3 1.6 %copy-start = (bf16[2,12,336,128]{3,2,1,0:T(8,128)(2,1)}, bf16[2,12,336,128]{3,2,1,0:T(8,128)(2,1)S(1)}, u32[]{:S(2)}) copy-start(bf16[2,12,336,128]{3,2,1,0:T(8,128)(2,1)S(1)} %pad_maximum_fusion.args_3_) | copy-start | bytes 6193156
  15.9 29.1 %collective-permute-start.2 = (bf16[1,12,304,128]{3,2,1,0:T(8,128)(2,1)}, bf16[1,12,304,128]{3,2,1,0:T(8,128)(2,1)S(1)}, u32[]{:S(2)}, u32[]{:S(2)}) collective-permute-start(bf16[1,12,304,128]{3,2,1,0:T(8,128)(2,1)} %pad_maximum_fusion.1), channel_id=1, source_target_pairs={{0,1},{1,2},{2,3},{3,4},{4,5},{5,6},{6,7},{8,9},{9,10},{10,11},{11... | collective-permute-start | bytes 2801672 | tf_op jit(solution)/shard_map/ppermute | solution.py:52
  19.7 25.2 %collective-permute-start.3 = (bf16[1,12,304,128]{3,2,1,0:T(8,128)(2,1)S(1)}, bf16[1,12,304,128]{3,2,1,0:T(8,128)(2,1)S(1)}, u32[]{:S(2)}, u32[]{:S(2)}) collective-permute-start(bf16[1,12,304,128]{3,2,1,0:T(8,128)(2,1)S(1)} %pad_maximum_fusion.2), channel_id=1, source_target_pairs={{1,0},{2,1},{3,2},{4,3},{5,4},{6,5},{7,6},{9,8},{10,9},{11,10},{12... | collective-permute-start | bytes 2801672 | tf_op jit(solution)/shard_map/ppermute | solution.py:53
  44.9 0.9 copy-start.2
  44.9 1.2 %copy-start.3 = (bf16[1,12,304,128]{3,2,1,0:T(8,128)(2,1)}, bf16[1,12,304,128]{3,2,1,0:T(8,128)(2,1)S(1)}, u32[]{:S(2)}) copy-start(bf16[1,12,304,128]{3,2,1,0:T(8,128)(2,1)S(1)} %collective-permute-done.3.args_5_) | copy-start | bytes 2801668
  59.8 23.1 %collective-permute-start.5 = (bf16[1,10,256,128]{3,2,1,0:T(8,128)(2,1)}, bf16[1,10,256,128]{3,2,1,0:T(8,128)(2,1)S(1)}, u32[]{:S(2)}, u32[]{:S(2)}) collective-permute-start(bf16[1,10,256,128]{3,2,1,0:T(8,128)(2,1)} %get-tuple-element.12.rest_2_), channel_id=1, source_target_pairs={{1,0},{2,1},{3,2},{4,3},{5,4},{6,5},{7,6},{9,8},{10,9},{11,10},{12... | collective-permute-start | bytes 1966088 | tf_op jit(solution)/shard_map/ppermute | solution.py:53
  65.6 20.8 %collective-permute-start.4 = (bf16[1,10,256,128]{3,2,1,0:T(8,128)(2,1)}, bf16[1,10,256,128]{3,2,1,0:T(8,128)(2,1)S(1)}, u32[]{:S(2)}, u32[]{:S(2)}) collective-permute-start(bf16[1,10,256,128]{3,2,1,0:T(8,128)(2,1)} %get-tuple-element.13.rest_3_), channel_id=1, source_target_pairs={{0,1},{1,2},{2,3},{3,4},{4,5},{5,6},{6,7},{8,9},{9,10},{10,11},{11... | collective-permute-start | bytes 1966088 | tf_op jit(solution)/shard_map/ppermute | solution.py:52
  82.9 3.5 %copy-start.4 = (bf16[1,10,256,128]{3,2,1,0:T(8,128)(2,1)}, bf16[1,10,256,128]{3,2,1,0:T(8,128)(2,1)S(1)}, u32[]{:S(2)}) copy-start(bf16[1,10,256,128]{3,2,1,0:T(8,128)(2,1)S(1)} %collective-permute-done.5.rest_5_) | copy-start | bytes 1966084
  86.4 0.9 copy-start.5

commit v13 on v12

--- a/solution.py
+++ b/solution.py
@@ -54,13 +54,16 @@
     return north, south
 
 
-def rows_kernel(plan, field_at, with_partial, target_off, emit, copies, targets_ref, edges_ref, taper_ref, *rest):
-    count = 1 + len(emit) + len(copies)
+def rows_kernel(
+    plan, field_at, with_partial, target_off, emit, copies, tiles, targets_ref, edges_ref, taper_ref, *rest
+):
+    count = 1 + len(emit) + len(copies) + (tiles == "save")
     outs = rest[-count:]
     rest = rest[: len(rest) - count]
     out_ref = outs[0]
     partial_ref = rest[0] if with_partial else None
     sources = rest[1:] if with_partial else rest
+    tiles_ref = outs[-1] if tiles == "save" else (sources[-1] if tiles == "load" else None)
     for (source, first, end), copy_ref in zip(copies, outs[1 + len(emit) :]):
         copy_ref[...] = sources[source][:, first:end, :K, :]
     columns, rank = out_ref.shape[2:]
@@ -68,7 +71,7 @@
     lon_blocks = partial_ref.shape[1] if emit else out_ref.shape[1]
     for p in range(lat_blocks):
 
-        def one_block(q, carry, p=p, uses=plan[p], side=None):
+        def one_block(q, carry, p=p, uses=plan[p], side=None, middle=False):
             if side is None:
                 target = targets_ref[p, q + target_off]
             else:
@@ -80,14 +83,22 @@
             for dr, members_at, members_row, field_from, row, members_off, field_off, trim in uses:
                 members_ref, field_ref = sources[members_at], sources[field_from]
                 for dc in range(3):
-                    gram = jnp.dot(
-                        target,
-                        members_ref[members_row, q + dc + members_off, :K, :],
-                        preferred_element_type=jnp.float32,
-                    )
-                    tile = gram * taper_ref[dr * 3 + dc]
-                    tile_high = tile.astype(jnp.bfloat16)
-                    tile_low = (tile - tile_high.astype(jnp.float32)).astype(jnp.bfloat16)
+                    slot = 3 * uses.index((dr, members_at, members_row, field_from, row, members_off, field_off, trim)) + dc
+                    if tiles == "load":
+                        tile_high = tiles_ref[p, q, slot, :columns, :]
+                        tile_low = tiles_ref[p, q, slot, columns:, :]
+                    else:
+                        gram = jnp.dot(
+                            target,
+                            members_ref[members_row, q + dc + members_off, :K, :],
+                            preferred_element_type=jnp.float32,
+                        )
+                        tile = gram * taper_ref[dr * 3 + dc]
+                        tile_high = tile.astype(jnp.bfloat16)
+                        tile_low = (tile - tile_high.astype(jnp.float32)).astype(jnp.bfloat16)
+                        if tiles == "save" and middle:
+                            tiles_ref[p, q - 1, slot, :columns, :] = tile_high
+                            tiles_ref[p, q - 1, slot, columns:, :] = tile_low
                     partner = field_ref.at[row, q + dc + field_off]
                     if trim:
                         kept = columns - STRIDE
@@ -127,7 +138,7 @@
             lax.fori_loop(0, lon_blocks, one_block, 0)
         else:
             one_block(0, 0, side=0)
-            lax.fori_loop(1, lon_blocks - 1, one_block, 0)
+            lax.fori_loop(1, lon_blocks - 1, functools.partial(one_block, middle=True), 0)
             one_block(lon_blocks - 1, 0, side=1)
 
 
@@ -135,12 +146,23 @@
     return rows_kernel(*args)
 
 
-def kernel_without_edges(plan, field_at, with_partial, target_off, emit, copies, targets_ref, *rest):
-    return rows_kernel(plan, field_at, with_partial, target_off, emit, copies, targets_ref, None, *rest)
+def kernel_without_edges(plan, field_at, with_partial, target_off, emit, copies, tiles, targets_ref, *rest):
+    return rows_kernel(plan, field_at, with_partial, target_off, emit, copies, tiles, targets_ref, None, *rest)
 
 
 def rows_call(
-    plan, field_at, targets, taper, partial, sources, out_like, target_off=0, emit=(), edges=None, copies=()
+    plan,
+    field_at,
+    targets,
+    taper,
+    partial,
+    sources,
+    out_like,
+    target_off=0,
+    emit=(),
+    edges=None,
+    copies=(),
+    tiles=None,
 ):
     lat_blocks, lon_blocks, columns, rank = (partial if emit else out_like).shape
     codes = sum(3 * len(uses) for uses in plan)
@@ -153,6 +175,10 @@
     for source, first, end in copies:
         held = sources[source]
         shapes.append(jax.ShapeDtypeStruct((held.shape[0], end - first, K, held.shape[3]), held.dtype))
+    if tiles == "save":
+        slots = max(3 * len(uses) for uses in plan)
+        inner = lon_blocks - 2
+        shapes.append(jax.ShapeDtypeStruct((lat_blocks, inner, slots, 2 * columns, rank), jnp.bfloat16))
     several = len(shapes) > 1
     moved = sum(x.size * x.dtype.itemsize for x in operands + shapes)
     vmem = pl.BlockSpec(memory_space=pltpu.VMEM)
@@ -165,6 +191,7 @@
             target_off,
             emit,
             copies,
+            tiles,
         ),
         out_shape=tuple(shapes) if several else shapes[0],
         in_specs=[vmem] * len(operands),
@@ -224,7 +251,7 @@
     like_wide = jax.ShapeDtypeStruct((lat_blocks, lon_blocks + 2) + panel.shape[2:], jnp.float32)
     own_fields = (0,) * lat_blocks
     span = (1, lon_blocks + 3)
-    partial, members = rows_call(
+    partial, members, own_tiles = rows_call(
         own_plan(lat_blocks, 0, own_fields, (0, 0)),
         K,
         targets,
@@ -235,6 +262,7 @@
         target_off=-1,
         edges=edges,
         copies=((0,) + span,),
+        tiles="save",
     )
     emit = tuple(0 if p == 0 else 1 for p in range(lat_blocks))
     first_product, first_row, last_row, members_north, members_south = rows_call(
@@ -258,8 +286,9 @@
         targets,
         taper,
         None,
-        (members, first_row, last_row),
+        (members, first_row, last_row, own_tiles),
         panel,
+        tiles="load",
     )
     second_product = rows_call(
         halo_plan(lat_blocks, (0, 1), (2, 3), (0, 0)),

time: 99.3 us -> 98.7 us (level)
  waiting for transfers between devices: 9.33 us -> 15.1 us
  Pallas kernels: 58.8 us -> 54.1 us
  starting transfers between devices: 21.1 us -> 19.9 us
    pallas_call x4, Pallas kernels: 58.8 us -> 54.1 us  [rows_call(): pl.pallas_call(functools.partial(kernel_with_edges if edges is not None e...]
    ppermute x2, waiting for transfers between devices: 0.01 us -> 3.33 us  [lat_halo(): lax.ppermute(first_row, 'lat', [(i + 1, i) for i in range(nlat - 1)])]
    ppermute x2, waiting for transfers between devices: 3.47 us -> 5.89 us  [lat_halo(): north = lax.ppermute(last_row, 'lat', [(i, i + 1) for i in range(nlat - 1)])]
    ppermute x2, starting transfers between devices: 9.93 us -> 8.79 us  [lat_halo(): lax.ppermute(first_row, 'lat', [(i + 1, i) for i in range(nlat - 1)])]
  transfers between devices with their start and end apart: 6 -> 6, of which waited for: 2 -> 3; matrix products, arithmetic and copies ran while one was open for 3% -> 3% of each run, Pallas kernels for 34% -> 30%
where the time goes in v13:
time: 98.7 us; the launch traced here: 98.1 us
  Pallas kernels  54.1 us (55%)
  starting transfers between devices  19.9 us (20%)
  waiting for transfers between devices  15.1 us (15%)
  local copies, waits for them, and re-layouts  5.11 us (5%)
  other arithmetic  3.01 us (3%)
    pallas_call x4, Pallas kernels, rows_call(): pl.pallas_call(functools.partial(kernel_with_edges if edges is not None e...  54.1 us
    ppermute x2, starting transfers between devices, lat_halo(): lax.ppermute(first_row, 'lat', [(i + 1, i) for i in range(nlat - 1)])  8.79 us
    ppermute x2, waiting for transfers between devices, lat_halo(): north = lax.ppermute(last_row, 'lat', [(i, i + 1) for i in range(nlat - 1)])  5.89 us
    ppermute x1, waiting for transfers between devices, lon_halo(): lax.ppermute(cells[:, -depth:], 'lon', [(i, (i + 1) % nlon) for i in rang...  5.85 us
    ppermute x2, starting transfers between devices, lat_halo(): north = lax.ppermute(last_row, 'lat', [(i, i + 1) for i in range(nlat - 1)])  5.73 us
    ppermute x1, starting transfers between devices, lon_halo(): lax.ppermute(cells[:, :depth], 'lon', [((i + 1) % nlon, i) for i in range...  5.35 us
    unnamed x15, local copies, waits for them, and re-layouts  3.44 us
    ppermute x2, waiting for transfers between devices, lat_halo(): lax.ppermute(first_row, 'lat', [(i + 1, i) for i in range(nlat - 1)])  3.33 us
  transfers between devices with their start and end apart: 6, of which 3 were waited for; matrix products, arithmetic and copies ran while one was open for 3% of the time, Pallas kernels for 30%

profile of v13, /device:TPU:2, one launch (start us, length us, event | category | flops | bytes accessed | tf_op | source)
XLA Modules:
  0.0 98.1 jit_solution(8321738172244641752)
XLA Ops:
  0.6 0.0 copy-start.1
  0.6 1.5 %reduce-precision_convert_fusion = (bf16[2,8,128,128]{3,2,1,0:T(8,128)(2,1)S(1)}, bf16[2,8,128,128]{3,2,1,0:T(8,128)(2,1)S(1)}) fusion(f32[2,8,128,128]{3,2,1,0:T(8,128)} %param.6), kind=kLoop, calls=%fused_computation.2 | loop fusion | flops 1048576 | bytes 2097152 | tf_op jit(solution)/shard_map/convert_element_type | solution.py:206
  2.2 0.0 copy-done.1
  2.2 0.1 collective-permute-start
  2.3 5.3 %collective-permute-start.1 = (bf16[2,2,336,128]{3,2,1,0:T(8,128)(2,1)S(1)}, bf16[2,2,336,128]{3,2,1,0:T(8,128)(2,1)S(1)}, u32[]{:S(2)}, u32[]{:S(2)}) collective-permute-start(bf16[2,2,336,128]{3,2,1,0:T(8,128)(2,1)S(1)} %get-tuple-element.22), channel_id=1, source_target_pairs={{8,0},{16,8},{24,16},{32,24},{40,32},{48,40},{56,48},{64,56},{72,6... | collective-permute-start | bytes 1032200 | tf_op jit(solution)/shard_map/ppermute | solution.py:46
  7.7 5.8 %collective-permute-done = bf16[2,2,336,128]{3,2,1,0:T(8,128)(2,1)S(1)} collective-permute-done((bf16[2,2,336,128]{3,2,1,0:T(8,128)(2,1)S(1)}, bf16[2,2,336,128]{3,2,1,0:T(8,128)(2,1)S(1)}, u32[]{:S(2)}, u32[]{:S(2)}) %collective-permute-start) | collective-permute-done | bytes 344096 | tf_op jit(solution)/shard_map/ppermute | solution.py:45
  13.5 0.0 collective-permute-done.1
  13.5 0.2 pad_maximum_fusion.args_3_
  13.7 0.0 copy-start
  13.8 0.1 fusion.1
  13.9 1.2 %pad_maximum_fusion.1 = bf16[1,12,304,128]{3,2,1,0:T(8,128)(2,1)} fusion(bf16[1,12,112,128]{3,2,1,0:T(8,128)(2,1)S(1)} %get-tuple-element.19, bf16[1,12,112,128]{3,2,1,0:T(8,128)(2,1)S(1)} %get-tuple-element.20, bf16[1,12,80,128]{3,2,1,0:T(8,128)(2,1)S(1)} %slice.40), kind=kLoop, calls=%fused_computation.4 | loop fusion | flops 2801664 | bytes 1867776 | tf_op jit(solution)/shard_map/concatenate | solution.py:245
  15.1 0.3 copy-done
  15.4 3.8 %collective-permute-start.2 = (bf16[1,12,304,128]{3,2,1,0:T(8,128)(2,1)}, bf16[1,12,304,128]{3,2,1,0:T(8,128)(2,1)S(1)}, u32[]{:S(2)}, u32[]{:S(2)}) collective-permute-start(bf16[1,12,304,128]{3,2,1,0:T(8,128)(2,1)} %pad_maximum_fusion.1), channel_id=1, source_target_pairs={{0,1},{1,2},{2,3},{3,4},{4,5},{5,6},{6,7},{8,9},{9,10},{10,11},{11... | collective-permute-start | bytes 2801672 | tf_op jit(solution)/shard_map/ppermute | solution.py:52
  19.2 0.1 pad_maximum_fusion.2
  19.2 0.0 copy-done.6
  19.3 4.1 %collective-permute-start.3 = (bf16[1,12,304,128]{3,2,1,0:T(8,128)(2,1)S(1)}, bf16[1,12,304,128]{3,2,1,0:T(8,128)(2,1)S(1)}, u32[]{:S(2)}, u32[]{:S(2)}) collective-permute-start(bf16[1,12,304,128]{3,2,1,0:T(8,128)(2,1)S(1)} %pad_maximum_fusion.2), channel_id=1, source_target_pairs={{1,0},{2,1},{3,2},{4,3},{5,4},{6,5},{7,6},{9,8},{10,9},{11,10},{12... | collective-permute-start | bytes 2801672 | tf_op jit(solution)/shard_map/ppermute | solution.py:53
  23.4 1.0 %copy.5 = bf16[2,8,80,128]{2,3,1,0:T(8,128)(2,1)} copy(bf16[2,8,80,128]{3,2,1,0:T(8,128)(2,1)S(1)} %copy-done.1) | data formatting | bytes 655360 | tf_op args[0]
  24.4 0.8 slice.39
  25.2 0.8 copy.7.args_1_
  26.0 19.6 %shard_map.50 = (f32[2,10,128,128]{3,2,1,0:T(8,128)}, bf16[2,10,80,128]{3,2,1,0:T(8,128)(2,1)}, bf16[2,8,6,256,128]{4,3,2,1,0:T(8,128)(2,1)}) custom-call(bf16[2,8,128,80]{3,2,1,0:T(8,128)(2,1)} %bitcast.3, bf16[2,2,128,80]{3,2,1,0:T(8,128)(2,1)} %copy.7.args_1_, f32[9,128,128]{2,1,0:T(8,128)} %constant.2.clone.args_2_.rest_0_, bf16[2,12,336,128]{3,2,1,0:T(8,128)(2,1)} %copy-done), custom_call_target="tpu_custom_call" | custom-call | flops 1824522240 | bytes 11075584 | tf_op jit(solution)/shard_map/pallas_call | solution.py:185
  45.6 0.0 collective-permute-done.2.args_4_
  45.6 0.0 collective-permute-done.3.args_5_
  45.6 0.9 copy-done.2
  46.5 0.3 copy-done.3
  46.8 13.6 %shard_map.51 = (f32[2,8,128,128]{3,2,1,0:T(8,128)}, bf16[1,10,256,128]{3,2,1,0:T(8,128)(2,1)}, bf16[1,10,256,128]{3,2,1,0:T(8,128)(2,1)}, bf16[1,10,80,128]{3,2,1,0:T(8,128)(2,1)}, bf16[1,10,80,128]{3,2,1,0:T(8,128)(2,1)}) custom-call(bf16[2,8,128,80]{3,2,1,0:T(8,128)(2,1)} %bitcast.4, bf16[2,2,128,80]{3,2,1,0:T(8,128)(2,1)} %copy.7.args_1_, ...), custom_call_target="tpu_custom_call" | custom-call | flops 912261120 | bytes 6946816 | tf_op jit(solution)/shard_map/pallas_call | solution.py:185
  60.4 4.7 %collective-permute-start.5 = (bf16[1,10,256,128]{3,2,1,0:T(8,128)(2,1)}, bf16[1,10,256,128]{3,2,1,0:T(8,128)(2,1)S(1)}, u32[]{:S(2)}, u32[]{:S(2)}) collective-permute-start(bf16[1,10,256,128]{3,2,1,0:T(8,128)(2,1)} %get-tuple-element.13.rest_2_), channel_id=1, source_target_pairs={{1,0},{2,1},{3,2},{4,3},{5,4},{6,5},{7,6},{9,8},{10,9},{11,10},{12... | collective-permute-start | bytes 1966088 | tf_op jit(solution)/shard_map/ppermute | solution.py:53
  65.1 1.9 %collective-permute-start.4 = (bf16[1,10,256,128]{3,2,1,0:T(8,128)(2,1)}, bf16[1,10,256,128]{3,2,1,0:T(8,128)(2,1)S(1)}, u32[]{:S(2)}, u32[]{:S(2)}) collective-permute-start(bf16[1,10,256,128]{3,2,1,0:T(8,128)(2,1)} %get-tuple-element.14.rest_3_), channel_id=1, source_target_pairs={{0,1},{1,2},{2,3},{3,4},{4,5},{5,6},{6,7},{8,9},{9,10},{10,11},{11... | collective-permute-start | bytes 1966088 | tf_op jit(solution)/shard_map/ppermute | solution.py:52
  67.0 9.6 %shard_map.52.rest_1_ = f32[2,8,128,128]{3,2,1,0:T(8,128)} custom-call(bf16[2,8,128,80]{3,2,1,0:T(8,128)(2,1)} %bitcast.5, f32[9,128,128]{2,1,0:T(8,128)} %constant.2.clone.args_2_.rest_0_, bf16[2,10,80,128]{3,2,1,0:T(8,128)(2,1)} %get-tuple-element.12.rest_1_, bf16[1,10,256,128]{3,2,1,0:T(8,128)(2,1)} %get-tuple-element.13.rest_2_, ...), custom_call_target="tpu_custom_call" | custom-call | flops 1459617792 | bytes 9977856 | tf_op jit(solution)/shard_map/pallas_call | solution.py:185
  76.6 3.3 %collective-permute-done.5.rest_5_ = bf16[1,10,256,128]{3,2,1,0:T(8,128)(2,1)S(1)} collective-permute-done((bf16[1,10,256,128]{3,2,1,0:T(8,128)(2,1)}, bf16[1,10,256,128]{3,2,1,0:T(8,128)(2,1)S(1)}, u32[]{:S(2)}, u32[]{:S(2)}) %collective-permute-start.5) | collective-permute-done | bytes 655392 | tf_op jit(solution)/shard_map/ppermute | solution.py:53
  80.0 5.9 %collective-permute-done.4.rest_4_ = bf16[1,10,256,128]{3,2,1,0:T(8,128)(2,1)S(1)} collective-permute-done((bf16[1,10,256,128]{3,2,1,0:T(8,128)(2,1)}, bf16[1,10,256,128]{3,2,1,0:T(8,128)(2,1)S(1)}, u32[]{:S(2)}, u32[]{:S(2)}) %collective-permute-start.4) | collective-permute-done | bytes 655392 | tf_op jit(solution)/shard_map/ppermute | solution.py:52
  85.9 0.9 copy-done.5
  86.7 11.3 %shard_map.53 = f32[2,8,128,128]{3,2,1,0:T(8,128)} custom-call(bf16[2,8,128,80]{3,2,1,0:T(8,128)(2,1)} %bitcast.6, f32[9,128,128]{2,1,0:T(8,128)} %constant.2.clone.args_2_.rest_0_, f32[2,8,128,128]{3,2,1,0:T(8,128)} %shard_map.52.rest_1_, bf16[1,10,80,128]{3,2,1,0:T(8,128)(2,1)} %get-tuple-element.16.rest_2_, ...), custom_call_target="tpu_custom_call" | custom-call | flops 729808896 | bytes 4734976 | tf_op jit(solution)/shard_map/pallas_call | solution.py:185
  (11 shorter events, 0.1 us)
Async XLA Ops:
  0.6 1.5 %copy-start.1 = (bf16[2,8,80,128]{3,2,1,0:T(8,128)(2,1)S(1)}, bf16[2,8,80,128]{3,2,1,0:T(8,128)(2,1)}, u32[]{:S(2)}) copy-start(bf16[2,8,80,128]{3,2,1,0:T(8,128)(2,1)} %param.5) | copy-start | bytes 983044
  2.2 11.3 %collective-permute-start = (bf16[2,2,336,128]{3,2,1,0:T(8,128)(2,1)S(1)}, bf16[2,2,336,128]{3,2,1,0:T(8,128)(2,1)S(1)}, u32[]{:S(2)}, u32[]{:S(2)}) collective-permute-start(bf16[2,2,336,128]{3,2,1,0:T(8,128)(2,1)S(1)} %get-tuple-element.21), channel_id=1, source_target_pairs={{0,8},{8,16},{16,24},{24,32},{32,40},{40,48},{48,56},{56,64},{64,7... | collective-permute-start | bytes 1032200 | tf_op jit(solution)/shard_map/ppermute | solution.py:45
  2.3 11.2 %collective-permute-start.1 = (bf16[2,2,336,128]{3,2,1,0:T(8,128)(2,1)S(1)}, bf16[2,2,336,128]{3,2,1,0:T(8,128)(2,1)S(1)}, u32[]{:S(2)}, u32[]{:S(2)}) collective-permute-start(bf16[2,2,336,128]{3,2,1,0:T(8,128)(2,1)S(1)} %get-tuple-element.22), channel_id=1, source_target_pairs={{8,0},{16,8},{24,16},{32,24},{40,32},{48,40},{56,48},{64,56},{72,6... | collective-permute-start | bytes 1032200 | tf_op jit(solution)/shard_map/ppermute | solution.py:46
  13.5 5.7 %copy-start.6 = (bf16[2,2,336,128]{3,2,1,0:T(8,128)(2,1)}, bf16[2,2,336,128]{3,2,1,0:T(8,128)(2,1)S(1)}, u32[]{:S(2)}) copy-start(bf16[2,2,336,128]{3,2,1,0:T(8,128)(2,1)S(1)} %collective-permute-done.1) | copy-start | bytes 1032196
  13.7 1.6 %copy-start = (bf16[2,12,336,128]{3,2,1,0:T(8,128)(2,1)}, bf16[2,12,336,128]{3,2,1,0:T(8,128)(2,1)S(1)}, u32[]{:S(2)}) copy-start(bf16[2,12,336,128]{3,2,1,0:T(8,128)(2,1)S(1)} %pad_maximum_fusion.args_3_) | copy-start | bytes 6193156
  15.4 30.2 %collective-permute-start.2 = (bf16[1,12,304,128]{3,2,1,0:T(8,128)(2,1)}, bf16[1,12,304,128]{3,2,1,0:T(8,128)(2,1)S(1)}, u32[]{:S(2)}, u32[]{:S(2)}) collective-permute-start(bf16[1,12,304,128]{3,2,1,0:T(8,128)(2,1)} %pad_maximum_fusion.1), channel_id=1, source_target_pairs={{0,1},{1,2},{2,3},{3,4},{4,5},{5,6},{6,7},{8,9},{9,10},{10,11},{11... | collective-permute-start | bytes 2801672 | tf_op jit(solution)/shard_map/ppermute | solution.py:52
  19.3 26.3 %collective-permute-start.3 = (bf16[1,12,304,128]{3,2,1,0:T(8,128)(2,1)S(1)}, bf16[1,12,304,128]{3,2,1,0:T(8,128)(2,1)S(1)}, u32[]{:S(2)}, u32[]{:S(2)}) collective-permute-start(bf16[1,12,304,128]{3,2,1,0:T(8,128)(2,1)S(1)} %pad_maximum_fusion.2), channel_id=1, source_target_pairs={{1,0},{2,1},{3,2},{4,3},{5,4},{6,5},{7,6},{9,8},{10,9},{11,10},{12... | collective-permute-start | bytes 2801672 | tf_op jit(solution)/shard_map/ppermute | solution.py:53
  45.6 0.9 copy-start.2
  45.6 1.3 %copy-start.3 = (bf16[1,12,304,128]{3,2,1,0:T(8,128)(2,1)}, bf16[1,12,304,128]{3,2,1,0:T(8,128)(2,1)S(1)}, u32[]{:S(2)}) copy-start(bf16[1,12,304,128]{3,2,1,0:T(8,128)(2,1)S(1)} %collective-permute-done.3.args_5_) | copy-start | bytes 2801668
  60.4 19.6 %collective-permute-start.5 = (bf16[1,10,256,128]{3,2,1,0:T(8,128)(2,1)}, bf16[1,10,256,128]{3,2,1,0:T(8,128)(2,1)S(1)}, u32[]{:S(2)}, u32[]{:S(2)}) collective-permute-start(bf16[1,10,256,128]{3,2,1,0:T(8,128)(2,1)} %get-tuple-element.13.rest_2_), channel_id=1, source_target_pairs={{1,0},{2,1},{3,2},{4,3},{5,4},{6,5},{7,6},{9,8},{10,9},{11,10},{12... | collective-permute-start | bytes 1966088 | tf_op jit(solution)/shard_map/ppermute | solution.py:53
  65.1 20.8 %collective-permute-start.4 = (bf16[1,10,256,128]{3,2,1,0:T(8,128)(2,1)}, bf16[1,10,256,128]{3,2,1,0:T(8,128)(2,1)S(1)}, u32[]{:S(2)}, u32[]{:S(2)}) collective-permute-start(bf16[1,10,256,128]{3,2,1,0:T(8,128)(2,1)} %get-tuple-element.14.rest_3_), channel_id=1, source_target_pairs={{0,1},{1,2},{2,3},{3,4},{4,5},{5,6},{6,7},{8,9},{9,10},{10,11},{11... | collective-permute-start | bytes 1966088 | tf_op jit(solution)/shard_map/ppermute | solution.py:52
  80.0 5.9 %copy-start.4 = (bf16[1,10,256,128]{3,2,1,0:T(8,128)(2,1)}, bf16[1,10,256,128]{3,2,1,0:T(8,128)(2,1)S(1)}, u32[]{:S(2)}) copy-start(bf16[1,10,256,128]{3,2,1,0:T(8,128)(2,1)S(1)} %collective-permute-done.5.rest_5_) | copy-start | bytes 1966084
  85.9 0.9 copy-start.5

commit v14 on v13

--- a/solution.py
+++ b/solution.py
@@ -57,14 +57,14 @@
 def rows_kernel(
     plan, field_at, with_partial, target_off, emit, copies, tiles, targets_ref, edges_ref, taper_ref, *rest
 ):
-    count = 1 + len(emit) + len(copies) + (tiles == "save")
+    count = 1 + 2 * len(emit) + len(copies) + (tiles == "save")
     outs = rest[-count:]
     rest = rest[: len(rest) - count]
     out_ref = outs[0]
     partial_ref = rest[0] if with_partial else None
     sources = rest[1:] if with_partial else rest
     tiles_ref = outs[-1] if tiles == "save" else (sources[-1] if tiles == "load" else None)
-    for (source, first, end), copy_ref in zip(copies, outs[1 + len(emit) :]):
+    for (source, first, end), copy_ref in zip(copies, outs[1 + 2 * len(emit) :]):
         copy_ref[...] = sources[source][:, first:end, :K, :]
     columns, rank = out_ref.shape[2:]
     lat_blocks = out_ref.shape[0]
@@ -130,6 +130,14 @@
                 row_ref = outs[1 + emit[p]]
                 row_ref[0, q, :columns, :] = high
                 row_ref[0, q, columns:, :] = low
+                kept = columns - STRIDE
+                sent_ref = outs[1 + len(emit) + emit[p]]
+                if p == 0:
+                    sent_ref[0, q, :kept, :] = high[:kept]
+                    sent_ref[0, q, kept:, :] = low[:kept]
+                else:
+                    sent_ref[0, q, :kept, :] = high[STRIDE:]
+                    sent_ref[0, q, kept:, :] = low[STRIDE:]
             else:
                 out_ref[p, q] = total
             return carry
@@ -172,6 +180,7 @@
     shapes = [jax.ShapeDtypeStruct(out_like.shape, jnp.float32)]
     if emit:
         shapes += [jax.ShapeDtypeStruct((1, lon_blocks, 2 * columns, rank), jnp.bfloat16)] * len(emit)
+        shapes += [jax.ShapeDtypeStruct((1, lon_blocks, 2 * (columns - STRIDE), rank), jnp.bfloat16)] * len(emit)
     for source, first, end in copies:
         held = sources[source]
         shapes.append(jax.ShapeDtypeStruct((held.shape[0], end - first, K, held.shape[3]), held.dtype))
@@ -265,7 +274,7 @@
         tiles="save",
     )
     emit = tuple(0 if p == 0 else 1 for p in range(lat_blocks))
-    first_product, first_row, last_row, members_north, members_south = rows_call(
+    first_product, first_row, last_row, sent_north, sent_south, members_north, members_south = rows_call(
         halo_plan(lat_blocks, (0, 1), (0, 1), (0, 0), trimmed=True),
         K,
         targets,
@@ -278,7 +287,7 @@
         edges=edges,
         copies=((0,) + span, (1,) + span),
     )
-    north2, south2 = lat_halo(first_row, last_row)
+    north2, south2 = lat_halo(sent_north, sent_south)
     row_fields = (1, 2) if lat_blocks == 2 else None
     partial = rows_call(
         own_plan(lat_blocks, 0, row_fields, (0, 0)),
@@ -291,7 +300,7 @@
         tiles="load",
     )
     second_product = rows_call(
-        halo_plan(lat_blocks, (0, 1), (2, 3), (0, 0)),
+        halo_plan(lat_blocks, (0, 1), (2, 3), (0, 0), trimmed=True),
         0,
         targets,
         taper,

time: 98.7 us -> 95.2 us (0.965)
  waiting for transfers between devices: 15.1 us -> 9.71 us
  starting transfers between devices: 19.9 us -> 21.3 us
    ppermute x2, waiting for transfers between devices: 5.89 us -> 2.32 us  [lat_halo(): north = lax.ppermute(last_row, 'lat', [(i, i + 1) for i in range(nlat - 1)])]
    ppermute x2, waiting for transfers between devices: 3.33 us -> 1.53 us  [lat_halo(): lax.ppermute(first_row, 'lat', [(i + 1, i) for i in range(nlat - 1)])]
  transfers between devices with their start and end apart: 6 -> 6, of which waited for: 3 -> 3; matrix products, arithmetic and copies ran while one was open for 3% -> 3% of each run, Pallas kernels for 30% -> 31%
where the time goes in v14:
time: 95.2 us; the launch traced here: 94.3 us
  Pallas kernels  54.5 us (57%)
  starting transfers between devices  21.3 us (22%)
  waiting for transfers between devices  9.71 us (10%)
  local copies, waits for them, and re-layouts  5.08 us (5%)
  other arithmetic  2.99 us (3%)
    pallas_call x4, Pallas kernels, rows_call(): pl.pallas_call(functools.partial(kernel_with_edges if edges is not None e...  54.5 us
    ppermute x2, starting transfers between devices, lat_halo(): lax.ppermute(first_row, 'lat', [(i + 1, i) for i in range(nlat - 1)])  9.64 us
    ppermute x2, starting transfers between devices, lat_halo(): north = lax.ppermute(last_row, 'lat', [(i, i + 1) for i in range(nlat - 1)])  6.24 us
    ppermute x1, waiting for transfers between devices, lon_halo(): lax.ppermute(cells[:, -depth:], 'lon', [(i, (i + 1) % nlon) for i in rang...  5.85 us
    ppermute x1, starting transfers between devices, lon_halo(): lax.ppermute(cells[:, :depth], 'lon', [((i + 1) % nlon, i) for i in range...  5.35 us
    unnamed x15, local copies, waits for them, and re-layouts  3.4 us
    ppermute x2, waiting for transfers between devices, lat_halo(): north = lax.ppermute(last_row, 'lat', [(i, i + 1) for i in range(nlat - 1)])  2.32 us
  transfers between devices with their start and end apart: 6, of which 3 were waited for; matrix products, arithmetic and copies ran while one was open for 3% of the time, Pallas kernels for 31%

profile of v14, /device:TPU:2, one launch (start us, length us, event | category | flops | bytes accessed | tf_op | source)
XLA Modules:
  0.0 94.3 jit_solution(11140885800698604836)
XLA Ops:
  0.6 0.0 copy-start.1
  0.6 1.5 %reduce-precision_convert_fusion = (bf16[2,8,128,128]{3,2,1,0:T(8,128)(2,1)S(1)}, bf16[2,8,128,128]{3,2,1,0:T(8,128)(2,1)S(1)}) fusion(f32[2,8,128,128]{3,2,1,0:T(8,128)} %param.6), kind=kLoop, calls=%fused_computation.2 | loop fusion | flops 1048576 | bytes 2097152 | tf_op jit(solution)/shard_map/convert_element_type | solution.py:215
  2.2 0.0 copy-done.1
  2.2 0.1 collective-permute-start
  2.3 5.3 %collective-permute-start.1 = (bf16[2,2,336,128]{3,2,1,0:T(8,128)(2,1)S(1)}, bf16[2,2,336,128]{3,2,1,0:T(8,128)(2,1)S(1)}, u32[]{:S(2)}, u32[]{:S(2)}) collective-permute-start(bf16[2,2,336,128]{3,2,1,0:T(8,128)(2,1)S(1)} %get-tuple-element.26), channel_id=1, source_target_pairs={{8,0},{16,8},{24,16},{32,24},{40,32},{48,40},{56,48},{64,56},{72,6... | collective-permute-start | bytes 1032200 | tf_op jit(solution)/shard_map/ppermute | solution.py:46
  7.7 5.8 %collective-permute-done = bf16[2,2,336,128]{3,2,1,0:T(8,128)(2,1)S(1)} collective-permute-done((bf16[2,2,336,128]{3,2,1,0:T(8,128)(2,1)S(1)}, bf16[2,2,336,128]{3,2,1,0:T(8,128)(2,1)S(1)}, u32[]{:S(2)}, u32[]{:S(2)}) %collective-permute-start) | collective-permute-done | bytes 344096 | tf_op jit(solution)/shard_map/ppermute | solution.py:45
  13.5 0.0 collective-permute-done.1
  13.5 0.2 pad_maximum_fusion.args_3_
  13.7 0.0 copy-start
  13.8 0.1 fusion.1
  13.9 1.2 %pad_maximum_fusion.1 = bf16[1,12,304,128]{3,2,1,0:T(8,128)(2,1)} fusion(bf16[1,12,112,128]{3,2,1,0:T(8,128)(2,1)S(1)} %get-tuple-element.23, bf16[1,12,112,128]{3,2,1,0:T(8,128)(2,1)S(1)} %get-tuple-element.24, bf16[1,12,80,128]{3,2,1,0:T(8,128)(2,1)S(1)} %slice.40), kind=kLoop, calls=%fused_computation.4 | loop fusion | flops 2801664 | bytes 1867776 | tf_op jit(solution)/shard_map/concatenate | solution.py:254
  15.0 0.3 copy-done
  15.4 3.8 %collective-permute-start.2 = (bf16[1,12,304,128]{3,2,1,0:T(8,128)(2,1)}, bf16[1,12,304,128]{3,2,1,0:T(8,128)(2,1)S(1)}, u32[]{:S(2)}, u32[]{:S(2)}) collective-permute-start(bf16[1,12,304,128]{3,2,1,0:T(8,128)(2,1)} %pad_maximum_fusion.1), channel_id=1, source_target_pairs={{0,1},{1,2},{2,3},{3,4},{4,5},{5,6},{6,7},{8,9},{9,10},{10,11},{11... | collective-permute-start | bytes 2801672 | tf_op jit(solution)/shard_map/ppermute | solution.py:52
  19.2 0.1 pad_maximum_fusion.2
  19.2 0.0 copy-done.6
  19.3 4.1 %collective-permute-start.3 = (bf16[1,12,304,128]{3,2,1,0:T(8,128)(2,1)S(1)}, bf16[1,12,304,128]{3,2,1,0:T(8,128)(2,1)S(1)}, u32[]{:S(2)}, u32[]{:S(2)}) collective-permute-start(bf16[1,12,304,128]{3,2,1,0:T(8,128)(2,1)S(1)} %pad_maximum_fusion.2), channel_id=1, source_target_pairs={{1,0},{2,1},{3,2},{4,3},{5,4},{6,5},{7,6},{9,8},{10,9},{11,10},{12... | collective-permute-start | bytes 2801672 | tf_op jit(solution)/shard_map/ppermute | solution.py:53
  23.4 1.0 %copy.5 = bf16[2,8,80,128]{2,3,1,0:T(8,128)(2,1)} copy(bf16[2,8,80,128]{3,2,1,0:T(8,128)(2,1)S(1)} %copy-done.1) | data formatting | bytes 655360 | tf_op args[0]
  24.4 0.8 slice.39
  25.2 0.8 copy.7.args_1_
  26.0 19.6 %shard_map.50 = (f32[2,10,128,128]{3,2,1,0:T(8,128)}, bf16[2,10,80,128]{3,2,1,0:T(8,128)(2,1)}, bf16[2,8,6,256,128]{4,3,2,1,0:T(8,128)(2,1)}) custom-call(bf16[2,8,128,80]{3,2,1,0:T(8,128)(2,1)} %bitcast.3, bf16[2,2,128,80]{3,2,1,0:T(8,128)(2,1)} %copy.7.args_1_, f32[9,128,128]{2,1,0:T(8,128)} %constant.2.clone.args_2_.rest_0_, bf16[2,12,336,128]{3,2,1,0:T(8,128)(2,1)} %copy-done), custom_call_target="tpu_custom_call" | custom-call | flops 1824522240 | bytes 11075584 | tf_op jit(solution)/shard_map/pallas_call | solution.py:194
  45.6 0.0 collective-permute-done.2.args_4_
  45.6 0.0 collective-permute-done.3.args_5_
  45.6 0.9 copy-done.2
  46.5 0.3 copy-done.3
  46.8 13.9 %shard_map.51 = (f32[2,8,128,128]{3,2,1,0:T(8,128)}, bf16[1,10,256,128]{3,2,1,0:T(8,128)(2,1)}, bf16[1,10,256,128]{3,2,1,0:T(8,128)(2,1)}, bf16[1,10,224,128]{3,...) custom-call(bf16[2,8,128,80]{3,2,1,0:T(8,128)(2,1)} %bitcast.4, ...), custom_call_target="tpu_custom_call" | custom-call | flops 912261120 | bytes 8093696 | tf_op jit(solution)/shard_map/pallas_call | solution.py:194
  60.8 2.4 %collective-permute-start.4 = (bf16[1,10,224,128]{3,2,1,0:T(8,128)(2,1)}, bf16[1,10,224,128]{3,2,1,0:T(8,128)(2,1)S(1)}, u32[]{:S(2)}, u32[]{:S(2)}) collective-permute-start(bf16[1,10,224,128]{3,2,1,0:T(8,128)(2,1)} %get-tuple-element.20), channel_id=1, source_target_pairs={{0,1},{1,2},{2,3},{3,4},{4,5},{5,6},{6,7},{8,9},{9,10},{10,11},{11... | collective-permute-start | bytes 1720328 | tf_op jit(solution)/shard_map/ppermute | solution.py:52
  63.2 5.5 %collective-permute-start.5 = (bf16[1,10,224,128]{3,2,1,0:T(8,128)(2,1)}, bf16[1,10,224,128]{3,2,1,0:T(8,128)(2,1)S(1)}, u32[]{:S(2)}, u32[]{:S(2)}) collective-permute-start(bf16[1,10,224,128]{3,2,1,0:T(8,128)(2,1)} %get-tuple-element.21), channel_id=1, source_target_pairs={{1,0},{2,1},{3,2},{4,3},{5,4},{6,5},{7,6},{9,8},{10,9},{11,10},{12... | collective-permute-start | bytes 1720328 | tf_op jit(solution)/shard_map/ppermute | solution.py:53
  68.7 9.7 %shard_map.52.rest_1_ = f32[2,8,128,128]{3,2,1,0:T(8,128)} custom-call(bf16[2,8,128,80]{3,2,1,0:T(8,128)(2,1)} %bitcast.5, f32[9,128,128]{2,1,0:T(8,128)} %constant.2.clone.args_2_.rest_0_, bf16[2,10,80,128]{3,2,1,0:T(8,128)(2,1)} %get-tuple-element.14.rest_1_, bf16[1,10,256,128]{3,2,1,0:T(8,128)(2,1)} %get-tuple-element.15.rest_2_, ...), custom_call_target="tpu_custom_call" | custom-call | flops 1459617792 | bytes 9977856 | tf_op jit(solution)/shard_map/pallas_call | solution.py:194
  78.4 2.3 %collective-permute-done.4.rest_4_ = bf16[1,10,224,128]{3,2,1,0:T(8,128)(2,1)S(1)} collective-permute-done((bf16[1,10,224,128]{3,2,1,0:T(8,128)(2,1)}, bf16[1,10,224,128]{3,2,1,0:T(8,128)(2,1)S(1)}, u32[]{:S(2)}, u32[]{:S(2)}) %collective-permute-start.4) | collective-permute-done | bytes 573472 | tf_op jit(solution)/shard_map/ppermute | solution.py:52
  80.7 1.5 %collective-permute-done.5.rest_5_ = bf16[1,10,224,128]{3,2,1,0:T(8,128)(2,1)S(1)} collective-permute-done((bf16[1,10,224,128]{3,2,1,0:T(8,128)(2,1)}, bf16[1,10,224,128]{3,2,1,0:T(8,128)(2,1)S(1)}, u32[]{:S(2)}, u32[]{:S(2)}) %collective-permute-start.5) | collective-permute-done | bytes 573472 | tf_op jit(solution)/shard_map/ppermute | solution.py:53
  82.2 0.8 copy-done.5
  83.0 11.3 %shard_map.53 = f32[2,8,128,128]{3,2,1,0:T(8,128)} custom-call(bf16[2,8,128,80]{3,2,1,0:T(8,128)(2,1)} %bitcast.6, f32[9,128,128]{2,1,0:T(8,128)} %constant.2.clone.args_2_.rest_0_, f32[2,8,128,128]{3,2,1,0:T(8,128)} %shard_map.52.rest_1_, bf16[1,10,80,128]{3,2,1,0:T(8,128)(2,1)} %get-tuple-element.18.rest_2_, ...), custom_call_target="tpu_custom_call" | custom-call | flops 729808896 | bytes 4571136 | tf_op jit(solution)/shard_map/pallas_call | solution.py:194
  (11 shorter events, 0.1 us)
Async XLA Ops:
  0.6 1.5 %copy-start.1 = (bf16[2,8,80,128]{3,2,1,0:T(8,128)(2,1)S(1)}, bf16[2,8,80,128]{3,2,1,0:T(8,128)(2,1)}, u32[]{:S(2)}) copy-start(bf16[2,8,80,128]{3,2,1,0:T(8,128)(2,1)} %param.5) | copy-start | bytes 983044
  2.2 11.3 %collective-permute-start = (bf16[2,2,336,128]{3,2,1,0:T(8,128)(2,1)S(1)}, bf16[2,2,336,128]{3,2,1,0:T(8,128)(2,1)S(1)}, u32[]{:S(2)}, u32[]{:S(2)}) collective-permute-start(bf16[2,2,336,128]{3,2,1,0:T(8,128)(2,1)S(1)} %get-tuple-element.25), channel_id=1, source_target_pairs={{0,8},{8,16},{16,24},{24,32},{32,40},{40,48},{48,56},{56,64},{64,7... | collective-permute-start | bytes 1032200 | tf_op jit(solution)/shard_map/ppermute | solution.py:45
  2.3 11.2 %collective-permute-start.1 = (bf16[2,2,336,128]{3,2,1,0:T(8,128)(2,1)S(1)}, bf16[2,2,336,128]{3,2,1,0:T(8,128)(2,1)S(1)}, u32[]{:S(2)}, u32[]{:S(2)}) collective-permute-start(bf16[2,2,336,128]{3,2,1,0:T(8,128)(2,1)S(1)} %get-tuple-element.26), channel_id=1, source_target_pairs={{8,0},{16,8},{24,16},{32,24},{40,32},{48,40},{56,48},{64,56},{72,6... | collective-permute-start | bytes 1032200 | tf_op jit(solution)/shard_map/ppermute | solution.py:46
  13.5 5.7 %copy-start.6 = (bf16[2,2,336,128]{3,2,1,0:T(8,128)(2,1)}, bf16[2,2,336,128]{3,2,1,0:T(8,128)(2,1)S(1)}, u32[]{:S(2)}) copy-start(bf16[2,2,336,128]{3,2,1,0:T(8,128)(2,1)S(1)} %collective-permute-done.1) | copy-start | bytes 1032196
  13.7 1.6 %copy-start = (bf16[2,12,336,128]{3,2,1,0:T(8,128)(2,1)}, bf16[2,12,336,128]{3,2,1,0:T(8,128)(2,1)S(1)}, u32[]{:S(2)}) copy-start(bf16[2,12,336,128]{3,2,1,0:T(8,128)(2,1)S(1)} %pad_maximum_fusion.args_3_) | copy-start | bytes 6193156
  15.4 30.2 %collective-permute-start.2 = (bf16[1,12,304,128]{3,2,1,0:T(8,128)(2,1)}, bf16[1,12,304,128]{3,2,1,0:T(8,128)(2,1)S(1)}, u32[]{:S(2)}, u32[]{:S(2)}) collective-permute-start(bf16[1,12,304,128]{3,2,1,0:T(8,128)(2,1)} %pad_maximum_fusion.1), channel_id=1, source_target_pairs={{0,1},{1,2},{2,3},{3,4},{4,5},{5,6},{6,7},{8,9},{9,10},{10,11},{11... | collective-permute-start | bytes 2801672 | tf_op jit(solution)/shard_map/ppermute | solution.py:52
  19.3 26.3 %collective-permute-start.3 = (bf16[1,12,304,128]{3,2,1,0:T(8,128)(2,1)S(1)}, bf16[1,12,304,128]{3,2,1,0:T(8,128)(2,1)S(1)}, u32[]{:S(2)}, u32[]{:S(2)}) collective-permute-start(bf16[1,12,304,128]{3,2,1,0:T(8,128)(2,1)S(1)} %pad_maximum_fusion.2), channel_id=1, source_target_pairs={{1,0},{2,1},{3,2},{4,3},{5,4},{6,5},{7,6},{9,8},{10,9},{11,10},{12... | collective-permute-start | bytes 2801672 | tf_op jit(solution)/shard_map/ppermute | solution.py:53
  45.6 0.9 copy-start.2
  45.6 1.3 %copy-start.3 = (bf16[1,12,304,128]{3,2,1,0:T(8,128)(2,1)}, bf16[1,12,304,128]{3,2,1,0:T(8,128)(2,1)S(1)}, u32[]{:S(2)}) copy-start(bf16[1,12,304,128]{3,2,1,0:T(8,128)(2,1)S(1)} %collective-permute-done.3.args_5_) | copy-start | bytes 2801668
  60.8 19.9 %collective-permute-start.4 = (bf16[1,10,224,128]{3,2,1,0:T(8,128)(2,1)}, bf16[1,10,224,128]{3,2,1,0:T(8,128)(2,1)S(1)}, u32[]{:S(2)}, u32[]{:S(2)}) collective-permute-start(bf16[1,10,224,128]{3,2,1,0:T(8,128)(2,1)} %get-tuple-element.20), channel_id=1, source_target_pairs={{0,1},{1,2},{2,3},{3,4},{4,5},{5,6},{6,7},{8,9},{9,10},{10,11},{11... | collective-permute-start | bytes 1720328 | tf_op jit(solution)/shard_map/ppermute | solution.py:52
  63.2 19.0 %collective-permute-start.5 = (bf16[1,10,224,128]{3,2,1,0:T(8,128)(2,1)}, bf16[1,10,224,128]{3,2,1,0:T(8,128)(2,1)S(1)}, u32[]{:S(2)}, u32[]{:S(2)}) collective-permute-start(bf16[1,10,224,128]{3,2,1,0:T(8,128)(2,1)} %get-tuple-element.21), channel_id=1, source_target_pairs={{1,0},{2,1},{3,2},{4,3},{5,4},{6,5},{7,6},{9,8},{10,9},{11,10},{12... | collective-permute-start | bytes 1720328 | tf_op jit(solution)/shard_map/ppermute | solution.py:53
  80.7 1.5 %copy-start.4 = (bf16[1,10,224,128]{3,2,1,0:T(8,128)(2,1)}, bf16[1,10,224,128]{3,2,1,0:T(8,128)(2,1)S(1)}, u32[]{:S(2)}) copy-start(bf16[1,10,224,128]{3,2,1,0:T(8,128)(2,1)S(1)} %collective-permute-done.4.rest_4_) | copy-start | bytes 1720324
  82.2 0.8 copy-start.5

commit v15 on v14

--- a/solution.py
+++ b/solution.py
@@ -274,7 +274,7 @@
         tiles="save",
     )
     emit = tuple(0 if p == 0 else 1 for p in range(lat_blocks))
-    first_product, first_row, last_row, sent_north, sent_south, members_north, members_south = rows_call(
+    first_product, first_row, last_row, sent_north, sent_south, members_north, members_south, halo_tiles = rows_call(
         halo_plan(lat_blocks, (0, 1), (0, 1), (0, 0), trimmed=True),
         K,
         targets,
@@ -286,6 +286,7 @@
         emit=emit,
         edges=edges,
         copies=((0,) + span, (1,) + span),
+        tiles="save",
     )
     north2, south2 = lat_halo(sent_north, sent_south)
     row_fields = (1, 2) if lat_blocks == 2 else None
@@ -305,8 +306,9 @@
         targets,
         taper,
         partial,
-        (members_north, members_south, north2, south2),
+        (members_north, members_south, north2, south2, halo_tiles),
         panel,
+        tiles="load",
     )
     return (first_product, second_product)
 

time: 95.2 us -> 92.5 us (0.972)
  Pallas kernels: 54.5 us -> 51.8 us
    pallas_call x4, Pallas kernels: 54.5 us -> 51.8 us  [rows_call(): pl.pallas_call(functools.partial(kernel_with_edges if edges is not None e...]
  transfers between devices with their start and end apart: 6 -> 6, of which waited for: 3 -> 3; matrix products, arithmetic and copies ran while one was open for 3% -> 3% of each run, Pallas kernels for 31% -> 32%
where the time goes in v15:
time: 92.5 us; the launch traced here: 91.6 us
  Pallas kernels  51.8 us (56%)
  starting transfers between devices  21.3 us (23%)
  waiting for transfers between devices  9.73 us (11%)
  local copies, waits for them, and re-layouts  5.06 us (5%)
  other arithmetic  2.97 us (3%)
    pallas_call x4, Pallas kernels, rows_call(): pl.pallas_call(functools.partial(kernel_with_edges if edges is not None e...  51.8 us
    ppermute x2, starting transfers between devices, lat_halo(): lax.ppermute(first_row, 'lat', [(i + 1, i) for i in range(nlat - 1)])  9.53 us
    ppermute x2, starting transfers between devices, lat_halo(): north = lax.ppermute(last_row, 'lat', [(i, i + 1) for i in range(nlat - 1)])  6.35 us
    ppermute x1, waiting for transfers between devices, lon_halo(): lax.ppermute(cells[:, -depth:], 'lon', [(i, (i + 1) % nlon) for i in rang...  5.85 us
    ppermute x1, starting transfers between devices, lon_halo(): lax.ppermute(cells[:, :depth], 'lon', [((i + 1) % nlon, i) for i in range...  5.35 us
    unnamed x15, local copies, waits for them, and re-layouts  3.38 us
    ppermute x2, waiting for transfers between devices, lat_halo(): north = lax.ppermute(last_row, 'lat', [(i, i + 1) for i in range(nlat - 1)])  2.35 us
  transfers between devices with their start and end apart: 6, of which 3 were waited for; matrix products, arithmetic and copies ran while one was open for 3% of the time, Pallas kernels for 32%

profile of v15, /device:TPU:2, one launch (start us, length us, event | category | flops | bytes accessed | tf_op | source)
XLA Modules:
  0.0 91.6 jit_solution(6967410314336641027)
XLA Ops:
  0.6 0.0 copy-start.1
  0.6 1.5 %reduce-precision_convert_fusion = (bf16[2,8,128,128]{3,2,1,0:T(8,128)(2,1)S(1)}, bf16[2,8,128,128]{3,2,1,0:T(8,128)(2,1)S(1)}) fusion(f32[2,8,128,128]{3,2,1,0:T(8,128)} %param.6), kind=kLoop, calls=%fused_computation.2 | loop fusion | flops 1048576 | bytes 2097152 | tf_op jit(solution)/shard_map/convert_element_type | solution.py:215
  2.2 0.0 copy-done.1
  2.2 0.1 collective-permute-start
  2.3 5.3 %collective-permute-start.1 = (bf16[2,2,336,128]{3,2,1,0:T(8,128)(2,1)S(1)}, bf16[2,2,336,128]{3,2,1,0:T(8,128)(2,1)S(1)}, u32[]{:S(2)}, u32[]{:S(2)}) collective-permute-start(bf16[2,2,336,128]{3,2,1,0:T(8,128)(2,1)S(1)} %get-tuple-element.28), channel_id=1, source_target_pairs={{8,0},{16,8},{24,16},{32,24},{40,32},{48,40},{56,48},{64,56},{72,6... | collective-permute-start | bytes 1032200 | tf_op jit(solution)/shard_map/ppermute | solution.py:46
  7.7 5.8 %collective-permute-done = bf16[2,2,336,128]{3,2,1,0:T(8,128)(2,1)S(1)} collective-permute-done((bf16[2,2,336,128]{3,2,1,0:T(8,128)(2,1)S(1)}, bf16[2,2,336,128]{3,2,1,0:T(8,128)(2,1)S(1)}, u32[]{:S(2)}, u32[]{:S(2)}) %collective-permute-start) | collective-permute-done | bytes 344096 | tf_op jit(solution)/shard_map/ppermute | solution.py:45
  13.5 0.0 collective-permute-done.1
  13.5 0.2 pad_maximum_fusion.args_3_
  13.8 0.1 fusion.1
  13.9 1.1 %pad_maximum_fusion.1 = bf16[1,12,304,128]{3,2,1,0:T(8,128)(2,1)} fusion(bf16[1,12,112,128]{3,2,1,0:T(8,128)(2,1)S(1)} %get-tuple-element.25, bf16[1,12,112,128]{3,2,1,0:T(8,128)(2,1)S(1)} %get-tuple-element.26, bf16[1,12,80,128]{3,2,1,0:T(8,128)(2,1)S(1)} %slice.40), kind=kLoop, calls=%fused_computation.4 | loop fusion | flops 2801664 | bytes 1867776 | tf_op jit(solution)/shard_map/concatenate | solution.py:254
  15.0 0.3 copy-done
  15.4 3.8 %collective-permute-start.2 = (bf16[1,12,304,128]{3,2,1,0:T(8,128)(2,1)}, bf16[1,12,304,128]{3,2,1,0:T(8,128)(2,1)S(1)}, u32[]{:S(2)}, u32[]{:S(2)}) collective-permute-start(bf16[1,12,304,128]{3,2,1,0:T(8,128)(2,1)} %pad_maximum_fusion.1), channel_id=1, source_target_pairs={{0,1},{1,2},{2,3},{3,4},{4,5},{5,6},{6,7},{8,9},{9,10},{10,11},{11... | collective-permute-start | bytes 2801672 | tf_op jit(solution)/shard_map/ppermute | solution.py:52
  19.2 0.1 pad_maximum_fusion.2
  19.2 0.0 copy-done.6
  19.3 4.1 %collective-permute-start.3 = (bf16[1,12,304,128]{3,2,1,0:T(8,128)(2,1)S(1)}, bf16[1,12,304,128]{3,2,1,0:T(8,128)(2,1)S(1)}, u32[]{:S(2)}, u32[]{:S(2)}) collective-permute-start(bf16[1,12,304,128]{3,2,1,0:T(8,128)(2,1)S(1)} %pad_maximum_fusion.2), channel_id=1, source_target_pairs={{1,0},{2,1},{3,2},{4,3},{5,4},{6,5},{7,6},{9,8},{10,9},{11,10},{12... | collective-permute-start | bytes 2801672 | tf_op jit(solution)/shard_map/ppermute | solution.py:53
  23.4 1.0 %copy.5 = bf16[2,8,80,128]{2,3,1,0:T(8,128)(2,1)} copy(bf16[2,8,80,128]{3,2,1,0:T(8,128)(2,1)S(1)} %copy-done.1) | data formatting | bytes 655360 | tf_op args[0]
  24.4 0.8 slice.39
  25.2 0.8 copy.7.args_1_
  26.0 19.5 %shard_map.50 = (f32[2,10,128,128]{3,2,1,0:T(8,128)}, bf16[2,10,80,128]{3,2,1,0:T(8,128)(2,1)}, bf16[2,8,6,256,128]{4,3,2,1,0:T(8,128)(2,1)}) custom-call(bf16[2,8,128,80]{3,2,1,0:T(8,128)(2,1)} %bitcast.3, bf16[2,2,128,80]{3,2,1,0:T(8,128)(2,1)} %copy.7.args_1_, f32[9,128,128]{2,1,0:T(8,128)} %constant.2.clone.args_2_.rest_0_, bf16[2,12,336,128]{3,2,1,0:T(8,128)(2,1)} %copy-done), custom_call_target="tpu_custom_call" | custom-call | flops 1824522240 | bytes 11075584 | tf_op jit(solution)/shard_map/pallas_call | solution.py:194
  45.4 0.0 collective-permute-done.2.args_4_
  45.5 0.0 collective-permute-done.3.args_5_
  45.5 0.9 copy-done.2
  46.4 0.3 copy-done.3
  46.7 15.0 %shard_map.51 = (f32[2,8,128,128]{3,2,1,0:T(8,128)}, bf16[1,10,256,128]{3,2,1,0:T(8,128)(2,1)}, bf16[1,10,256,128]{3,2,1,0:T(8,128)(2,1)}, bf16[1,10,224,128]{3,...) custom-call(bf16[2,8,128,80]{3,2,1,0:T(8,128)(2,1)} %bitcast.4, ...), custom_call_target="tpu_custom_call" | custom-call | flops 912261120 | bytes 11239424 | tf_op jit(solution)/shard_map/pallas_call | solution.py:194
  61.7 2.5 %collective-permute-start.4 = (bf16[1,10,224,128]{3,2,1,0:T(8,128)(2,1)}, bf16[1,10,224,128]{3,2,1,0:T(8,128)(2,1)S(1)}, u32[]{:S(2)}, u32[]{:S(2)}) collective-permute-start(bf16[1,10,224,128]{3,2,1,0:T(8,128)(2,1)} %get-tuple-element.21), channel_id=1, source_target_pairs={{0,1},{1,2},{2,3},{3,4},{4,5},{5,6},{6,7},{8,9},{9,10},{10,11},{11... | collective-permute-start | bytes 1720328 | tf_op jit(solution)/shard_map/ppermute | solution.py:52
  64.2 5.4 %collective-permute-start.5 = (bf16[1,10,224,128]{3,2,1,0:T(8,128)(2,1)}, bf16[1,10,224,128]{3,2,1,0:T(8,128)(2,1)S(1)}, u32[]{:S(2)}, u32[]{:S(2)}) collective-permute-start(bf16[1,10,224,128]{3,2,1,0:T(8,128)(2,1)} %get-tuple-element.22), channel_id=1, source_target_pairs={{1,0},{2,1},{3,2},{4,3},{5,4},{6,5},{7,6},{9,8},{10,9},{11,10},{12... | collective-permute-start | bytes 1720328 | tf_op jit(solution)/shard_map/ppermute | solution.py:53
  69.6 9.6 %shard_map.52.rest_1_ = f32[2,8,128,128]{3,2,1,0:T(8,128)} custom-call(bf16[2,8,128,80]{3,2,1,0:T(8,128)(2,1)} %bitcast.5, f32[9,128,128]{2,1,0:T(8,128)} %constant.2.clone.args_2_.rest_0_, bf16[2,10,80,128]{3,2,1,0:T(8,128)(2,1)} %get-tuple-element.15.rest_1_, bf16[1,10,256,128]{3,2,1,0:T(8,128)(2,1)} %get-tuple-element.16.rest_2_, ...), custom_call_target="tpu_custom_call" | custom-call | flops 1459617792 | bytes 9977856 | tf_op jit(solution)/shard_map/pallas_call | solution.py:194
  79.2 2.3 %collective-permute-done.4.rest_4_ = bf16[1,10,224,128]{3,2,1,0:T(8,128)(2,1)S(1)} collective-permute-done((bf16[1,10,224,128]{3,2,1,0:T(8,128)(2,1)}, bf16[1,10,224,128]{3,2,1,0:T(8,128)(2,1)S(1)}, u32[]{:S(2)}, u32[]{:S(2)}) %collective-permute-start.4) | collective-permute-done | bytes 573472 | tf_op jit(solution)/shard_map/ppermute | solution.py:52
  81.6 1.5 %collective-permute-done.5.rest_5_ = bf16[1,10,224,128]{3,2,1,0:T(8,128)(2,1)S(1)} collective-permute-done((bf16[1,10,224,128]{3,2,1,0:T(8,128)(2,1)}, bf16[1,10,224,128]{3,2,1,0:T(8,128)(2,1)S(1)}, u32[]{:S(2)}, u32[]{:S(2)}) %collective-permute-start.5) | collective-permute-done | bytes 573472 | tf_op jit(solution)/shard_map/ppermute | solution.py:53
  83.1 0.0 copy-done.4
  83.1 0.8 copy-done.5
  83.9 7.7 %shard_map.53 = f32[2,8,128,128]{3,2,1,0:T(8,128)} custom-call(bf16[2,8,128,80]{3,2,1,0:T(8,128)(2,1)} %bitcast.6, f32[9,128,128]{2,1,0:T(8,128)} %constant.2.clone.args_2_.rest_0_, f32[2,8,128,128]{3,2,1,0:T(8,128)} %shard_map.52.rest_1_, bf16[1,10,80,128]{3,2,1,0:T(8,128)(2,1)} %get-tuple-element.19.rest_2_, ...), custom_call_target="tpu_custom_call" | custom-call | flops 729808896 | bytes 7716864 | tf_op jit(solution)/shard_map/pallas_call | solution.py:194
  (11 shorter events, 0.1 us)
Async XLA Ops:
  0.6 1.5 %copy-start.1 = (bf16[2,8,80,128]{3,2,1,0:T(8,128)(2,1)S(1)}, bf16[2,8,80,128]{3,2,1,0:T(8,128)(2,1)}, u32[]{:S(2)}) copy-start(bf16[2,8,80,128]{3,2,1,0:T(8,128)(2,1)} %param.5) | copy-start | bytes 983044
  2.2 11.3 %collective-permute-start = (bf16[2,2,336,128]{3,2,1,0:T(8,128)(2,1)S(1)}, bf16[2,2,336,128]{3,2,1,0:T(8,128)(2,1)S(1)}, u32[]{:S(2)}, u32[]{:S(2)}) collective-permute-start(bf16[2,2,336,128]{3,2,1,0:T(8,128)(2,1)S(1)} %get-tuple-element.27), channel_id=1, source_target_pairs={{0,8},{8,16},{16,24},{24,32},{32,40},{40,48},{48,56},{56,64},{64,7... | collective-permute-start | bytes 1032200 | tf_op jit(solution)/shard_map/ppermute | solution.py:45
  2.3 11.2 %collective-permute-start.1 = (bf16[2,2,336,128]{3,2,1,0:T(8,128)(2,1)S(1)}, bf16[2,2,336,128]{3,2,1,0:T(8,128)(2,1)S(1)}, u32[]{:S(2)}, u32[]{:S(2)}) collective-permute-start(bf16[2,2,336,128]{3,2,1,0:T(8,128)(2,1)S(1)} %get-tuple-element.28), channel_id=1, source_target_pairs={{8,0},{16,8},{24,16},{32,24},{40,32},{48,40},{56,48},{64,56},{72,6... | collective-permute-start | bytes 1032200 | tf_op jit(solution)/shard_map/ppermute | solution.py:46
  13.5 5.7 %copy-start.6 = (bf16[2,2,336,128]{3,2,1,0:T(8,128)(2,1)}, bf16[2,2,336,128]{3,2,1,0:T(8,128)(2,1)S(1)}, u32[]{:S(2)}) copy-start(bf16[2,2,336,128]{3,2,1,0:T(8,128)(2,1)S(1)} %collective-permute-done.1) | copy-start | bytes 1032196
  13.7 1.6 %copy-start = (bf16[2,12,336,128]{3,2,1,0:T(8,128)(2,1)}, bf16[2,12,336,128]{3,2,1,0:T(8,128)(2,1)S(1)}, u32[]{:S(2)}) copy-start(bf16[2,12,336,128]{3,2,1,0:T(8,128)(2,1)S(1)} %pad_maximum_fusion.args_3_) | copy-start | bytes 6193156
  15.4 30.1 %collective-permute-start.2 = (bf16[1,12,304,128]{3,2,1,0:T(8,128)(2,1)}, bf16[1,12,304,128]{3,2,1,0:T(8,128)(2,1)S(1)}, u32[]{:S(2)}, u32[]{:S(2)}) collective-permute-start(bf16[1,12,304,128]{3,2,1,0:T(8,128)(2,1)} %pad_maximum_fusion.1), channel_id=1, source_target_pairs={{0,1},{1,2},{2,3},{3,4},{4,5},{5,6},{6,7},{8,9},{9,10},{10,11},{11... | collective-permute-start | bytes 2801672 | tf_op jit(solution)/shard_map/ppermute | solution.py:52
  19.3 26.2 %collective-permute-start.3 = (bf16[1,12,304,128]{3,2,1,0:T(8,128)(2,1)S(1)}, bf16[1,12,304,128]{3,2,1,0:T(8,128)(2,1)S(1)}, u32[]{:S(2)}, u32[]{:S(2)}) collective-permute-start(bf16[1,12,304,128]{3,2,1,0:T(8,128)(2,1)S(1)} %pad_maximum_fusion.2), channel_id=1, source_target_pairs={{1,0},{2,1},{3,2},{4,3},{5,4},{6,5},{7,6},{9,8},{10,9},{11,10},{12... | collective-permute-start | bytes 2801672 | tf_op jit(solution)/shard_map/ppermute | solution.py:53
  45.5 0.9 %copy-start.2 = (bf16[1,12,304,128]{3,2,1,0:T(8,128)(2,1)}, bf16[1,12,304,128]{3,2,1,0:T(8,128)(2,1)S(1)}, u32[]{:S(2)}) copy-start(bf16[1,12,304,128]{3,2,1,0:T(8,128)(2,1)S(1)} %collective-permute-done.2.args_4_) | copy-start | bytes 2801668
  45.5 1.2 %copy-start.3 = (bf16[1,12,304,128]{3,2,1,0:T(8,128)(2,1)}, bf16[1,12,304,128]{3,2,1,0:T(8,128)(2,1)S(1)}, u32[]{:S(2)}) copy-start(bf16[1,12,304,128]{3,2,1,0:T(8,128)(2,1)S(1)} %collective-permute-done.3.args_5_) | copy-start | bytes 2801668
  61.7 19.9 %collective-permute-start.4 = (bf16[1,10,224,128]{3,2,1,0:T(8,128)(2,1)}, bf16[1,10,224,128]{3,2,1,0:T(8,128)(2,1)S(1)}, u32[]{:S(2)}, u32[]{:S(2)}) collective-permute-start(bf16[1,10,224,128]{3,2,1,0:T(8,128)(2,1)} %get-tuple-element.21), channel_id=1, source_target_pairs={{0,1},{1,2},{2,3},{3,4},{4,5},{5,6},{6,7},{8,9},{9,10},{10,11},{11... | collective-permute-start | bytes 1720328 | tf_op jit(solution)/shard_map/ppermute | solution.py:52
  64.2 18.9 %collective-permute-start.5 = (bf16[1,10,224,128]{3,2,1,0:T(8,128)(2,1)}, bf16[1,10,224,128]{3,2,1,0:T(8,128)(2,1)S(1)}, u32[]{:S(2)}, u32[]{:S(2)}) collective-permute-start(bf16[1,10,224,128]{3,2,1,0:T(8,128)(2,1)} %get-tuple-element.22), channel_id=1, source_target_pairs={{1,0},{2,1},{3,2},{4,3},{5,4},{6,5},{7,6},{9,8},{10,9},{11,10},{12... | collective-permute-start | bytes 1720328 | tf_op jit(solution)/shard_map/ppermute | solution.py:53
  81.6 1.5 %copy-start.4 = (bf16[1,10,224,128]{3,2,1,0:T(8,128)(2,1)}, bf16[1,10,224,128]{3,2,1,0:T(8,128)(2,1)S(1)}, u32[]{:S(2)}) copy-start(bf16[1,10,224,128]{3,2,1,0:T(8,128)(2,1)S(1)} %collective-permute-done.4.rest_4_) | copy-start | bytes 1720324
  83.1 0.8 copy-start.5

commit v16 on v15

--- a/solution.py
+++ b/solution.py
@@ -55,15 +55,16 @@
 
 
 def rows_kernel(
-    plan, field_at, with_partial, target_off, emit, copies, tiles, targets_ref, edges_ref, taper_ref, *rest
+    plan, field_at, with_partial, target_off, emit, copies, tiles, extra, targets_ref, edges_ref, taper_ref, *rest
 ):
-    count = 1 + 2 * len(emit) + len(copies) + (tiles == "save")
+    count = 1 + 2 * len(emit) + len(copies) + (tiles == "save") + bool(extra)
     outs = rest[-count:]
     rest = rest[: len(rest) - count]
     out_ref = outs[0]
     partial_ref = rest[0] if with_partial else None
     sources = rest[1:] if with_partial else rest
     tiles_ref = outs[-1] if tiles == "save" else (sources[-1] if tiles == "load" else None)
+    extra_ref = outs[-1] if extra else None
     for (source, first, end), copy_ref in zip(copies, outs[1 + 2 * len(emit) :]):
         copy_ref[...] = sources[source][:, first:end, :K, :]
     columns, rank = out_ref.shape[2:]
@@ -117,6 +118,18 @@
                     total = total + jnp.dot(tile_high, field_high, preferred_element_type=jnp.float32)
                     total = total + jnp.dot(tile_high, field_low, preferred_element_type=jnp.float32)
                     total = total + jnp.dot(tile_low, field_high, preferred_element_type=jnp.float32)
+            for index, (dr, members_at, members_row, _, _, members_off, _, _) in enumerate(extra[p] if extra else ()):
+                for dc in range(3):
+                    gram = jnp.dot(
+                        target,
+                        sources[members_at][members_row, q + dc + members_off, :K, :],
+                        preferred_element_type=jnp.float32,
+                    )
+                    tile = gram * taper_ref[dr * 3 + dc]
+                    tile_high = tile.astype(jnp.bfloat16)
+                    tile_low = (tile - tile_high.astype(jnp.float32)).astype(jnp.bfloat16)
+                    extra_ref[p, q, 3 * index + dc, :columns, :] = tile_high
+                    extra_ref[p, q, 3 * index + dc, columns:, :] = tile_low
             if emit:
                 inner = out_ref.shape[1]
                 shift = (lon_blocks - inner) // 2
@@ -154,8 +167,8 @@
     return rows_kernel(*args)
 
 
-def kernel_without_edges(plan, field_at, with_partial, target_off, emit, copies, tiles, targets_ref, *rest):
-    return rows_kernel(plan, field_at, with_partial, target_off, emit, copies, tiles, targets_ref, None, *rest)
+def kernel_without_edges(plan, field_at, with_partial, target_off, emit, copies, tiles, extra, targets_ref, *rest):
+    return rows_kernel(plan, field_at, with_partial, target_off, emit, copies, tiles, extra, targets_ref, None, *rest)
 
 
 def rows_call(
@@ -171,6 +184,7 @@
     edges=None,
     copies=(),
     tiles=None,
+    extra=(),
 ):
     lat_blocks, lon_blocks, columns, rank = (partial if emit else out_like).shape
     codes = sum(3 * len(uses) for uses in plan)
@@ -188,6 +202,9 @@
         slots = max(3 * len(uses) for uses in plan)
         inner = lon_blocks - 2
         shapes.append(jax.ShapeDtypeStruct((lat_blocks, inner, slots, 2 * columns, rank), jnp.bfloat16))
+    if extra:
+        slots = max(3 * len(uses) for uses in extra)
+        shapes.append(jax.ShapeDtypeStruct((lat_blocks, lon_blocks, slots, 2 * columns, rank), jnp.bfloat16))
     several = len(shapes) > 1
     moved = sum(x.size * x.dtype.itemsize for x in operands + shapes)
     vmem = pl.BlockSpec(memory_space=pltpu.VMEM)
@@ -201,6 +218,7 @@
             emit,
             copies,
             tiles,
+            extra,
         ),
         out_shape=tuple(shapes) if several else shapes[0],
         in_specs=[vmem] * len(operands),
@@ -274,7 +292,7 @@
         tiles="save",
     )
     emit = tuple(0 if p == 0 else 1 for p in range(lat_blocks))
-    first_product, first_row, last_row, sent_north, sent_south, members_north, members_south, halo_tiles = rows_call(
+    first_product, first_row, last_row, sent_north, sent_south, members_north, members_south = rows_call(
         halo_plan(lat_blocks, (0, 1), (0, 1), (0, 0), trimmed=True),
         K,
         targets,
@@ -286,19 +304,19 @@
         emit=emit,
         edges=edges,
         copies=((0,) + span, (1,) + span),
-        tiles="save",
     )
     north2, south2 = lat_halo(sent_north, sent_south)
     row_fields = (1, 2) if lat_blocks == 2 else None
-    partial = rows_call(
+    partial, halo_tiles = rows_call(
         own_plan(lat_blocks, 0, row_fields, (0, 0)),
         0,
         targets,
         taper,
         None,
-        (members, first_row, last_row, own_tiles),
+        (members, first_row, last_row, members_north, members_south, own_tiles),
         panel,
         tiles="load",
+        extra=halo_plan(lat_blocks, (3, 4), (3, 4), (0, 0)),
     )
     second_product = rows_call(
         halo_plan(lat_blocks, (0, 1), (2, 3), (0, 0), trimmed=True),

time: 92.5 us -> 91.7 us (level)
  waiting for transfers between devices: 9.73 us -> 8.04 us
    ppermute x2, waiting for transfers between devices: 2.35 us -> 0.66 us  [lat_halo(): north = lax.ppermute(last_row, 'lat', [(i, i + 1) for i in range(nlat - 1)])]
  transfers between devices with their start and end apart: 6 -> 6, of which waited for: 3 -> 3; matrix products, arithmetic and copies ran while one was open for 3% -> 3% of each run, Pallas kernels for 32% -> 34%
where the time goes in v16:
time: 91.7 us; the launch traced here: 90.8 us
  Pallas kernels  52.6 us (57%)
  starting transfers between devices  21.3 us (23%)
  waiting for transfers between devices  8.04 us (9%)
  local copies, waits for them, and re-layouts  5.09 us (6%)
  other arithmetic  3.01 us (3%)
    pallas_call x4, Pallas kernels, rows_call(): pl.pallas_call(functools.partial(kernel_with_edges if edges is not None e...  52.6 us
    ppermute x2, starting transfers between devices, lat_halo(): lax.ppermute(first_row, 'lat', [(i + 1, i) for i in range(nlat - 1)])  9.64 us
    ppermute x2, starting transfers between devices, lat_halo(): north = lax.ppermute(last_row, 'lat', [(i, i + 1) for i in range(nlat - 1)])  6.23 us
    ppermute x1, waiting for transfers between devices, lon_halo(): lax.ppermute(cells[:, -depth:], 'lon', [(i, (i + 1) % nlon) for i in rang...  5.85 us
    ppermute x1, starting transfers between devices, lon_halo(): lax.ppermute(cells[:, :depth], 'lon', [((i + 1) % nlon, i) for i in range...  5.35 us
    unnamed x15, local copies, waits for them, and re-layouts  3.4 us
  transfers between devices with their start and end apart: 6, of which 3 were waited for; matrix products, arithmetic and copies ran while one was open for 3% of the time, Pallas kernels for 34%

profile of v16, /device:TPU:2, one launch (start us, length us, event | category | flops | bytes accessed | tf_op | source)
XLA Modules:
  0.0 90.8 jit_solution(4669164113534044443)
XLA Ops:
  0.6 0.0 copy-start.1
  0.6 1.5 %reduce-precision_convert_fusion = (bf16[2,8,128,128]{3,2,1,0:T(8,128)(2,1)S(1)}, bf16[2,8,128,128]{3,2,1,0:T(8,128)(2,1)S(1)}) fusion(f32[2,8,128,128]{3,2,1,0:T(8,128)} %param.6), kind=kLoop, calls=%fused_computation.2 | loop fusion | flops 1048576 | bytes 2097152 | tf_op jit(solution)/shard_map/convert_element_type | solution.py:233
  2.2 0.0 copy-done.1
  2.2 0.1 collective-permute-start
  2.3 5.3 %collective-permute-start.1 = (bf16[2,2,336,128]{3,2,1,0:T(8,128)(2,1)S(1)}, bf16[2,2,336,128]{3,2,1,0:T(8,128)(2,1)S(1)}, u32[]{:S(2)}, u32[]{:S(2)}) collective-permute-start(bf16[2,2,336,128]{3,2,1,0:T(8,128)(2,1)S(1)} %get-tuple-element.30), channel_id=1, source_target_pairs={{8,0},{16,8},{24,16},{32,24},{40,32},{48,40},{56,48},{64,56},{72,6... | collective-permute-start | bytes 1032200 | tf_op jit(solution)/shard_map/ppermute | solution.py:46
  7.7 5.8 %collective-permute-done = bf16[2,2,336,128]{3,2,1,0:T(8,128)(2,1)S(1)} collective-permute-done((bf16[2,2,336,128]{3,2,1,0:T(8,128)(2,1)S(1)}, bf16[2,2,336,128]{3,2,1,0:T(8,128)(2,1)S(1)}, u32[]{:S(2)}, u32[]{:S(2)}) %collective-permute-start) | collective-permute-done | bytes 344096 | tf_op jit(solution)/shard_map/ppermute | solution.py:45
  13.5 0.0 collective-permute-done.1
  13.5 0.2 pad_maximum_fusion.args_3_
  13.7 0.0 copy-start
  13.8 0.1 fusion.1
  13.9 1.2 %pad_maximum_fusion.1 = bf16[1,12,304,128]{3,2,1,0:T(8,128)(2,1)} fusion(bf16[1,12,112,128]{3,2,1,0:T(8,128)(2,1)S(1)} %get-tuple-element.27, bf16[1,12,112,128]{3,2,1,0:T(8,128)(2,1)S(1)} %get-tuple-element.28, bf16[1,12,80,128]{3,2,1,0:T(8,128)(2,1)S(1)} %slice.40), kind=kLoop, calls=%fused_computation.4 | loop fusion | flops 2801664 | bytes 1867776 | tf_op jit(solution)/shard_map/concatenate | solution.py:272
  15.1 0.3 copy-done
  15.4 3.8 %collective-permute-start.2 = (bf16[1,12,304,128]{3,2,1,0:T(8,128)(2,1)}, bf16[1,12,304,128]{3,2,1,0:T(8,128)(2,1)S(1)}, u32[]{:S(2)}, u32[]{:S(2)}) collective-permute-start(bf16[1,12,304,128]{3,2,1,0:T(8,128)(2,1)} %pad_maximum_fusion.1), channel_id=1, source_target_pairs={{0,1},{1,2},{2,3},{3,4},{4,5},{5,6},{6,7},{8,9},{9,10},{10,11},{11... | collective-permute-start | bytes 2801672 | tf_op jit(solution)/shard_map/ppermute | solution.py:52
  19.2 0.1 pad_maximum_fusion.2
  19.3 0.0 copy-done.6
  19.3 4.1 %collective-permute-start.3 = (bf16[1,12,304,128]{3,2,1,0:T(8,128)(2,1)S(1)}, bf16[1,12,304,128]{3,2,1,0:T(8,128)(2,1)S(1)}, u32[]{:S(2)}, u32[]{:S(2)}) collective-permute-start(bf16[1,12,304,128]{3,2,1,0:T(8,128)(2,1)S(1)} %pad_maximum_fusion.2), channel_id=1, source_target_pairs={{1,0},{2,1},{3,2},{4,3},{5,4},{6,5},{7,6},{9,8},{10,9},{11,10},{12... | collective-permute-start | bytes 2801672 | tf_op jit(solution)/shard_map/ppermute | solution.py:53
  23.4 1.0 %copy.5 = bf16[2,8,80,128]{2,3,1,0:T(8,128)(2,1)} copy(bf16[2,8,80,128]{3,2,1,0:T(8,128)(2,1)S(1)} %copy-done.1) | data formatting | bytes 655360 | tf_op args[0]
  24.4 0.8 slice.39
  25.2 0.8 copy.7.args_1_
  26.0 19.6 %shard_map.50 = (f32[2,10,128,128]{3,2,1,0:T(8,128)}, bf16[2,10,80,128]{3,2,1,0:T(8,128)(2,1)}, bf16[2,8,6,256,128]{4,3,2,1,0:T(8,128)(2,1)}) custom-call(bf16[2,8,128,80]{3,2,1,0:T(8,128)(2,1)} %bitcast.3, bf16[2,2,128,80]{3,2,1,0:T(8,128)(2,1)} %copy.7.args_1_, f32[9,128,128]{2,1,0:T(8,128)} %constant.2.clone.args_2_.rest_0_, bf16[2,12,336,128]{3,2,1,0:T(8,128)(2,1)} %copy-done), custom_call_target="tpu_custom_call" | custom-call | flops 1824522240 | bytes 11075584 | tf_op jit(solution)/shard_map/pallas_call | solution.py:211
  45.6 0.0 collective-permute-done.2.args_4_
  45.6 0.0 collective-permute-done.3.args_5_
  45.6 0.9 copy-done.2
  46.5 0.3 copy-done.3
  46.8 14.0 %shard_map.51 = (f32[2,8,128,128]{3,2,1,0:T(8,128)}, bf16[1,10,256,128]{3,2,1,0:T(8,128)(2,1)}, bf16[1,10,256,128]{3,2,1,0:T(8,128)(2,1)}, bf16[1,10,224,128]{3,...) custom-call(bf16[2,8,128,80]{3,2,1,0:T(8,128)(2,1)} %bitcast.4, ...), custom_call_target="tpu_custom_call" | custom-call | flops 912261120 | bytes 8093696 | tf_op jit(solution)/shard_map/pallas_call | solution.py:211
  60.8 2.4 %collective-permute-start.4 = (bf16[1,10,224,128]{3,2,1,0:T(8,128)(2,1)}, bf16[1,10,224,128]{3,2,1,0:T(8,128)(2,1)S(1)}, u32[]{:S(2)}, u32[]{:S(2)}) collective-permute-start(bf16[1,10,224,128]{3,2,1,0:T(8,128)(2,1)} %get-tuple-element.23), channel_id=1, source_target_pairs={{0,1},{1,2},{2,3},{3,4},{4,5},{5,6},{6,7},{8,9},{9,10},{10,11},{11... | collective-permute-start | bytes 1720328 | tf_op jit(solution)/shard_map/ppermute | solution.py:52
  63.2 5.5 %collective-permute-start.5 = (bf16[1,10,224,128]{3,2,1,0:T(8,128)(2,1)}, bf16[1,10,224,128]{3,2,1,0:T(8,128)(2,1)S(1)}, u32[]{:S(2)}, u32[]{:S(2)}) collective-permute-start(bf16[1,10,224,128]{3,2,1,0:T(8,128)(2,1)} %get-tuple-element.24), channel_id=1, source_target_pairs={{1,0},{2,1},{3,2},{4,3},{5,4},{6,5},{7,6},{9,8},{10,9},{11,10},{12... | collective-permute-start | bytes 1720328 | tf_op jit(solution)/shard_map/ppermute | solution.py:53
  68.8 11.3 %shard_map.52 = (f32[2,8,128,128]{3,2,1,0:T(8,128)}, bf16[2,8,3,256,128]{4,3,2,1,0:T(8,128)(2,1)}) custom-call(bf16[2,8,128,80]{3,2,1,0:T(8,128)(2,1)} %bitcast.5, f32[9,128,128]{2,1,0:T(8,128)} %constant.2.clone.args_2_.rest_0_, bf16[2,10,80,128]{3,2,1,0:T(8,128)(2,1)} %get-tuple-element.16.rest_1_, bf16[1,10,256,128]{3,2,1,0:T(8,128)(2,1)} %get-tuple-element.17.rest_2_, ...), custom_call_target="tpu_custom_call" | custom-call | flops 1459617792 | bytes 13533184 | tf_op jit(solution)/shard_map/pallas_call | solution.py:211
  80.1 0.7 collective-permute-done.4.rest_4_
  80.7 1.5 %collective-permute-done.5.rest_5_ = bf16[1,10,224,128]{3,2,1,0:T(8,128)(2,1)S(1)} collective-permute-done((bf16[1,10,224,128]{3,2,1,0:T(8,128)(2,1)}, bf16[1,10,224,128]{3,2,1,0:T(8,128)(2,1)S(1)}, u32[]{:S(2)}, u32[]{:S(2)}) %collective-permute-start.5) | collective-permute-done | bytes 573472 | tf_op jit(solution)/shard_map/ppermute | solution.py:53
  82.3 0.8 copy-done.5
  83.1 7.7 %shard_map.53 = f32[2,8,128,128]{3,2,1,0:T(8,128)} custom-call(bf16[2,8,128,80]{3,2,1,0:T(8,128)(2,1)} %bitcast.6, f32[9,128,128]{2,1,0:T(8,128)} %constant.2.clone.args_2_.rest_0_, f32[2,8,128,128]{3,2,1,0:T(8,128)} %get-tuple-element.22.rest_1_, bf16[1,10,80,128]{3,2,1,0:T(8,128)(2,1)} %get-tuple-element.19.rest_4_.rest_2_, ...), custom_call_target="tpu_custom_call" | custom-call | flops 729808896 | bytes 7716864 | tf_op jit(solution)/shard_map/pallas_call | solution.py:211
  (11 shorter events, 0.1 us)
Async XLA Ops:
  0.6 1.5 %copy-start.1 = (bf16[2,8,80,128]{3,2,1,0:T(8,128)(2,1)S(1)}, bf16[2,8,80,128]{3,2,1,0:T(8,128)(2,1)}, u32[]{:S(2)}) copy-start(bf16[2,8,80,128]{3,2,1,0:T(8,128)(2,1)} %param.5) | copy-start | bytes 983044
  2.2 11.3 %collective-permute-start = (bf16[2,2,336,128]{3,2,1,0:T(8,128)(2,1)S(1)}, bf16[2,2,336,128]{3,2,1,0:T(8,128)(2,1)S(1)}, u32[]{:S(2)}, u32[]{:S(2)}) collective-permute-start(bf16[2,2,336,128]{3,2,1,0:T(8,128)(2,1)S(1)} %get-tuple-element.29), channel_id=1, source_target_pairs={{0,8},{8,16},{16,24},{24,32},{32,40},{40,48},{48,56},{56,64},{64,7... | collective-permute-start | bytes 1032200 | tf_op jit(solution)/shard_map/ppermute | solution.py:45
  2.3 11.2 %collective-permute-start.1 = (bf16[2,2,336,128]{3,2,1,0:T(8,128)(2,1)S(1)}, bf16[2,2,336,128]{3,2,1,0:T(8,128)(2,1)S(1)}, u32[]{:S(2)}, u32[]{:S(2)}) collective-permute-start(bf16[2,2,336,128]{3,2,1,0:T(8,128)(2,1)S(1)} %get-tuple-element.30), channel_id=1, source_target_pairs={{8,0},{16,8},{24,16},{32,24},{40,32},{48,40},{56,48},{64,56},{72,6... | collective-permute-start | bytes 1032200 | tf_op jit(solution)/shard_map/ppermute | solution.py:46
  13.5 5.7 %copy-start.6 = (bf16[2,2,336,128]{3,2,1,0:T(8,128)(2,1)}, bf16[2,2,336,128]{3,2,1,0:T(8,128)(2,1)S(1)}, u32[]{:S(2)}) copy-start(bf16[2,2,336,128]{3,2,1,0:T(8,128)(2,1)S(1)} %collective-permute-done.1) | copy-start | bytes 1032196
  13.7 1.7 %copy-start = (bf16[2,12,336,128]{3,2,1,0:T(8,128)(2,1)}, bf16[2,12,336,128]{3,2,1,0:T(8,128)(2,1)S(1)}, u32[]{:S(2)}) copy-start(bf16[2,12,336,128]{3,2,1,0:T(8,128)(2,1)S(1)} %pad_maximum_fusion.args_3_) | copy-start | bytes 6193156
  15.4 30.2 %collective-permute-start.2 = (bf16[1,12,304,128]{3,2,1,0:T(8,128)(2,1)}, bf16[1,12,304,128]{3,2,1,0:T(8,128)(2,1)S(1)}, u32[]{:S(2)}, u32[]{:S(2)}) collective-permute-start(bf16[1,12,304,128]{3,2,1,0:T(8,128)(2,1)} %pad_maximum_fusion.1), channel_id=1, source_target_pairs={{0,1},{1,2},{2,3},{3,4},{4,5},{5,6},{6,7},{8,9},{9,10},{10,11},{11... | collective-permute-start | bytes 2801672 | tf_op jit(solution)/shard_map/ppermute | solution.py:52
  19.3 26.3 %collective-permute-start.3 = (bf16[1,12,304,128]{3,2,1,0:T(8,128)(2,1)S(1)}, bf16[1,12,304,128]{3,2,1,0:T(8,128)(2,1)S(1)}, u32[]{:S(2)}, u32[]{:S(2)}) collective-permute-start(bf16[1,12,304,128]{3,2,1,0:T(8,128)(2,1)S(1)} %pad_maximum_fusion.2), channel_id=1, source_target_pairs={{1,0},{2,1},{3,2},{4,3},{5,4},{6,5},{7,6},{9,8},{10,9},{11,10},{12... | collective-permute-start | bytes 2801672 | tf_op jit(solution)/shard_map/ppermute | solution.py:53
  45.6 0.9 %copy-start.2 = (bf16[1,12,304,128]{3,2,1,0:T(8,128)(2,1)}, bf16[1,12,304,128]{3,2,1,0:T(8,128)(2,1)S(1)}, u32[]{:S(2)}) copy-start(bf16[1,12,304,128]{3,2,1,0:T(8,128)(2,1)S(1)} %collective-permute-done.2.args_4_) | copy-start | bytes 2801668
  45.6 1.2 %copy-start.3 = (bf16[1,12,304,128]{3,2,1,0:T(8,128)(2,1)}, bf16[1,12,304,128]{3,2,1,0:T(8,128)(2,1)S(1)}, u32[]{:S(2)}) copy-start(bf16[1,12,304,128]{3,2,1,0:T(8,128)(2,1)S(1)} %collective-permute-done.3.args_5_) | copy-start | bytes 2801668
  60.8 19.9 %collective-permute-start.4 = (bf16[1,10,224,128]{3,2,1,0:T(8,128)(2,1)}, bf16[1,10,224,128]{3,2,1,0:T(8,128)(2,1)S(1)}, u32[]{:S(2)}, u32[]{:S(2)}) collective-permute-start(bf16[1,10,224,128]{3,2,1,0:T(8,128)(2,1)} %get-tuple-element.23), channel_id=1, source_target_pairs={{0,1},{1,2},{2,3},{3,4},{4,5},{5,6},{6,7},{8,9},{9,10},{10,11},{11... | collective-permute-start | bytes 1720328 | tf_op jit(solution)/shard_map/ppermute | solution.py:52
  63.2 19.0 %collective-permute-start.5 = (bf16[1,10,224,128]{3,2,1,0:T(8,128)(2,1)}, bf16[1,10,224,128]{3,2,1,0:T(8,128)(2,1)S(1)}, u32[]{:S(2)}, u32[]{:S(2)}) collective-permute-start(bf16[1,10,224,128]{3,2,1,0:T(8,128)(2,1)} %get-tuple-element.24), channel_id=1, source_target_pairs={{1,0},{2,1},{3,2},{4,3},{5,4},{6,5},{7,6},{9,8},{10,9},{11,10},{12... | collective-permute-start | bytes 1720328 | tf_op jit(solution)/shard_map/ppermute | solution.py:53
  80.7 1.5 %copy-start.4 = (bf16[1,10,224,128]{3,2,1,0:T(8,128)(2,1)}, bf16[1,10,224,128]{3,2,1,0:T(8,128)(2,1)S(1)}, u32[]{:S(2)}) copy-start(bf16[1,10,224,128]{3,2,1,0:T(8,128)(2,1)S(1)} %collective-permute-done.4.rest_4_) | copy-start | bytes 1720324
  82.3 0.8 copy-start.5

commit v17 on v16

--- a/solution.py
+++ b/solution.py
@@ -292,7 +292,7 @@
         tiles="save",
     )
     emit = tuple(0 if p == 0 else 1 for p in range(lat_blocks))
-    first_product, first_row, last_row, sent_north, sent_south, members_north, members_south = rows_call(
+    first_product, first_row, last_row, sent_north, sent_south = rows_call(
         halo_plan(lat_blocks, (0, 1), (0, 1), (0, 0), trimmed=True),
         K,
         targets,
@@ -303,7 +303,6 @@
         target_off=-1,
         emit=emit,
         edges=edges,
-        copies=((0,) + span, (1,) + span),
     )
     north2, south2 = lat_halo(sent_north, sent_south)
     row_fields = (1, 2) if lat_blocks == 2 else None
@@ -313,18 +312,18 @@
         targets,
         taper,
         None,
-        (members, first_row, last_row, members_north, members_south, own_tiles),
+        (members, first_row, last_row, north, south, own_tiles),
         panel,
         tiles="load",
-        extra=halo_plan(lat_blocks, (3, 4), (3, 4), (0, 0)),
+        extra=halo_plan(lat_blocks, (3, 4), (3, 4), (1, 0)),
     )
     second_product = rows_call(
-        halo_plan(lat_blocks, (0, 1), (2, 3), (0, 0), trimmed=True),
+        halo_plan(lat_blocks, (0, 1), (0, 1), (0, 0), trimmed=True),
         0,
         targets,
         taper,
         partial,
-        (members_north, members_south, north2, south2, halo_tiles),
+        (north2, south2, halo_tiles),
         panel,
         tiles="load",
     )

time: 91.7 us -> 91.3 us (level)
  transfers between devices with their start and end apart: 6 -> 6, of which waited for: 3 -> 3; matrix products, arithmetic and copies ran while one was open for 3% -> 3% of each run, Pallas kernels for 34% -> 35%
where the time goes in v17:
time: 91.3 us; the launch traced here: 90.4 us
  Pallas kernels  52.7 us (58%)
  starting transfers between devices  21.3 us (23%)
  waiting for transfers between devices  7.61 us (8%)
  local copies, waits for them, and re-layouts  5.04 us (6%)
  other arithmetic  3.01 us (3%)
    pallas_call x4, Pallas kernels, rows_call(): pl.pallas_call(functools.partial(kernel_with_edges if edges is not None e...  52.7 us
    ppermute x2, starting transfers between devices, lat_halo(): lax.ppermute(first_row, 'lat', [(i + 1, i) for i in range(nlat - 1)])  9.62 us
    ppermute x2, starting transfers between devices, lat_halo(): north = lax.ppermute(last_row, 'lat', [(i, i + 1) for i in range(nlat - 1)])  6.26 us
    ppermute x1, waiting for transfers between devices, lon_halo(): lax.ppermute(cells[:, -depth:], 'lon', [(i, (i + 1) % nlon) for i in rang...  5.85 us
    ppermute x1, starting transfers between devices, lon_halo(): lax.ppermute(cells[:, :depth], 'lon', [((i + 1) % nlon, i) for i in range...  5.35 us
    unnamed x15, local copies, waits for them, and re-layouts  3.36 us
  transfers between devices with their start and end apart: 6, of which 3 were waited for; matrix products, arithmetic and copies ran while one was open for 3% of the time, Pallas kernels for 35%

profile of v17, /device:TPU:2, one launch (start us, length us, event | category | flops | bytes accessed | tf_op | source)
XLA Modules:
  0.0 90.4 jit_solution(13585040977075599446)
XLA Ops:
  0.6 0.0 copy-start.3
  0.6 1.5 %reduce-precision_convert_fusion = (bf16[2,8,128,128]{3,2,1,0:T(8,128)(2,1)S(1)}, bf16[2,8,128,128]{3,2,1,0:T(8,128)(2,1)S(1)}) fusion(f32[2,8,128,128]{3,2,1,0:T(8,128)} %param.6), kind=kLoop, calls=%fused_computation.2 | loop fusion | flops 1048576 | bytes 2097152 | tf_op jit(solution)/shard_map/convert_element_type | solution.py:233
  2.2 0.0 copy-done.3
  2.2 0.1 collective-permute-start
  2.3 5.3 %collective-permute-start.1 = (bf16[2,2,336,128]{3,2,1,0:T(8,128)(2,1)S(1)}, bf16[2,2,336,128]{3,2,1,0:T(8,128)(2,1)S(1)}, u32[]{:S(2)}, u32[]{:S(2)}) collective-permute-start(bf16[2,2,336,128]{3,2,1,0:T(8,128)(2,1)S(1)} %get-tuple-element.26), channel_id=1, source_target_pairs={{8,0},{16,8},{24,16},{32,24},{40,32},{48,40},{56,48},{64,56},{72,6... | collective-permute-start | bytes 1032200 | tf_op jit(solution)/shard_map/ppermute | solution.py:46
  7.7 5.8 %collective-permute-done = bf16[2,2,336,128]{3,2,1,0:T(8,128)(2,1)S(1)} collective-permute-done((bf16[2,2,336,128]{3,2,1,0:T(8,128)(2,1)S(1)}, bf16[2,2,336,128]{3,2,1,0:T(8,128)(2,1)S(1)}, u32[]{:S(2)}, u32[]{:S(2)}) %collective-permute-start) | collective-permute-done | bytes 344096 | tf_op jit(solution)/shard_map/ppermute | solution.py:45
  13.5 0.0 collective-permute-done.1
  13.5 0.2 pad_maximum_fusion.args_3_
  13.7 0.0 copy-start
  13.8 0.1 fusion.1
  13.9 1.2 %pad_maximum_fusion.1 = bf16[1,12,304,128]{3,2,1,0:T(8,128)(2,1)} fusion(bf16[1,12,112,128]{3,2,1,0:T(8,128)(2,1)S(1)} %get-tuple-element.23, bf16[1,12,112,128]{3,2,1,0:T(8,128)(2,1)S(1)} %get-tuple-element.24, bf16[1,12,80,128]{3,2,1,0:T(8,128)(2,1)S(1)} %slice.40), kind=kLoop, calls=%fused_computation.4 | loop fusion | flops 2801664 | bytes 1867776 | tf_op jit(solution)/shard_map/concatenate | solution.py:272
  15.1 0.3 copy-done
  15.4 3.8 %collective-permute-start.2 = (bf16[1,12,304,128]{3,2,1,0:T(8,128)(2,1)}, bf16[1,12,304,128]{3,2,1,0:T(8,128)(2,1)S(1)}, u32[]{:S(2)}, u32[]{:S(2)}) collective-permute-start(bf16[1,12,304,128]{3,2,1,0:T(8,128)(2,1)} %pad_maximum_fusion.1), channel_id=1, source_target_pairs={{0,1},{1,2},{2,3},{3,4},{4,5},{5,6},{6,7},{8,9},{9,10},{10,11},{11... | collective-permute-start | bytes 2801672 | tf_op jit(solution)/shard_map/ppermute | solution.py:52
  19.2 0.1 pad_maximum_fusion.2
  19.3 4.1 %collective-permute-start.3 = (bf16[1,12,304,128]{3,2,1,0:T(8,128)(2,1)S(1)}, bf16[1,12,304,128]{3,2,1,0:T(8,128)(2,1)S(1)}, u32[]{:S(2)}, u32[]{:S(2)}) collective-permute-start(bf16[1,12,304,128]{3,2,1,0:T(8,128)(2,1)S(1)} %pad_maximum_fusion.2), channel_id=1, source_target_pairs={{1,0},{2,1},{3,2},{4,3},{5,4},{6,5},{7,6},{9,8},{10,9},{11,10},{12... | collective-permute-start | bytes 2801672 | tf_op jit(solution)/shard_map/ppermute | solution.py:53
  23.4 1.0 %copy.5 = bf16[2,8,80,128]{2,3,1,0:T(8,128)(2,1)} copy(bf16[2,8,80,128]{3,2,1,0:T(8,128)(2,1)S(1)} %copy-done.3) | data formatting | bytes 655360 | tf_op args[0]
  24.4 0.8 slice.39
  25.2 0.8 copy.7.args_1_
  26.0 19.6 %shard_map.50 = (f32[2,10,128,128]{3,2,1,0:T(8,128)}, bf16[2,10,80,128]{3,2,1,0:T(8,128)(2,1)}, bf16[2,8,6,256,128]{4,3,2,1,0:T(8,128)(2,1)}) custom-call(bf16[2,8,128,80]{3,2,1,0:T(8,128)(2,1)} %bitcast.3, bf16[2,2,128,80]{3,2,1,0:T(8,128)(2,1)} %copy.7.args_1_, f32[9,128,128]{2,1,0:T(8,128)} %constant.2.clone.args_2_.rest_0_, bf16[2,12,336,128]{3,2,1,0:T(8,128)(2,1)} %copy-done), custom_call_target="tpu_custom_call" | custom-call | flops 1824522240 | bytes 11075584 | tf_op jit(solution)/shard_map/pallas_call | solution.py:211
  45.6 0.0 collective-permute-done.2.args_4_.rest_4_
  45.6 0.0 collective-permute-done.3.args_5_.rest_5_
  45.6 0.9 copy-done.1
  46.5 0.3 copy-done.2
  46.8 13.8 %shard_map.51 = (f32[2,8,128,128]{3,2,1,0:T(8,128)}, bf16[1,10,256,128]{3,2,1,0:T(8,128)(2,1)}, bf16[1,10,256,128]{3,2,1,0:T(8,128)(2,1)}, bf16[1,10,224,128]{3,2,1,0:T(8,128)(2,1)}, bf16[1,10,224,128]{3,2,1,0:T(8,128)(2,1)}) custom-call(bf16[2,8,128,80]{3,2,1,0:T(8,128)(2,1)} %bitcast.4, bf16[2,2,128,80]{3,2,1,0:T(8,128)(2,1)} %copy.7.args_1_, ...), custom_call_target="tpu_custom_call" | custom-call | flops 912261120 | bytes 7684096 | tf_op jit(solution)/shard_map/pallas_call | solution.py:211
  60.6 2.4 %collective-permute-start.4 = (bf16[1,10,224,128]{3,2,1,0:T(8,128)(2,1)}, bf16[1,10,224,128]{3,2,1,0:T(8,128)(2,1)S(1)}, u32[]{:S(2)}, u32[]{:S(2)}) collective-permute-start(bf16[1,10,224,128]{3,2,1,0:T(8,128)(2,1)} %get-tuple-element.19), channel_id=1, source_target_pairs={{0,1},{1,2},{2,3},{3,4},{4,5},{5,6},{6,7},{8,9},{9,10},{10,11},{11... | collective-permute-start | bytes 1720328 | tf_op jit(solution)/shard_map/ppermute | solution.py:52
  63.0 5.5 %collective-permute-start.5 = (bf16[1,10,224,128]{3,2,1,0:T(8,128)(2,1)}, bf16[1,10,224,128]{3,2,1,0:T(8,128)(2,1)S(1)}, u32[]{:S(2)}, u32[]{:S(2)}) collective-permute-start(bf16[1,10,224,128]{3,2,1,0:T(8,128)(2,1)} %get-tuple-element.20), channel_id=1, source_target_pairs={{1,0},{2,1},{3,2},{4,3},{5,4},{6,5},{7,6},{9,8},{10,9},{11,10},{12... | collective-permute-start | bytes 1720328 | tf_op jit(solution)/shard_map/ppermute | solution.py:53
  68.5 11.8 %shard_map.52 = (f32[2,8,128,128]{3,2,1,0:T(8,128)}, bf16[2,8,3,256,128]{4,3,2,1,0:T(8,128)(2,1)}) custom-call(bf16[2,8,128,80]{3,2,1,0:T(8,128)(2,1)} %bitcast.5, f32[9,128,128]{2,1,0:T(8,128)} %constant.2.clone.args_2_.rest_0_, bf16[2,10,80,128]{3,2,1,0:T(8,128)(2,1)} %get-tuple-element.14.rest_1_, bf16[1,10,256,128]{3,2,1,0:T(8,128)(2,1)} %get-tuple-element.15.rest_2_, ...), custom_call_target="tpu_custom_call" | custom-call | flops 1459617792 | bytes 14991360 | tf_op jit(solution)/shard_map/pallas_call | solution.py:211
  80.3 0.2 collective-permute-done.4.rest_2_
  80.5 1.5 %collective-permute-done.5.rest_3_ = bf16[1,10,224,128]{3,2,1,0:T(8,128)(2,1)S(1)} collective-permute-done((bf16[1,10,224,128]{3,2,1,0:T(8,128)(2,1)}, bf16[1,10,224,128]{3,2,1,0:T(8,128)(2,1)S(1)}, u32[]{:S(2)}, u32[]{:S(2)}) %collective-permute-start.5) | collective-permute-done | bytes 573472 | tf_op jit(solution)/shard_map/ppermute | solution.py:53
  82.0 0.0 copy-done.4
  82.0 0.8 copy-done.5
  82.9 7.6 %shard_map.53 = f32[2,8,128,128]{3,2,1,0:T(8,128)} custom-call(bf16[2,8,128,80]{3,2,1,0:T(8,128)(2,1)} %bitcast.6, f32[9,128,128]{2,1,0:T(8,128)} %constant.2.clone.args_2_.rest_0_, f32[2,8,128,128]{3,2,1,0:T(8,128)} %get-tuple-element.18.rest_1_, bf16[1,10,224,128]{3,2,1,0:T(8,128)(2,1)} %copy-done.4, bf16[1,10,224,128]{3,2,1,0:T(8,128)(2,1)} %copy-done.5, ...), custom_call_target="tpu_custom_call" | custom-call | flops 729808896 | bytes 7307264 | tf_op jit(solution)/shard_map/pallas_call | solution.py:211
  (11 shorter events, 0.1 us)
Async XLA Ops:
  0.6 1.5 %copy-start.3 = (bf16[2,8,80,128]{3,2,1,0:T(8,128)(2,1)S(1)}, bf16[2,8,80,128]{3,2,1,0:T(8,128)(2,1)}, u32[]{:S(2)}) copy-start(bf16[2,8,80,128]{3,2,1,0:T(8,128)(2,1)} %param.5) | copy-start | bytes 983044
  2.2 11.3 %collective-permute-start = (bf16[2,2,336,128]{3,2,1,0:T(8,128)(2,1)S(1)}, bf16[2,2,336,128]{3,2,1,0:T(8,128)(2,1)S(1)}, u32[]{:S(2)}, u32[]{:S(2)}) collective-permute-start(bf16[2,2,336,128]{3,2,1,0:T(8,128)(2,1)S(1)} %get-tuple-element.25), channel_id=1, source_target_pairs={{0,8},{8,16},{16,24},{24,32},{32,40},{40,48},{48,56},{56,64},{64,7... | collective-permute-start | bytes 1032200 | tf_op jit(solution)/shard_map/ppermute | solution.py:45
  2.3 11.2 %collective-permute-start.1 = (bf16[2,2,336,128]{3,2,1,0:T(8,128)(2,1)S(1)}, bf16[2,2,336,128]{3,2,1,0:T(8,128)(2,1)S(1)}, u32[]{:S(2)}, u32[]{:S(2)}) collective-permute-start(bf16[2,2,336,128]{3,2,1,0:T(8,128)(2,1)S(1)} %get-tuple-element.26), channel_id=1, source_target_pairs={{8,0},{16,8},{24,16},{32,24},{40,32},{48,40},{56,48},{64,56},{72,6... | collective-permute-start | bytes 1032200 | tf_op jit(solution)/shard_map/ppermute | solution.py:46
  13.5 5.7 %copy-start.6 = (bf16[2,2,336,128]{3,2,1,0:T(8,128)(2,1)}, bf16[2,2,336,128]{3,2,1,0:T(8,128)(2,1)S(1)}, u32[]{:S(2)}) copy-start(bf16[2,2,336,128]{3,2,1,0:T(8,128)(2,1)S(1)} %collective-permute-done.1) | copy-start | bytes 1032196
  13.7 1.7 %copy-start = (bf16[2,12,336,128]{3,2,1,0:T(8,128)(2,1)}, bf16[2,12,336,128]{3,2,1,0:T(8,128)(2,1)S(1)}, u32[]{:S(2)}) copy-start(bf16[2,12,336,128]{3,2,1,0:T(8,128)(2,1)S(1)} %pad_maximum_fusion.args_3_) | copy-start | bytes 6193156
  15.4 30.2 %collective-permute-start.2 = (bf16[1,12,304,128]{3,2,1,0:T(8,128)(2,1)}, bf16[1,12,304,128]{3,2,1,0:T(8,128)(2,1)S(1)}, u32[]{:S(2)}, u32[]{:S(2)}) collective-permute-start(bf16[1,12,304,128]{3,2,1,0:T(8,128)(2,1)} %pad_maximum_fusion.1), channel_id=1, source_target_pairs={{0,1},{1,2},{2,3},{3,4},{4,5},{5,6},{6,7},{8,9},{9,10},{10,11},{11... | collective-permute-start | bytes 2801672 | tf_op jit(solution)/shard_map/ppermute | solution.py:52
  19.3 26.3 %collective-permute-start.3 = (bf16[1,12,304,128]{3,2,1,0:T(8,128)(2,1)S(1)}, bf16[1,12,304,128]{3,2,1,0:T(8,128)(2,1)S(1)}, u32[]{:S(2)}, u32[]{:S(2)}) collective-permute-start(bf16[1,12,304,128]{3,2,1,0:T(8,128)(2,1)S(1)} %pad_maximum_fusion.2), channel_id=1, source_target_pairs={{1,0},{2,1},{3,2},{4,3},{5,4},{6,5},{7,6},{9,8},{10,9},{11,10},{12... | collective-permute-start | bytes 2801672 | tf_op jit(solution)/shard_map/ppermute | solution.py:53
  45.6 0.9 %copy-start.1 = (bf16[1,12,304,128]{3,2,1,0:T(8,128)(2,1)}, bf16[1,12,304,128]{3,2,1,0:T(8,128)(2,1)S(1)}, u32[]{:S(2)}) copy-start(bf16[1,12,304,128]{3,2,1,0:T(8,128)(2,1)S(1)} %collective-permute-done.2.args_4_.rest_4_) | copy-start | bytes 2801668
  45.6 1.2 %copy-start.2 = (bf16[1,12,304,128]{3,2,1,0:T(8,128)(2,1)}, bf16[1,12,304,128]{3,2,1,0:T(8,128)(2,1)S(1)}, u32[]{:S(2)}) copy-start(bf16[1,12,304,128]{3,2,1,0:T(8,128)(2,1)S(1)} %collective-permute-done.3.args_5_.rest_5_) | copy-start | bytes 2801668
  60.6 19.9 %collective-permute-start.4 = (bf16[1,10,224,128]{3,2,1,0:T(8,128)(2,1)}, bf16[1,10,224,128]{3,2,1,0:T(8,128)(2,1)S(1)}, u32[]{:S(2)}, u32[]{:S(2)}) collective-permute-start(bf16[1,10,224,128]{3,2,1,0:T(8,128)(2,1)} %get-tuple-element.19), channel_id=1, source_target_pairs={{0,1},{1,2},{2,3},{3,4},{4,5},{5,6},{6,7},{8,9},{9,10},{10,11},{11... | collective-permute-start | bytes 1720328 | tf_op jit(solution)/shard_map/ppermute | solution.py:52
  63.0 19.0 %collective-permute-start.5 = (bf16[1,10,224,128]{3,2,1,0:T(8,128)(2,1)}, bf16[1,10,224,128]{3,2,1,0:T(8,128)(2,1)S(1)}, u32[]{:S(2)}, u32[]{:S(2)}) collective-permute-start(bf16[1,10,224,128]{3,2,1,0:T(8,128)(2,1)} %get-tuple-element.20), channel_id=1, source_target_pairs={{1,0},{2,1},{3,2},{4,3},{5,4},{6,5},{7,6},{9,8},{10,9},{11,10},{12... | collective-permute-start | bytes 1720328 | tf_op jit(solution)/shard_map/ppermute | solution.py:53
  80.5 1.5 %copy-start.4 = (bf16[1,10,224,128]{3,2,1,0:T(8,128)(2,1)}, bf16[1,10,224,128]{3,2,1,0:T(8,128)(2,1)S(1)}, u32[]{:S(2)}) copy-start(bf16[1,10,224,128]{3,2,1,0:T(8,128)(2,1)S(1)} %collective-permute-done.4.rest_2_) | copy-start | bytes 1720324
  82.0 0.8 copy-start.5
